TPU v7x, 128 devices: a whole 4x4x4 slice. The times are simulated.
128 devices in a mesh: gx: 8 (over y, core), gy: 16 (over x, z).
Axes of the slice: x: 4, y: 4, z: 4, core: 2. Of those that a mesh axis runs over, the one named last changes fastest.
Arguments:
- bricks: bfloat16 [32768, 1536], P(('gx', 'gy')), may hold values from -6 to 6
- brick_target: int32 [32768, 1], P(('gx', 'gy')), may hold values from 0 to 127; in each aligned block of 256 rows (0 to 255, 256 to 511, ...) at most 6 rows name the same one
- brick_slot: int32 [32768], P(('gx', 'gy')), may hold values from 0 to 511
- screen: float32 [256, 1024, 128], P('gx', 'gy'), may hold values from 0.05 to 2
- coarse_guess: float32 [256, 1024, 128], P('gx', 'gy'), may hold values from -18 to 18
Outputs:
- solution_field: float32 [256, 1024, 128], P('gx', 'gy')
- residual: float32 [256, 1024, 128], P('gx', 'gy')
Inputs may be any that keep to these rules, and one draw needn't show every extreme that they name: `brick_target`: among the 256 bricks of one device, no target is named more than 6 times, a bound that some block reaches.
All inputs are finite; a program needn't handle non-finite values.
Results may differ from a plain program's by a relative error of at most 0.0003.
Values may be sent and summed in bfloat16 or wider, within the bound.
No kernel may reach another device: no remote copies, remote signals or barrier semaphores. Data moves between devices by JAX's collectives and lax.ppermute only.
A program may use at most 128 MiB of HBM per device.

v0:
```python
import jax
import jax.numpy as jnp
from jax import lax
from jax.sharding import Mesh
from jax.sharding import PartitionSpec as P

ITERS = 2
GX_GY = ("gx_0", "gx_1", "gy_0", "gy_1")
GX = ("gx_0", "gx_1")
GY = ("gy_0", "gy_1")


def extended(shard, sides, width):
    edges = {}
    for axis, dim in sides:
        count, length = (lax.axis_size(axis), shard.shape[dim])
        up = [(i, (i + 1) % count) for i in range(count - 1)]
        last = lax.slice_in_dim(shard, length - width, length, axis=dim)
        first = lax.slice_in_dim(shard, 0, width, axis=dim)
        edges[dim] = (
            lax.ppermute(last, axis, up),
            lax.ppermute(first, axis, [(b, a) for a, b in up]),
        )
    done = []
    for _, dim in sides:
        low, high = edges[dim]
        around = [(width, width) if d in done else (0, 0) for d in range(shard.ndim)]
        shard = jnp.concatenate([jnp.pad(low, around), shard, jnp.pad(high, around)], axis=dim)
        done.append(dim)
    return shard


def over_axes(shard, axes):
    for axis in axes:
        shard = lax.psum(shard, axis)
    return shard


def with_halo(block, sides, width):
    for axis, dim in sides:
        count = lax.axis_size(axis)
        forward = [(i, i + 1) for i in range(count - 1)]
        backward = [(target, source) for source, target in forward]
        low = lax.ppermute(
            lax.slice_in_dim(block, block.shape[dim] - width, None, axis=dim), axis, forward
        )
        high = lax.ppermute(lax.slice_in_dim(block, 0, width, axis=dim), axis, backward)
        block = jnp.concatenate([low, block, high], axis=dim)
    return block


def build_send(bricks, brick_target, brick_slot, peers, capacity):
    target = brick_target[:, 0]
    onehot = (target[:, None] == jnp.arange(peers, dtype=jnp.int32)[None, :]).astype(jnp.int32)
    earlier = jnp.cumsum(onehot, axis=0) - onehot
    order = jnp.sum(earlier * onehot, axis=1)
    place = target * capacity + order
    payload = jnp.zeros((peers * capacity, bricks.shape[1]), bricks.dtype).at[place].set(bricks)
    slots = jnp.zeros((peers * capacity,), jnp.int32).at[place].set(brick_slot)
    return (payload, slots)


def next_along_z(field):
    edge = jnp.zeros(field.shape[:-1] + (1,), field.dtype)
    return jnp.concatenate([field[..., 1:], edge], axis=-1)


def prior_along_z(field):
    edge = jnp.zeros(field.shape[:-1] + (1,), field.dtype)
    return jnp.concatenate([edge, field[..., :-1]], axis=-1)


def operate(field, screen):
    padded = extended(field, ((GX, 0), (GY, 1)), 1)
    beside = padded[2:, 1:-1] + padded[:-2, 1:-1]
    beside = beside + padded[1:-1, 2:] + padded[1:-1, :-2]
    beside = beside + next_along_z(field) + prior_along_z(field)
    return (6.0 + screen) * field - beside


def paired_total(first, second):
    return (over_axes(first, GX_GY), over_axes(second, GX_GY))


def component_grid(blocks, comp, span_x, span_y, span_z):
    part_blocks = blocks[:, comp, :].reshape(span_x, span_y, span_z, 8, 8, 8)
    grid = part_blocks.transpose(0, 3, 1, 4, 2, 5)
    return grid.reshape(span_x * 8, span_y * 8, span_z * 8)


def body(bricks, brick_target, brick_slot, screen, coarse_guess):
    peers = lax.axis_size(GX_GY)
    capacity = max(2, 3 * bricks.shape[0] // peers)
    payload, slots = build_send(bricks, brick_target, brick_slot, peers, capacity)
    arrived, landed = (
        lax.all_to_all(
            payload.reshape(peers, capacity, 1536), GX_GY, split_axis=0, concat_axis=0, tiled=True
        ),
        lax.all_to_all(
            slots.reshape(peers, capacity), GX_GY, split_axis=0, concat_axis=0, tiled=True
        ),
    )
    width_x, width_y, depth = screen.shape
    span_x = width_x // 8
    span_y = width_y // 8
    span_z = depth // 8
    blocks = jnp.zeros((span_x * span_y * span_z, 1536), jnp.float32)
    blocks = blocks.at[landed.reshape(-1)].add(arrived.reshape(-1, 1536).astype(jnp.float32))
    blocks = blocks.reshape(span_x * span_y * span_z, 3, 512)
    normal_x = component_grid(blocks, 0, span_x, span_y, span_z)
    normal_y = component_grid(blocks, 1, span_x, span_y, span_z)
    normal_z = component_grid(blocks, 2, span_x, span_y, span_z)
    along_x = with_halo(normal_x, ((GX, 0),), 1)
    along_y = with_halo(normal_y, ((GY, 1),), 1)
    total = along_x[2:] - along_x[:-2]
    total = total + (along_y[:, 2:] - along_y[:, :-2])
    total = total + (next_along_z(normal_z) - prior_along_z(normal_z))
    source = -0.5 * total
    inverse = 1.0 / (6.0 + screen)
    solution = coarse_guess
    residual = source - operate(solution, screen)
    precond = residual * inverse
    image = operate(precond, screen)
    gamma, delta = paired_total(jnp.sum(residual * precond), jnp.sum(image * precond))
    alpha = gamma / delta
    direction = precond
    along = image
    for step in range(ITERS):
        solution = solution + alpha * direction
        residual = residual - alpha * along
        if step + 1 < ITERS:
            precond = residual * inverse
            image = operate(precond, screen)
            gamma_next, delta = paired_total(jnp.sum(residual * precond), jnp.sum(image * precond))
            ratio = gamma_next / gamma
            alpha = gamma_next / (delta - ratio * gamma_next / alpha)
            direction = precond + ratio * direction
            along = image + ratio * along
            gamma = gamma_next
    return (solution, residual)


def solution(mesh):
    split = Mesh(mesh.devices.reshape(4, 2, 4, 4), ("gx_0", "gx_1", "gy_0", "gy_1"))
    placed = (P(GX_GY, None), P(GX_GY, None), P(GX_GY), P(GX, GY, None), P(GX, GY, None))
    return jax.shard_map(
        body,
        mesh=split,
        in_specs=placed,
        out_specs=(P(GX, GY, None), P(GX, GY, None)),
        check_vma=False,
    )
```

profile of v0, /device:TPU:0, one launch (start us, length us, event | category | flops | bytes accessed | tf_op | source)
XLA Modules:
  0.0 315.9 jit_solution(11609887403149342128)
XLA Ops:
  5.6 11.2 %all-to-all-start = ((s32[128,1,6]{2,1,0:T(1,128)}), s32[128,1,6]{2,1,0:T(1,128)S(1)}, u32[]{:S(2)}, u32[]{:S(2)}) async-start(s32[128,1,6]{2,1,0:T(1,128)} %bitcast.7), calls=%async_computation | async-start | bytes 131072 | tf_op jit(solution)/shard_map/all_to_all | solution.py:99
  26.2 6.5 %all-to-all-start.1 = ((bf16[128,6,1536]{2,1,0:T(8,128)(2,1)}), bf16[128,6,1536]{2,1,0:T(8,128)(2,1)}, u32[]{:S(2)}, u32[]{:S(2)}) async-start(bf16[128,6,1536]{2,1,0:T(8,128)(2,1)} %reshape.77), calls=%async_computation.1 | async-start | bytes 6291456 | tf_op jit(solution)/shard_map/all_to_all | solution.py:96
  36.7 4.7 %collective-permute-start.7 = (f32[32,1,128]{2,1,0:T(1,128)S(1)}, f32[32,1,128]{2,1,0:T(1,128)S(1)}, u32[]{:S(2)}, u32[]{:S(2)}) collective-permute-start(f32[32,1,128]{2,1,0:T(1,128)S(1)} %get-tuple-element.48), channel_id=1, source_target_pairs={{0,1},{1,2},{2,3},{3,4},{4,5},{5,6},{6,7},{7,8},{8,9},{9,10},{10,1... | collective-permute-start | bytes 49160 | tf_op jit(solution)/shard_map/ppermute | solution.py:21
  46.8 26.3 %all-to-all-done.1 = bf16[128,6,1536]{2,1,0:T(8,128)(2,1)} async-done(((bf16[128,6,1536]{2,1,0:T(8,128)(2,1)}), bf16[128,6,1536]{2,1,0:T(8,128)(2,1)}, u32[]{:S(2)}, u32[]{:S(2)}) %all-to-all-start.1) | async-done | bytes 2359328 | tf_op jit(solution)/shard_map/all_to_all | solution.py:96
  73.0 5.3 %reshape.103 = f32[768,1536]{1,0:T(8,128)} reshape(bf16[128,6,1536]{2,1,0:T(8,128)(2,1)} %all-to-all-done.1) | data formatting | bytes 7077888 | tf_op jit(solution)/shard_map/convert_element_type | solution.py:108
  78.3 13.5 %scatter_custom_fusion.2 = f32[512,1536]{1,0:T(8,128)} fusion(s32[768]{0:T(1024)S(1)} %fusion.39, f32[768,1536]{1,0:T(8,128)} %reshape.103, f32[]{:T(128)} %constant.9.clone.1), kind=kCustom, calls=%fused_computation.3 | custom fusion | flops 1179648 | bytes 3146240 | tf_op jit(solution)/shard_map/scatter-add | solution.py:108
  98.6 4.9 %reshape_squeeze.9 = f32[4,8,16,8,8,8]{2,1,0,5,4,3:T(8,128)} reshape(f32[512,1,512]{0,2,1:T(8,128)S(1)} %get-tuple-element.26) | data formatting | bytes 2097152 | tf_op jit(solution)/shard_map/reshape;squeeze | solution.py:86
  103.5 12.4 %copy.23 = f32[4,8,8,8,16,8]{5,4,3,2,1,0:T(8,128)} copy(f32[4,8,8,8,16,8]{4,2,0,5,3,1:T(8,128)} %bitcast.34) | data formatting | bytes 2097152 | tf_op jit(solution)/shard_map/transpose | solution.py:87
  115.9 11.8 %reshape.79 = f32[32,64,128]{2,1,0:T(8,128)S(1)} reshape(f32[4,8,8,8,16,8]{5,4,3,2,1,0:T(8,128)} %copy.23) | data formatting | bytes 2097152 | tf_op jit(solution)/shard_map/reshape | solution.py:88
  132.2 4.9 %reshape_squeeze.10 = f32[4,8,16,8,8,8]{2,1,0,5,4,3:T(8,128)} reshape(f32[512,1,512]{0,2,1:T(8,128)S(1)} %get-tuple-element.28) | data formatting | bytes 2097152 | tf_op jit(solution)/shard_map/reshape;squeeze | solution.py:86
  137.1 12.4 %copy.24 = f32[4,8,8,8,16,8]{5,4,3,2,1,0:T(8,128)} copy(f32[4,8,8,8,16,8]{4,2,0,5,3,1:T(8,128)} %bitcast.35) | data formatting | bytes 2097152 | tf_op jit(solution)/shard_map/transpose | solution.py:87
  149.4 11.8 %reshape.80 = f32[32,64,128]{2,1,0:T(8,128)S(1)} reshape(f32[4,8,8,8,16,8]{5,4,3,2,1,0:T(8,128)} %copy.24) | data formatting | bytes 2097152 | tf_op jit(solution)/shard_map/reshape | solution.py:88
  162.6 6.2 %reshape_squeeze.11 = f32[4,8,16,8,8,8]{2,1,0,5,4,3:T(8,128)} reshape(f32[512,1,512]{0,2,1:T(8,128)} %get-tuple-element.27) | data formatting | bytes 2097152 | tf_op jit(solution)/shard_map/reshape;squeeze | solution.py:86
  168.7 12.4 %copy.25 = f32[4,8,8,8,16,8]{5,4,3,2,1,0:T(8,128)} copy(f32[4,8,8,8,16,8]{4,2,0,5,3,1:T(8,128)} %bitcast.36) | data formatting | bytes 2097152 | tf_op jit(solution)/shard_map/transpose | solution.py:87
  181.1 11.8 %reshape.81 = f32[32,64,128]{2,1,0:T(8,128)S(1)} reshape(f32[4,8,8,8,16,8]{5,4,3,2,1,0:T(8,128)} %copy.25) | data formatting | bytes 2097152 | tf_op jit(solution)/shard_map/reshape | solution.py:88
  192.9 4.8 %collective-permute-start.3 = (f32[32,1,128]{2,1,0:T(1,128)S(1)}, f32[32,1,128]{2,1,0:T(1,128)S(1)}, u32[]{:S(2)}, u32[]{:S(2)}) collective-permute-start(f32[32,1,128]{2,1,0:T(1,128)S(1)} %get-tuple-element.44), channel_id=1, source_target_pairs={{0,1},{1,2},{2,3},{3,4},{4,5},{5,6},{6,7},{7,8},{8,9},{9,10},{10,1... | collective-permute-start | bytes 49160 | tf_op jit(solution)/shard_map/ppermute | solution.py:44
  208.6 4.8 %collective-permute-start.11 = (f32[32,1,128]{2,1,0:T(1,128)S(1)}, f32[32,1,128]{2,1,0:T(1,128)S(1)}, u32[]{:S(2)}, u32[]{:S(2)}) collective-permute-start(f32[32,1,128]{2,1,0:T(1,128)S(1)} %get-tuple-element.36), channel_id=1, source_target_pairs={{0,1},{1,2},{2,3},{3,4},{4,5},{5,6},{6,7},{7,8},{8,9},{9,10},{10,1... | collective-permute-start | bytes 49160 | tf_op jit(solution)/shard_map/ppermute | solution.py:21
  217.3 9.8 %all-reduce.19 = (f32[]{:T(128)}, f32[]{:T(128)}) all-reduce(f32[]{:T(128)} %get-tuple-element.5, f32[]{:T(128)} %get-tuple-element.4), channel_id=1, replica_groups=mesh['gx_0'=4,'gx_1'=2,'gy_0'=4,'gy_1'=4] {'gx_0'}, use_global_device_ids=true, to_apply=%region_7.8 | all-reduce | flops 2 | bytes 16 | tf_op jit(solution)/shard_map/psum | solution.py:35
  230.2 16.7 %all-reduce.17 = (f32[]{:T(128)}, f32[]{:T(128)}) all-reduce(f32[]{:T(128)} %get-tuple-element.20, f32[]{:T(128)} %get-tuple-element.21), channel_id=1, replica_groups=mesh['gx_0'=4,'gx_1'=2,'gy_0'=4,'gy_1'=4] {'gy_0'}, use_global_device_ids=true, to_apply=%region_9.10 | all-reduce | flops 2 | bytes 16 | tf_op jit(solution)/shard_map/psum | solution.py:35
  246.9 8.4 %all-reduce.15 = (f32[]{:T(128)}, f32[]{:T(128)}) all-reduce(f32[]{:T(128)} %get-tuple-element.12, f32[]{:T(128)} %get-tuple-element.13), channel_id=1, replica_groups=mesh['gx_0'=4,'gx_1'=2,'gy_0'=4,'gy_1'=4] {'gy_1'}, use_global_device_ids=true, to_apply=%region_10.11 | all-reduce | flops 2 | bytes 16 | tf_op jit(solution)/shard_map/psum | solution.py:35
  264.8 4.5 %collective-permute-start.15 = (f32[32,1,128]{2,1,0:T(1,128)S(1)}, f32[32,1,128]{2,1,0:T(1,128)S(1)}, u32[]{:S(2)}, u32[]{:S(2)}) collective-permute-start(f32[32,1,128]{2,1,0:T(1,128)S(1)} %get-tuple-element.30), channel_id=1, source_target_pairs={{0,1},{1,2},{2,3},{3,4},{4,5},{5,6},{6,7},{7,8},{8,9},{9,10},{10,1... | collective-permute-start | bytes 49160 | tf_op jit(solution)/shard_map/ppermute | solution.py:21
  273.3 8.4 %all-reduce.18 = (f32[]{:T(128)}, f32[]{:T(128)}) all-reduce(f32[]{:T(128)} %get-tuple-element.3, f32[]{:T(128)} %get-tuple-element.2), channel_id=1, replica_groups=mesh['gx_0'=4,'gx_1'=2,'gy_0'=4,'gy_1'=4] {'gx_0'}, use_global_device_ids=true, to_apply=%region_17.18 | all-reduce | flops 2 | bytes 16 | tf_op jit(solution)/shard_map/psum | solution.py:35
  284.9 14.3 %all-reduce.16 = (f32[]{:T(128)}, f32[]{:T(128)}) all-reduce(f32[]{:T(128)} %get-tuple-element.18, f32[]{:T(128)} %get-tuple-element.19), channel_id=1, replica_groups=mesh['gx_0'=4,'gx_1'=2,'gy_0'=4,'gy_1'=4] {'gy_0'}, use_global_device_ids=true, to_apply=%region_19.20 | all-reduce | flops 2 | bytes 16 | tf_op jit(solution)/shard_map/psum | solution.py:35
  299.1 8.4 %all-reduce.14 = (f32[]{:T(128)}, f32[]{:T(128)}) all-reduce(f32[]{:T(128)} %get-tuple-element.10, f32[]{:T(128)} %get-tuple-element.11), channel_id=1, replica_groups=mesh['gx_0'=4,'gx_1'=2,'gy_0'=4,'gy_1'=4] {'gy_1'}, use_global_device_ids=true, to_apply=%region_20.21 | all-reduce | flops 2 | bytes 16 | tf_op jit(solution)/shard_map/psum | solution.py:35
  (91 shorter events, 73.1 us)
Async XLA Ops:
  5.6 20.6 %all-to-all-start = ((s32[128,1,6]{2,1,0:T(1,128)}), s32[128,1,6]{2,1,0:T(1,128)S(1)}, u32[]{:S(2)}, u32[]{:S(2)}) async-start(s32[128,1,6]{2,1,0:T(1,128)} %bitcast.7), calls=%async_computation | async-start | bytes 131072 | tf_op jit(solution)/shard_map/all_to_all | solution.py:99
  22.5 10.2 %copy-start = (f32[32,64,128]{2,1,0:T(8,128)S(1)}, f32[32,64,128]{2,1,0:T(8,128)}, u32[]{:S(2)}) copy-start(f32[32,64,128]{2,1,0:T(8,128)} %param.9) | copy-start | bytes 3145732
  26.2 46.8 %all-to-all-start.1 = ((bf16[128,6,1536]{2,1,0:T(8,128)(2,1)}), bf16[128,6,1536]{2,1,0:T(8,128)(2,1)}, u32[]{:S(2)}, u32[]{:S(2)}) async-start(bf16[128,6,1536]{2,1,0:T(8,128)(2,1)} %reshape.77), calls=%async_computation.1 | async-start | bytes 6291456 | tf_op jit(solution)/shard_map/all_to_all | solution.py:96
  32.7 11.7 %collective-permute-start.5 = (f32[1,64,128]{2,1,0:T(8,128)S(1)}, f32[1,64,128]{2,1,0:T(8,128)S(1)}, u32[]{:S(2)}, u32[]{:S(2)}) collective-permute-start(f32[1,64,128]{2,1,0:T(8,128)S(1)} %get-tuple-element.50), channel_id=1, source_target_pairs={{0,16},{16,32},{32,48},{48,64},{64,80},{80,96},{96,112},{1,17},{17... | collective-permute-start | bytes 98312 | tf_op jit(solution)/shard_map/ppermute | solution.py:21
  34.0 12.1 %collective-permute-start.4 = (f32[1,64,128]{2,1,0:T(8,128)S(1)}, f32[1,64,128]{2,1,0:T(8,128)S(1)}, u32[]{:S(2)}, u32[]{:S(2)}) collective-permute-start(f32[1,64,128]{2,1,0:T(8,128)S(1)} %get-tuple-element.49), channel_id=1, source_target_pairs={{16,0},{32,16},{48,32},{64,48},{80,64},{96,80},{112,96},{17,1},{33... | collective-permute-start | bytes 98312 | tf_op jit(solution)/shard_map/ppermute | solution.py:22
  35.4 157.6 %collective-permute-start.6 = (f32[32,1,128]{2,1,0:T(1,128)S(1)}, f32[32,1,128]{2,1,0:T(1,128)S(1)}, u32[]{:S(2)}, u32[]{:S(2)}) collective-permute-start(f32[32,1,128]{2,1,0:T(1,128)S(1)} %get-tuple-element.47), channel_id=1, source_target_pairs={{1,0},{2,1},{3,2},{4,3},{5,4},{6,5},{7,6},{8,7},{9,8},{10,9},{11,1... | collective-permute-start | bytes 49160 | tf_op jit(solution)/shard_map/ppermute | solution.py:22
  36.7 161.4 %collective-permute-start.7 = (f32[32,1,128]{2,1,0:T(1,128)S(1)}, f32[32,1,128]{2,1,0:T(1,128)S(1)}, u32[]{:S(2)}, u32[]{:S(2)}) collective-permute-start(f32[32,1,128]{2,1,0:T(1,128)S(1)} %get-tuple-element.48), channel_id=1, source_target_pairs={{0,1},{1,2},{2,3},{3,4},{4,5},{5,6},{6,7},{7,8},{8,9},{9,10},{10,1... | collective-permute-start | bytes 49160 | tf_op jit(solution)/shard_map/ppermute | solution.py:21
  127.6 71.5 %collective-permute-start = (f32[1,64,128]{2,1,0:T(8,128)S(1)}, f32[1,64,128]{2,1,0:T(8,128)S(1)}, u32[]{:S(2)}, u32[]{:S(2)}) collective-permute-start(f32[1,64,128]{2,1,0:T(8,128)S(1)} %get-tuple-element.41), channel_id=1, source_target_pairs={{16,0},{32,16},{48,32},{64,48},{80,64},{96,80},{112,96},{17,1},{33... | collective-permute-start | bytes 98312 | tf_op jit(solution)/shard_map/ppermute | solution.py:47
  128.9 70.2 %collective-permute-start.1 = (f32[1,64,128]{2,1,0:T(8,128)S(1)}, f32[1,64,128]{2,1,0:T(8,128)S(1)}, u32[]{:S(2)}, u32[]{:S(2)}) collective-permute-start(f32[1,64,128]{2,1,0:T(8,128)S(1)} %get-tuple-element.42), channel_id=1, source_target_pairs={{0,16},{16,32},{32,48},{48,64},{64,80},{80,96},{96,112},{1,17},{17... | collective-permute-start | bytes 98312 | tf_op jit(solution)/shard_map/ppermute | solution.py:44
  161.2 7.5 %copy-start.6 = (f32[32,64,128]{2,1,0:T(8,128)}, f32[32,64,128]{2,1,0:T(8,128)S(1)}, u32[]{:S(2)}) copy-start(f32[32,64,128]{2,1,0:T(8,128)S(1)} %reshape.80) | copy-start | bytes 3145732
  161.3 36.9 %collective-permute-start.2 = (f32[32,1,128]{2,1,0:T(1,128)S(1)}, f32[32,1,128]{2,1,0:T(1,128)S(1)}, u32[]{:S(2)}, u32[]{:S(2)}) collective-permute-start(f32[32,1,128]{2,1,0:T(1,128)S(1)} %get-tuple-element.43), channel_id=1, source_target_pairs={{1,0},{2,1},{3,2},{4,3},{5,4},{6,5},{7,6},{8,7},{9,8},{10,9},{11,1... | collective-permute-start | bytes 49160 | tf_op jit(solution)/shard_map/ppermute | solution.py:47
  192.9 6.2 %collective-permute-start.3 = (f32[32,1,128]{2,1,0:T(1,128)S(1)}, f32[32,1,128]{2,1,0:T(1,128)S(1)}, u32[]{:S(2)}, u32[]{:S(2)}) collective-permute-start(f32[32,1,128]{2,1,0:T(1,128)S(1)} %get-tuple-element.44), channel_id=1, source_target_pairs={{0,1},{1,2},{2,3},{3,4},{4,5},{5,6},{6,7},{7,8},{8,9},{9,10},{10,1... | collective-permute-start | bytes 49160 | tf_op jit(solution)/shard_map/ppermute | solution.py:44
  202.9 14.4 %copy-start.1 = (f32[32,64,128]{2,1,0:T(8,128)}, f32[32,64,128]{2,1,0:T(8,128)S(1)}, u32[]{:S(2)}) copy-start(f32[32,64,128]{2,1,0:T(8,128)S(1)} %get-tuple-element.25) | copy-start | bytes 3145732
  202.9 11.9 %collective-permute-start.8 = (f32[1,64,128]{2,1,0:T(8,128)S(1)}, f32[1,64,128]{2,1,0:T(8,128)S(1)}, u32[]{:S(2)}, u32[]{:S(2)}) collective-permute-start(f32[1,64,128]{2,1,0:T(8,128)S(1)} %get-tuple-element.38), channel_id=1, source_target_pairs={{16,0},{32,16},{48,32},{64,48},{80,64},{96,80},{112,96},{17,1},{33... | collective-permute-start | bytes 98312 | tf_op jit(solution)/shard_map/ppermute | solution.py:22
  204.2 10.6 %collective-permute-start.9 = (f32[1,64,128]{2,1,0:T(8,128)S(1)}, f32[1,64,128]{2,1,0:T(8,128)S(1)}, u32[]{:S(2)}, u32[]{:S(2)}) collective-permute-start(f32[1,64,128]{2,1,0:T(8,128)S(1)} %get-tuple-element.37), channel_id=1, source_target_pairs={{0,16},{16,32},{32,48},{48,64},{64,80},{80,96},{96,112},{1,17},{17... | collective-permute-start | bytes 98312 | tf_op jit(solution)/shard_map/ppermute | solution.py:21
  207.3 6.5 %collective-permute-start.10 = (f32[32,1,128]{2,1,0:T(1,128)S(1)}, f32[32,1,128]{2,1,0:T(1,128)S(1)}, u32[]{:S(2)}, u32[]{:S(2)}) collective-permute-start(f32[32,1,128]{2,1,0:T(1,128)S(1)} %get-tuple-element.35), channel_id=1, source_target_pairs={{1,0},{2,1},{3,2},{4,3},{5,4},{6,5},{7,6},{8,7},{9,8},{10,9},{11,1... | collective-permute-start | bytes 49160 | tf_op jit(solution)/shard_map/ppermute | solution.py:22
  208.6 6.3 %collective-permute-start.11 = (f32[32,1,128]{2,1,0:T(1,128)S(1)}, f32[32,1,128]{2,1,0:T(1,128)S(1)}, u32[]{:S(2)}, u32[]{:S(2)}) collective-permute-start(f32[32,1,128]{2,1,0:T(1,128)S(1)} %get-tuple-element.36), channel_id=1, source_target_pairs={{0,1},{1,2},{2,3},{3,4},{4,5},{5,6},{6,7},{7,8},{8,9},{9,10},{10,1... | collective-permute-start | bytes 49160 | tf_op jit(solution)/shard_map/ppermute | solution.py:21
  258.8 12.0 %copy-start.2 = (f32[32,64,128]{2,1,0:T(8,128)S(1)}, f32[32,64,128]{2,1,0:T(8,128)}, u32[]{:S(2)}) copy-start(f32[32,64,128]{2,1,0:T(8,128)} %copy-done.1) | copy-start | bytes 3145732
  258.8 12.0 %copy-start.4 = (f32[32,64,128]{2,1,0:T(8,128)S(1)}, f32[32,64,128]{2,1,0:T(8,128)}, u32[]{:S(2)}) copy-start(f32[32,64,128]{2,1,0:T(8,128)} %param.8) | copy-start | bytes 3145732
  258.8 12.0 %copy-start.5 = (f32[32,64,128]{2,1,0:T(8,128)S(1)}, f32[32,64,128]{2,1,0:T(8,128)}, u32[]{:S(2)}) copy-start(f32[32,64,128]{2,1,0:T(8,128)} %get-tuple-element.23) | copy-start | bytes 3145732
  258.8 11.9 %collective-permute-start.12 = (f32[1,64,128]{2,1,0:T(8,128)S(1)}, f32[1,64,128]{2,1,0:T(8,128)S(1)}, u32[]{:S(2)}, u32[]{:S(2)}) collective-permute-start(f32[1,64,128]{2,1,0:T(8,128)S(1)} %get-tuple-element.32), channel_id=1, source_target_pairs={{16,0},{32,16},{48,32},{64,48},{80,64},{96,80},{112,96},{17,1},{33... | collective-permute-start | bytes 98312 | tf_op jit(solution)/shard_map/ppermute | solution.py:22
  260.4 10.3 %collective-permute-start.13 = (f32[1,64,128]{2,1,0:T(8,128)S(1)}, f32[1,64,128]{2,1,0:T(8,128)S(1)}, u32[]{:S(2)}, u32[]{:S(2)}) collective-permute-start(f32[1,64,128]{2,1,0:T(8,128)S(1)} %get-tuple-element.31), channel_id=1, source_target_pairs={{0,16},{16,32},{32,48},{48,64},{64,80},{80,96},{96,112},{1,17},{17... | collective-permute-start | bytes 98312 | tf_op jit(solution)/shard_map/ppermute | solution.py:21
  263.5 6.2 %collective-permute-start.14 = (f32[32,1,128]{2,1,0:T(1,128)S(1)}, f32[32,1,128]{2,1,0:T(1,128)S(1)}, u32[]{:S(2)}, u32[]{:S(2)}) collective-permute-start(f32[32,1,128]{2,1,0:T(1,128)S(1)} %get-tuple-element.29), channel_id=1, source_target_pairs={{1,0},{2,1},{3,2},{4,3},{5,4},{6,5},{7,6},{8,7},{9,8},{10,9},{11,1... | collective-permute-start | bytes 49160 | tf_op jit(solution)/shard_map/ppermute | solution.py:22
  264.8 6.0 %collective-permute-start.15 = (f32[32,1,128]{2,1,0:T(1,128)S(1)}, f32[32,1,128]{2,1,0:T(1,128)S(1)}, u32[]{:S(2)}, u32[]{:S(2)}) collective-permute-start(f32[32,1,128]{2,1,0:T(1,128)S(1)} %get-tuple-element.30), channel_id=1, source_target_pairs={{0,1},{1,2},{2,3},{3,4},{4,5},{5,6},{6,7},{7,8},{8,9},{9,10},{10,1... | collective-permute-start | bytes 49160 | tf_op jit(solution)/shard_map/ppermute | solution.py:21
  (4 other events, 25.2 us)
where the time goes:
time: 319 us; the launch traced here: 316 us
  local copies, waits for them, and re-layouts  115 us (36%)
  blocking collectives  72.2 us (23%)
  starting transfers between devices  57.8 us (18%)
  waiting for transfers between devices  33.1 us (10%)
  other arithmetic  30.8 us (10%)
  between operations  6.86 us (2%)
    psum x8, blocking collectives, over_axes(): shard = lax.psum(shard, axis)  72.2 us
    transpose x3, local copies, waits for them, and re-layouts, component_grid(): grid = part_blocks.transpose(0, 3, 1, 4, 2, 5)  37.1 us
    reshape x3, local copies, waits for them, and re-layouts, component_grid(): return grid.reshape(span_x * 8, span_y * 8, span_z * 8)  35.3 us
    all_to_all x1, waiting for transfers between devices, body(): lax.all_to_all(payload.reshape(peers, capacity, 1536), GX_GY, split_axis=...  26.3 us
    ppermute x6, starting transfers between devices, extended(): lax.ppermute(last, axis, up)  21.5 us
    another operation x3, local copies, waits for them, and re-layouts, component_grid(): part_blocks = blocks[:, comp, :].reshape(span_x, span_y, span_z, 8, 8, 8)  15.9 us
    scatter-add x1, other arithmetic, body(): blocks.at[landed.reshape(-1)]  13.5 us
    all_to_all x1, starting transfers between devices, body(): lax.all_to_all(slots.reshape(peers, capacity), GX_GY, split_axis=0, conca...  11.2 us
  transfers between devices with their start and end apart: 18, of which 5 were waited for; matrix products, arithmetic and copies ran while one was open for 40% of the time, Pallas kernels for 0%

commit v1 on v0

--- a/solution.py
+++ b/solution.py
@@ -79,7 +79,8 @@
 
 
 def paired_total(first, second):
-    return (over_axes(first, GX_GY), over_axes(second, GX_GY))
+    both = lax.psum(jnp.stack([first, second]), GX_GY)
+    return (both[0], both[1])
 
 
 def component_grid(blocks, comp, span_x, span_y, span_z):

time: 319 us -> 387 us (1.21)
  blocking collectives: 72.2 us -> 136 us
    psum x8 -> x2, blocking collectives: 72.2 us -> 136 us  [paired_total(): both = lax.psum(jnp.stack([first, second]), GX_GY)]
  transfers between devices with their start and end apart: 18 -> 18, of which waited for: 5 -> 5; matrix products, arithmetic and copies ran while one was open for 40% -> 33% of each run, Pallas kernels for 0% -> 0%
where the time goes in v1:
time: 387 us; the launch traced here: 384 us
  blocking collectives  136 us (35%)
  local copies, waits for them, and re-layouts  116 us (30%)
  starting transfers between devices  57.8 us (15%)
  other arithmetic  33.3 us (9%)
  waiting for transfers between devices  33 us (9%)
  between operations  7.02 us (2%)
    psum x2, blocking collectives, paired_total(): both = lax.psum(jnp.stack([first, second]), GX_GY)  136 us
    transpose x3, local copies, waits for them, and re-layouts, component_grid(): grid = part_blocks.transpose(0, 3, 1, 4, 2, 5)  37 us
    reshape x3, local copies, waits for them, and re-layouts, component_grid(): return grid.reshape(span_x * 8, span_y * 8, span_z * 8)  35.3 us
    all_to_all x1, waiting for transfers between devices, body(): lax.all_to_all(payload.reshape(peers, capacity, 1536), GX_GY, split_axis=...  26.1 us
    ppermute x6, starting transfers between devices, extended(): lax.ppermute(last, axis, up)  21.5 us
    another operation x3, local copies, waits for them, and re-layouts, component_grid(): part_blocks = blocks[:, comp, :].reshape(span_x, span_y, span_z, 8, 8, 8)  15.9 us
    scatter-add x1, other arithmetic, body(): blocks.at[landed.reshape(-1)]  13.5 us
    all_to_all x1, starting transfers between devices, body(): lax.all_to_all(slots.reshape(peers, capacity), GX_GY, split_axis=0, conca...  11.2 us
  transfers between devices with their start and end apart: 18, of which 5 were waited for; matrix products, arithmetic and copies ran while one was open for 33% of the time, Pallas kernels for 0%

profile of v1, /device:TPU:0, one launch (start us, length us, event | category | flops | bytes accessed | tf_op | source)
XLA Modules:
  0.0 383.7 jit_solution(14861949810085420257)
XLA Ops:
  5.6 11.2 %all-to-all-start = ((s32[128,1,6]{2,1,0:T(1,128)}), s32[128,1,6]{2,1,0:T(1,128)S(1)}, u32[]{:S(2)}, u32[]{:S(2)}) async-start(s32[128,1,6]{2,1,0:T(1,128)} %bitcast.7), calls=%async_computation | async-start | bytes 131072 | tf_op jit(solution)/shard_map/all_to_all | solution.py:100
  22.5 3.8 all-to-all-done
  26.2 6.5 %all-to-all-start.1 = ((bf16[128,6,1536]{2,1,0:T(8,128)(2,1)}), bf16[128,6,1536]{2,1,0:T(8,128)(2,1)}, u32[]{:S(2)}, u32[]{:S(2)}) async-start(bf16[128,6,1536]{2,1,0:T(8,128)(2,1)} %reshape.77), calls=%async_computation.1 | async-start | bytes 6291456 | tf_op jit(solution)/shard_map/all_to_all | solution.py:97
  36.7 4.7 %collective-permute-start.7 = (f32[32,1,128]{2,1,0:T(1,128)S(1)}, f32[32,1,128]{2,1,0:T(1,128)S(1)}, u32[]{:S(2)}, u32[]{:S(2)}) collective-permute-start(f32[32,1,128]{2,1,0:T(1,128)S(1)} %get-tuple-element.32), channel_id=1, source_target_pairs={{0,1},{1,2},{2,3},{3,4},{4,5},{5,6},{6,7},{7,8},{8,9},{9,10},{10,1... | collective-permute-start | bytes 49160 | tf_op jit(solution)/shard_map/ppermute | solution.py:21
  46.9 26.1 %all-to-all-done.1 = bf16[128,6,1536]{2,1,0:T(8,128)(2,1)} async-done(((bf16[128,6,1536]{2,1,0:T(8,128)(2,1)}), bf16[128,6,1536]{2,1,0:T(8,128)(2,1)}, u32[]{:S(2)}, u32[]{:S(2)}) %all-to-all-start.1) | async-done | bytes 2359328 | tf_op jit(solution)/shard_map/all_to_all | solution.py:97
  73.0 5.3 %reshape.103 = f32[768,1536]{1,0:T(8,128)} reshape(bf16[128,6,1536]{2,1,0:T(8,128)(2,1)} %all-to-all-done.1) | data formatting | bytes 7077888 | tf_op jit(solution)/shard_map/convert_element_type | solution.py:109
  78.3 13.5 %scatter_custom_fusion.2 = f32[512,1536]{1,0:T(8,128)} fusion(s32[768]{0:T(1024)S(1)} %fusion.39, f32[768,1536]{1,0:T(8,128)} %reshape.103, f32[]{:T(128)} %constant.9.clone.1), kind=kCustom, calls=%fused_computation.3 | custom fusion | flops 1179648 | bytes 3146240 | tf_op jit(solution)/shard_map/scatter-add | solution.py:109
  91.8 3.5 copy.22
  98.6 4.8 %reshape_squeeze.9 = f32[4,8,16,8,8,8]{2,1,0,5,4,3:T(8,128)} reshape(f32[512,1,512]{0,2,1:T(8,128)S(1)} %get-tuple-element.10) | data formatting | bytes 2097152 | tf_op jit(solution)/shard_map/reshape;squeeze | solution.py:87
  103.4 12.3 %copy.23 = f32[4,8,8,8,16,8]{5,4,3,2,1,0:T(8,128)} copy(f32[4,8,8,8,16,8]{4,2,0,5,3,1:T(8,128)} %bitcast.42) | data formatting | bytes 2097152 | tf_op jit(solution)/shard_map/transpose | solution.py:88
  115.8 11.8 %reshape.79 = f32[32,64,128]{2,1,0:T(8,128)S(1)} reshape(f32[4,8,8,8,16,8]{5,4,3,2,1,0:T(8,128)} %copy.23) | data formatting | bytes 2097152 | tf_op jit(solution)/shard_map/reshape | solution.py:89
  132.1 4.9 %reshape_squeeze.10 = f32[4,8,16,8,8,8]{2,1,0,5,4,3:T(8,128)} reshape(f32[512,1,512]{0,2,1:T(8,128)S(1)} %get-tuple-element.12) | data formatting | bytes 2097152 | tf_op jit(solution)/shard_map/reshape;squeeze | solution.py:87
  137.0 12.3 %copy.24 = f32[4,8,8,8,16,8]{5,4,3,2,1,0:T(8,128)} copy(f32[4,8,8,8,16,8]{4,2,0,5,3,1:T(8,128)} %bitcast.43) | data formatting | bytes 2097152 | tf_op jit(solution)/shard_map/transpose | solution.py:88
  149.3 11.8 %reshape.80 = f32[32,64,128]{2,1,0:T(8,128)S(1)} reshape(f32[4,8,8,8,16,8]{5,4,3,2,1,0:T(8,128)} %copy.24) | data formatting | bytes 2097152 | tf_op jit(solution)/shard_map/reshape | solution.py:89
  162.4 6.2 %reshape_squeeze.11 = f32[4,8,16,8,8,8]{2,1,0,5,4,3:T(8,128)} reshape(f32[512,1,512]{0,2,1:T(8,128)} %get-tuple-element.11) | data formatting | bytes 2097152 | tf_op jit(solution)/shard_map/reshape;squeeze | solution.py:87
  168.6 12.3 %copy.25 = f32[4,8,8,8,16,8]{5,4,3,2,1,0:T(8,128)} copy(f32[4,8,8,8,16,8]{4,2,0,5,3,1:T(8,128)} %bitcast.44) | data formatting | bytes 2097152 | tf_op jit(solution)/shard_map/transpose | solution.py:88
  181.0 11.8 %reshape.81 = f32[32,64,128]{2,1,0:T(8,128)S(1)} reshape(f32[4,8,8,8,16,8]{5,4,3,2,1,0:T(8,128)} %copy.25) | data formatting | bytes 2097152 | tf_op jit(solution)/shard_map/reshape | solution.py:89
  192.8 4.8 %collective-permute-start.3 = (f32[32,1,128]{2,1,0:T(1,128)S(1)}, f32[32,1,128]{2,1,0:T(1,128)S(1)}, u32[]{:S(2)}, u32[]{:S(2)}) collective-permute-start(f32[32,1,128]{2,1,0:T(1,128)S(1)} %get-tuple-element.28), channel_id=1, source_target_pairs={{0,1},{1,2},{2,3},{3,4},{4,5},{5,6},{6,7},{7,8},{8,9},{9,10},{10,1... | collective-permute-start | bytes 49160 | tf_op jit(solution)/shard_map/ppermute | solution.py:44
  199.1 3.5 fusion.33
  208.3 4.8 %collective-permute-start.11 = (f32[32,1,128]{2,1,0:T(1,128)S(1)}, f32[32,1,128]{2,1,0:T(1,128)S(1)}, u32[]{:S(2)}, u32[]{:S(2)}) collective-permute-start(f32[32,1,128]{2,1,0:T(1,128)S(1)} %get-tuple-element.20), channel_id=1, source_target_pairs={{0,1},{1,2},{2,3},{3,4},{4,5},{5,6},{6,7},{7,8},{8,9},{9,10},{10,1... | collective-permute-start | bytes 49160 | tf_op jit(solution)/shard_map/ppermute | solution.py:21
  218.3 68.6 %psum.14 = f32[2]{0:T(128)S(1)} all-reduce(f32[2]{0:T(128)S(1)} %pad_maximum_fusion.20), channel_id=1, replica_groups=mesh['gx_0'=4,'gx_1'=2,'gy_0'=4,'gy_1'=4] {'gx_0','gx_1','gy_0','gy_1'}, use_global_device_ids=true, to_apply=%region_8.9 | all-reduce | flops 2 | bytes 16 | tf_op jit(solution)/shard_map/psum | solution.py:82
  297.0 4.5 %collective-permute-start.15 = (f32[32,1,128]{2,1,0:T(1,128)S(1)}, f32[32,1,128]{2,1,0:T(1,128)S(1)}, u32[]{:S(2)}, u32[]{:S(2)}) collective-permute-start(f32[32,1,128]{2,1,0:T(1,128)S(1)} %get-tuple-element.14), channel_id=1, source_target_pairs={{0,1},{1,2},{2,3},{3,4},{4,5},{5,6},{6,7},{7,8},{8,9},{9,10},{10,1... | collective-permute-start | bytes 49160 | tf_op jit(solution)/shard_map/ppermute | solution.py:21
  306.9 67.8 %psum.15 = f32[2]{0:T(128)S(1)} all-reduce(f32[2]{0:T(128)S(1)} %pad_maximum_fusion.21), channel_id=1, replica_groups=mesh['gx_0'=4,'gx_1'=2,'gy_0'=4,'gy_1'=4] {'gx_0','gx_1','gy_0','gy_1'}, use_global_device_ids=true, to_apply=%region_11.12 | all-reduce | flops 2 | bytes 16 | tf_op jit(solution)/shard_map/psum | solution.py:82
  379.8 3.9 %multiply_subtract_fusion = (f32[32,64,128]{2,1,0:T(8,128)}, f32[32,64,128]{2,1,0:T(8,128)}) fusion(f32[32,64,128]{2,1,0:T(8,128)} %get-tuple-element.6, f32[32,64,128]{2,1,0:T(8,128)} %get-tuple-element.7, f32[]{:T(128)S(6)} %div.21, f32[]{:T(128)S(6)} %div.23, f32[32,64,128]{2,1,0:T(8,128)} %copy-done.1, f32[]{:T(128)S(6)} %div.20, ...), kind=kLoop, calls=%fused_computation.63 | loop fusion | flops 3145728 | bytes 8388620 | tf_op jit(solution)/shard_map/sub | solution.py:131
  (89 shorter events, 56.0 us)
Async XLA Ops:
  5.6 20.6 %all-to-all-start = ((s32[128,1,6]{2,1,0:T(1,128)}), s32[128,1,6]{2,1,0:T(1,128)S(1)}, u32[]{:S(2)}, u32[]{:S(2)}) async-start(s32[128,1,6]{2,1,0:T(1,128)} %bitcast.7), calls=%async_computation | async-start | bytes 131072 | tf_op jit(solution)/shard_map/all_to_all | solution.py:100
  22.5 10.2 %copy-start = (f32[32,64,128]{2,1,0:T(8,128)S(1)}, f32[32,64,128]{2,1,0:T(8,128)}, u32[]{:S(2)}) copy-start(f32[32,64,128]{2,1,0:T(8,128)} %param.9) | copy-start | bytes 3145732
  26.2 46.8 %all-to-all-start.1 = ((bf16[128,6,1536]{2,1,0:T(8,128)(2,1)}), bf16[128,6,1536]{2,1,0:T(8,128)(2,1)}, u32[]{:S(2)}, u32[]{:S(2)}) async-start(bf16[128,6,1536]{2,1,0:T(8,128)(2,1)} %reshape.77), calls=%async_computation.1 | async-start | bytes 6291456 | tf_op jit(solution)/shard_map/all_to_all | solution.py:97
  32.7 11.9 %collective-permute-start.5 = (f32[1,64,128]{2,1,0:T(8,128)S(1)}, f32[1,64,128]{2,1,0:T(8,128)S(1)}, u32[]{:S(2)}, u32[]{:S(2)}) collective-permute-start(f32[1,64,128]{2,1,0:T(8,128)S(1)} %get-tuple-element.34), channel_id=1, source_target_pairs={{0,16},{16,32},{32,48},{48,64},{64,80},{80,96},{96,112},{1,17},{17... | collective-permute-start | bytes 98312 | tf_op jit(solution)/shard_map/ppermute | solution.py:21
  34.0 12.3 %collective-permute-start.4 = (f32[1,64,128]{2,1,0:T(8,128)S(1)}, f32[1,64,128]{2,1,0:T(8,128)S(1)}, u32[]{:S(2)}, u32[]{:S(2)}) collective-permute-start(f32[1,64,128]{2,1,0:T(8,128)S(1)} %get-tuple-element.33), channel_id=1, source_target_pairs={{16,0},{32,16},{48,32},{64,48},{80,64},{96,80},{112,96},{17,1},{33... | collective-permute-start | bytes 98312 | tf_op jit(solution)/shard_map/ppermute | solution.py:22
  35.4 157.4 %collective-permute-start.6 = (f32[32,1,128]{2,1,0:T(1,128)S(1)}, f32[32,1,128]{2,1,0:T(1,128)S(1)}, u32[]{:S(2)}, u32[]{:S(2)}) collective-permute-start(f32[32,1,128]{2,1,0:T(1,128)S(1)} %get-tuple-element.31), channel_id=1, source_target_pairs={{1,0},{2,1},{3,2},{4,3},{5,4},{6,5},{7,6},{8,7},{9,8},{10,9},{11,1... | collective-permute-start | bytes 49160 | tf_op jit(solution)/shard_map/ppermute | solution.py:22
  36.7 161.3 %collective-permute-start.7 = (f32[32,1,128]{2,1,0:T(1,128)S(1)}, f32[32,1,128]{2,1,0:T(1,128)S(1)}, u32[]{:S(2)}, u32[]{:S(2)}) collective-permute-start(f32[32,1,128]{2,1,0:T(1,128)S(1)} %get-tuple-element.32), channel_id=1, source_target_pairs={{0,1},{1,2},{2,3},{3,4},{4,5},{5,6},{6,7},{7,8},{8,9},{9,10},{10,1... | collective-permute-start | bytes 49160 | tf_op jit(solution)/shard_map/ppermute | solution.py:21
  127.6 71.5 %collective-permute-start = (f32[1,64,128]{2,1,0:T(8,128)S(1)}, f32[1,64,128]{2,1,0:T(8,128)S(1)}, u32[]{:S(2)}, u32[]{:S(2)}) collective-permute-start(f32[1,64,128]{2,1,0:T(8,128)S(1)} %get-tuple-element.25), channel_id=1, source_target_pairs={{16,0},{32,16},{48,32},{64,48},{80,64},{96,80},{112,96},{17,1},{33... | collective-permute-start | bytes 98312 | tf_op jit(solution)/shard_map/ppermute | solution.py:47
  128.9 70.2 %collective-permute-start.1 = (f32[1,64,128]{2,1,0:T(8,128)S(1)}, f32[1,64,128]{2,1,0:T(8,128)S(1)}, u32[]{:S(2)}, u32[]{:S(2)}) collective-permute-start(f32[1,64,128]{2,1,0:T(8,128)S(1)} %get-tuple-element.26), channel_id=1, source_target_pairs={{0,16},{16,32},{32,48},{48,64},{64,80},{80,96},{96,112},{1,17},{17... | collective-permute-start | bytes 98312 | tf_op jit(solution)/shard_map/ppermute | solution.py:44
  161.1 7.5 %copy-start.6 = (f32[32,64,128]{2,1,0:T(8,128)}, f32[32,64,128]{2,1,0:T(8,128)S(1)}, u32[]{:S(2)}) copy-start(f32[32,64,128]{2,1,0:T(8,128)S(1)} %reshape.80) | copy-start | bytes 3145732
  161.1 36.9 %collective-permute-start.2 = (f32[32,1,128]{2,1,0:T(1,128)S(1)}, f32[32,1,128]{2,1,0:T(1,128)S(1)}, u32[]{:S(2)}, u32[]{:S(2)}) collective-permute-start(f32[32,1,128]{2,1,0:T(1,128)S(1)} %get-tuple-element.27), channel_id=1, source_target_pairs={{1,0},{2,1},{3,2},{4,3},{5,4},{6,5},{7,6},{8,7},{9,8},{10,9},{11,1... | collective-permute-start | bytes 49160 | tf_op jit(solution)/shard_map/ppermute | solution.py:47
  192.8 6.2 %collective-permute-start.3 = (f32[32,1,128]{2,1,0:T(1,128)S(1)}, f32[32,1,128]{2,1,0:T(1,128)S(1)}, u32[]{:S(2)}, u32[]{:S(2)}) collective-permute-start(f32[32,1,128]{2,1,0:T(1,128)S(1)} %get-tuple-element.28), channel_id=1, source_target_pairs={{0,1},{1,2},{2,3},{3,4},{4,5},{5,6},{6,7},{7,8},{8,9},{9,10},{10,1... | collective-permute-start | bytes 49160 | tf_op jit(solution)/shard_map/ppermute | solution.py:44
  202.6 14.4 %copy-start.1 = (f32[32,64,128]{2,1,0:T(8,128)}, f32[32,64,128]{2,1,0:T(8,128)S(1)}, u32[]{:S(2)}) copy-start(f32[32,64,128]{2,1,0:T(8,128)S(1)} %get-tuple-element.9) | copy-start | bytes 3145732
  202.6 11.9 %collective-permute-start.8 = (f32[1,64,128]{2,1,0:T(8,128)S(1)}, f32[1,64,128]{2,1,0:T(8,128)S(1)}, u32[]{:S(2)}, u32[]{:S(2)}) collective-permute-start(f32[1,64,128]{2,1,0:T(8,128)S(1)} %get-tuple-element.22), channel_id=1, source_target_pairs={{16,0},{32,16},{48,32},{64,48},{80,64},{96,80},{112,96},{17,1},{33... | collective-permute-start | bytes 98312 | tf_op jit(solution)/shard_map/ppermute | solution.py:22
  203.9 10.6 %collective-permute-start.9 = (f32[1,64,128]{2,1,0:T(8,128)S(1)}, f32[1,64,128]{2,1,0:T(8,128)S(1)}, u32[]{:S(2)}, u32[]{:S(2)}) collective-permute-start(f32[1,64,128]{2,1,0:T(8,128)S(1)} %get-tuple-element.21), channel_id=1, source_target_pairs={{0,16},{16,32},{32,48},{48,64},{64,80},{80,96},{96,112},{1,17},{17... | collective-permute-start | bytes 98312 | tf_op jit(solution)/shard_map/ppermute | solution.py:21
  207.0 6.5 %collective-permute-start.10 = (f32[32,1,128]{2,1,0:T(1,128)S(1)}, f32[32,1,128]{2,1,0:T(1,128)S(1)}, u32[]{:S(2)}, u32[]{:S(2)}) collective-permute-start(f32[32,1,128]{2,1,0:T(1,128)S(1)} %get-tuple-element.19), channel_id=1, source_target_pairs={{1,0},{2,1},{3,2},{4,3},{5,4},{6,5},{7,6},{8,7},{9,8},{10,9},{11,1... | collective-permute-start | bytes 49160 | tf_op jit(solution)/shard_map/ppermute | solution.py:22
  208.3 6.3 %collective-permute-start.11 = (f32[32,1,128]{2,1,0:T(1,128)S(1)}, f32[32,1,128]{2,1,0:T(1,128)S(1)}, u32[]{:S(2)}, u32[]{:S(2)}) collective-permute-start(f32[32,1,128]{2,1,0:T(1,128)S(1)} %get-tuple-element.20), channel_id=1, source_target_pairs={{0,1},{1,2},{2,3},{3,4},{4,5},{5,6},{6,7},{7,8},{8,9},{9,10},{10,1... | collective-permute-start | bytes 49160 | tf_op jit(solution)/shard_map/ppermute | solution.py:21
  291.0 12.0 %copy-start.2 = (f32[32,64,128]{2,1,0:T(8,128)S(1)}, f32[32,64,128]{2,1,0:T(8,128)}, u32[]{:S(2)}) copy-start(f32[32,64,128]{2,1,0:T(8,128)} %copy-done.1) | copy-start | bytes 3145732
  291.0 12.0 %copy-start.4 = (f32[32,64,128]{2,1,0:T(8,128)S(1)}, f32[32,64,128]{2,1,0:T(8,128)}, u32[]{:S(2)}) copy-start(f32[32,64,128]{2,1,0:T(8,128)} %param.8) | copy-start | bytes 3145732
  291.0 12.0 %copy-start.5 = (f32[32,64,128]{2,1,0:T(8,128)S(1)}, f32[32,64,128]{2,1,0:T(8,128)}, u32[]{:S(2)}) copy-start(f32[32,64,128]{2,1,0:T(8,128)} %get-tuple-element.7) | copy-start | bytes 3145732
  291.1 11.9 %collective-permute-start.12 = (f32[1,64,128]{2,1,0:T(8,128)S(1)}, f32[1,64,128]{2,1,0:T(8,128)S(1)}, u32[]{:S(2)}, u32[]{:S(2)}) collective-permute-start(f32[1,64,128]{2,1,0:T(8,128)S(1)} %get-tuple-element.16), channel_id=1, source_target_pairs={{16,0},{32,16},{48,32},{64,48},{80,64},{96,80},{112,96},{17,1},{33... | collective-permute-start | bytes 98312 | tf_op jit(solution)/shard_map/ppermute | solution.py:22
  292.6 10.3 %collective-permute-start.13 = (f32[1,64,128]{2,1,0:T(8,128)S(1)}, f32[1,64,128]{2,1,0:T(8,128)S(1)}, u32[]{:S(2)}, u32[]{:S(2)}) collective-permute-start(f32[1,64,128]{2,1,0:T(8,128)S(1)} %get-tuple-element.15), channel_id=1, source_target_pairs={{0,16},{16,32},{32,48},{48,64},{64,80},{80,96},{96,112},{1,17},{17... | collective-permute-start | bytes 98312 | tf_op jit(solution)/shard_map/ppermute | solution.py:21
  295.7 6.2 %collective-permute-start.14 = (f32[32,1,128]{2,1,0:T(1,128)S(1)}, f32[32,1,128]{2,1,0:T(1,128)S(1)}, u32[]{:S(2)}, u32[]{:S(2)}) collective-permute-start(f32[32,1,128]{2,1,0:T(1,128)S(1)} %get-tuple-element.13), channel_id=1, source_target_pairs={{1,0},{2,1},{3,2},{4,3},{5,4},{6,5},{7,6},{8,7},{9,8},{10,9},{11,1... | collective-permute-start | bytes 49160 | tf_op jit(solution)/shard_map/ppermute | solution.py:22
  297.0 6.0 %collective-permute-start.15 = (f32[32,1,128]{2,1,0:T(1,128)S(1)}, f32[32,1,128]{2,1,0:T(1,128)S(1)}, u32[]{:S(2)}, u32[]{:S(2)}) collective-permute-start(f32[32,1,128]{2,1,0:T(1,128)S(1)} %get-tuple-element.14), channel_id=1, source_target_pairs={{0,1},{1,2},{2,3},{3,4},{4,5},{5,6},{6,7},{7,8},{8,9},{9,10},{10,1... | collective-permute-start | bytes 49160 | tf_op jit(solution)/shard_map/ppermute | solution.py:21
  (4 other events, 25.2 us)

commit v2 on v0

--- a/solution.py
+++ b/solution.py
@@ -3,6 +3,8 @@
 from jax import lax
 from jax.sharding import Mesh
 from jax.sharding import PartitionSpec as P
+from jax.experimental import pallas as pl
+from jax.experimental.pallas import tpu as pltpu
 
 ITERS = 2
 GX_GY = ("gx_0", "gx_1", "gy_0", "gy_1")
@@ -88,6 +90,52 @@
     return grid.reshape(span_x * 8, span_y * 8, span_z * 8)
 
 
+def relayout_kernel(blk_ref, out_ref):
+    sub = lax.broadcasted_iota(jnp.int32, (8, 128), 0)
+    lane = lax.broadcasted_iota(jnp.int32, (8, 128), 1)
+    grp = (lane // 8) % 8
+    low_half = lane < 64
+    swaps = []
+    for m in (4, 2, 1):
+        first = ((sub & m) == 0) & ((grp & m) != 0)
+        second = ((sub & m) != 0) & ((grp & m) == 0)
+        swaps.append((m, first, second))
+
+    def transpose_groups(x):
+        for m, first, second in swaps:
+            a = pltpu.roll(pltpu.roll(x, 8 - m, 0), 8 * m, 1)
+            b = pltpu.roll(pltpu.roll(x, m, 0), 128 - 8 * m, 1)
+            x = jnp.where(first, a, jnp.where(second, b, x))
+        return x
+
+    def step(i, carry):
+        uh = i % 4
+        c = (i // 4) % 3
+        ly = (i // 12) % 8
+        lx = i // 96
+        row = pl.multiple_of((lx * 8 + ly) * 16, 16)
+        col = pl.multiple_of((c * 4 + uh) * 128, 128)
+        s0 = blk_ref[pl.ds(row, 8), pl.ds(col, 128)]
+        s1 = blk_ref[pl.ds(row + 8, 8), pl.ds(col, 128)]
+        u0 = jnp.where(low_half, s0, pltpu.roll(s1, 64, 1))
+        u1 = jnp.where(low_half, pltpu.roll(s0, 64, 1), s1)
+        y = pl.multiple_of(ly * 8, 8)
+        out_ref[c, lx * 8 + uh * 2, pl.ds(y, 8), :] = transpose_groups(u0)
+        out_ref[c, lx * 8 + uh * 2 + 1, pl.ds(y, 8), :] = transpose_groups(u1)
+        return carry
+
+    lax.fori_loop(0, 384, step, 0)
+
+
+def to_grid(blocks, span_x, span_y, depth):
+    return pl.pallas_call(
+        relayout_kernel,
+        out_shape=jax.ShapeDtypeStruct((3, span_x * 8, span_y * 8, depth), jnp.float32),
+        in_specs=[pl.BlockSpec(memory_space=pltpu.VMEM)],
+        out_specs=pl.BlockSpec(memory_space=pltpu.VMEM),
+    )(blocks)
+
+
 def body(bricks, brick_target, brick_slot, screen, coarse_guess):
     peers = lax.axis_size(GX_GY)
     capacity = max(2, 3 * bricks.shape[0] // peers)
@@ -104,12 +152,15 @@
     span_x = width_x // 8
     span_y = width_y // 8
     span_z = depth // 8
-    blocks = jnp.zeros((span_x * span_y * span_z, 1536), jnp.float32)
-    blocks = blocks.at[landed.reshape(-1)].add(arrived.reshape(-1, 1536).astype(jnp.float32))
-    blocks = blocks.reshape(span_x * span_y * span_z, 3, 512)
-    normal_x = component_grid(blocks, 0, span_x, span_y, span_z)
-    normal_y = component_grid(blocks, 1, span_x, span_y, span_z)
-    normal_z = component_grid(blocks, 2, span_x, span_y, span_z)
+    picks = landed.reshape(-1, 1) == jnp.arange(span_x * span_y * span_z, dtype=jnp.int32)[None, :]
+    blocks = jnp.einsum(
+        "ks,kj->sj",
+        picks.astype(jnp.bfloat16),
+        arrived.reshape(-1, 1536),
+        preferred_element_type=jnp.float32,
+    )
+    normals = to_grid(blocks, span_x, span_y, depth)
+    normal_x, normal_y, normal_z = normals[0], normals[1], normals[2]
     along_x = with_halo(normal_x, ((GX, 0),), 1)
     along_y = with_halo(normal_y, ((GY, 1),), 1)
     total = along_x[2:] - along_x[:-2]

time: 319 us -> 328 us (1.028)
  Pallas kernels: 0 us -> 114 us
  local copies, waits for them, and re-layouts: 115 us -> 22.5 us
  other arithmetic: 30.8 us -> 17.2 us
  matrix products: 0 us -> 4.83 us
    pallas_call x0 -> x1, Pallas kernels: none -> 114 us  [to_grid(): pl.pallas_call(relayout_kernel, out_shape=jax.ShapeDtypeStruct((3, span_x...]
    transpose x3 -> x0, local copies, waits for them, and re-layouts: 37.1 us -> none  [component_grid(): grid = part_blocks.transpose(0, 3, 1, 4, 2, 5)]
    reshape x4 -> x1, local copies, waits for them, and re-layouts: 35.4 us -> 5.03 us  [body(): arrived.reshape(-1, 1536)]
    another operation x6 -> x3, local copies, waits for them, and re-layouts: 15.9 us -> 0.02 us  [the longest x3 15.9 us: component_grid(): part_blocks = blocks[:, comp, :].reshape(span_x, span_y, span_z, 8, 8, 8)]
    scatter-add x1 -> x0, other arithmetic: 13.5 us -> none  [body(): blocks.at[landed.reshape(-1)]]
    convert_element_type x1 -> x0, local copies, waits for them, and re-layouts: 5.28 us -> none  [body(): arrived.reshape(-1, 1536).astype(jnp.float32)]
    ppermute x6, waiting for transfers between devices: 0.02 us -> 5.18 us  [extended(): lax.ppermute(first, axis, [(b, a) for a, b in up])]
    dot_general x0 -> x1, matrix products: none -> 4.83 us  [body(): jnp.einsum('ks,kj->sj', picks.astype(jnp.bfloat16), arrived.reshape(-1, 1...]
  transfers between devices with their start and end apart: 18 -> 18, of which waited for: 5 -> 5; matrix products, arithmetic and copies ran while one was open for 40% -> 8% of each run, Pallas kernels for 0% -> 35%
where the time goes in v2:
time: 328 us; the launch traced here: 327 us
  Pallas kernels  114 us (35%)
  blocking collectives  71.6 us (22%)
  starting transfers between devices  55.7 us (17%)
  waiting for transfers between devices  34.2 us (10%)
  local copies, waits for them, and re-layouts  22.5 us (7%)
  other arithmetic  17.2 us (5%)
  between operations  6.84 us (2%)
  matrix products  4.83 us (1%)
    pallas_call x1, Pallas kernels, to_grid(): pl.pallas_call(relayout_kernel, out_shape=jax.ShapeDtypeStruct((3, span_x...  114 us
    psum x8, blocking collectives, over_axes(): shard = lax.psum(shard, axis)  71.6 us
    all_to_all x1, waiting for transfers between devices, body(): lax.all_to_all(payload.reshape(peers, capacity, 1536), GX_GY, split_axis=...  24.9 us
    ppermute x6, starting transfers between devices, extended(): lax.ppermute(last, axis, up)  19.8 us
    all_to_all x1, starting transfers between devices, body(): lax.all_to_all(slots.reshape(peers, capacity), GX_GY, split_axis=0, conca...  11.2 us
    ppermute x6, starting transfers between devices, extended(): lax.ppermute(first, axis, [(b, a) for a, b in up])  8.02 us
    ppermute x2, starting transfers between devices, with_halo(): lax.ppermute(lax.slice_in_dim(block, block.shape[dim] - width, None, axis...  7.58 us
  transfers between devices with their start and end apart: 18, of which 5 were waited for; matrix products, arithmetic and copies ran while one was open for 8% of the time, Pallas kernels for 35%

profile of v2, /device:TPU:0, one launch (start us, length us, event | category | flops | bytes accessed | tf_op | source)
XLA Modules:
  0.0 327.3 jit_solution(1004834260044999897)
XLA Ops:
  5.6 11.2 %all-to-all-start = ((s32[128,1,6]{2,1,0:T(1,128)}), s32[128,1,6]{2,1,0:T(1,128)S(1)}, u32[]{:S(2)}, u32[]{:S(2)}) async-start(s32[128,1,6]{2,1,0:T(1,128)} %bitcast.7), calls=%async_computation | async-start | bytes 131072 | tf_op jit(solution)/shard_map/all_to_all | solution.py:147
  16.8 3.2 scatter_custom_fusion.1
  22.5 3.7 %all-to-all-done = s32[128,1,6]{2,1,0:T(1,128)S(1)} async-done(((s32[128,1,6]{2,1,0:T(1,128)}), s32[128,1,6]{2,1,0:T(1,128)S(1)}, u32[]{:S(2)}, u32[]{:S(2)}) %all-to-all-start) | async-done | bytes 3104 | tf_op jit(solution)/shard_map/all_to_all | solution.py:147
  26.2 6.5 %all-to-all-start.1 = ((bf16[128,6,1536]{2,1,0:T(8,128)(2,1)}), bf16[128,6,1536]{2,1,0:T(8,128)(2,1)}, u32[]{:S(2)}, u32[]{:S(2)}) async-start(bf16[128,6,1536]{2,1,0:T(8,128)(2,1)} %reshape.37), calls=%async_computation.1 | async-start | bytes 6291456 | tf_op jit(solution)/shard_map/all_to_all | solution.py:144
  34.1 4.5 %collective-permute-start.7 = (f32[32,1,128]{2,1,0:T(1,128)S(1)}, f32[32,1,128]{2,1,0:T(1,128)S(1)}, u32[]{:S(2)}, u32[]{:S(2)}) collective-permute-start(f32[32,1,128]{2,1,0:T(1,128)S(1)} %get-tuple-element.48), channel_id=1, source_target_pairs={{0,1},{1,2},{2,3},{3,4},{4,5},{5,6},{6,7},{7,8},{8,9},{9,10},{10,1... | collective-permute-start | bytes 49160 | tf_op jit(solution)/shard_map/ppermute | solution.py:23
  40.0 3.0 collective-permute-start.5
  48.2 24.9 %all-to-all-done.1 = bf16[128,6,1536]{2,1,0:T(8,128)(2,1)} async-done(((bf16[128,6,1536]{2,1,0:T(8,128)(2,1)}), bf16[128,6,1536]{2,1,0:T(8,128)(2,1)}, u32[]{:S(2)}, u32[]{:S(2)}) %all-to-all-start.1) | async-done | bytes 2359328 | tf_op jit(solution)/shard_map/all_to_all | solution.py:144
  73.1 5.0 %reshape.38 = bf16[768,1536]{1,0:T(8,128)(2,1)} reshape(bf16[128,6,1536]{2,1,0:T(8,128)(2,1)} %all-to-all-done.1) | data formatting | bytes 4718592 | tf_op jit(solution)/shard_map/reshape | solution.py:159
  78.1 4.8 %fusion.blk_ref = f32[512,1536]{1,0:T(8,128)} fusion(bf16[768,1536]{1,0:T(8,128)(2,1)} %reshape.38, s32[768]{0:T(1024)S(1)} %eq.48), kind=kOutput, calls=%fused_computation.3 | convolution fusion | flops 1208352768 | bytes 5508096 | tf_op jit(solution)/shard_map/ks,kj->sj/dot_general | solution.py:156
  82.9 114.4 %shard_map.68 = f32[3,32,64,128]{3,2,1,0:T(8,128)} custom-call(f32[512,1536]{1,0:T(8,128)} %fusion.blk_ref), custom_call_target="tpu_custom_call" | custom-call | tf_op jit(solution)/shard_map/pallas_call | solution.py:131
  201.7 4.5 %collective-permute-start.3 = (f32[32,1,128]{2,1,0:T(1,128)S(1)}, f32[32,1,128]{2,1,0:T(1,128)S(1)}, u32[]{:S(2)}, u32[]{:S(2)}) collective-permute-start(f32[32,1,128]{2,1,0:T(1,128)S(1)} %get-tuple-element.44), channel_id=1, source_target_pairs={{0,1},{1,2},{2,3},{3,4},{4,5},{5,6},{6,7},{7,8},{8,9},{9,10},{10,1... | collective-permute-start | bytes 49160 | tf_op jit(solution)/shard_map/ppermute | solution.py:46
  211.4 3.5 %fusion.33 = (f32[32,64,128]{2,1,0:T(8,128)S(1)}, f32[32,64,128]{2,1,0:T(8,128)S(1)}) fusion(f32[32,64,128]{2,1,0:T(8,128)S(1)} %copy-done.3, f32[32,64,127]{2,1,0:T(8,128)S(1)} %copy-done.6, f32[32,64,127]{2,1,0:T(8,128)S(1)} %get-tuple-element.51, f32[34,64,128]{2,1,0:T(8,128)} %constant_dynamic-update-slice_fusion, ...), kind=kLoop, calls=%fused_computation.75 | loop fusion | flops 8126464 | bytes 11763712 | tf_op jit(solution)/shard_map/mul | solution.py:173
  216.3 4.5 %collective-permute-start.11 = (f32[32,1,128]{2,1,0:T(1,128)S(1)}, f32[32,1,128]{2,1,0:T(1,128)S(1)}, u32[]{:S(2)}, u32[]{:S(2)}) collective-permute-start(f32[32,1,128]{2,1,0:T(1,128)S(1)} %get-tuple-element.38), channel_id=1, source_target_pairs={{0,1},{1,2},{2,3},{3,4},{4,5},{5,6},{6,7},{7,8},{8,9},{9,10},{10,1... | collective-permute-start | bytes 49160 | tf_op jit(solution)/shard_map/ppermute | solution.py:23
  224.4 3.8 %collective-permute-done.8 = f32[1,64,128]{2,1,0:T(8,128)S(1)} collective-permute-done((f32[1,64,128]{2,1,0:T(8,128)S(1)}, f32[1,64,128]{2,1,0:T(8,128)S(1)}, u32[]{:S(2)}, u32[]{:S(2)}) %collective-permute-start.8) | collective-permute-done | bytes 32800 | tf_op jit(solution)/shard_map/ppermute | solution.py:24
  230.7 11.5 %all-reduce.19 = (f32[]{:T(128)}, f32[]{:T(128)}) all-reduce(f32[]{:T(128)} %get-tuple-element.5, f32[]{:T(128)} %get-tuple-element.4), channel_id=1, replica_groups=mesh['gx_0'=4,'gx_1'=2,'gy_0'=4,'gy_1'=4] {'gx_0'}, use_global_device_ids=true, to_apply=%region_6.7 | all-reduce | flops 2 | bytes 16 | tf_op jit(solution)/shard_map/psum | solution.py:37
  242.2 3.1 all-reduce.21
  245.3 12.2 %all-reduce.17 = (f32[]{:T(128)}, f32[]{:T(128)}) all-reduce(f32[]{:T(128)} %get-tuple-element.20, f32[]{:T(128)} %get-tuple-element.21), channel_id=1, replica_groups=mesh['gx_0'=4,'gx_1'=2,'gy_0'=4,'gy_1'=4] {'gy_0'}, use_global_device_ids=true, to_apply=%region_8.9 | all-reduce | flops 2 | bytes 16 | tf_op jit(solution)/shard_map/psum | solution.py:37
  257.5 10.9 %all-reduce.15 = (f32[]{:T(128)}, f32[]{:T(128)}) all-reduce(f32[]{:T(128)} %get-tuple-element.12, f32[]{:T(128)} %get-tuple-element.13), channel_id=1, replica_groups=mesh['gx_0'=4,'gx_1'=2,'gy_0'=4,'gy_1'=4] {'gy_1'}, use_global_device_ids=true, to_apply=%region_9.10 | all-reduce | flops 2 | bytes 16 | tf_op jit(solution)/shard_map/psum | solution.py:37
  273.5 4.5 %collective-permute-start.15 = (f32[32,1,128]{2,1,0:T(1,128)S(1)}, f32[32,1,128]{2,1,0:T(1,128)S(1)}, u32[]{:S(2)}, u32[]{:S(2)}) collective-permute-start(f32[32,1,128]{2,1,0:T(1,128)S(1)} %get-tuple-element.32), channel_id=1, source_target_pairs={{0,1},{1,2},{2,3},{3,4},{4,5},{5,6},{6,7},{7,8},{8,9},{9,10},{10,1... | collective-permute-start | bytes 49160 | tf_op jit(solution)/shard_map/ppermute | solution.py:23
  285.0 10.9 %all-reduce.18 = (f32[]{:T(128)}, f32[]{:T(128)}) all-reduce(f32[]{:T(128)} %get-tuple-element.3, f32[]{:T(128)} %get-tuple-element.2), channel_id=1, replica_groups=mesh['gx_0'=4,'gx_1'=2,'gy_0'=4,'gy_1'=4] {'gx_0'}, use_global_device_ids=true, to_apply=%region_16.17 | all-reduce | flops 2 | bytes 16 | tf_op jit(solution)/shard_map/psum | solution.py:37
  295.9 3.1 all-reduce.20
  299.1 9.5 %all-reduce.16 = (f32[]{:T(128)}, f32[]{:T(128)}) all-reduce(f32[]{:T(128)} %get-tuple-element.18, f32[]{:T(128)} %get-tuple-element.19), channel_id=1, replica_groups=mesh['gx_0'=4,'gx_1'=2,'gy_0'=4,'gy_1'=4] {'gy_0'}, use_global_device_ids=true, to_apply=%region_18.19 | all-reduce | flops 2 | bytes 16 | tf_op jit(solution)/shard_map/psum | solution.py:37
  308.6 10.3 %all-reduce.14 = (f32[]{:T(128)}, f32[]{:T(128)}) all-reduce(f32[]{:T(128)} %get-tuple-element.10, f32[]{:T(128)} %get-tuple-element.11), channel_id=1, replica_groups=mesh['gx_0'=4,'gx_1'=2,'gy_0'=4,'gy_1'=4] {'gy_1'}, use_global_device_ids=true, to_apply=%region_19.20 | all-reduce | flops 2 | bytes 16 | tf_op jit(solution)/shard_map/psum | solution.py:37
  323.3 3.9 %multiply_subtract_fusion = (f32[32,64,128]{2,1,0:T(8,128)}, f32[32,64,128]{2,1,0:T(8,128)}) fusion(f32[32,64,128]{2,1,0:T(8,128)} %get-tuple-element.22, f32[32,64,128]{2,1,0:T(8,128)} %get-tuple-element.23, f32[]{:T(128)S(6)} %div.21, f32[]{:T(128)S(6)} %div.23, f32[32,64,128]{2,1,0:T(8,128)} %copy-done.1, f32[]{:T(128)S(6)} %div.20, ...), kind=kLoop, calls=%fused_computation.65 | loop fusion | flops 3145728 | bytes 8388620 | tf_op jit(solution)/shard_map/sub | solution.py:181
  (75 shorter events, 42.6 us)
Async XLA Ops:
  5.6 20.6 %all-to-all-start = ((s32[128,1,6]{2,1,0:T(1,128)}), s32[128,1,6]{2,1,0:T(1,128)S(1)}, u32[]{:S(2)}, u32[]{:S(2)}) async-start(s32[128,1,6]{2,1,0:T(1,128)} %bitcast.7), calls=%async_computation | async-start | bytes 131072 | tf_op jit(solution)/shard_map/all_to_all | solution.py:147
  26.2 46.9 %all-to-all-start.1 = ((bf16[128,6,1536]{2,1,0:T(8,128)(2,1)}), bf16[128,6,1536]{2,1,0:T(8,128)(2,1)}, u32[]{:S(2)}, u32[]{:S(2)}) async-start(bf16[128,6,1536]{2,1,0:T(8,128)(2,1)} %reshape.37), calls=%async_computation.1 | async-start | bytes 6291456 | tf_op jit(solution)/shard_map/all_to_all | solution.py:144
  32.8 174.7 %collective-permute-start.6 = (f32[32,1,128]{2,1,0:T(1,128)S(1)}, f32[32,1,128]{2,1,0:T(1,128)S(1)}, u32[]{:S(2)}, u32[]{:S(2)}) collective-permute-start(f32[32,1,128]{2,1,0:T(1,128)S(1)} %get-tuple-element.47), channel_id=1, source_target_pairs={{1,0},{2,1},{3,2},{4,3},{5,4},{6,5},{7,6},{8,7},{9,8},{10,9},{11,1... | collective-permute-start | bytes 49160 | tf_op jit(solution)/shard_map/ppermute | solution.py:24
  34.1 176.8 %collective-permute-start.7 = (f32[32,1,128]{2,1,0:T(1,128)S(1)}, f32[32,1,128]{2,1,0:T(1,128)S(1)}, u32[]{:S(2)}, u32[]{:S(2)}) collective-permute-start(f32[32,1,128]{2,1,0:T(1,128)S(1)} %get-tuple-element.48), channel_id=1, source_target_pairs={{0,1},{1,2},{2,3},{3,4},{4,5},{5,6},{6,7},{7,8},{8,9},{9,10},{10,1... | collective-permute-start | bytes 49160 | tf_op jit(solution)/shard_map/ppermute | solution.py:23
  38.7 8.9 %collective-permute-start.4 = (f32[1,64,128]{2,1,0:T(8,128)S(1)}, f32[1,64,128]{2,1,0:T(8,128)S(1)}, u32[]{:S(2)}, u32[]{:S(2)}) collective-permute-start(f32[1,64,128]{2,1,0:T(8,128)S(1)} %get-tuple-element.49), channel_id=1, source_target_pairs={{16,0},{32,16},{48,32},{64,48},{80,64},{96,80},{112,96},{17,1},{33... | collective-permute-start | bytes 98312 | tf_op jit(solution)/shard_map/ppermute | solution.py:24
  40.0 5.8 %collective-permute-start.5 = (f32[1,64,128]{2,1,0:T(8,128)S(1)}, f32[1,64,128]{2,1,0:T(8,128)S(1)}, u32[]{:S(2)}, u32[]{:S(2)}) collective-permute-start(f32[1,64,128]{2,1,0:T(8,128)S(1)} %get-tuple-element.50), channel_id=1, source_target_pairs={{0,16},{16,32},{32,48},{48,64},{64,80},{80,96},{96,112},{1,17},{17... | collective-permute-start | bytes 98312 | tf_op jit(solution)/shard_map/ppermute | solution.py:23
  199.4 12.0 %copy-start.3 = (f32[32,64,128]{2,1,0:T(8,128)S(1)}, f32[32,64,128]{2,1,0:T(8,128)}, u32[]{:S(2)}) copy-start(f32[32,64,128]{2,1,0:T(8,128)} %param.8) | copy-start | bytes 3145732
  199.4 12.0 %copy-start.6 = (f32[32,64,127]{2,1,0:T(8,128)S(1)}, f32[32,64,127]{2,1,0:T(8,128)}, u32[]{:S(2)}) copy-start(f32[32,64,127]{2,1,0:T(8,128)} %get-tuple-element.52) | copy-start | bytes 3121156
  200.4 10.6 %collective-permute-start.2 = (f32[32,1,128]{2,1,0:T(1,128)S(1)}, f32[32,1,128]{2,1,0:T(1,128)S(1)}, u32[]{:S(2)}, u32[]{:S(2)}) collective-permute-start(f32[32,1,128]{2,1,0:T(1,128)S(1)} %get-tuple-element.43), channel_id=1, source_target_pairs={{1,0},{2,1},{3,2},{4,3},{5,4},{6,5},{7,6},{8,7},{9,8},{10,9},{11,1... | collective-permute-start | bytes 49160 | tf_op jit(solution)/shard_map/ppermute | solution.py:49
  201.7 9.3 %collective-permute-start.3 = (f32[32,1,128]{2,1,0:T(1,128)S(1)}, f32[32,1,128]{2,1,0:T(1,128)S(1)}, u32[]{:S(2)}, u32[]{:S(2)}) collective-permute-start(f32[32,1,128]{2,1,0:T(1,128)S(1)} %get-tuple-element.44), channel_id=1, source_target_pairs={{0,1},{1,2},{2,3},{3,4},{4,5},{5,6},{6,7},{7,8},{8,9},{9,10},{10,1... | collective-permute-start | bytes 49160 | tf_op jit(solution)/shard_map/ppermute | solution.py:46
  206.2 4.7 %collective-permute-start = (f32[1,64,128]{2,1,0:T(8,128)S(1)}, f32[1,64,128]{2,1,0:T(8,128)S(1)}, u32[]{:S(2)}, u32[]{:S(2)}) collective-permute-start(f32[1,64,128]{2,1,0:T(8,128)S(1)} %get-tuple-element.26), channel_id=1, source_target_pairs={{16,0},{32,16},{48,32},{64,48},{80,64},{96,80},{112,96},{17,1},{33... | collective-permute-start | bytes 98312 | tf_op jit(solution)/shard_map/ppermute | solution.py:49
  207.5 3.9 %collective-permute-start.1 = (f32[1,64,128]{2,1,0:T(8,128)S(1)}, f32[1,64,128]{2,1,0:T(8,128)S(1)}, u32[]{:S(2)}, u32[]{:S(2)}) collective-permute-start(f32[1,64,128]{2,1,0:T(8,128)S(1)} %get-tuple-element.27), channel_id=1, source_target_pairs={{0,16},{16,32},{32,48},{48,64},{64,80},{80,96},{96,112},{1,17},{17... | collective-permute-start | bytes 98312 | tf_op jit(solution)/shard_map/ppermute | solution.py:46
  214.9 15.7 %copy-start.1 = (f32[32,64,128]{2,1,0:T(8,128)}, f32[32,64,128]{2,1,0:T(8,128)S(1)}, u32[]{:S(2)}) copy-start(f32[32,64,128]{2,1,0:T(8,128)S(1)} %get-tuple-element.25) | copy-start | bytes 3145732
  215.0 9.4 %collective-permute-start.10 = (f32[32,1,128]{2,1,0:T(1,128)S(1)}, f32[32,1,128]{2,1,0:T(1,128)S(1)}, u32[]{:S(2)}, u32[]{:S(2)}) collective-permute-start(f32[32,1,128]{2,1,0:T(1,128)S(1)} %get-tuple-element.37), channel_id=1, source_target_pairs={{1,0},{2,1},{3,2},{4,3},{5,4},{6,5},{7,6},{8,7},{9,8},{10,9},{11,1... | collective-permute-start | bytes 49160 | tf_op jit(solution)/shard_map/ppermute | solution.py:24
  216.3 8.1 %collective-permute-start.11 = (f32[32,1,128]{2,1,0:T(1,128)S(1)}, f32[32,1,128]{2,1,0:T(1,128)S(1)}, u32[]{:S(2)}, u32[]{:S(2)}) collective-permute-start(f32[32,1,128]{2,1,0:T(1,128)S(1)} %get-tuple-element.38), channel_id=1, source_target_pairs={{0,1},{1,2},{2,3},{3,4},{4,5},{5,6},{6,7},{7,8},{8,9},{9,10},{10,1... | collective-permute-start | bytes 49160 | tf_op jit(solution)/shard_map/ppermute | solution.py:23
  220.9 3.6 %collective-permute-start.9 = (f32[1,64,128]{2,1,0:T(8,128)S(1)}, f32[1,64,128]{2,1,0:T(8,128)S(1)}, u32[]{:S(2)}, u32[]{:S(2)}) collective-permute-start(f32[1,64,128]{2,1,0:T(8,128)S(1)} %get-tuple-element.39), channel_id=1, source_target_pairs={{0,16},{16,32},{32,48},{48,64},{64,80},{80,96},{96,112},{1,17},{17... | collective-permute-start | bytes 98312 | tf_op jit(solution)/shard_map/ppermute | solution.py:23
  222.7 5.5 %collective-permute-start.8 = (f32[1,64,128]{2,1,0:T(8,128)S(1)}, f32[1,64,128]{2,1,0:T(8,128)S(1)}, u32[]{:S(2)}, u32[]{:S(2)}) collective-permute-start(f32[1,64,128]{2,1,0:T(8,128)S(1)} %get-tuple-element.40), channel_id=1, source_target_pairs={{16,0},{32,16},{48,32},{64,48},{80,64},{96,80},{112,96},{17,1},{33... | collective-permute-start | bytes 98312 | tf_op jit(solution)/shard_map/ppermute | solution.py:24
  271.9 10.6 %copy-start.2 = (f32[32,64,128]{2,1,0:T(8,128)S(1)}, f32[32,64,128]{2,1,0:T(8,128)}, u32[]{:S(2)}) copy-start(f32[32,64,128]{2,1,0:T(8,128)} %copy-done.1) | copy-start | bytes 3145732
  271.9 10.6 %copy-start.4 = (f32[32,64,128]{2,1,0:T(8,128)S(1)}, f32[32,64,128]{2,1,0:T(8,128)}, u32[]{:S(2)}) copy-start(f32[32,64,128]{2,1,0:T(8,128)} %param.8) | copy-start | bytes 3145732
  271.9 10.6 %copy-start.5 = (f32[32,64,128]{2,1,0:T(8,128)S(1)}, f32[32,64,128]{2,1,0:T(8,128)}, u32[]{:S(2)}) copy-start(f32[32,64,128]{2,1,0:T(8,128)} %get-tuple-element.23) | copy-start | bytes 3145732
  272.0 9.1 %collective-permute-start.14 = (f32[32,1,128]{2,1,0:T(1,128)S(1)}, f32[32,1,128]{2,1,0:T(1,128)S(1)}, u32[]{:S(2)}, u32[]{:S(2)}) collective-permute-start(f32[32,1,128]{2,1,0:T(1,128)S(1)} %get-tuple-element.31), channel_id=1, source_target_pairs={{1,0},{2,1},{3,2},{4,3},{5,4},{6,5},{7,6},{8,7},{9,8},{10,9},{11,1... | collective-permute-start | bytes 49160 | tf_op jit(solution)/shard_map/ppermute | solution.py:24
  273.5 7.5 %collective-permute-start.15 = (f32[32,1,128]{2,1,0:T(1,128)S(1)}, f32[32,1,128]{2,1,0:T(1,128)S(1)}, u32[]{:S(2)}, u32[]{:S(2)}) collective-permute-start(f32[32,1,128]{2,1,0:T(1,128)S(1)} %get-tuple-element.32), channel_id=1, source_target_pairs={{0,1},{1,2},{2,3},{3,4},{4,5},{5,6},{6,7},{7,8},{8,9},{9,10},{10,1... | collective-permute-start | bytes 49160 | tf_op jit(solution)/shard_map/ppermute | solution.py:23
  278.1 3.0 collective-permute-start.13
  279.4 3.1 collective-permute-start.12
  (1 other events, 10.2 us)

commit v3 on v2

--- a/solution.py
+++ b/solution.py
@@ -109,22 +109,24 @@
         return x
 
     def step(i, carry):
-        uh = i % 4
-        c = (i // 4) % 3
-        ly = (i // 12) % 8
-        lx = i // 96
-        row = pl.multiple_of((lx * 8 + ly) * 16, 16)
-        col = pl.multiple_of((c * 4 + uh) * 128, 128)
-        s0 = blk_ref[pl.ds(row, 8), pl.ds(col, 128)]
-        s1 = blk_ref[pl.ds(row + 8, 8), pl.ds(col, 128)]
-        u0 = jnp.where(low_half, s0, pltpu.roll(s1, 64, 1))
-        u1 = jnp.where(low_half, pltpu.roll(s0, 64, 1), s1)
+        ly = i % 8
+        lx = i // 8
+        row = pl.multiple_of(i * 16, 16)
         y = pl.multiple_of(ly * 8, 8)
-        out_ref[c, lx * 8 + uh * 2, pl.ds(y, 8), :] = transpose_groups(u0)
-        out_ref[c, lx * 8 + uh * 2 + 1, pl.ds(y, 8), :] = transpose_groups(u1)
+        top = blk_ref[pl.ds(row, 8), :]
+        bottom = blk_ref[pl.ds(row + 8, 8), :]
+        for c in range(3):
+            for uh in range(4):
+                col = (c * 4 + uh) * 128
+                s0 = top[:, col:col + 128]
+                s1 = bottom[:, col:col + 128]
+                u0 = jnp.where(low_half, s0, pltpu.roll(s1, 64, 1))
+                u1 = jnp.where(low_half, pltpu.roll(s0, 64, 1), s1)
+                out_ref[c, lx * 8 + uh * 2, pl.ds(y, 8), :] = transpose_groups(u0)
+                out_ref[c, lx * 8 + uh * 2 + 1, pl.ds(y, 8), :] = transpose_groups(u1)
         return carry
 
-    lax.fori_loop(0, 384, step, 0)
+    lax.fori_loop(0, 32, step, 0)
 
 
 def to_grid(blocks, span_x, span_y, depth):

time: 328 us -> 229 us (0.70)
  Pallas kernels: 114 us -> 14.7 us
    pallas_call x1, Pallas kernels: 114 us -> 14.7 us  [to_grid(): pl.pallas_call(relayout_kernel, out_shape=jax.ShapeDtypeStruct((3, span_x...]
  transfers between devices with their start and end apart: 18 -> 18, of which waited for: 5 -> 5; matrix products, arithmetic and copies ran while one was open for 8% -> 11% of each run, Pallas kernels for 35% -> 6%
where the time goes in v3:
time: 229 us; the launch traced here: 228 us
  blocking collectives  71.6 us (31%)
  starting transfers between devices  55.7 us (24%)
  waiting for transfers between devices  34.2 us (15%)
  local copies, waits for them, and re-layouts  22.5 us (10%)
  other arithmetic  17.2 us (8%)
  Pallas kernels  14.7 us (6%)
  between operations  6.84 us (3%)
  matrix products  4.83 us (2%)
    psum x8, blocking collectives, over_axes(): shard = lax.psum(shard, axis)  71.6 us
    all_to_all x1, waiting for transfers between devices, body(): lax.all_to_all(payload.reshape(peers, capacity, 1536), GX_GY, split_axis=...  24.9 us
    ppermute x6, starting transfers between devices, extended(): lax.ppermute(last, axis, up)  19.8 us
    pallas_call x1, Pallas kernels, to_grid(): pl.pallas_call(relayout_kernel, out_shape=jax.ShapeDtypeStruct((3, span_x...  14.7 us
    all_to_all x1, starting transfers between devices, body(): lax.all_to_all(slots.reshape(peers, capacity), GX_GY, split_axis=0, conca...  11.2 us
    ppermute x6, starting transfers between devices, extended(): lax.ppermute(first, axis, [(b, a) for a, b in up])  8.02 us
    ppermute x2, starting transfers between devices, with_halo(): lax.ppermute(lax.slice_in_dim(block, block.shape[dim] - width, None, axis...  7.58 us
    all_to_all x1, starting transfers between devices, body(): lax.all_to_all(payload.reshape(peers, capacity, 1536), GX_GY, split_axis=...  6.54 us
  transfers between devices with their start and end apart: 18, of which 5 were waited for; matrix products, arithmetic and copies ran while one was open for 11% of the time, Pallas kernels for 6%

profile of v3, /device:TPU:0, one launch (start us, length us, event | category | flops | bytes accessed | tf_op | source)
XLA Modules:
  0.0 227.6 jit_solution(15866204321261008192)
XLA Ops:
  5.6 11.2 %all-to-all-start = ((s32[128,1,6]{2,1,0:T(1,128)}), s32[128,1,6]{2,1,0:T(1,128)S(1)}, u32[]{:S(2)}, u32[]{:S(2)}) async-start(s32[128,1,6]{2,1,0:T(1,128)} %bitcast.7), calls=%async_computation | async-start | bytes 131072 | tf_op jit(solution)/shard_map/all_to_all | solution.py:149
  16.8 3.2 %scatter_custom_fusion.1 = bf16[768,1536]{1,0:T(8,128)(2,1)S(1)} fusion(s32[256]{0:T(256)S(1)} %bitcast.38, bf16[256,1536]{1,0:T(8,128)(2,1)} %param.5, bf16[]{:T(256)} %constant.11.clone.1), kind=kCustom, calls=%fused_computation.4 | custom fusion | bytes 2359808 | tf_op jit(solution)/shard_map/scatter | solution.py:60
  22.5 3.7 %all-to-all-done = s32[128,1,6]{2,1,0:T(1,128)S(1)} async-done(((s32[128,1,6]{2,1,0:T(1,128)}), s32[128,1,6]{2,1,0:T(1,128)S(1)}, u32[]{:S(2)}, u32[]{:S(2)}) %all-to-all-start) | async-done | bytes 3104 | tf_op jit(solution)/shard_map/all_to_all | solution.py:149
  26.2 6.5 %all-to-all-start.1 = ((bf16[128,6,1536]{2,1,0:T(8,128)(2,1)}), bf16[128,6,1536]{2,1,0:T(8,128)(2,1)}, u32[]{:S(2)}, u32[]{:S(2)}) async-start(bf16[128,6,1536]{2,1,0:T(8,128)(2,1)} %reshape.37), calls=%async_computation.1 | async-start | bytes 6291456 | tf_op jit(solution)/shard_map/all_to_all | solution.py:146
  34.1 4.5 %collective-permute-start.7 = (f32[32,1,128]{2,1,0:T(1,128)S(1)}, f32[32,1,128]{2,1,0:T(1,128)S(1)}, u32[]{:S(2)}, u32[]{:S(2)}) collective-permute-start(f32[32,1,128]{2,1,0:T(1,128)S(1)} %get-tuple-element.48), channel_id=1, source_target_pairs={{0,1},{1,2},{2,3},{3,4},{4,5},{5,6},{6,7},{7,8},{8,9},{9,10},{10,1... | collective-permute-start | bytes 49160 | tf_op jit(solution)/shard_map/ppermute | solution.py:23
  48.2 24.9 %all-to-all-done.1 = bf16[128,6,1536]{2,1,0:T(8,128)(2,1)} async-done(((bf16[128,6,1536]{2,1,0:T(8,128)(2,1)}), bf16[128,6,1536]{2,1,0:T(8,128)(2,1)}, u32[]{:S(2)}, u32[]{:S(2)}) %all-to-all-start.1) | async-done | bytes 2359328 | tf_op jit(solution)/shard_map/all_to_all | solution.py:146
  73.1 5.0 %reshape.38 = bf16[768,1536]{1,0:T(8,128)(2,1)} reshape(bf16[128,6,1536]{2,1,0:T(8,128)(2,1)} %all-to-all-done.1) | data formatting | bytes 4718592 | tf_op jit(solution)/shard_map/reshape | solution.py:161
  78.1 4.8 %fusion.blk_ref = f32[512,1536]{1,0:T(8,128)} fusion(bf16[768,1536]{1,0:T(8,128)(2,1)} %reshape.38, s32[768]{0:T(1024)S(1)} %eq.48), kind=kOutput, calls=%fused_computation.3 | convolution fusion | flops 1208352768 | bytes 5508096 | tf_op jit(solution)/shard_map/ks,kj->sj/dot_general | solution.py:158
  82.9 14.7 %shard_map.68 = f32[3,32,64,128]{3,2,1,0:T(8,128)} custom-call(f32[512,1536]{1,0:T(8,128)} %fusion.blk_ref), custom_call_target="tpu_custom_call" | custom-call | tf_op jit(solution)/shard_map/pallas_call | solution.py:133
  102.0 4.5 %collective-permute-start.3 = (f32[32,1,128]{2,1,0:T(1,128)S(1)}, f32[32,1,128]{2,1,0:T(1,128)S(1)}, u32[]{:S(2)}, u32[]{:S(2)}) collective-permute-start(f32[32,1,128]{2,1,0:T(1,128)S(1)} %get-tuple-element.44), channel_id=1, source_target_pairs={{0,1},{1,2},{2,3},{3,4},{4,5},{5,6},{6,7},{7,8},{8,9},{9,10},{10,1... | collective-permute-start | bytes 49160 | tf_op jit(solution)/shard_map/ppermute | solution.py:46
  107.9 3.0 %collective-permute-start.1 = (f32[1,64,128]{2,1,0:T(8,128)S(1)}, f32[1,64,128]{2,1,0:T(8,128)S(1)}, u32[]{:S(2)}, u32[]{:S(2)}) collective-permute-start(f32[1,64,128]{2,1,0:T(8,128)S(1)} %get-tuple-element.27), channel_id=1, source_target_pairs={{0,16},{16,32},{32,48},{48,64},{64,80},{80,96},{96,112},{1,17},{17... | collective-permute-start | bytes 98312 | tf_op jit(solution)/shard_map/ppermute | solution.py:46
  111.8 3.5 %fusion.33 = (f32[32,64,128]{2,1,0:T(8,128)S(1)}, f32[32,64,128]{2,1,0:T(8,128)S(1)}) fusion(f32[32,64,128]{2,1,0:T(8,128)S(1)} %copy-done.3, f32[32,64,127]{2,1,0:T(8,128)S(1)} %copy-done.6, f32[32,64,127]{2,1,0:T(8,128)S(1)} %get-tuple-element.51, f32[34,64,128]{2,1,0:T(8,128)} %constant_dynamic-update-slice_fusion, ...), kind=kLoop, calls=%fused_computation.75 | loop fusion | flops 8126464 | bytes 11763712 | tf_op jit(solution)/shard_map/mul | solution.py:175
  116.6 4.5 %collective-permute-start.11 = (f32[32,1,128]{2,1,0:T(1,128)S(1)}, f32[32,1,128]{2,1,0:T(1,128)S(1)}, u32[]{:S(2)}, u32[]{:S(2)}) collective-permute-start(f32[32,1,128]{2,1,0:T(1,128)S(1)} %get-tuple-element.38), channel_id=1, source_target_pairs={{0,1},{1,2},{2,3},{3,4},{4,5},{5,6},{6,7},{7,8},{8,9},{9,10},{10,1... | collective-permute-start | bytes 49160 | tf_op jit(solution)/shard_map/ppermute | solution.py:23
  124.8 3.8 %collective-permute-done.8 = f32[1,64,128]{2,1,0:T(8,128)S(1)} collective-permute-done((f32[1,64,128]{2,1,0:T(8,128)S(1)}, f32[1,64,128]{2,1,0:T(8,128)S(1)}, u32[]{:S(2)}, u32[]{:S(2)}) %collective-permute-start.8) | collective-permute-done | bytes 32800 | tf_op jit(solution)/shard_map/ppermute | solution.py:24
  131.0 11.5 %all-reduce.19 = (f32[]{:T(128)}, f32[]{:T(128)}) all-reduce(f32[]{:T(128)} %get-tuple-element.5, f32[]{:T(128)} %get-tuple-element.4), channel_id=1, replica_groups=mesh['gx_0'=4,'gx_1'=2,'gy_0'=4,'gy_1'=4] {'gx_0'}, use_global_device_ids=true, to_apply=%region_6.7 | all-reduce | flops 2 | bytes 16 | tf_op jit(solution)/shard_map/psum | solution.py:37
  142.5 3.1 %all-reduce.21 = (f32[]{:T(128)}, f32[]{:T(128)}) all-reduce(f32[]{:T(128)} %get-tuple-element.16, f32[]{:T(128)} %get-tuple-element.17), channel_id=1, replica_groups=mesh['gx_0'=4,'gx_1'=2,'gy_0'=4,'gy_1'=4] {'gx_1'}, use_global_device_ids=true, to_apply=%region_7.8 | all-reduce | flops 2 | bytes 16 | tf_op jit(solution)/shard_map/psum | solution.py:37
  145.6 12.4 %all-reduce.17 = (f32[]{:T(128)}, f32[]{:T(128)}) all-reduce(f32[]{:T(128)} %get-tuple-element.20, f32[]{:T(128)} %get-tuple-element.21), channel_id=1, replica_groups=mesh['gx_0'=4,'gx_1'=2,'gy_0'=4,'gy_1'=4] {'gy_0'}, use_global_device_ids=true, to_apply=%region_8.9 | all-reduce | flops 2 | bytes 16 | tf_op jit(solution)/shard_map/psum | solution.py:37
  158.0 10.7 %all-reduce.15 = (f32[]{:T(128)}, f32[]{:T(128)}) all-reduce(f32[]{:T(128)} %get-tuple-element.12, f32[]{:T(128)} %get-tuple-element.13), channel_id=1, replica_groups=mesh['gx_0'=4,'gx_1'=2,'gy_0'=4,'gy_1'=4] {'gy_1'}, use_global_device_ids=true, to_apply=%region_9.10 | all-reduce | flops 2 | bytes 16 | tf_op jit(solution)/shard_map/psum | solution.py:37
  173.8 4.5 %collective-permute-start.15 = (f32[32,1,128]{2,1,0:T(1,128)S(1)}, f32[32,1,128]{2,1,0:T(1,128)S(1)}, u32[]{:S(2)}, u32[]{:S(2)}) collective-permute-start(f32[32,1,128]{2,1,0:T(1,128)S(1)} %get-tuple-element.32), channel_id=1, source_target_pairs={{0,1},{1,2},{2,3},{3,4},{4,5},{5,6},{6,7},{7,8},{8,9},{9,10},{10,1... | collective-permute-start | bytes 49160 | tf_op jit(solution)/shard_map/ppermute | solution.py:23
  185.4 10.9 %all-reduce.18 = (f32[]{:T(128)}, f32[]{:T(128)}) all-reduce(f32[]{:T(128)} %get-tuple-element.3, f32[]{:T(128)} %get-tuple-element.2), channel_id=1, replica_groups=mesh['gx_0'=4,'gx_1'=2,'gy_0'=4,'gy_1'=4] {'gx_0'}, use_global_device_ids=true, to_apply=%region_16.17 | all-reduce | flops 2 | bytes 16 | tf_op jit(solution)/shard_map/psum | solution.py:37
  196.2 3.1 %all-reduce.20 = (f32[]{:T(128)}, f32[]{:T(128)}) all-reduce(f32[]{:T(128)} %get-tuple-element.14, f32[]{:T(128)} %get-tuple-element.15), channel_id=1, replica_groups=mesh['gx_0'=4,'gx_1'=2,'gy_0'=4,'gy_1'=4] {'gx_1'}, use_global_device_ids=true, to_apply=%region_17.18 | all-reduce | flops 2 | bytes 16 | tf_op jit(solution)/shard_map/psum | solution.py:37
  199.4 9.5 %all-reduce.16 = (f32[]{:T(128)}, f32[]{:T(128)}) all-reduce(f32[]{:T(128)} %get-tuple-element.18, f32[]{:T(128)} %get-tuple-element.19), channel_id=1, replica_groups=mesh['gx_0'=4,'gx_1'=2,'gy_0'=4,'gy_1'=4] {'gy_0'}, use_global_device_ids=true, to_apply=%region_18.19 | all-reduce | flops 2 | bytes 16 | tf_op jit(solution)/shard_map/psum | solution.py:37
  208.9 10.3 %all-reduce.14 = (f32[]{:T(128)}, f32[]{:T(128)}) all-reduce(f32[]{:T(128)} %get-tuple-element.10, f32[]{:T(128)} %get-tuple-element.11), channel_id=1, replica_groups=mesh['gx_0'=4,'gx_1'=2,'gy_0'=4,'gy_1'=4] {'gy_1'}, use_global_device_ids=true, to_apply=%region_19.20 | all-reduce | flops 2 | bytes 16 | tf_op jit(solution)/shard_map/psum | solution.py:37
  223.7 3.9 %multiply_subtract_fusion = (f32[32,64,128]{2,1,0:T(8,128)}, f32[32,64,128]{2,1,0:T(8,128)}) fusion(f32[32,64,128]{2,1,0:T(8,128)} %get-tuple-element.22, f32[32,64,128]{2,1,0:T(8,128)} %get-tuple-element.23, f32[]{:T(128)S(6)} %div.21, f32[]{:T(128)S(6)} %div.23, f32[32,64,128]{2,1,0:T(8,128)} %copy-done.1, f32[]{:T(128)S(6)} %div.20, ...), kind=kLoop, calls=%fused_computation.65 | loop fusion | flops 3145728 | bytes 8388620 | tf_op jit(solution)/shard_map/sub | solution.py:183
  (75 shorter events, 42.6 us)
Async XLA Ops:
  5.6 20.6 %all-to-all-start = ((s32[128,1,6]{2,1,0:T(1,128)}), s32[128,1,6]{2,1,0:T(1,128)S(1)}, u32[]{:S(2)}, u32[]{:S(2)}) async-start(s32[128,1,6]{2,1,0:T(1,128)} %bitcast.7), calls=%async_computation | async-start | bytes 131072 | tf_op jit(solution)/shard_map/all_to_all | solution.py:149
  26.2 46.9 %all-to-all-start.1 = ((bf16[128,6,1536]{2,1,0:T(8,128)(2,1)}), bf16[128,6,1536]{2,1,0:T(8,128)(2,1)}, u32[]{:S(2)}, u32[]{:S(2)}) async-start(bf16[128,6,1536]{2,1,0:T(8,128)(2,1)} %reshape.37), calls=%async_computation.1 | async-start | bytes 6291456 | tf_op jit(solution)/shard_map/all_to_all | solution.py:146
  32.8 75.1 %collective-permute-start.6 = (f32[32,1,128]{2,1,0:T(1,128)S(1)}, f32[32,1,128]{2,1,0:T(1,128)S(1)}, u32[]{:S(2)}, u32[]{:S(2)}) collective-permute-start(f32[32,1,128]{2,1,0:T(1,128)S(1)} %get-tuple-element.47), channel_id=1, source_target_pairs={{1,0},{2,1},{3,2},{4,3},{5,4},{6,5},{7,6},{8,7},{9,8},{10,9},{11,1... | collective-permute-start | bytes 49160 | tf_op jit(solution)/shard_map/ppermute | solution.py:24
  34.1 77.2 %collective-permute-start.7 = (f32[32,1,128]{2,1,0:T(1,128)S(1)}, f32[32,1,128]{2,1,0:T(1,128)S(1)}, u32[]{:S(2)}, u32[]{:S(2)}) collective-permute-start(f32[32,1,128]{2,1,0:T(1,128)S(1)} %get-tuple-element.48), channel_id=1, source_target_pairs={{0,1},{1,2},{2,3},{3,4},{4,5},{5,6},{6,7},{7,8},{8,9},{9,10},{10,1... | collective-permute-start | bytes 49160 | tf_op jit(solution)/shard_map/ppermute | solution.py:23
  38.7 8.9 %collective-permute-start.4 = (f32[1,64,128]{2,1,0:T(8,128)S(1)}, f32[1,64,128]{2,1,0:T(8,128)S(1)}, u32[]{:S(2)}, u32[]{:S(2)}) collective-permute-start(f32[1,64,128]{2,1,0:T(8,128)S(1)} %get-tuple-element.49), channel_id=1, source_target_pairs={{16,0},{32,16},{48,32},{64,48},{80,64},{96,80},{112,96},{17,1},{33... | collective-permute-start | bytes 98312 | tf_op jit(solution)/shard_map/ppermute | solution.py:24
  40.0 5.8 %collective-permute-start.5 = (f32[1,64,128]{2,1,0:T(8,128)S(1)}, f32[1,64,128]{2,1,0:T(8,128)S(1)}, u32[]{:S(2)}, u32[]{:S(2)}) collective-permute-start(f32[1,64,128]{2,1,0:T(8,128)S(1)} %get-tuple-element.50), channel_id=1, source_target_pairs={{0,16},{16,32},{32,48},{48,64},{64,80},{80,96},{96,112},{1,17},{17... | collective-permute-start | bytes 98312 | tf_op jit(solution)/shard_map/ppermute | solution.py:23
  99.7 12.0 %copy-start.3 = (f32[32,64,128]{2,1,0:T(8,128)S(1)}, f32[32,64,128]{2,1,0:T(8,128)}, u32[]{:S(2)}) copy-start(f32[32,64,128]{2,1,0:T(8,128)} %param.8) | copy-start | bytes 3145732
  99.8 12.0 %copy-start.6 = (f32[32,64,127]{2,1,0:T(8,128)S(1)}, f32[32,64,127]{2,1,0:T(8,128)}, u32[]{:S(2)}) copy-start(f32[32,64,127]{2,1,0:T(8,128)} %get-tuple-element.52) | copy-start | bytes 3121156
  100.7 10.6 %collective-permute-start.2 = (f32[32,1,128]{2,1,0:T(1,128)S(1)}, f32[32,1,128]{2,1,0:T(1,128)S(1)}, u32[]{:S(2)}, u32[]{:S(2)}) collective-permute-start(f32[32,1,128]{2,1,0:T(1,128)S(1)} %get-tuple-element.43), channel_id=1, source_target_pairs={{1,0},{2,1},{3,2},{4,3},{5,4},{6,5},{7,6},{8,7},{9,8},{10,9},{11,1... | collective-permute-start | bytes 49160 | tf_op jit(solution)/shard_map/ppermute | solution.py:49
  102.0 9.3 %collective-permute-start.3 = (f32[32,1,128]{2,1,0:T(1,128)S(1)}, f32[32,1,128]{2,1,0:T(1,128)S(1)}, u32[]{:S(2)}, u32[]{:S(2)}) collective-permute-start(f32[32,1,128]{2,1,0:T(1,128)S(1)} %get-tuple-element.44), channel_id=1, source_target_pairs={{0,1},{1,2},{2,3},{3,4},{4,5},{5,6},{6,7},{7,8},{8,9},{9,10},{10,1... | collective-permute-start | bytes 49160 | tf_op jit(solution)/shard_map/ppermute | solution.py:46
  106.6 4.7 %collective-permute-start = (f32[1,64,128]{2,1,0:T(8,128)S(1)}, f32[1,64,128]{2,1,0:T(8,128)S(1)}, u32[]{:S(2)}, u32[]{:S(2)}) collective-permute-start(f32[1,64,128]{2,1,0:T(8,128)S(1)} %get-tuple-element.26), channel_id=1, source_target_pairs={{16,0},{32,16},{48,32},{64,48},{80,64},{96,80},{112,96},{17,1},{33... | collective-permute-start | bytes 98312 | tf_op jit(solution)/shard_map/ppermute | solution.py:49
  107.9 3.9 %collective-permute-start.1 = (f32[1,64,128]{2,1,0:T(8,128)S(1)}, f32[1,64,128]{2,1,0:T(8,128)S(1)}, u32[]{:S(2)}, u32[]{:S(2)}) collective-permute-start(f32[1,64,128]{2,1,0:T(8,128)S(1)} %get-tuple-element.27), channel_id=1, source_target_pairs={{0,16},{16,32},{32,48},{48,64},{64,80},{80,96},{96,112},{1,17},{17... | collective-permute-start | bytes 98312 | tf_op jit(solution)/shard_map/ppermute | solution.py:46
  115.3 15.7 %copy-start.1 = (f32[32,64,128]{2,1,0:T(8,128)}, f32[32,64,128]{2,1,0:T(8,128)S(1)}, u32[]{:S(2)}) copy-start(f32[32,64,128]{2,1,0:T(8,128)S(1)} %get-tuple-element.25) | copy-start | bytes 3145732
  115.3 9.4 %collective-permute-start.10 = (f32[32,1,128]{2,1,0:T(1,128)S(1)}, f32[32,1,128]{2,1,0:T(1,128)S(1)}, u32[]{:S(2)}, u32[]{:S(2)}) collective-permute-start(f32[32,1,128]{2,1,0:T(1,128)S(1)} %get-tuple-element.37), channel_id=1, source_target_pairs={{1,0},{2,1},{3,2},{4,3},{5,4},{6,5},{7,6},{8,7},{9,8},{10,9},{11,1... | collective-permute-start | bytes 49160 | tf_op jit(solution)/shard_map/ppermute | solution.py:24
  116.6 8.1 %collective-permute-start.11 = (f32[32,1,128]{2,1,0:T(1,128)S(1)}, f32[32,1,128]{2,1,0:T(1,128)S(1)}, u32[]{:S(2)}, u32[]{:S(2)}) collective-permute-start(f32[32,1,128]{2,1,0:T(1,128)S(1)} %get-tuple-element.38), channel_id=1, source_target_pairs={{0,1},{1,2},{2,3},{3,4},{4,5},{5,6},{6,7},{7,8},{8,9},{9,10},{10,1... | collective-permute-start | bytes 49160 | tf_op jit(solution)/shard_map/ppermute | solution.py:23
  121.2 3.6 %collective-permute-start.9 = (f32[1,64,128]{2,1,0:T(8,128)S(1)}, f32[1,64,128]{2,1,0:T(8,128)S(1)}, u32[]{:S(2)}, u32[]{:S(2)}) collective-permute-start(f32[1,64,128]{2,1,0:T(8,128)S(1)} %get-tuple-element.39), channel_id=1, source_target_pairs={{0,16},{16,32},{32,48},{48,64},{64,80},{80,96},{96,112},{1,17},{17... | collective-permute-start | bytes 98312 | tf_op jit(solution)/shard_map/ppermute | solution.py:23
  123.1 5.5 %collective-permute-start.8 = (f32[1,64,128]{2,1,0:T(8,128)S(1)}, f32[1,64,128]{2,1,0:T(8,128)S(1)}, u32[]{:S(2)}, u32[]{:S(2)}) collective-permute-start(f32[1,64,128]{2,1,0:T(8,128)S(1)} %get-tuple-element.40), channel_id=1, source_target_pairs={{16,0},{32,16},{48,32},{64,48},{80,64},{96,80},{112,96},{17,1},{33... | collective-permute-start | bytes 98312 | tf_op jit(solution)/shard_map/ppermute | solution.py:24
  172.2 10.6 %copy-start.2 = (f32[32,64,128]{2,1,0:T(8,128)S(1)}, f32[32,64,128]{2,1,0:T(8,128)}, u32[]{:S(2)}) copy-start(f32[32,64,128]{2,1,0:T(8,128)} %copy-done.1) | copy-start | bytes 3145732
  172.2 10.6 %copy-start.4 = (f32[32,64,128]{2,1,0:T(8,128)S(1)}, f32[32,64,128]{2,1,0:T(8,128)}, u32[]{:S(2)}) copy-start(f32[32,64,128]{2,1,0:T(8,128)} %param.8) | copy-start | bytes 3145732
  172.2 10.6 %copy-start.5 = (f32[32,64,128]{2,1,0:T(8,128)S(1)}, f32[32,64,128]{2,1,0:T(8,128)}, u32[]{:S(2)}) copy-start(f32[32,64,128]{2,1,0:T(8,128)} %get-tuple-element.23) | copy-start | bytes 3145732
  172.3 9.1 %collective-permute-start.14 = (f32[32,1,128]{2,1,0:T(1,128)S(1)}, f32[32,1,128]{2,1,0:T(1,128)S(1)}, u32[]{:S(2)}, u32[]{:S(2)}) collective-permute-start(f32[32,1,128]{2,1,0:T(1,128)S(1)} %get-tuple-element.31), channel_id=1, source_target_pairs={{1,0},{2,1},{3,2},{4,3},{5,4},{6,5},{7,6},{8,7},{9,8},{10,9},{11,1... | collective-permute-start | bytes 49160 | tf_op jit(solution)/shard_map/ppermute | solution.py:24
  173.8 7.5 %collective-permute-start.15 = (f32[32,1,128]{2,1,0:T(1,128)S(1)}, f32[32,1,128]{2,1,0:T(1,128)S(1)}, u32[]{:S(2)}, u32[]{:S(2)}) collective-permute-start(f32[32,1,128]{2,1,0:T(1,128)S(1)} %get-tuple-element.32), channel_id=1, source_target_pairs={{0,1},{1,2},{2,3},{3,4},{4,5},{5,6},{6,7},{7,8},{8,9},{9,10},{10,1... | collective-permute-start | bytes 49160 | tf_op jit(solution)/shard_map/ppermute | solution.py:23
  178.4 3.0 %collective-permute-start.13 = (f32[1,64,128]{2,1,0:T(8,128)S(1)}, f32[1,64,128]{2,1,0:T(8,128)S(1)}, u32[]{:S(2)}, u32[]{:S(2)}) collective-permute-start(f32[1,64,128]{2,1,0:T(8,128)S(1)} %get-tuple-element.33), channel_id=1, source_target_pairs={{0,16},{16,32},{32,48},{48,64},{64,80},{80,96},{96,112},{1,17},{17... | collective-permute-start | bytes 98312 | tf_op jit(solution)/shard_map/ppermute | solution.py:23
  179.7 3.1 %collective-permute-start.12 = (f32[1,64,128]{2,1,0:T(8,128)S(1)}, f32[1,64,128]{2,1,0:T(8,128)S(1)}, u32[]{:S(2)}, u32[]{:S(2)}) collective-permute-start(f32[1,64,128]{2,1,0:T(8,128)S(1)} %get-tuple-element.34), channel_id=1, source_target_pairs={{16,0},{32,16},{48,32},{64,48},{80,64},{96,80},{112,96},{17,1},{33... | collective-permute-start | bytes 98312 | tf_op jit(solution)/shard_map/ppermute | solution.py:24
  (1 other events, 10.2 us)

commit v4 on v3

--- a/solution.py
+++ b/solution.py
@@ -6,7 +6,6 @@
 from jax.experimental import pallas as pl
 from jax.experimental.pallas import tpu as pltpu
 
-ITERS = 2
 GX_GY = ("gx_0", "gx_1", "gy_0", "gy_1")
 GX = ("gx_0", "gx_1")
 GY = ("gy_0", "gy_1")
@@ -80,10 +79,6 @@
     return (6.0 + screen) * field - beside
 
 
-def paired_total(first, second):
-    return (over_axes(first, GX_GY), over_axes(second, GX_GY))
-
-
 def component_grid(blocks, comp, span_x, span_y, span_z):
     part_blocks = blocks[:, comp, :].reshape(span_x, span_y, span_z, 8, 8, 8)
     grid = part_blocks.transpose(0, 3, 1, 4, 2, 5)
@@ -170,26 +165,35 @@
     total = total + (next_along_z(normal_z) - prior_along_z(normal_z))
     source = -0.5 * total
     inverse = 1.0 / (6.0 + screen)
-    solution = coarse_guess
-    residual = source - operate(solution, screen)
+    residual = source - operate(coarse_guess, screen)
     precond = residual * inverse
     image = operate(precond, screen)
-    gamma, delta = paired_total(jnp.sum(residual * precond), jnp.sum(image * precond))
+    scaled = image * inverse
+    scaled_image = operate(scaled, screen)
+    sums = over_axes(
+        jnp.stack(
+            [
+                jnp.sum(residual * precond),
+                jnp.sum(precond * image),
+                jnp.sum(image * scaled),
+                jnp.sum(scaled * scaled_image),
+            ]
+        ),
+        GX_GY,
+    )
+    gamma, delta, energy, curvature = sums[0], sums[1], sums[2], sums[3]
     alpha = gamma / delta
-    direction = precond
-    along = image
-    for step in range(ITERS):
-        solution = solution + alpha * direction
-        residual = residual - alpha * along
-        if step + 1 < ITERS:
-            precond = residual * inverse
-            image = operate(precond, screen)
-            gamma_next, delta = paired_total(jnp.sum(residual * precond), jnp.sum(image * precond))
-            ratio = gamma_next / gamma
-            alpha = gamma_next / (delta - ratio * gamma_next / alpha)
-            direction = precond + ratio * direction
-            along = image + ratio * along
-            gamma = gamma_next
+    gamma_next = alpha * alpha * energy - gamma
+    ratio = gamma_next / gamma
+    grow = 1.0 + ratio
+    delta_next = grow * grow * delta - 2.0 * grow * alpha * energy + alpha * alpha * curvature
+    alpha_next = gamma_next / delta_next
+    solution = coarse_guess + alpha * precond
+    residual = residual - alpha * image
+    direction = residual * inverse + ratio * precond
+    along = image - alpha * scaled_image + ratio * image
+    solution = solution + alpha_next * direction
+    residual = residual - alpha_next * along
     return (solution, residual)
 
 

time: 229 us -> 192 us (0.84)
  blocking collectives: 71.6 us -> 37.1 us
    psum x8 -> x4, blocking collectives: 71.6 us -> 37.1 us  [over_axes(): shard = lax.psum(shard, axis)]
    another operation x3 -> x4, other arithmetic: 0.25 us -> 2.76 us  [the longest x1 2.5 us: body(): jnp.stack([jnp.sum(residual * precond), jnp.sum(precond * image), jnp.sum...]
    mul x2 -> x1, other arithmetic: 5.66 us -> 3.47 us  [body(): precond = residual * inverse]
    reduce_sum x2 -> x1, other arithmetic: 4.97 us -> 3.3 us  [body(): jnp.sum(residual * precond)]
  transfers between devices with their start and end apart: 18 -> 18, of which waited for: 5 -> 4; matrix products, arithmetic and copies ran while one was open for 11% -> 11% of each run, Pallas kernels for 6% -> 8%
where the time goes in v4:
time: 192 us; the launch traced here: 191 us
  starting transfers between devices  57 us (30%)
  blocking collectives  37.1 us (19%)
  waiting for transfers between devices  35.4 us (18%)
  local copies, waits for them, and re-layouts  21.7 us (11%)
  other arithmetic  16 us (8%)
  Pallas kernels  14.7 us (8%)
  between operations  6.1 us (3%)
  matrix products  3.17 us (2%)
    psum x4, blocking collectives, over_axes(): shard = lax.psum(shard, axis)  37.1 us
    all_to_all x1, waiting for transfers between devices, body(): lax.all_to_all(payload.reshape(peers, capacity, 1536), GX_GY, split_axis=...  26.8 us
    ppermute x6, starting transfers between devices, extended(): lax.ppermute(last, axis, up)  21.2 us
    pallas_call x1, Pallas kernels, to_grid(): pl.pallas_call(relayout_kernel, out_shape=jax.ShapeDtypeStruct((3, span_x...  14.7 us
    all_to_all x1, starting transfers between devices, body(): lax.all_to_all(slots.reshape(peers, capacity), GX_GY, split_axis=0, conca...  11.2 us
    ppermute x6, starting transfers between devices, extended(): lax.ppermute(first, axis, [(b, a) for a, b in up])  7.91 us
    ppermute x2, starting transfers between devices, with_halo(): lax.ppermute(lax.slice_in_dim(block, block.shape[dim] - width, None, axis...  7.58 us
    all_to_all x1, starting transfers between devices, body(): lax.all_to_all(payload.reshape(peers, capacity, 1536), GX_GY, split_axis=...  6.54 us
  transfers between devices with their start and end apart: 18, of which 4 were waited for; matrix products, arithmetic and copies ran while one was open for 11% of the time, Pallas kernels for 8%

profile of v4, /device:TPU:0, one launch (start us, length us, event | category | flops | bytes accessed | tf_op | source)
XLA Modules:
  0.0 191.2 jit_solution(15005136902162465399)
XLA Ops:
  5.6 11.2 %all-to-all-start = ((s32[128,1,6]{2,1,0:T(1,128)}), s32[128,1,6]{2,1,0:T(1,128)S(1)}, u32[]{:S(2)}, u32[]{:S(2)}) async-start(s32[128,1,6]{2,1,0:T(1,128)} %bitcast.7), calls=%async_computation | async-start | bytes 131072 | tf_op jit(solution)/shard_map/all_to_all | solution.py:144
  16.8 3.2 %scatter_custom_fusion.1 = bf16[768,1536]{1,0:T(8,128)(2,1)S(1)} fusion(s32[256]{0:T(256)S(1)} %bitcast.46, bf16[256,1536]{1,0:T(8,128)(2,1)} %param.5, bf16[]{:T(256)} %constant.12.clone.1), kind=kCustom, calls=%fused_computation.4 | custom fusion | bytes 2359808 | tf_op jit(solution)/shard_map/scatter | solution.py:59
  20.0 2.5 %reshape.37 = bf16[128,6,1536]{2,1,0:T(8,128)(2,1)} reshape(bf16[768,1536]{1,0:T(8,128)(2,1)S(1)} %scatter_custom_fusion.1) | data formatting | bytes 4718592 | tf_op jit(solution)/shard_map/reshape | solution.py:142
  22.5 3.7 %all-to-all-done = s32[128,1,6]{2,1,0:T(1,128)S(1)} async-done(((s32[128,1,6]{2,1,0:T(1,128)}), s32[128,1,6]{2,1,0:T(1,128)S(1)}, u32[]{:S(2)}, u32[]{:S(2)}) %all-to-all-start) | async-done | bytes 3104 | tf_op jit(solution)/shard_map/all_to_all | solution.py:144
  26.2 6.5 %all-to-all-start.1 = ((bf16[128,6,1536]{2,1,0:T(8,128)(2,1)}), bf16[128,6,1536]{2,1,0:T(8,128)(2,1)}, u32[]{:S(2)}, u32[]{:S(2)}) async-start(bf16[128,6,1536]{2,1,0:T(8,128)(2,1)} %reshape.37), calls=%async_computation.1 | async-start | bytes 6291456 | tf_op jit(solution)/shard_map/all_to_all | solution.py:141
  36.0 5.1 %collective-permute-start.7 = (f32[32,1,128]{2,1,0:T(1,128)}, f32[32,1,128]{2,1,0:T(1,128)}, u32[]{:S(2)}, u32[]{:S(2)}) collective-permute-start(f32[32,1,128]{2,1,0:T(1,128)} %get-tuple-element.35), channel_id=1, source_target_pairs={{0,1},{1,2},{2,3},{3,4},{4,5},{5,6},{6,7},{7,8},{8,9},{9,10},{10,1... | collective-permute-start | bytes 49160 | tf_op jit(solution)/shard_map/ppermute | solution.py:22
  46.3 26.8 %all-to-all-done.1 = bf16[128,6,1536]{2,1,0:T(8,128)(2,1)} async-done(((bf16[128,6,1536]{2,1,0:T(8,128)(2,1)}), bf16[128,6,1536]{2,1,0:T(8,128)(2,1)}, u32[]{:S(2)}, u32[]{:S(2)}) %all-to-all-start.1) | async-done | bytes 2359328 | tf_op jit(solution)/shard_map/all_to_all | solution.py:141
  73.1 3.7 %reshape.38 = bf16[768,1536]{1,0:T(8,128)(2,1)S(1)} reshape(bf16[128,6,1536]{2,1,0:T(8,128)(2,1)} %all-to-all-done.1) | data formatting | bytes 4718592 | tf_op jit(solution)/shard_map/reshape | solution.py:156
  76.8 3.2 %fusion.blk_ref = f32[512,1536]{1,0:T(8,128)} fusion(bf16[768,1536]{1,0:T(8,128)(2,1)S(1)} %reshape.38, s32[768]{0:T(1024)S(1)} %eq.48), kind=kOutput, calls=%fused_computation.3 | convolution fusion | flops 1208352768 | bytes 5508096 | tf_op jit(solution)/shard_map/ks,kj->sj/dot_general | solution.py:153
  80.0 14.7 %shard_map.68 = f32[3,32,64,128]{3,2,1,0:T(8,128)} custom-call(f32[512,1536]{1,0:T(8,128)} %fusion.blk_ref), custom_call_target="tpu_custom_call" | custom-call | tf_op jit(solution)/shard_map/pallas_call | solution.py:128
  98.9 4.5 %collective-permute-start.3 = (f32[32,1,128]{2,1,0:T(1,128)S(1)}, f32[32,1,128]{2,1,0:T(1,128)S(1)}, u32[]{:S(2)}, u32[]{:S(2)}) collective-permute-start(f32[32,1,128]{2,1,0:T(1,128)S(1)} %get-tuple-element.31), channel_id=1, source_target_pairs={{0,1},{1,2},{2,3},{3,4},{4,5},{5,6},{6,7},{7,8},{8,9},{9,10},{10,1... | collective-permute-start | bytes 49160 | tf_op jit(solution)/shard_map/ppermute | solution.py:45
  104.7 3.0 %collective-permute-start.1 = (f32[1,64,128]{2,1,0:T(8,128)S(1)}, f32[1,64,128]{2,1,0:T(8,128)S(1)}, u32[]{:S(2)}, u32[]{:S(2)}) collective-permute-start(f32[1,64,128]{2,1,0:T(8,128)S(1)} %get-tuple-element.12), channel_id=1, source_target_pairs={{0,16},{16,32},{32,48},{48,64},{64,80},{80,96},{96,112},{1,17},{17... | collective-permute-start | bytes 98312 | tf_op jit(solution)/shard_map/ppermute | solution.py:45
  109.0 3.5 %fusion.40 = (f32[32,64,128]{2,1,0:T(8,128)S(1)}, f32[32,64,128]{2,1,0:T(8,128)S(1)}) fusion(f32[32,64,128]{2,1,0:T(8,128)S(1)} %copy-done.1, f32[32,64,127]{2,1,0:T(8,128)S(1)} %get-tuple-element.44, f32[32,64,127]{2,1,0:T(8,128)S(1)} %get-tuple-element.45, f32[34,64,128]{2,1,0:T(8,128)} %constant_dynamic-update-slice_fusion, ...), kind=kLoop, calls=%fused_computation.94 | loop fusion | flops 8126464 | bytes 11763712 | tf_op jit(solution)/shard_map/mul | solution.py:169
  113.8 4.5 %collective-permute-start.11 = (f32[32,1,128]{2,1,0:T(1,128)S(1)}, f32[32,1,128]{2,1,0:T(1,128)S(1)}, u32[]{:S(2)}, u32[]{:S(2)}) collective-permute-start(f32[32,1,128]{2,1,0:T(1,128)S(1)} %get-tuple-element.25), channel_id=1, source_target_pairs={{0,1},{1,2},{2,3},{3,4},{4,5},{5,6},{6,7},{7,8},{8,9},{9,10},{10,1... | collective-permute-start | bytes 49160 | tf_op jit(solution)/shard_map/ppermute | solution.py:22
  121.8 3.5 %collective-permute-done.8 = f32[1,64,128]{2,1,0:T(8,128)S(1)} collective-permute-done((f32[1,64,128]{2,1,0:T(8,128)S(1)}, f32[1,64,128]{2,1,0:T(8,128)S(1)}, u32[]{:S(2)}, u32[]{:S(2)}) %collective-permute-start.8) | collective-permute-done | bytes 32800 | tf_op jit(solution)/shard_map/ppermute | solution.py:23
  127.4 4.5 %collective-permute-start.15 = (f32[32,1,128]{2,1,0:T(1,128)S(1)}, f32[32,1,128]{2,1,0:T(1,128)S(1)}, u32[]{:S(2)}, u32[]{:S(2)}) collective-permute-start(f32[32,1,128]{2,1,0:T(1,128)S(1)} %get-tuple-element.19), channel_id=1, source_target_pairs={{0,1},{1,2},{2,3},{3,4},{4,5},{5,6},{6,7},{7,8},{8,9},{9,10},{10,1... | collective-permute-start | bytes 49160 | tf_op jit(solution)/shard_map/ppermute | solution.py:22
  132.0 4.0 %collective-permute-start.13 = (f32[1,64,128]{2,1,0:T(8,128)S(1)}, f32[1,64,128]{2,1,0:T(8,128)S(1)}, u32[]{:S(2)}, u32[]{:S(2)}) collective-permute-start(f32[1,64,128]{2,1,0:T(8,128)S(1)} %get-tuple-element.20), channel_id=1, source_target_pairs={{0,16},{16,32},{32,48},{48,64},{64,80},{80,96},{96,112},{1,17},{17... | collective-permute-start | bytes 98312 | tf_op jit(solution)/shard_map/ppermute | solution.py:22
  139.1 3.3 %multiply_reduce_fusion.3 = (f32[]{:T(128)}, f32[]{:T(128)}, f32[]{:T(128)}, f32[]{:T(128)}, f32[32,64,128]{2,1,0:T(8,128)}) fusion(f32[32,64,128]{2,1,0:T(8,128)S(1)} %get-tuple-element.10, f32[32,64,128]{2,1,0:T(8,128)S(1)} %copy-done.1, f32[32,64,128]{2,1,0:T(8,128)S(1)} %get-tuple-element.8, f32[32,64,128]{2,1,0:T(8,128)S(1)} %get-tuple-element.7, ...), kind=kLoop, calls=%fused_computation.71 | loop fusion | flops 8388604 | bytes 7421968 | tf_op jit(solution)/shard_map/reduce_sum | solution.py:176
  142.4 2.5 %pad_maximum_fusion.20 = f32[4]{0:T(128)S(1)} fusion(f32[1]{0:T(128)} %bitcast.16, f32[1]{0:T(128)} %bitcast.15, f32[1]{0:T(128)} %bitcast.14, f32[1]{0:T(128)} %bitcast.13), kind=kLoop, calls=%fused_computation.92 | loop fusion | flops 12 | bytes 32 | tf_op jit(solution)/shard_map/stack | solution.py:174
  144.9 10.8 %psum.28 = f32[4]{0:T(128)S(1)} all-reduce(f32[4]{0:T(128)S(1)} %pad_maximum_fusion.20), channel_id=1, replica_groups=mesh['gx_0'=4,'gx_1'=2,'gy_0'=4,'gy_1'=4] {'gx_0'}, use_global_device_ids=true, to_apply=%region_9.10 | all-reduce | flops 4 | bytes 32 | tf_op jit(solution)/shard_map/psum | solution.py:36
  155.7 2.5 %psum.29 = f32[4]{0:T(128)S(1)} all-reduce(f32[4]{0:T(128)S(1)} %psum.28), channel_id=1, replica_groups=mesh['gx_0'=4,'gx_1'=2,'gy_0'=4,'gy_1'=4] {'gx_1'}, use_global_device_ids=true, to_apply=%region_10.11 | all-reduce | flops 4 | bytes 32 | tf_op jit(solution)/shard_map/psum | solution.py:36
  158.2 13.7 %psum.30 = f32[4]{0:T(128)S(1)} all-reduce(f32[4]{0:T(128)S(1)} %psum.29), channel_id=1, replica_groups=mesh['gx_0'=4,'gx_1'=2,'gy_0'=4,'gy_1'=4] {'gy_0'}, use_global_device_ids=true, to_apply=%region_11.12 | all-reduce | flops 4 | bytes 32 | tf_op jit(solution)/shard_map/psum | solution.py:36
  171.9 10.1 %psum.31 = f32[4]{0:T(128)S(1)} all-reduce(f32[4]{0:T(128)S(1)} %psum.30), channel_id=1, replica_groups=mesh['gx_0'=4,'gx_1'=2,'gy_0'=4,'gy_1'=4] {'gy_1'}, use_global_device_ids=true, to_apply=%region_12.13 | all-reduce | flops 4 | bytes 32 | tf_op jit(solution)/shard_map/psum | solution.py:36
  187.7 3.5 %multiply_subtract_fusion = (f32[32,64,128]{2,1,0:T(8,128)}, f32[32,64,128]{2,1,0:T(8,128)}) fusion(f32[32,64,128]{2,1,0:T(8,128)} %copy-done.2, f32[32,64,128]{2,1,0:T(8,128)} %get-tuple-element.6, f32[32,64,128]{2,1,0:T(8,128)S(1)} %get-tuple-element.10, f32[]{:T(128)S(6)} %div.18, f32[]{:T(128)S(6)} %div.19, f32[]{:T(128)S(6)} %div.17, ...), kind=kLoop, calls=%fused_computation.65 | loop fusion | flops 4718592 | bytes 7340044 | tf_op jit(solution)/shard_map/sub | solution.py:196
  (63 shorter events, 30.4 us)
Async XLA Ops:
  5.6 20.6 %all-to-all-start = ((s32[128,1,6]{2,1,0:T(1,128)}), s32[128,1,6]{2,1,0:T(1,128)S(1)}, u32[]{:S(2)}, u32[]{:S(2)}) async-start(s32[128,1,6]{2,1,0:T(1,128)} %bitcast.7), calls=%async_computation | async-start | bytes 131072 | tf_op jit(solution)/shard_map/all_to_all | solution.py:144
  22.5 10.2 %copy-start = (f32[32,64,128]{2,1,0:T(8,128)S(1)}, f32[32,64,128]{2,1,0:T(8,128)}, u32[]{:S(2)}) copy-start(f32[32,64,128]{2,1,0:T(8,128)} %param.9) | copy-start | bytes 3145732
  26.2 46.9 %all-to-all-start.1 = ((bf16[128,6,1536]{2,1,0:T(8,128)(2,1)}), bf16[128,6,1536]{2,1,0:T(8,128)(2,1)}, u32[]{:S(2)}, u32[]{:S(2)}) async-start(bf16[128,6,1536]{2,1,0:T(8,128)(2,1)} %reshape.37), calls=%async_computation.1 | async-start | bytes 6291456 | tf_op jit(solution)/shard_map/all_to_all | solution.py:141
  32.8 11.1 %collective-permute-start.5 = (f32[1,64,128]{2,1,0:T(8,128)S(1)}, f32[1,64,128]{2,1,0:T(8,128)S(1)}, u32[]{:S(2)}, u32[]{:S(2)}) collective-permute-start(f32[1,64,128]{2,1,0:T(8,128)S(1)} %get-tuple-element.37), channel_id=1, source_target_pairs={{0,16},{16,32},{32,48},{48,64},{64,80},{80,96},{96,112},{1,17},{17... | collective-permute-start | bytes 98312 | tf_op jit(solution)/shard_map/ppermute | solution.py:22
  34.7 70.0 %collective-permute-start.6 = (f32[32,1,128]{2,1,0:T(1,128)}, f32[32,1,128]{2,1,0:T(1,128)S(1)}, u32[]{:S(2)}, u32[]{:S(2)}) collective-permute-start(f32[32,1,128]{2,1,0:T(1,128)} %get-tuple-element.34), channel_id=1, source_target_pairs={{1,0},{2,1},{3,2},{4,3},{5,4},{6,5},{7,6},{8,7},{9,8},{10,9},{11,1... | collective-permute-start | bytes 49160 | tf_op jit(solution)/shard_map/ppermute | solution.py:23
  36.0 72.5 %collective-permute-start.7 = (f32[32,1,128]{2,1,0:T(1,128)}, f32[32,1,128]{2,1,0:T(1,128)}, u32[]{:S(2)}, u32[]{:S(2)}) collective-permute-start(f32[32,1,128]{2,1,0:T(1,128)} %get-tuple-element.35), channel_id=1, source_target_pairs={{0,1},{1,2},{2,3},{3,4},{4,5},{5,6},{6,7},{7,8},{8,9},{9,10},{10,1... | collective-permute-start | bytes 49160 | tf_op jit(solution)/shard_map/ppermute | solution.py:22
  41.2 4.5 %collective-permute-start.4 = (f32[1,64,128]{2,1,0:T(8,128)S(1)}, f32[1,64,128]{2,1,0:T(8,128)S(1)}, u32[]{:S(2)}, u32[]{:S(2)}) collective-permute-start(f32[1,64,128]{2,1,0:T(8,128)S(1)} %get-tuple-element.36), channel_id=1, source_target_pairs={{16,0},{32,16},{48,32},{64,48},{80,64},{96,80},{112,96},{17,1},{33... | collective-permute-start | bytes 98312 | tf_op jit(solution)/shard_map/ppermute | solution.py:23
  97.6 11.0 %collective-permute-start.2 = (f32[32,1,128]{2,1,0:T(1,128)S(1)}, f32[32,1,128]{2,1,0:T(1,128)S(1)}, u32[]{:S(2)}, u32[]{:S(2)}) collective-permute-start(f32[32,1,128]{2,1,0:T(1,128)S(1)} %get-tuple-element.30), channel_id=1, source_target_pairs={{1,0},{2,1},{3,2},{4,3},{5,4},{6,5},{7,6},{8,7},{9,8},{10,9},{11,1... | collective-permute-start | bytes 49160 | tf_op jit(solution)/shard_map/ppermute | solution.py:48
  98.9 9.7 %collective-permute-start.3 = (f32[32,1,128]{2,1,0:T(1,128)S(1)}, f32[32,1,128]{2,1,0:T(1,128)S(1)}, u32[]{:S(2)}, u32[]{:S(2)}) collective-permute-start(f32[32,1,128]{2,1,0:T(1,128)S(1)} %get-tuple-element.31), channel_id=1, source_target_pairs={{0,1},{1,2},{2,3},{3,4},{4,5},{5,6},{6,7},{7,8},{8,9},{9,10},{10,1... | collective-permute-start | bytes 49160 | tf_op jit(solution)/shard_map/ppermute | solution.py:45
  103.4 5.2 %collective-permute-start = (f32[1,64,128]{2,1,0:T(8,128)S(1)}, f32[1,64,128]{2,1,0:T(8,128)S(1)}, u32[]{:S(2)}, u32[]{:S(2)}) collective-permute-start(f32[1,64,128]{2,1,0:T(8,128)S(1)} %get-tuple-element.11), channel_id=1, source_target_pairs={{16,0},{32,16},{48,32},{64,48},{80,64},{96,80},{112,96},{17,1},{33... | collective-permute-start | bytes 98312 | tf_op jit(solution)/shard_map/ppermute | solution.py:48
  104.7 3.9 %collective-permute-start.1 = (f32[1,64,128]{2,1,0:T(8,128)S(1)}, f32[1,64,128]{2,1,0:T(8,128)S(1)}, u32[]{:S(2)}, u32[]{:S(2)}) collective-permute-start(f32[1,64,128]{2,1,0:T(8,128)S(1)} %get-tuple-element.12), channel_id=1, source_target_pairs={{0,16},{16,32},{32,48},{48,64},{64,80},{80,96},{96,112},{1,17},{17... | collective-permute-start | bytes 98312 | tf_op jit(solution)/shard_map/ppermute | solution.py:45
  107.8 1.2 copy-start.1
  112.5 9.3 %collective-permute-start.10 = (f32[32,1,128]{2,1,0:T(1,128)S(1)}, f32[32,1,128]{2,1,0:T(1,128)S(1)}, u32[]{:S(2)}, u32[]{:S(2)}) collective-permute-start(f32[32,1,128]{2,1,0:T(1,128)S(1)} %get-tuple-element.24), channel_id=1, source_target_pairs={{1,0},{2,1},{3,2},{4,3},{5,4},{6,5},{7,6},{8,7},{9,8},{10,9},{11,1... | collective-permute-start | bytes 49160 | tf_op jit(solution)/shard_map/ppermute | solution.py:23
  113.8 8.0 %collective-permute-start.11 = (f32[32,1,128]{2,1,0:T(1,128)S(1)}, f32[32,1,128]{2,1,0:T(1,128)S(1)}, u32[]{:S(2)}, u32[]{:S(2)}) collective-permute-start(f32[32,1,128]{2,1,0:T(1,128)S(1)} %get-tuple-element.25), channel_id=1, source_target_pairs={{0,1},{1,2},{2,3},{3,4},{4,5},{5,6},{6,7},{7,8},{8,9},{9,10},{10,1... | collective-permute-start | bytes 49160 | tf_op jit(solution)/shard_map/ppermute | solution.py:22
  118.4 3.4 %collective-permute-start.9 = (f32[1,64,128]{2,1,0:T(8,128)S(1)}, f32[1,64,128]{2,1,0:T(8,128)S(1)}, u32[]{:S(2)}, u32[]{:S(2)}) collective-permute-start(f32[1,64,128]{2,1,0:T(8,128)S(1)} %get-tuple-element.26), channel_id=1, source_target_pairs={{0,16},{16,32},{32,48},{48,64},{64,80},{80,96},{96,112},{1,17},{17... | collective-permute-start | bytes 98312 | tf_op jit(solution)/shard_map/ppermute | solution.py:22
  120.1 5.3 %collective-permute-start.8 = (f32[1,64,128]{2,1,0:T(8,128)S(1)}, f32[1,64,128]{2,1,0:T(8,128)S(1)}, u32[]{:S(2)}, u32[]{:S(2)}) collective-permute-start(f32[1,64,128]{2,1,0:T(8,128)S(1)} %get-tuple-element.27), channel_id=1, source_target_pairs={{16,0},{32,16},{48,32},{64,48},{80,64},{96,80},{112,96},{17,1},{33... | collective-permute-start | bytes 98312 | tf_op jit(solution)/shard_map/ppermute | solution.py:23
  126.0 16.4 %copy-start.2 = (f32[32,64,128]{2,1,0:T(8,128)}, f32[32,64,128]{2,1,0:T(8,128)S(1)}, u32[]{:S(2)}) copy-start(f32[32,64,128]{2,1,0:T(8,128)S(1)} %get-tuple-element.8) | copy-start | bytes 3145732
  126.1 11.7 %collective-permute-start.14 = (f32[32,1,128]{2,1,0:T(1,128)S(1)}, f32[32,1,128]{2,1,0:T(1,128)S(1)}, u32[]{:S(2)}, u32[]{:S(2)}) collective-permute-start(f32[32,1,128]{2,1,0:T(1,128)S(1)} %get-tuple-element.18), channel_id=1, source_target_pairs={{1,0},{2,1},{3,2},{4,3},{5,4},{6,5},{7,6},{8,7},{9,8},{10,9},{11,1... | collective-permute-start | bytes 49160 | tf_op jit(solution)/shard_map/ppermute | solution.py:23
  127.4 10.4 %collective-permute-start.15 = (f32[32,1,128]{2,1,0:T(1,128)S(1)}, f32[32,1,128]{2,1,0:T(1,128)S(1)}, u32[]{:S(2)}, u32[]{:S(2)}) collective-permute-start(f32[32,1,128]{2,1,0:T(1,128)S(1)} %get-tuple-element.19), channel_id=1, source_target_pairs={{0,1},{1,2},{2,3},{3,4},{4,5},{5,6},{6,7},{7,8},{8,9},{9,10},{10,1... | collective-permute-start | bytes 49160 | tf_op jit(solution)/shard_map/ppermute | solution.py:22
  132.0 5.9 %collective-permute-start.13 = (f32[1,64,128]{2,1,0:T(8,128)S(1)}, f32[1,64,128]{2,1,0:T(8,128)S(1)}, u32[]{:S(2)}, u32[]{:S(2)}) collective-permute-start(f32[1,64,128]{2,1,0:T(8,128)S(1)} %get-tuple-element.20), channel_id=1, source_target_pairs={{0,16},{16,32},{32,48},{48,64},{64,80},{80,96},{96,112},{1,17},{17... | collective-permute-start | bytes 98312 | tf_op jit(solution)/shard_map/ppermute | solution.py:22
  135.9 3.2 %collective-permute-start.12 = (f32[1,64,128]{2,1,0:T(8,128)S(1)}, f32[1,64,128]{2,1,0:T(8,128)S(1)}, u32[]{:S(2)}, u32[]{:S(2)}) collective-permute-start(f32[1,64,128]{2,1,0:T(8,128)S(1)} %get-tuple-element.21), channel_id=1, source_target_pairs={{16,0},{32,16},{48,32},{64,48},{80,64},{96,80},{112,96},{17,1},{33... | collective-permute-start | bytes 98312 | tf_op jit(solution)/shard_map/ppermute | solution.py:23

commit v5 on v4

--- a/solution.py
+++ b/solution.py
@@ -56,9 +56,15 @@
     earlier = jnp.cumsum(onehot, axis=0) - onehot
     order = jnp.sum(earlier * onehot, axis=1)
     place = target * capacity + order
-    payload = jnp.zeros((peers * capacity, bricks.shape[1]), bricks.dtype).at[place].set(bricks)
-    slots = jnp.zeros((peers * capacity,), jnp.int32).at[place].set(brick_slot)
-    return (payload, slots)
+    high = (brick_slot // 32).astype(jnp.bfloat16)
+    low = (brick_slot % 32).astype(jnp.bfloat16)
+    tag = jnp.zeros((bricks.shape[0], 128), jnp.bfloat16).at[:, 0].set(high).at[:, 1].set(low)
+    rows = jnp.concatenate([bricks, tag], axis=1)
+    chosen = place[None, :] == jnp.arange(peers * capacity, dtype=jnp.int32)[:, None]
+    payload = jnp.einsum(
+        "pk,kj->pj", chosen.astype(jnp.bfloat16), rows, preferred_element_type=jnp.float32
+    )
+    return payload.astype(jnp.bfloat16)
 
 
 def next_along_z(field):
@@ -136,15 +142,12 @@
 def body(bricks, brick_target, brick_slot, screen, coarse_guess):
     peers = lax.axis_size(GX_GY)
     capacity = max(2, 3 * bricks.shape[0] // peers)
-    payload, slots = build_send(bricks, brick_target, brick_slot, peers, capacity)
-    arrived, landed = (
-        lax.all_to_all(
-            payload.reshape(peers, capacity, 1536), GX_GY, split_axis=0, concat_axis=0, tiled=True
-        ),
-        lax.all_to_all(
-            slots.reshape(peers, capacity), GX_GY, split_axis=0, concat_axis=0, tiled=True
-        ),
-    )
+    payload = build_send(bricks, brick_target, brick_slot, peers, capacity)
+    arrived = lax.all_to_all(
+        payload.reshape(peers, capacity, payload.shape[1]), GX_GY, split_axis=0, concat_axis=0, tiled=True
+    ).reshape(peers * capacity, payload.shape[1])
+    tag = arrived[:, 1536:1538].astype(jnp.int32)
+    landed = tag[:, 0] * 32 + tag[:, 1]
     width_x, width_y, depth = screen.shape
     span_x = width_x // 8
     span_y = width_y // 8
@@ -153,7 +156,7 @@
     blocks = jnp.einsum(
         "ks,kj->sj",
         picks.astype(jnp.bfloat16),
-        arrived.reshape(-1, 1536),
+        arrived[:, :1536],
         preferred_element_type=jnp.float32,
     )
     normals = to_grid(blocks, span_x, span_y, depth)

time: 192 us -> 190 us (0.990)
  starting transfers between devices: 57 us -> 50.2 us
  local copies, waits for them, and re-layouts: 21.7 us -> 16.7 us
  other arithmetic: 16 us -> 20 us
  matrix products: 3.17 us -> 6.86 us
  waiting for transfers between devices: 35.4 us -> 37.4 us
    all_to_all x2 -> x1, starting transfers between devices: 17.7 us -> 11.6 us  [body(): lax.all_to_all(payload.reshape(peers, capacity, payload.shape[1]), GX_GY,...]
    scatter x2 -> x3, local copies, waits for them, and re-layouts: 4.79 us -> 0.16 us  [build_send(): jnp.zeros((bricks.shape[0], 128), jnp.bfloat16).at[:, 0].set(high).at[:, 1]]
    dot_general x1 -> x2, matrix products: 3.17 us -> 6.86 us  [the longest x1 4.84 us: body(): jnp.einsum('ks,kj->sj', picks.astype(jnp.bfloat16), arrived[:, :1536], pr...]
    another operation x3 -> x6, other arithmetic: 0.25 us -> 3.51 us
    all_to_all x2 -> x1, waiting for transfers between devices: 30.5 us -> 31.6 us  [body(): lax.all_to_all(payload.reshape(peers, capacity, payload.shape[1]), GX_GY,...]
  transfers between devices with their start and end apart: 18 -> 17, of which waited for: 4 -> 4; matrix products, arithmetic and copies ran while one was open for 11% -> 10% of each run, Pallas kernels for 8% -> 8%
where the time goes in v5:
time: 190 us; the launch traced here: 189 us
  starting transfers between devices  50.2 us (26%)
  waiting for transfers between devices  37.4 us (20%)
  blocking collectives  37 us (19%)
  other arithmetic  20 us (11%)
  local copies, waits for them, and re-layouts  16.7 us (9%)
  Pallas kernels  14.7 us (8%)
  matrix products  6.86 us (4%)
  between operations  6.16 us (3%)
    psum x4, blocking collectives, over_axes(): shard = lax.psum(shard, axis)  37 us
    all_to_all x1, waiting for transfers between devices, body(): lax.all_to_all(payload.reshape(peers, capacity, payload.shape[1]), GX_GY,...  31.6 us
    ppermute x6, starting transfers between devices, extended(): lax.ppermute(last, axis, up)  20.7 us
    pallas_call x1, Pallas kernels, to_grid(): pl.pallas_call(relayout_kernel, out_shape=jax.ShapeDtypeStruct((3, span_x...  14.7 us
    all_to_all x1, starting transfers between devices, body(): lax.all_to_all(payload.reshape(peers, capacity, payload.shape[1]), GX_GY,...  11.6 us
    ppermute x6, starting transfers between devices, extended(): lax.ppermute(first, axis, [(b, a) for a, b in up])  7.75 us
    ppermute x2, starting transfers between devices, with_halo(): lax.ppermute(lax.slice_in_dim(block, block.shape[dim] - width, None, axis...  7.58 us
    ppermute x6, waiting for transfers between devices, extended(): lax.ppermute(first, axis, [(b, a) for a, b in up])  5.75 us
  transfers between devices with their start and end apart: 17, of which 4 were waited for; matrix products, arithmetic and copies ran while one was open for 10% of the time, Pallas kernels for 8%

profile of v5, /device:TPU:0, one launch (start us, length us, event | category | flops | bytes accessed | tf_op | source)
XLA Modules:
  0.0 189.1 jit_solution(556939881565369146)
XLA Ops:
  1.9 2.0 %broadcast_select_fusion = (bf16[256]{0:T(256)(128)(2,1)S(1)}, bf16[256]{0:T(256)(128)(2,1)S(1)}) fusion(pred[]{:T(512)} %compare_reduce_fusion, s32[256]{0:T(256)} %param.11, pred[]{:T(512)} %compare_reduce_fusion.1), kind=kLoop, calls=%fused_computation.105 | loop fusion | flops 5888 | bytes 2050 | tf_op jit(solution)/shard_map/select.12
  6.7 2.0 %convolution_convert_fusion = bf16[768,1664]{1,0:T(8,128)(2,1)S(1)} fusion(bf16[256,128]{1,0:T(8,128)(2,1)S(1)} %copy.10, bf16[256,1536]{1,0:T(8,128)(2,1)} %param.9, s32[256]{0:T(256)S(1)} %multiply_add_fusion.1), kind=kOutput, calls=%fused_computation | convolution fusion | flops 657489920 | bytes 3408896 | tf_op jit(solution)/shard_map/pk,kj->pj/dot_general | solution.py:64
  8.8 2.6 %reshape.93 = bf16[128,6,1664]{2,1,0:T(8,128)(2,1)} reshape(bf16[768,1664]{1,0:T(8,128)(2,1)S(1)} %convolution_convert_fusion) | data formatting | bytes 5111808 | tf_op jit(solution)/shard_map/reshape | solution.py:147
  11.4 11.6 %all-to-all-start = ((bf16[128,6,1664]{2,1,0:T(8,128)(2,1)}), bf16[128,6,1664]{2,1,0:T(8,128)(2,1)}, u32[]{:S(2)}, u32[]{:S(2)}) async-start(bf16[128,6,1664]{2,1,0:T(8,128)(2,1)} %reshape.93), calls=%async_computation | async-start | bytes 6815744 | tf_op jit(solution)/shard_map/all_to_all | solution.py:146
  25.7 4.5 %collective-permute-start.7 = (f32[32,1,128]{2,1,0:T(1,128)S(1)}, f32[32,1,128]{2,1,0:T(1,128)S(1)}, u32[]{:S(2)}, u32[]{:S(2)}) collective-permute-start(f32[32,1,128]{2,1,0:T(1,128)S(1)} %get-tuple-element.59), channel_id=1, source_target_pairs={{0,1},{1,2},{2,3},{3,4},{4,5},{5,6},{6,7},{7,8},{8,9},{9,10},{10,1... | collective-permute-start | bytes 49160 | tf_op jit(solution)/shard_map/ppermute | solution.py:22
  34.5 31.6 %all-to-all-done = bf16[128,6,1664]{2,1,0:T(8,128)(2,1)} async-done(((bf16[128,6,1664]{2,1,0:T(8,128)(2,1)}), bf16[128,6,1664]{2,1,0:T(8,128)(2,1)}, u32[]{:S(2)}, u32[]{:S(2)}) %all-to-all-start) | async-done | bytes 2555936 | tf_op jit(solution)/shard_map/all_to_all | solution.py:146
  66.1 5.4 %reshape.94 = bf16[768,1664]{1,0:T(8,128)(2,1)} reshape(bf16[128,6,1664]{2,1,0:T(8,128)(2,1)} %all-to-all-done) | data formatting | bytes 5111808 | tf_op jit(solution)/shard_map/reshape | solution.py:148
  72.7 4.8 %fusion.blk_ref = f32[512,1536]{1,0:T(8,128)} fusion(bf16[768,1664]{1,0:T(8,128)(2,1)} %reshape.94, s32[768]{0:T(1024)S(1)} %fusion.34), kind=kOutput, calls=%fused_computation.1 | convolution fusion | flops 1208352768 | bytes 5508096 | tf_op jit(solution)/shard_map/ks,kj->sj/dot_general | solution.py:156
  77.6 14.7 %shard_map.68 = f32[3,32,64,128]{3,2,1,0:T(8,128)} custom-call(f32[512,1536]{1,0:T(8,128)} %fusion.blk_ref), custom_call_target="tpu_custom_call" | custom-call | tf_op jit(solution)/shard_map/pallas_call | solution.py:134
  92.3 2.1 %slice_bitcast_fusion.2 = (f32[32,64,128]{2,1,0:T(8,128)S(1)}, f32[32,64,128]{2,1,0:T(8,128)S(1)}, f32[32,64,128]{2,1,0:T(8,128)S(1)}) fusion(f32[3,32,64,128]{3,2,1,0:T(8,128)} %shard_map.68), kind=kLoop, calls=%fused_computation.62 | loop fusion | bytes 6291456 | tf_op jit(solution)/shard_map/squeeze | solution.py:163
  96.5 4.5 %collective-permute-start.3 = (f32[32,1,128]{2,1,0:T(1,128)S(1)}, f32[32,1,128]{2,1,0:T(1,128)S(1)}, u32[]{:S(2)}, u32[]{:S(2)}) collective-permute-start(f32[32,1,128]{2,1,0:T(1,128)S(1)} %get-tuple-element.55), channel_id=1, source_target_pairs={{0,1},{1,2},{2,3},{3,4},{4,5},{5,6},{6,7},{7,8},{8,9},{9,10},{10,1... | collective-permute-start | bytes 49160 | tf_op jit(solution)/shard_map/ppermute | solution.py:45
  102.3 3.0 %collective-permute-start.1 = (f32[1,64,128]{2,1,0:T(8,128)S(1)}, f32[1,64,128]{2,1,0:T(8,128)S(1)}, u32[]{:S(2)}, u32[]{:S(2)}) collective-permute-start(f32[1,64,128]{2,1,0:T(8,128)S(1)} %get-tuple-element.36), channel_id=1, source_target_pairs={{0,16},{16,32},{32,48},{48,64},{64,80},{80,96},{96,112},{1,17},{17... | collective-permute-start | bytes 98312 | tf_op jit(solution)/shard_map/ppermute | solution.py:45
  106.6 3.6 %fusion.45 = (f32[32,64,128]{2,1,0:T(8,128)S(1)}, f32[32,64,128]{2,1,0:T(8,128)S(1)}) fusion(f32[32,64,128]{2,1,0:T(8,128)S(1)} %copy-done.1, f32[32,64,127]{2,1,0:T(8,128)S(1)} %get-tuple-element.70, f32[32,64,127]{2,1,0:T(8,128)S(1)} %get-tuple-element.71, f32[34,64,128]{2,1,0:T(8,128)} %constant_dynamic-update-slice_fusion, ...), kind=kLoop, calls=%fused_computation.114 | loop fusion | flops 8126464 | bytes 11763712 | tf_op jit(solution)/shard_map/mul | solution.py:172
  111.6 4.5 %collective-permute-start.11 = (f32[32,1,128]{2,1,0:T(1,128)S(1)}, f32[32,1,128]{2,1,0:T(1,128)S(1)}, u32[]{:S(2)}, u32[]{:S(2)}) collective-permute-start(f32[32,1,128]{2,1,0:T(1,128)S(1)} %get-tuple-element.49), channel_id=1, source_target_pairs={{0,1},{1,2},{2,3},{3,4},{4,5},{5,6},{6,7},{7,8},{8,9},{9,10},{10,1... | collective-permute-start | bytes 49160 | tf_op jit(solution)/shard_map/ppermute | solution.py:22
  119.6 3.5 %collective-permute-done.8 = f32[1,64,128]{2,1,0:T(8,128)S(1)} collective-permute-done((f32[1,64,128]{2,1,0:T(8,128)S(1)}, f32[1,64,128]{2,1,0:T(8,128)S(1)}, u32[]{:S(2)}, u32[]{:S(2)}) %collective-permute-start.8) | collective-permute-done | bytes 32800 | tf_op jit(solution)/shard_map/ppermute | solution.py:23
  125.2 4.5 %collective-permute-start.15 = (f32[32,1,128]{2,1,0:T(1,128)S(1)}, f32[32,1,128]{2,1,0:T(1,128)S(1)}, u32[]{:S(2)}, u32[]{:S(2)}) collective-permute-start(f32[32,1,128]{2,1,0:T(1,128)S(1)} %get-tuple-element.43), channel_id=1, source_target_pairs={{0,1},{1,2},{2,3},{3,4},{4,5},{5,6},{6,7},{7,8},{8,9},{9,10},{10,1... | collective-permute-start | bytes 49160 | tf_op jit(solution)/shard_map/ppermute | solution.py:22
  129.8 4.0 %collective-permute-start.13 = (f32[1,64,128]{2,1,0:T(8,128)S(1)}, f32[1,64,128]{2,1,0:T(8,128)S(1)}, u32[]{:S(2)}, u32[]{:S(2)}) collective-permute-start(f32[1,64,128]{2,1,0:T(8,128)S(1)} %get-tuple-element.44), channel_id=1, source_target_pairs={{0,16},{16,32},{32,48},{48,64},{64,80},{80,96},{96,112},{1,17},{17... | collective-permute-start | bytes 98312 | tf_op jit(solution)/shard_map/ppermute | solution.py:22
  136.9 3.3 %multiply_reduce_fusion.3 = (f32[]{:T(128)}, f32[]{:T(128)}, f32[]{:T(128)}, f32[]{:T(128)}, f32[32,64,128]{2,1,0:T(8,128)}) fusion(f32[32,64,128]{2,1,0:T(8,128)S(1)} %get-tuple-element.34, f32[32,64,128]{2,1,0:T(8,128)S(1)} %copy-done.1, f32[32,64,128]{2,1,0:T(8,128)S(1)} %get-tuple-element.32, f32[32,64,128]{2,1,0:T(8,128)S(1)} %get-tuple-element.31, ...), kind=kLoop, calls=%fused_computation.69 | loop fusion | flops 8388604 | bytes 7421968 | tf_op jit(solution)/shard_map/reduce_sum | solution.py:179
  140.2 2.6 %pad_maximum_fusion.20 = f32[4]{0:T(128)S(1)} fusion(f32[1]{0:T(128)} %bitcast.13, f32[1]{0:T(128)} %bitcast.12, f32[1]{0:T(128)} %bitcast.11, f32[1]{0:T(128)} %bitcast.10), kind=kLoop, calls=%fused_computation.108 | loop fusion | flops 12 | bytes 32 | tf_op jit(solution)/shard_map/stack | solution.py:177
  142.8 10.8 %psum.28 = f32[4]{0:T(128)S(1)} all-reduce(f32[4]{0:T(128)S(1)} %pad_maximum_fusion.20), channel_id=1, replica_groups=mesh['gx_0'=4,'gx_1'=2,'gy_0'=4,'gy_1'=4] {'gx_0'}, use_global_device_ids=true, to_apply=%region_9.10 | all-reduce | flops 4 | bytes 32 | tf_op jit(solution)/shard_map/psum | solution.py:36
  153.7 2.5 %psum.29 = f32[4]{0:T(128)S(1)} all-reduce(f32[4]{0:T(128)S(1)} %psum.28), channel_id=1, replica_groups=mesh['gx_0'=4,'gx_1'=2,'gy_0'=4,'gy_1'=4] {'gx_1'}, use_global_device_ids=true, to_apply=%region_10.11 | all-reduce | flops 4 | bytes 32 | tf_op jit(solution)/shard_map/psum | solution.py:36
  156.1 13.5 %psum.30 = f32[4]{0:T(128)S(1)} all-reduce(f32[4]{0:T(128)S(1)} %psum.29), channel_id=1, replica_groups=mesh['gx_0'=4,'gx_1'=2,'gy_0'=4,'gy_1'=4] {'gy_0'}, use_global_device_ids=true, to_apply=%region_11.12 | all-reduce | flops 4 | bytes 32 | tf_op jit(solution)/shard_map/psum | solution.py:36
  169.6 10.2 %psum.31 = f32[4]{0:T(128)S(1)} all-reduce(f32[4]{0:T(128)S(1)} %psum.30), channel_id=1, replica_groups=mesh['gx_0'=4,'gx_1'=2,'gy_0'=4,'gy_1'=4] {'gy_1'}, use_global_device_ids=true, to_apply=%region_12.13 | all-reduce | flops 4 | bytes 32 | tf_op jit(solution)/shard_map/psum | solution.py:36
  185.6 3.5 %multiply_subtract_fusion = (f32[32,64,128]{2,1,0:T(8,128)}, f32[32,64,128]{2,1,0:T(8,128)}) fusion(f32[32,64,128]{2,1,0:T(8,128)} %copy-done.2, f32[32,64,128]{2,1,0:T(8,128)} %get-tuple-element.30, f32[32,64,128]{2,1,0:T(8,128)S(1)} %get-tuple-element.34, f32[]{:T(128)S(6)} %div.34, f32[]{:T(128)S(6)} %div.35, f32[]{:T(128)S(6)} %div.33, ...), kind=kLoop, calls=%fused_computation.63 | loop fusion | flops 4718592 | bytes 7340044 | tf_op jit(solution)/shard_map/sub | solution.py:199
  (66 shorter events, 27.4 us)
Async XLA Ops:
  11.4 11.7 %copy-start = (f32[32,64,128]{2,1,0:T(8,128)S(1)}, f32[32,64,128]{2,1,0:T(8,128)}, u32[]{:S(2)}) copy-start(f32[32,64,128]{2,1,0:T(8,128)} %param.13) | copy-start | bytes 3145732
  11.4 54.7 %all-to-all-start = ((bf16[128,6,1664]{2,1,0:T(8,128)(2,1)}), bf16[128,6,1664]{2,1,0:T(8,128)(2,1)}, u32[]{:S(2)}, u32[]{:S(2)}) async-start(bf16[128,6,1664]{2,1,0:T(8,128)(2,1)} %reshape.93), calls=%async_computation | async-start | bytes 6815744 | tf_op jit(solution)/shard_map/all_to_all | solution.py:146
  23.1 8.5 %collective-permute-start.5 = (f32[1,64,128]{2,1,0:T(8,128)S(1)}, f32[1,64,128]{2,1,0:T(8,128)S(1)}, u32[]{:S(2)}, u32[]{:S(2)}) collective-permute-start(f32[1,64,128]{2,1,0:T(8,128)S(1)} %get-tuple-element.61), channel_id=1, source_target_pairs={{0,16},{16,32},{32,48},{48,64},{64,80},{80,96},{96,112},{1,17},{17... | collective-permute-start | bytes 98312 | tf_op jit(solution)/shard_map/ppermute | solution.py:22
  24.4 77.9 %collective-permute-start.6 = (f32[32,1,128]{2,1,0:T(1,128)S(1)}, f32[32,1,128]{2,1,0:T(1,128)S(1)}, u32[]{:S(2)}, u32[]{:S(2)}) collective-permute-start(f32[32,1,128]{2,1,0:T(1,128)S(1)} %get-tuple-element.58), channel_id=1, source_target_pairs={{1,0},{2,1},{3,2},{4,3},{5,4},{6,5},{7,6},{8,7},{9,8},{10,9},{11,1... | collective-permute-start | bytes 49160 | tf_op jit(solution)/shard_map/ppermute | solution.py:23
  25.7 80.4 %collective-permute-start.7 = (f32[32,1,128]{2,1,0:T(1,128)S(1)}, f32[32,1,128]{2,1,0:T(1,128)S(1)}, u32[]{:S(2)}, u32[]{:S(2)}) collective-permute-start(f32[32,1,128]{2,1,0:T(1,128)S(1)} %get-tuple-element.59), channel_id=1, source_target_pairs={{0,1},{1,2},{2,3},{3,4},{4,5},{5,6},{6,7},{7,8},{8,9},{9,10},{10,1... | collective-permute-start | bytes 49160 | tf_op jit(solution)/shard_map/ppermute | solution.py:22
  30.2 3.7 %collective-permute-start.4 = (f32[1,64,128]{2,1,0:T(8,128)S(1)}, f32[1,64,128]{2,1,0:T(8,128)S(1)}, u32[]{:S(2)}, u32[]{:S(2)}) collective-permute-start(f32[1,64,128]{2,1,0:T(8,128)S(1)} %get-tuple-element.60), channel_id=1, source_target_pairs={{16,0},{32,16},{48,32},{64,48},{80,64},{96,80},{112,96},{17,1},{33... | collective-permute-start | bytes 98312 | tf_op jit(solution)/shard_map/ppermute | solution.py:23
  95.2 11.0 %collective-permute-start.2 = (f32[32,1,128]{2,1,0:T(1,128)S(1)}, f32[32,1,128]{2,1,0:T(1,128)S(1)}, u32[]{:S(2)}, u32[]{:S(2)}) collective-permute-start(f32[32,1,128]{2,1,0:T(1,128)S(1)} %get-tuple-element.54), channel_id=1, source_target_pairs={{1,0},{2,1},{3,2},{4,3},{5,4},{6,5},{7,6},{8,7},{9,8},{10,9},{11,1... | collective-permute-start | bytes 49160 | tf_op jit(solution)/shard_map/ppermute | solution.py:48
  96.5 9.7 %collective-permute-start.3 = (f32[32,1,128]{2,1,0:T(1,128)S(1)}, f32[32,1,128]{2,1,0:T(1,128)S(1)}, u32[]{:S(2)}, u32[]{:S(2)}) collective-permute-start(f32[32,1,128]{2,1,0:T(1,128)S(1)} %get-tuple-element.55), channel_id=1, source_target_pairs={{0,1},{1,2},{2,3},{3,4},{4,5},{5,6},{6,7},{7,8},{8,9},{9,10},{10,1... | collective-permute-start | bytes 49160 | tf_op jit(solution)/shard_map/ppermute | solution.py:45
  101.0 5.1 %collective-permute-start = (f32[1,64,128]{2,1,0:T(8,128)S(1)}, f32[1,64,128]{2,1,0:T(8,128)S(1)}, u32[]{:S(2)}, u32[]{:S(2)}) collective-permute-start(f32[1,64,128]{2,1,0:T(8,128)S(1)} %get-tuple-element.35), channel_id=1, source_target_pairs={{16,0},{32,16},{48,32},{64,48},{80,64},{96,80},{112,96},{17,1},{33... | collective-permute-start | bytes 98312 | tf_op jit(solution)/shard_map/ppermute | solution.py:48
  102.3 3.9 %collective-permute-start.1 = (f32[1,64,128]{2,1,0:T(8,128)S(1)}, f32[1,64,128]{2,1,0:T(8,128)S(1)}, u32[]{:S(2)}, u32[]{:S(2)}) collective-permute-start(f32[1,64,128]{2,1,0:T(8,128)S(1)} %get-tuple-element.36), channel_id=1, source_target_pairs={{0,16},{16,32},{32,48},{48,64},{64,80},{80,96},{96,112},{1,17},{17... | collective-permute-start | bytes 98312 | tf_op jit(solution)/shard_map/ppermute | solution.py:45
  105.4 1.2 copy-start.1
  110.3 9.3 %collective-permute-start.10 = (f32[32,1,128]{2,1,0:T(1,128)S(1)}, f32[32,1,128]{2,1,0:T(1,128)S(1)}, u32[]{:S(2)}, u32[]{:S(2)}) collective-permute-start(f32[32,1,128]{2,1,0:T(1,128)S(1)} %get-tuple-element.48), channel_id=1, source_target_pairs={{1,0},{2,1},{3,2},{4,3},{5,4},{6,5},{7,6},{8,7},{9,8},{10,9},{11,1... | collective-permute-start | bytes 49160 | tf_op jit(solution)/shard_map/ppermute | solution.py:23
  111.6 8.0 %collective-permute-start.11 = (f32[32,1,128]{2,1,0:T(1,128)S(1)}, f32[32,1,128]{2,1,0:T(1,128)S(1)}, u32[]{:S(2)}, u32[]{:S(2)}) collective-permute-start(f32[32,1,128]{2,1,0:T(1,128)S(1)} %get-tuple-element.49), channel_id=1, source_target_pairs={{0,1},{1,2},{2,3},{3,4},{4,5},{5,6},{6,7},{7,8},{8,9},{9,10},{10,1... | collective-permute-start | bytes 49160 | tf_op jit(solution)/shard_map/ppermute | solution.py:22
  116.1 3.5 %collective-permute-start.9 = (f32[1,64,128]{2,1,0:T(8,128)S(1)}, f32[1,64,128]{2,1,0:T(8,128)S(1)}, u32[]{:S(2)}, u32[]{:S(2)}) collective-permute-start(f32[1,64,128]{2,1,0:T(8,128)S(1)} %get-tuple-element.50), channel_id=1, source_target_pairs={{0,16},{16,32},{32,48},{48,64},{64,80},{80,96},{96,112},{1,17},{17... | collective-permute-start | bytes 98312 | tf_op jit(solution)/shard_map/ppermute | solution.py:22
  117.9 5.3 %collective-permute-start.8 = (f32[1,64,128]{2,1,0:T(8,128)S(1)}, f32[1,64,128]{2,1,0:T(8,128)S(1)}, u32[]{:S(2)}, u32[]{:S(2)}) collective-permute-start(f32[1,64,128]{2,1,0:T(8,128)S(1)} %get-tuple-element.51), channel_id=1, source_target_pairs={{16,0},{32,16},{48,32},{64,48},{80,64},{96,80},{112,96},{17,1},{33... | collective-permute-start | bytes 98312 | tf_op jit(solution)/shard_map/ppermute | solution.py:23
  123.9 16.4 %copy-start.2 = (f32[32,64,128]{2,1,0:T(8,128)}, f32[32,64,128]{2,1,0:T(8,128)S(1)}, u32[]{:S(2)}) copy-start(f32[32,64,128]{2,1,0:T(8,128)S(1)} %get-tuple-element.32) | copy-start | bytes 3145732
  123.9 11.5 %collective-permute-start.14 = (f32[32,1,128]{2,1,0:T(1,128)S(1)}, f32[32,1,128]{2,1,0:T(1,128)S(1)}, u32[]{:S(2)}, u32[]{:S(2)}) collective-permute-start(f32[32,1,128]{2,1,0:T(1,128)S(1)} %get-tuple-element.42), channel_id=1, source_target_pairs={{1,0},{2,1},{3,2},{4,3},{5,4},{6,5},{7,6},{8,7},{9,8},{10,9},{11,1... | collective-permute-start | bytes 49160 | tf_op jit(solution)/shard_map/ppermute | solution.py:23
  125.2 10.2 %collective-permute-start.15 = (f32[32,1,128]{2,1,0:T(1,128)S(1)}, f32[32,1,128]{2,1,0:T(1,128)S(1)}, u32[]{:S(2)}, u32[]{:S(2)}) collective-permute-start(f32[32,1,128]{2,1,0:T(1,128)S(1)} %get-tuple-element.43), channel_id=1, source_target_pairs={{0,1},{1,2},{2,3},{3,4},{4,5},{5,6},{6,7},{7,8},{8,9},{9,10},{10,1... | collective-permute-start | bytes 49160 | tf_op jit(solution)/shard_map/ppermute | solution.py:22
  129.8 5.7 %collective-permute-start.13 = (f32[1,64,128]{2,1,0:T(8,128)S(1)}, f32[1,64,128]{2,1,0:T(8,128)S(1)}, u32[]{:S(2)}, u32[]{:S(2)}) collective-permute-start(f32[1,64,128]{2,1,0:T(8,128)S(1)} %get-tuple-element.44), channel_id=1, source_target_pairs={{0,16},{16,32},{32,48},{48,64},{64,80},{80,96},{96,112},{1,17},{17... | collective-permute-start | bytes 98312 | tf_op jit(solution)/shard_map/ppermute | solution.py:22
  133.8 3.2 %collective-permute-start.12 = (f32[1,64,128]{2,1,0:T(8,128)S(1)}, f32[1,64,128]{2,1,0:T(8,128)S(1)}, u32[]{:S(2)}, u32[]{:S(2)}) collective-permute-start(f32[1,64,128]{2,1,0:T(8,128)S(1)} %get-tuple-element.45), channel_id=1, source_target_pairs={{16,0},{32,16},{48,32},{64,48},{80,64},{96,80},{112,96},{17,1},{33... | collective-permute-start | bytes 98312 | tf_op jit(solution)/shard_map/ppermute | solution.py:23

commit v6 on v5

--- a/solution.py
+++ b/solution.py
@@ -182,7 +182,7 @@
                 jnp.sum(scaled * scaled_image),
             ]
         ),
-        GX_GY,
+        (GX, GY),
     )
     gamma, delta, energy, curvature = sums[0], sums[1], sums[2], sums[3]
     alpha = gamma / delta

time: 190 us -> 208 us (1.095)
  blocking collectives: 37 us -> 54.6 us
    psum x4 -> x2, blocking collectives: 37 us -> 54.6 us  [over_axes(): shard = lax.psum(shard, axis)]
  transfers between devices with their start and end apart: 17 -> 17, of which waited for: 4 -> 4; matrix products, arithmetic and copies ran while one was open for 10% -> 9% of each run, Pallas kernels for 8% -> 7%
where the time goes in v6:
time: 208 us; the launch traced here: 207 us
  blocking collectives  54.6 us (26%)
  starting transfers between devices  50.2 us (24%)
  waiting for transfers between devices  37.4 us (18%)
  other arithmetic  19.9 us (10%)
  local copies, waits for them, and re-layouts  16.7 us (8%)
  Pallas kernels  14.7 us (7%)
  matrix products  6.84 us (3%)
  between operations  6.23 us (3%)
    psum x2, blocking collectives, over_axes(): shard = lax.psum(shard, axis)  54.6 us
    all_to_all x1, waiting for transfers between devices, body(): lax.all_to_all(payload.reshape(peers, capacity, payload.shape[1]), GX_GY,...  31.6 us
    ppermute x6, starting transfers between devices, extended(): lax.ppermute(last, axis, up)  20.7 us
    pallas_call x1, Pallas kernels, to_grid(): pl.pallas_call(relayout_kernel, out_shape=jax.ShapeDtypeStruct((3, span_x...  14.7 us
    all_to_all x1, starting transfers between devices, body(): lax.all_to_all(payload.reshape(peers, capacity, payload.shape[1]), GX_GY,...  11.6 us
    ppermute x6, starting transfers between devices, extended(): lax.ppermute(first, axis, [(b, a) for a, b in up])  7.75 us
    ppermute x2, starting transfers between devices, with_halo(): lax.ppermute(lax.slice_in_dim(block, block.shape[dim] - width, None, axis...  7.58 us
    ppermute x6, waiting for transfers between devices, extended(): lax.ppermute(first, axis, [(b, a) for a, b in up])  5.75 us
  transfers between devices with their start and end apart: 17, of which 4 were waited for; matrix products, arithmetic and copies ran while one was open for 9% of the time, Pallas kernels for 7%

profile of v6, /device:TPU:0, one launch (start us, length us, event | category | flops | bytes accessed | tf_op | source)
XLA Modules:
  0.0 206.5 jit_solution(3054867778553826565)
XLA Ops:
  1.9 2.0 broadcast_select_fusion
  6.7 2.0 convolution_convert_fusion
  8.8 2.6 %reshape.93 = bf16[128,6,1664]{2,1,0:T(8,128)(2,1)} reshape(bf16[768,1664]{1,0:T(8,128)(2,1)S(1)} %convolution_convert_fusion) | data formatting | bytes 5111808 | tf_op jit(solution)/shard_map/reshape | solution.py:147
  11.4 11.6 %all-to-all-start = ((bf16[128,6,1664]{2,1,0:T(8,128)(2,1)}), bf16[128,6,1664]{2,1,0:T(8,128)(2,1)}, u32[]{:S(2)}, u32[]{:S(2)}) async-start(bf16[128,6,1664]{2,1,0:T(8,128)(2,1)} %reshape.93), calls=%async_computation | async-start | bytes 6815744 | tf_op jit(solution)/shard_map/all_to_all | solution.py:146
  25.7 4.5 %collective-permute-start.7 = (f32[32,1,128]{2,1,0:T(1,128)S(1)}, f32[32,1,128]{2,1,0:T(1,128)S(1)}, u32[]{:S(2)}, u32[]{:S(2)}) collective-permute-start(f32[32,1,128]{2,1,0:T(1,128)S(1)} %get-tuple-element.59), channel_id=1, source_target_pairs={{0,1},{1,2},{2,3},{3,4},{4,5},{5,6},{6,7},{7,8},{8,9},{9,10},{10,1... | collective-permute-start | bytes 49160 | tf_op jit(solution)/shard_map/ppermute | solution.py:22
  34.5 31.6 %all-to-all-done = bf16[128,6,1664]{2,1,0:T(8,128)(2,1)} async-done(((bf16[128,6,1664]{2,1,0:T(8,128)(2,1)}), bf16[128,6,1664]{2,1,0:T(8,128)(2,1)}, u32[]{:S(2)}, u32[]{:S(2)}) %all-to-all-start) | async-done | bytes 2555936 | tf_op jit(solution)/shard_map/all_to_all | solution.py:146
  66.1 5.4 %reshape.94 = bf16[768,1664]{1,0:T(8,128)(2,1)} reshape(bf16[128,6,1664]{2,1,0:T(8,128)(2,1)} %all-to-all-done) | data formatting | bytes 5111808 | tf_op jit(solution)/shard_map/reshape | solution.py:148
  72.7 4.8 %fusion.blk_ref = f32[512,1536]{1,0:T(8,128)} fusion(bf16[768,1664]{1,0:T(8,128)(2,1)} %reshape.94, s32[768]{0:T(1024)S(1)} %fusion.34), kind=kOutput, calls=%fused_computation.1 | convolution fusion | flops 1208352768 | bytes 5508096 | tf_op jit(solution)/shard_map/ks,kj->sj/dot_general | solution.py:156
  77.5 14.7 %shard_map.68 = f32[3,32,64,128]{3,2,1,0:T(8,128)} custom-call(f32[512,1536]{1,0:T(8,128)} %fusion.blk_ref), custom_call_target="tpu_custom_call" | custom-call | tf_op jit(solution)/shard_map/pallas_call | solution.py:134
  92.2 2.1 %slice_bitcast_fusion.2 = (f32[32,64,128]{2,1,0:T(8,128)S(1)}, f32[32,64,128]{2,1,0:T(8,128)S(1)}, f32[32,64,128]{2,1,0:T(8,128)S(1)}) fusion(f32[3,32,64,128]{3,2,1,0:T(8,128)} %shard_map.68), kind=kLoop, calls=%fused_computation.62 | loop fusion | bytes 6291456 | tf_op jit(solution)/shard_map/squeeze | solution.py:163
  96.4 4.5 %collective-permute-start.3 = (f32[32,1,128]{2,1,0:T(1,128)S(1)}, f32[32,1,128]{2,1,0:T(1,128)S(1)}, u32[]{:S(2)}, u32[]{:S(2)}) collective-permute-start(f32[32,1,128]{2,1,0:T(1,128)S(1)} %get-tuple-element.55), channel_id=1, source_target_pairs={{0,1},{1,2},{2,3},{3,4},{4,5},{5,6},{6,7},{7,8},{8,9},{9,10},{10,1... | collective-permute-start | bytes 49160 | tf_op jit(solution)/shard_map/ppermute | solution.py:45
  102.3 3.0 %collective-permute-start.1 = (f32[1,64,128]{2,1,0:T(8,128)S(1)}, f32[1,64,128]{2,1,0:T(8,128)S(1)}, u32[]{:S(2)}, u32[]{:S(2)}) collective-permute-start(f32[1,64,128]{2,1,0:T(8,128)S(1)} %get-tuple-element.36), channel_id=1, source_target_pairs={{0,16},{16,32},{32,48},{48,64},{64,80},{80,96},{96,112},{1,17},{17... | collective-permute-start | bytes 98312 | tf_op jit(solution)/shard_map/ppermute | solution.py:45
  106.5 3.6 %fusion.45 = (f32[32,64,128]{2,1,0:T(8,128)S(1)}, f32[32,64,128]{2,1,0:T(8,128)S(1)}) fusion(f32[32,64,128]{2,1,0:T(8,128)S(1)} %copy-done.1, f32[32,64,127]{2,1,0:T(8,128)S(1)} %get-tuple-element.70, f32[32,64,127]{2,1,0:T(8,128)S(1)} %get-tuple-element.71, f32[34,64,128]{2,1,0:T(8,128)} %constant_dynamic-update-slice_fusion, ...), kind=kLoop, calls=%fused_computation.114 | loop fusion | flops 8126464 | bytes 11763712 | tf_op jit(solution)/shard_map/mul | solution.py:172
  111.5 4.5 %collective-permute-start.11 = (f32[32,1,128]{2,1,0:T(1,128)S(1)}, f32[32,1,128]{2,1,0:T(1,128)S(1)}, u32[]{:S(2)}, u32[]{:S(2)}) collective-permute-start(f32[32,1,128]{2,1,0:T(1,128)S(1)} %get-tuple-element.49), channel_id=1, source_target_pairs={{0,1},{1,2},{2,3},{3,4},{4,5},{5,6},{6,7},{7,8},{8,9},{9,10},{10,1... | collective-permute-start | bytes 49160 | tf_op jit(solution)/shard_map/ppermute | solution.py:22
  116.0 1.8 collective-permute-start.9
  119.5 3.5 %collective-permute-done.8 = f32[1,64,128]{2,1,0:T(8,128)S(1)} collective-permute-done((f32[1,64,128]{2,1,0:T(8,128)S(1)}, f32[1,64,128]{2,1,0:T(8,128)S(1)}, u32[]{:S(2)}, u32[]{:S(2)}) %collective-permute-start.8) | collective-permute-done | bytes 32800 | tf_op jit(solution)/shard_map/ppermute | solution.py:23
  125.1 4.5 %collective-permute-start.15 = (f32[32,1,128]{2,1,0:T(1,128)S(1)}, f32[32,1,128]{2,1,0:T(1,128)S(1)}, u32[]{:S(2)}, u32[]{:S(2)}) collective-permute-start(f32[32,1,128]{2,1,0:T(1,128)S(1)} %get-tuple-element.43), channel_id=1, source_target_pairs={{0,1},{1,2},{2,3},{3,4},{4,5},{5,6},{6,7},{7,8},{8,9},{9,10},{10,1... | collective-permute-start | bytes 49160 | tf_op jit(solution)/shard_map/ppermute | solution.py:22
  129.7 4.0 %collective-permute-start.13 = (f32[1,64,128]{2,1,0:T(8,128)S(1)}, f32[1,64,128]{2,1,0:T(8,128)S(1)}, u32[]{:S(2)}, u32[]{:S(2)}) collective-permute-start(f32[1,64,128]{2,1,0:T(8,128)S(1)} %get-tuple-element.44), channel_id=1, source_target_pairs={{0,16},{16,32},{32,48},{48,64},{64,80},{80,96},{96,112},{1,17},{17... | collective-permute-start | bytes 98312 | tf_op jit(solution)/shard_map/ppermute | solution.py:22
  135.3 1.5 collective-permute-done.12
  136.8 3.3 %multiply_reduce_fusion.3 = (f32[]{:T(128)}, f32[]{:T(128)}, f32[]{:T(128)}, f32[]{:T(128)}, f32[32,64,128]{2,1,0:T(8,128)}) fusion(f32[32,64,128]{2,1,0:T(8,128)S(1)} %get-tuple-element.34, f32[32,64,128]{2,1,0:T(8,128)S(1)} %copy-done.1, f32[32,64,128]{2,1,0:T(8,128)S(1)} %get-tuple-element.32, f32[32,64,128]{2,1,0:T(8,128)S(1)} %get-tuple-element.31, ...), kind=kLoop, calls=%fused_computation.69 | loop fusion | flops 8388604 | bytes 7421968 | tf_op jit(solution)/shard_map/reduce_sum | solution.py:179
  140.1 2.5 %pad_maximum_fusion.20 = f32[4]{0:T(128)S(1)} fusion(f32[1]{0:T(128)} %bitcast.13, f32[1]{0:T(128)} %bitcast.12, f32[1]{0:T(128)} %bitcast.11, f32[1]{0:T(128)} %bitcast.10), kind=kLoop, calls=%fused_computation.108 | loop fusion | flops 12 | bytes 32 | tf_op jit(solution)/shard_map/stack | solution.py:177
  142.7 15.0 %psum.14 = f32[4]{0:T(128)S(1)} all-reduce(f32[4]{0:T(128)S(1)} %pad_maximum_fusion.20), channel_id=1, replica_groups=mesh['gx_0'=4,'gx_1'=2,'gy_0'=4,'gy_1'=4] {'gx_0','gx_1'}, use_global_device_ids=true, to_apply=%region_9.10 | all-reduce | flops 4 | bytes 32 | tf_op jit(solution)/shard_map/psum | solution.py:36
  157.7 39.5 %psum.15 = f32[4]{0:T(128)S(1)} all-reduce(f32[4]{0:T(128)S(1)} %psum.14), channel_id=1, replica_groups=mesh['gx_0'=4,'gx_1'=2,'gy_0'=4,'gy_1'=4] {'gy_0','gy_1'}, use_global_device_ids=true, to_apply=%region_10.11 | all-reduce | flops 4 | bytes 32 | tf_op jit(solution)/shard_map/psum | solution.py:36
  203.0 3.5 %multiply_subtract_fusion = (f32[32,64,128]{2,1,0:T(8,128)}, f32[32,64,128]{2,1,0:T(8,128)}) fusion(f32[32,64,128]{2,1,0:T(8,128)} %copy-done.2, f32[32,64,128]{2,1,0:T(8,128)} %get-tuple-element.30, f32[32,64,128]{2,1,0:T(8,128)S(1)} %get-tuple-element.34, f32[]{:T(128)S(6)} %div.34, f32[]{:T(128)S(6)} %div.35, f32[]{:T(128)S(6)} %div.33, ...), kind=kLoop, calls=%fused_computation.63 | loop fusion | flops 4718592 | bytes 7340044 | tf_op jit(solution)/shard_map/sub | solution.py:199
  (64 shorter events, 24.1 us)
Async XLA Ops:
  11.4 11.7 %copy-start = (f32[32,64,128]{2,1,0:T(8,128)S(1)}, f32[32,64,128]{2,1,0:T(8,128)}, u32[]{:S(2)}) copy-start(f32[32,64,128]{2,1,0:T(8,128)} %param.13) | copy-start | bytes 3145732
  11.4 54.7 %all-to-all-start = ((bf16[128,6,1664]{2,1,0:T(8,128)(2,1)}), bf16[128,6,1664]{2,1,0:T(8,128)(2,1)}, u32[]{:S(2)}, u32[]{:S(2)}) async-start(bf16[128,6,1664]{2,1,0:T(8,128)(2,1)} %reshape.93), calls=%async_computation | async-start | bytes 6815744 | tf_op jit(solution)/shard_map/all_to_all | solution.py:146
  23.1 8.5 %collective-permute-start.5 = (f32[1,64,128]{2,1,0:T(8,128)S(1)}, f32[1,64,128]{2,1,0:T(8,128)S(1)}, u32[]{:S(2)}, u32[]{:S(2)}) collective-permute-start(f32[1,64,128]{2,1,0:T(8,128)S(1)} %get-tuple-element.61), channel_id=1, source_target_pairs={{0,16},{16,32},{32,48},{48,64},{64,80},{80,96},{96,112},{1,17},{17... | collective-permute-start | bytes 98312 | tf_op jit(solution)/shard_map/ppermute | solution.py:22
  24.4 77.9 %collective-permute-start.6 = (f32[32,1,128]{2,1,0:T(1,128)S(1)}, f32[32,1,128]{2,1,0:T(1,128)S(1)}, u32[]{:S(2)}, u32[]{:S(2)}) collective-permute-start(f32[32,1,128]{2,1,0:T(1,128)S(1)} %get-tuple-element.58), channel_id=1, source_target_pairs={{1,0},{2,1},{3,2},{4,3},{5,4},{6,5},{7,6},{8,7},{9,8},{10,9},{11,1... | collective-permute-start | bytes 49160 | tf_op jit(solution)/shard_map/ppermute | solution.py:23
  25.7 80.5 %collective-permute-start.7 = (f32[32,1,128]{2,1,0:T(1,128)S(1)}, f32[32,1,128]{2,1,0:T(1,128)S(1)}, u32[]{:S(2)}, u32[]{:S(2)}) collective-permute-start(f32[32,1,128]{2,1,0:T(1,128)S(1)} %get-tuple-element.59), channel_id=1, source_target_pairs={{0,1},{1,2},{2,3},{3,4},{4,5},{5,6},{6,7},{7,8},{8,9},{9,10},{10,1... | collective-permute-start | bytes 49160 | tf_op jit(solution)/shard_map/ppermute | solution.py:22
  30.2 3.7 %collective-permute-start.4 = (f32[1,64,128]{2,1,0:T(8,128)S(1)}, f32[1,64,128]{2,1,0:T(8,128)S(1)}, u32[]{:S(2)}, u32[]{:S(2)}) collective-permute-start(f32[1,64,128]{2,1,0:T(8,128)S(1)} %get-tuple-element.60), channel_id=1, source_target_pairs={{16,0},{32,16},{48,32},{64,48},{80,64},{96,80},{112,96},{17,1},{33... | collective-permute-start | bytes 98312 | tf_op jit(solution)/shard_map/ppermute | solution.py:23
  95.1 11.0 %collective-permute-start.2 = (f32[32,1,128]{2,1,0:T(1,128)S(1)}, f32[32,1,128]{2,1,0:T(1,128)S(1)}, u32[]{:S(2)}, u32[]{:S(2)}) collective-permute-start(f32[32,1,128]{2,1,0:T(1,128)S(1)} %get-tuple-element.54), channel_id=1, source_target_pairs={{1,0},{2,1},{3,2},{4,3},{5,4},{6,5},{7,6},{8,7},{9,8},{10,9},{11,1... | collective-permute-start | bytes 49160 | tf_op jit(solution)/shard_map/ppermute | solution.py:48
  96.4 9.8 %collective-permute-start.3 = (f32[32,1,128]{2,1,0:T(1,128)S(1)}, f32[32,1,128]{2,1,0:T(1,128)S(1)}, u32[]{:S(2)}, u32[]{:S(2)}) collective-permute-start(f32[32,1,128]{2,1,0:T(1,128)S(1)} %get-tuple-element.55), channel_id=1, source_target_pairs={{0,1},{1,2},{2,3},{3,4},{4,5},{5,6},{6,7},{7,8},{8,9},{9,10},{10,1... | collective-permute-start | bytes 49160 | tf_op jit(solution)/shard_map/ppermute | solution.py:45
  100.9 5.2 %collective-permute-start = (f32[1,64,128]{2,1,0:T(8,128)S(1)}, f32[1,64,128]{2,1,0:T(8,128)S(1)}, u32[]{:S(2)}, u32[]{:S(2)}) collective-permute-start(f32[1,64,128]{2,1,0:T(8,128)S(1)} %get-tuple-element.35), channel_id=1, source_target_pairs={{16,0},{32,16},{48,32},{64,48},{80,64},{96,80},{112,96},{17,1},{33... | collective-permute-start | bytes 98312 | tf_op jit(solution)/shard_map/ppermute | solution.py:48
  102.3 3.9 %collective-permute-start.1 = (f32[1,64,128]{2,1,0:T(8,128)S(1)}, f32[1,64,128]{2,1,0:T(8,128)S(1)}, u32[]{:S(2)}, u32[]{:S(2)}) collective-permute-start(f32[1,64,128]{2,1,0:T(8,128)S(1)} %get-tuple-element.36), channel_id=1, source_target_pairs={{0,16},{16,32},{32,48},{48,64},{64,80},{80,96},{96,112},{1,17},{17... | collective-permute-start | bytes 98312 | tf_op jit(solution)/shard_map/ppermute | solution.py:45
  105.3 1.2 copy-start.1
  110.2 9.3 %collective-permute-start.10 = (f32[32,1,128]{2,1,0:T(1,128)S(1)}, f32[32,1,128]{2,1,0:T(1,128)S(1)}, u32[]{:S(2)}, u32[]{:S(2)}) collective-permute-start(f32[32,1,128]{2,1,0:T(1,128)S(1)} %get-tuple-element.48), channel_id=1, source_target_pairs={{1,0},{2,1},{3,2},{4,3},{5,4},{6,5},{7,6},{8,7},{9,8},{10,9},{11,1... | collective-permute-start | bytes 49160 | tf_op jit(solution)/shard_map/ppermute | solution.py:23
  111.5 8.0 %collective-permute-start.11 = (f32[32,1,128]{2,1,0:T(1,128)S(1)}, f32[32,1,128]{2,1,0:T(1,128)S(1)}, u32[]{:S(2)}, u32[]{:S(2)}) collective-permute-start(f32[32,1,128]{2,1,0:T(1,128)S(1)} %get-tuple-element.49), channel_id=1, source_target_pairs={{0,1},{1,2},{2,3},{3,4},{4,5},{5,6},{6,7},{7,8},{8,9},{9,10},{10,1... | collective-permute-start | bytes 49160 | tf_op jit(solution)/shard_map/ppermute | solution.py:22
  116.0 3.5 %collective-permute-start.9 = (f32[1,64,128]{2,1,0:T(8,128)S(1)}, f32[1,64,128]{2,1,0:T(8,128)S(1)}, u32[]{:S(2)}, u32[]{:S(2)}) collective-permute-start(f32[1,64,128]{2,1,0:T(8,128)S(1)} %get-tuple-element.50), channel_id=1, source_target_pairs={{0,16},{16,32},{32,48},{48,64},{64,80},{80,96},{96,112},{1,17},{17... | collective-permute-start | bytes 98312 | tf_op jit(solution)/shard_map/ppermute | solution.py:22
  117.8 5.3 %collective-permute-start.8 = (f32[1,64,128]{2,1,0:T(8,128)S(1)}, f32[1,64,128]{2,1,0:T(8,128)S(1)}, u32[]{:S(2)}, u32[]{:S(2)}) collective-permute-start(f32[1,64,128]{2,1,0:T(8,128)S(1)} %get-tuple-element.51), channel_id=1, source_target_pairs={{16,0},{32,16},{48,32},{64,48},{80,64},{96,80},{112,96},{17,1},{33... | collective-permute-start | bytes 98312 | tf_op jit(solution)/shard_map/ppermute | solution.py:23
  123.7 16.4 %copy-start.2 = (f32[32,64,128]{2,1,0:T(8,128)}, f32[32,64,128]{2,1,0:T(8,128)S(1)}, u32[]{:S(2)}) copy-start(f32[32,64,128]{2,1,0:T(8,128)S(1)} %get-tuple-element.32) | copy-start | bytes 3145732
  123.8 11.5 %collective-permute-start.14 = (f32[32,1,128]{2,1,0:T(1,128)S(1)}, f32[32,1,128]{2,1,0:T(1,128)S(1)}, u32[]{:S(2)}, u32[]{:S(2)}) collective-permute-start(f32[32,1,128]{2,1,0:T(1,128)S(1)} %get-tuple-element.42), channel_id=1, source_target_pairs={{1,0},{2,1},{3,2},{4,3},{5,4},{6,5},{7,6},{8,7},{9,8},{10,9},{11,1... | collective-permute-start | bytes 49160 | tf_op jit(solution)/shard_map/ppermute | solution.py:23
  125.1 10.2 %collective-permute-start.15 = (f32[32,1,128]{2,1,0:T(1,128)S(1)}, f32[32,1,128]{2,1,0:T(1,128)S(1)}, u32[]{:S(2)}, u32[]{:S(2)}) collective-permute-start(f32[32,1,128]{2,1,0:T(1,128)S(1)} %get-tuple-element.43), channel_id=1, source_target_pairs={{0,1},{1,2},{2,3},{3,4},{4,5},{5,6},{6,7},{7,8},{8,9},{9,10},{10,1... | collective-permute-start | bytes 49160 | tf_op jit(solution)/shard_map/ppermute | solution.py:22
  129.7 5.7 %collective-permute-start.13 = (f32[1,64,128]{2,1,0:T(8,128)S(1)}, f32[1,64,128]{2,1,0:T(8,128)S(1)}, u32[]{:S(2)}, u32[]{:S(2)}) collective-permute-start(f32[1,64,128]{2,1,0:T(8,128)S(1)} %get-tuple-element.44), channel_id=1, source_target_pairs={{0,16},{16,32},{32,48},{48,64},{64,80},{80,96},{96,112},{1,17},{17... | collective-permute-start | bytes 98312 | tf_op jit(solution)/shard_map/ppermute | solution.py:22
  133.6 3.2 %collective-permute-start.12 = (f32[1,64,128]{2,1,0:T(8,128)S(1)}, f32[1,64,128]{2,1,0:T(8,128)S(1)}, u32[]{:S(2)}, u32[]{:S(2)}) collective-permute-start(f32[1,64,128]{2,1,0:T(8,128)S(1)} %get-tuple-element.45), channel_id=1, source_target_pairs={{16,0},{32,16},{48,32},{64,48},{80,64},{96,80},{112,96},{17,1},{33... | collective-permute-start | bytes 98312 | tf_op jit(solution)/shard_map/ppermute | solution.py:23

commit v7 on v6

--- a/solution.py
+++ b/solution.py
@@ -6,9 +6,10 @@
 from jax.experimental import pallas as pl
 from jax.experimental.pallas import tpu as pltpu
 
-GX_GY = ("gx_0", "gx_1", "gy_0", "gy_1")
-GX = ("gx_0", "gx_1")
-GY = ("gy_0", "gy_1")
+GX = ("y_hi", "y_lo", "core")
+GY = ("x_hi", "x_lo", "z_hi", "z_lo")
+GX_GY = GX + GY
+PAIRS = ("core", "y_lo", "y_hi", "z_lo", "z_hi", "x_lo", "x_hi")
 
 
 def extended(shard, sides, width):
@@ -182,7 +183,7 @@
                 jnp.sum(scaled * scaled_image),
             ]
         ),
-        (GX, GY),
+        PAIRS,
     )
     gamma, delta, energy, curvature = sums[0], sums[1], sums[2], sums[3]
     alpha = gamma / delta
@@ -201,7 +202,7 @@
 
 
 def solution(mesh):
-    split = Mesh(mesh.devices.reshape(4, 2, 4, 4), ("gx_0", "gx_1", "gy_0", "gy_1"))
+    split = Mesh(mesh.devices.reshape((2,) * 7), GX_GY)
     placed = (P(GX_GY, None), P(GX_GY, None), P(GX_GY), P(GX, GY, None), P(GX, GY, None))
     return jax.shard_map(
         body,

time: 208 us -> 196 us (0.942)
  blocking collectives: 54.6 us -> 42.6 us
    psum x2 -> x7, blocking collectives: 54.6 us -> 42.6 us  [over_axes(): shard = lax.psum(shard, axis)]
  transfers between devices with their start and end apart: 17 -> 17, of which waited for: 4 -> 4; matrix products, arithmetic and copies ran while one was open for 9% -> 9% of each run, Pallas kernels for 7% -> 8%
where the time goes in v7:
time: 196 us; the launch traced here: 195 us
  starting transfers between devices  50.2 us (26%)
  blocking collectives  42.6 us (22%)
  waiting for transfers between devices  37.4 us (19%)
  other arithmetic  20 us (10%)
  local copies, waits for them, and re-layouts  16.7 us (9%)
  Pallas kernels  14.7 us (8%)
  matrix products  6.86 us (4%)
  between operations  6.16 us (3%)
    psum x7, blocking collectives, over_axes(): shard = lax.psum(shard, axis)  42.6 us
    all_to_all x1, waiting for transfers between devices, body(): lax.all_to_all(payload.reshape(peers, capacity, payload.shape[1]), GX_GY,...  31.6 us
    ppermute x6, starting transfers between devices, extended(): lax.ppermute(last, axis, up)  20.7 us
    pallas_call x1, Pallas kernels, to_grid(): pl.pallas_call(relayout_kernel, out_shape=jax.ShapeDtypeStruct((3, span_x...  14.7 us
    all_to_all x1, starting transfers between devices, body(): lax.all_to_all(payload.reshape(peers, capacity, payload.shape[1]), GX_GY,...  11.6 us
    ppermute x6, starting transfers between devices, extended(): lax.ppermute(first, axis, [(b, a) for a, b in up])  7.75 us
    ppermute x2, starting transfers between devices, with_halo(): lax.ppermute(lax.slice_in_dim(block, block.shape[dim] - width, None, axis...  7.58 us
    ppermute x6, waiting for transfers between devices, extended(): lax.ppermute(first, axis, [(b, a) for a, b in up])  5.75 us
  transfers between devices with their start and end apart: 17, of which 4 were waited for; matrix products, arithmetic and copies ran while one was open for 9% of the time, Pallas kernels for 8%

profile of v7, /device:TPU:0, one launch (start us, length us, event | category | flops | bytes accessed | tf_op | source)
XLA Modules:
  0.0 194.7 jit_solution(1708859992933379489)
XLA Ops:
  8.8 2.6 %reshape.93 = bf16[128,6,1664]{2,1,0:T(8,128)(2,1)} reshape(bf16[768,1664]{1,0:T(8,128)(2,1)S(1)} %convolution_convert_fusion) | data formatting | bytes 5111808 | tf_op jit(solution)/shard_map/reshape | solution.py:148
  11.4 11.6 %all-to-all-start = ((bf16[128,6,1664]{2,1,0:T(8,128)(2,1)}), bf16[128,6,1664]{2,1,0:T(8,128)(2,1)}, u32[]{:S(2)}, u32[]{:S(2)}) async-start(bf16[128,6,1664]{2,1,0:T(8,128)(2,1)} %reshape.93), calls=%async_computation | async-start | bytes 6815744 | tf_op jit(solution)/shard_map/all_to_all | solution.py:147
  25.7 4.5 %collective-permute-start.7 = (f32[32,1,128]{2,1,0:T(1,128)S(1)}, f32[32,1,128]{2,1,0:T(1,128)S(1)}, u32[]{:S(2)}, u32[]{:S(2)}) collective-permute-start(f32[32,1,128]{2,1,0:T(1,128)S(1)} %get-tuple-element.59), channel_id=1, source_target_pairs={{0,1},{1,2},{2,3},{3,4},{4,5},{5,6},{6,7},{7,8},{8,9},{9,10},{10,1... | collective-permute-start | bytes 49160 | tf_op jit(solution)/shard_map/ppermute | solution.py:23
  34.5 31.6 %all-to-all-done = bf16[128,6,1664]{2,1,0:T(8,128)(2,1)} async-done(((bf16[128,6,1664]{2,1,0:T(8,128)(2,1)}), bf16[128,6,1664]{2,1,0:T(8,128)(2,1)}, u32[]{:S(2)}, u32[]{:S(2)}) %all-to-all-start) | async-done | bytes 2555936 | tf_op jit(solution)/shard_map/all_to_all | solution.py:147
  66.1 5.4 %reshape.94 = bf16[768,1664]{1,0:T(8,128)(2,1)} reshape(bf16[128,6,1664]{2,1,0:T(8,128)(2,1)} %all-to-all-done) | data formatting | bytes 5111808 | tf_op jit(solution)/shard_map/reshape | solution.py:149
  72.7 4.8 %fusion.blk_ref = f32[512,1536]{1,0:T(8,128)} fusion(bf16[768,1664]{1,0:T(8,128)(2,1)} %reshape.94, s32[768]{0:T(1024)S(1)} %fusion.34), kind=kOutput, calls=%fused_computation.1 | convolution fusion | flops 1208352768 | bytes 5508096 | tf_op jit(solution)/shard_map/ks,kj->sj/dot_general | solution.py:157
  77.6 14.7 %shard_map.68 = f32[3,32,64,128]{3,2,1,0:T(8,128)} custom-call(f32[512,1536]{1,0:T(8,128)} %fusion.blk_ref), custom_call_target="tpu_custom_call" | custom-call | tf_op jit(solution)/shard_map/pallas_call | solution.py:135
  96.5 4.5 %collective-permute-start.3 = (f32[32,1,128]{2,1,0:T(1,128)S(1)}, f32[32,1,128]{2,1,0:T(1,128)S(1)}, u32[]{:S(2)}, u32[]{:S(2)}) collective-permute-start(f32[32,1,128]{2,1,0:T(1,128)S(1)} %get-tuple-element.55), channel_id=1, source_target_pairs={{0,1},{1,2},{2,3},{3,4},{4,5},{5,6},{6,7},{7,8},{8,9},{9,10},{10,1... | collective-permute-start | bytes 49160 | tf_op jit(solution)/shard_map/ppermute | solution.py:46
  102.3 3.0 %collective-permute-start.1 = (f32[1,64,128]{2,1,0:T(8,128)S(1)}, f32[1,64,128]{2,1,0:T(8,128)S(1)}, u32[]{:S(2)}, u32[]{:S(2)}) collective-permute-start(f32[1,64,128]{2,1,0:T(8,128)S(1)} %get-tuple-element.36), channel_id=1, source_target_pairs={{0,16},{16,32},{32,48},{48,64},{64,80},{80,96},{96,112},{1,17},{17... | collective-permute-start | bytes 98312 | tf_op jit(solution)/shard_map/ppermute | solution.py:46
  106.6 3.6 %fusion.45 = (f32[32,64,128]{2,1,0:T(8,128)S(1)}, f32[32,64,128]{2,1,0:T(8,128)S(1)}) fusion(f32[32,64,128]{2,1,0:T(8,128)S(1)} %copy-done.1, f32[32,64,127]{2,1,0:T(8,128)S(1)} %get-tuple-element.70, f32[32,64,127]{2,1,0:T(8,128)S(1)} %get-tuple-element.71, f32[34,64,128]{2,1,0:T(8,128)} %constant_dynamic-update-slice_fusion, ...), kind=kLoop, calls=%fused_computation.114 | loop fusion | flops 8126464 | bytes 11763712 | tf_op jit(solution)/shard_map/mul | solution.py:173
  111.6 4.5 %collective-permute-start.11 = (f32[32,1,128]{2,1,0:T(1,128)S(1)}, f32[32,1,128]{2,1,0:T(1,128)S(1)}, u32[]{:S(2)}, u32[]{:S(2)}) collective-permute-start(f32[32,1,128]{2,1,0:T(1,128)S(1)} %get-tuple-element.49), channel_id=1, source_target_pairs={{0,1},{1,2},{2,3},{3,4},{4,5},{5,6},{6,7},{7,8},{8,9},{9,10},{10,1... | collective-permute-start | bytes 49160 | tf_op jit(solution)/shard_map/ppermute | solution.py:23
  119.6 3.5 %collective-permute-done.8 = f32[1,64,128]{2,1,0:T(8,128)S(1)} collective-permute-done((f32[1,64,128]{2,1,0:T(8,128)S(1)}, f32[1,64,128]{2,1,0:T(8,128)S(1)}, u32[]{:S(2)}, u32[]{:S(2)}) %collective-permute-start.8) | collective-permute-done | bytes 32800 | tf_op jit(solution)/shard_map/ppermute | solution.py:24
  125.2 4.5 %collective-permute-start.15 = (f32[32,1,128]{2,1,0:T(1,128)S(1)}, f32[32,1,128]{2,1,0:T(1,128)S(1)}, u32[]{:S(2)}, u32[]{:S(2)}) collective-permute-start(f32[32,1,128]{2,1,0:T(1,128)S(1)} %get-tuple-element.43), channel_id=1, source_target_pairs={{0,1},{1,2},{2,3},{3,4},{4,5},{5,6},{6,7},{7,8},{8,9},{9,10},{10,1... | collective-permute-start | bytes 49160 | tf_op jit(solution)/shard_map/ppermute | solution.py:23
  129.8 4.0 %collective-permute-start.13 = (f32[1,64,128]{2,1,0:T(8,128)S(1)}, f32[1,64,128]{2,1,0:T(8,128)S(1)}, u32[]{:S(2)}, u32[]{:S(2)}) collective-permute-start(f32[1,64,128]{2,1,0:T(8,128)S(1)} %get-tuple-element.44), channel_id=1, source_target_pairs={{0,16},{16,32},{32,48},{48,64},{64,80},{80,96},{96,112},{1,17},{17... | collective-permute-start | bytes 98312 | tf_op jit(solution)/shard_map/ppermute | solution.py:23
  136.9 3.3 %multiply_reduce_fusion.3 = (f32[]{:T(128)}, f32[]{:T(128)}, f32[]{:T(128)}, f32[]{:T(128)}, f32[32,64,128]{2,1,0:T(8,128)}) fusion(f32[32,64,128]{2,1,0:T(8,128)S(1)} %get-tuple-element.34, f32[32,64,128]{2,1,0:T(8,128)S(1)} %copy-done.1, f32[32,64,128]{2,1,0:T(8,128)S(1)} %get-tuple-element.32, f32[32,64,128]{2,1,0:T(8,128)S(1)} %get-tuple-element.31, ...), kind=kLoop, calls=%fused_computation.69 | loop fusion | flops 8388604 | bytes 7421968 | tf_op jit(solution)/shard_map/reduce_sum | solution.py:180
  140.2 2.6 %pad_maximum_fusion.20 = f32[4]{0:T(128)S(1)} fusion(f32[1]{0:T(128)} %bitcast.13, f32[1]{0:T(128)} %bitcast.12, f32[1]{0:T(128)} %bitcast.11, f32[1]{0:T(128)} %bitcast.10), kind=kLoop, calls=%fused_computation.108 | loop fusion | flops 12 | bytes 32 | tf_op jit(solution)/shard_map/stack | solution.py:178
  142.8 4.7 %psum.49 = f32[4]{0:T(128)S(1)} all-reduce(f32[4]{0:T(128)S(1)} %pad_maximum_fusion.20), channel_id=1, replica_groups=mesh['y_hi'=2,'y_lo'=2,'core'=2,'x_hi'=2,'x_lo'=2,'z_hi'=2,'z_lo'=2] {'c..., use_global_device_ids=true, to_apply=%region_9.10 | all-reduce | flops 4 | bytes 32 | tf_op jit(solution)/shard_map/psum | solution.py:37
  147.6 4.9 %psum.50 = f32[4]{0:T(128)S(1)} all-reduce(f32[4]{0:T(128)S(1)} %psum.49), channel_id=1, replica_groups=mesh['y_hi'=2,'y_lo'=2,'core'=2,'x_hi'=2,'x_lo'=2,'z_hi'=2,'z_lo'=2] {'y..., use_global_device_ids=true, to_apply=%region_10.11 | all-reduce | flops 4 | bytes 32 | tf_op jit(solution)/shard_map/psum | solution.py:37
  152.5 6.4 %psum.51 = f32[4]{0:T(128)S(1)} all-reduce(f32[4]{0:T(128)S(1)} %psum.50), channel_id=1, replica_groups=mesh['y_hi'=2,'y_lo'=2,'core'=2,'x_hi'=2,'x_lo'=2,'z_hi'=2,'z_lo'=2] {'y..., use_global_device_ids=true, to_apply=%region_11.12 | all-reduce | flops 4 | bytes 32 | tf_op jit(solution)/shard_map/psum | solution.py:37
  158.9 4.9 %psum.52 = f32[4]{0:T(128)S(1)} all-reduce(f32[4]{0:T(128)S(1)} %psum.51), channel_id=1, replica_groups=mesh['y_hi'=2,'y_lo'=2,'core'=2,'x_hi'=2,'x_lo'=2,'z_hi'=2,'z_lo'=2] {'z..., use_global_device_ids=true, to_apply=%region_12.13 | all-reduce | flops 4 | bytes 32 | tf_op jit(solution)/shard_map/psum | solution.py:37
  163.8 10.3 %psum.53 = f32[4]{0:T(128)S(1)} all-reduce(f32[4]{0:T(128)S(1)} %psum.52), channel_id=1, replica_groups=mesh['y_hi'=2,'y_lo'=2,'core'=2,'x_hi'=2,'x_lo'=2,'z_hi'=2,'z_lo'=2] {'z..., use_global_device_ids=true, to_apply=%region_13.14 | all-reduce | flops 4 | bytes 32 | tf_op jit(solution)/shard_map/psum | solution.py:37
  174.1 4.9 %psum.54 = f32[4]{0:T(128)S(1)} all-reduce(f32[4]{0:T(128)S(1)} %psum.53), channel_id=1, replica_groups=mesh['y_hi'=2,'y_lo'=2,'core'=2,'x_hi'=2,'x_lo'=2,'z_hi'=2,'z_lo'=2] {'x..., use_global_device_ids=true, to_apply=%region_14.15 | all-reduce | flops 4 | bytes 32 | tf_op jit(solution)/shard_map/psum | solution.py:37
  179.0 6.4 %psum.55 = f32[4]{0:T(128)S(1)} all-reduce(f32[4]{0:T(128)S(1)} %psum.54), channel_id=1, replica_groups=mesh['y_hi'=2,'y_lo'=2,'core'=2,'x_hi'=2,'x_lo'=2,'z_hi'=2,'z_lo'=2] {'x..., use_global_device_ids=true, to_apply=%region_15.16 | all-reduce | flops 4 | bytes 32 | tf_op jit(solution)/shard_map/psum | solution.py:37
  191.2 3.5 %multiply_subtract_fusion = (f32[32,64,128]{2,1,0:T(8,128)}, f32[32,64,128]{2,1,0:T(8,128)}) fusion(f32[32,64,128]{2,1,0:T(8,128)} %copy-done.2, f32[32,64,128]{2,1,0:T(8,128)} %get-tuple-element.30, f32[32,64,128]{2,1,0:T(8,128)S(1)} %get-tuple-element.34, f32[]{:T(128)S(6)} %div.34, f32[]{:T(128)S(6)} %div.35, f32[]{:T(128)S(6)} %div.33, ...), kind=kLoop, calls=%fused_computation.63 | loop fusion | flops 4718592 | bytes 7340044 | tf_op jit(solution)/shard_map/sub | solution.py:200
  (69 shorter events, 33.4 us)
Async XLA Ops:
  11.4 11.7 %copy-start = (f32[32,64,128]{2,1,0:T(8,128)S(1)}, f32[32,64,128]{2,1,0:T(8,128)}, u32[]{:S(2)}) copy-start(f32[32,64,128]{2,1,0:T(8,128)} %param.13) | copy-start | bytes 3145732
  11.4 54.7 %all-to-all-start = ((bf16[128,6,1664]{2,1,0:T(8,128)(2,1)}), bf16[128,6,1664]{2,1,0:T(8,128)(2,1)}, u32[]{:S(2)}, u32[]{:S(2)}) async-start(bf16[128,6,1664]{2,1,0:T(8,128)(2,1)} %reshape.93), calls=%async_computation | async-start | bytes 6815744 | tf_op jit(solution)/shard_map/all_to_all | solution.py:147
  23.1 8.5 %collective-permute-start.5 = (f32[1,64,128]{2,1,0:T(8,128)S(1)}, f32[1,64,128]{2,1,0:T(8,128)S(1)}, u32[]{:S(2)}, u32[]{:S(2)}) collective-permute-start(f32[1,64,128]{2,1,0:T(8,128)S(1)} %get-tuple-element.61), channel_id=1, source_target_pairs={{0,16},{16,32},{32,48},{48,64},{64,80},{80,96},{96,112},{1,17},{17... | collective-permute-start | bytes 98312 | tf_op jit(solution)/shard_map/ppermute | solution.py:23
  24.4 77.9 %collective-permute-start.6 = (f32[32,1,128]{2,1,0:T(1,128)S(1)}, f32[32,1,128]{2,1,0:T(1,128)S(1)}, u32[]{:S(2)}, u32[]{:S(2)}) collective-permute-start(f32[32,1,128]{2,1,0:T(1,128)S(1)} %get-tuple-element.58), channel_id=1, source_target_pairs={{1,0},{2,1},{3,2},{4,3},{5,4},{6,5},{7,6},{8,7},{9,8},{10,9},{11,1... | collective-permute-start | bytes 49160 | tf_op jit(solution)/shard_map/ppermute | solution.py:24
  25.7 80.4 %collective-permute-start.7 = (f32[32,1,128]{2,1,0:T(1,128)S(1)}, f32[32,1,128]{2,1,0:T(1,128)S(1)}, u32[]{:S(2)}, u32[]{:S(2)}) collective-permute-start(f32[32,1,128]{2,1,0:T(1,128)S(1)} %get-tuple-element.59), channel_id=1, source_target_pairs={{0,1},{1,2},{2,3},{3,4},{4,5},{5,6},{6,7},{7,8},{8,9},{9,10},{10,1... | collective-permute-start | bytes 49160 | tf_op jit(solution)/shard_map/ppermute | solution.py:23
  30.2 3.7 %collective-permute-start.4 = (f32[1,64,128]{2,1,0:T(8,128)S(1)}, f32[1,64,128]{2,1,0:T(8,128)S(1)}, u32[]{:S(2)}, u32[]{:S(2)}) collective-permute-start(f32[1,64,128]{2,1,0:T(8,128)S(1)} %get-tuple-element.60), channel_id=1, source_target_pairs={{16,0},{32,16},{48,32},{64,48},{80,64},{96,80},{112,96},{17,1},{33... | collective-permute-start | bytes 98312 | tf_op jit(solution)/shard_map/ppermute | solution.py:24
  95.2 11.0 %collective-permute-start.2 = (f32[32,1,128]{2,1,0:T(1,128)S(1)}, f32[32,1,128]{2,1,0:T(1,128)S(1)}, u32[]{:S(2)}, u32[]{:S(2)}) collective-permute-start(f32[32,1,128]{2,1,0:T(1,128)S(1)} %get-tuple-element.54), channel_id=1, source_target_pairs={{1,0},{2,1},{3,2},{4,3},{5,4},{6,5},{7,6},{8,7},{9,8},{10,9},{11,1... | collective-permute-start | bytes 49160 | tf_op jit(solution)/shard_map/ppermute | solution.py:49
  96.5 9.7 %collective-permute-start.3 = (f32[32,1,128]{2,1,0:T(1,128)S(1)}, f32[32,1,128]{2,1,0:T(1,128)S(1)}, u32[]{:S(2)}, u32[]{:S(2)}) collective-permute-start(f32[32,1,128]{2,1,0:T(1,128)S(1)} %get-tuple-element.55), channel_id=1, source_target_pairs={{0,1},{1,2},{2,3},{3,4},{4,5},{5,6},{6,7},{7,8},{8,9},{9,10},{10,1... | collective-permute-start | bytes 49160 | tf_op jit(solution)/shard_map/ppermute | solution.py:46
  101.0 5.1 %collective-permute-start = (f32[1,64,128]{2,1,0:T(8,128)S(1)}, f32[1,64,128]{2,1,0:T(8,128)S(1)}, u32[]{:S(2)}, u32[]{:S(2)}) collective-permute-start(f32[1,64,128]{2,1,0:T(8,128)S(1)} %get-tuple-element.35), channel_id=1, source_target_pairs={{16,0},{32,16},{48,32},{64,48},{80,64},{96,80},{112,96},{17,1},{33... | collective-permute-start | bytes 98312 | tf_op jit(solution)/shard_map/ppermute | solution.py:49
  102.3 3.9 %collective-permute-start.1 = (f32[1,64,128]{2,1,0:T(8,128)S(1)}, f32[1,64,128]{2,1,0:T(8,128)S(1)}, u32[]{:S(2)}, u32[]{:S(2)}) collective-permute-start(f32[1,64,128]{2,1,0:T(8,128)S(1)} %get-tuple-element.36), channel_id=1, source_target_pairs={{0,16},{16,32},{32,48},{48,64},{64,80},{80,96},{96,112},{1,17},{17... | collective-permute-start | bytes 98312 | tf_op jit(solution)/shard_map/ppermute | solution.py:46
  105.4 1.2 copy-start.1
  110.3 9.3 %collective-permute-start.10 = (f32[32,1,128]{2,1,0:T(1,128)S(1)}, f32[32,1,128]{2,1,0:T(1,128)S(1)}, u32[]{:S(2)}, u32[]{:S(2)}) collective-permute-start(f32[32,1,128]{2,1,0:T(1,128)S(1)} %get-tuple-element.48), channel_id=1, source_target_pairs={{1,0},{2,1},{3,2},{4,3},{5,4},{6,5},{7,6},{8,7},{9,8},{10,9},{11,1... | collective-permute-start | bytes 49160 | tf_op jit(solution)/shard_map/ppermute | solution.py:24
  111.6 8.0 %collective-permute-start.11 = (f32[32,1,128]{2,1,0:T(1,128)S(1)}, f32[32,1,128]{2,1,0:T(1,128)S(1)}, u32[]{:S(2)}, u32[]{:S(2)}) collective-permute-start(f32[32,1,128]{2,1,0:T(1,128)S(1)} %get-tuple-element.49), channel_id=1, source_target_pairs={{0,1},{1,2},{2,3},{3,4},{4,5},{5,6},{6,7},{7,8},{8,9},{9,10},{10,1... | collective-permute-start | bytes 49160 | tf_op jit(solution)/shard_map/ppermute | solution.py:23
  116.1 3.5 %collective-permute-start.9 = (f32[1,64,128]{2,1,0:T(8,128)S(1)}, f32[1,64,128]{2,1,0:T(8,128)S(1)}, u32[]{:S(2)}, u32[]{:S(2)}) collective-permute-start(f32[1,64,128]{2,1,0:T(8,128)S(1)} %get-tuple-element.50), channel_id=1, source_target_pairs={{0,16},{16,32},{32,48},{48,64},{64,80},{80,96},{96,112},{1,17},{17... | collective-permute-start | bytes 98312 | tf_op jit(solution)/shard_map/ppermute | solution.py:23
  117.9 5.3 %collective-permute-start.8 = (f32[1,64,128]{2,1,0:T(8,128)S(1)}, f32[1,64,128]{2,1,0:T(8,128)S(1)}, u32[]{:S(2)}, u32[]{:S(2)}) collective-permute-start(f32[1,64,128]{2,1,0:T(8,128)S(1)} %get-tuple-element.51), channel_id=1, source_target_pairs={{16,0},{32,16},{48,32},{64,48},{80,64},{96,80},{112,96},{17,1},{33... | collective-permute-start | bytes 98312 | tf_op jit(solution)/shard_map/ppermute | solution.py:24
  123.9 16.4 %copy-start.2 = (f32[32,64,128]{2,1,0:T(8,128)}, f32[32,64,128]{2,1,0:T(8,128)S(1)}, u32[]{:S(2)}) copy-start(f32[32,64,128]{2,1,0:T(8,128)S(1)} %get-tuple-element.32) | copy-start | bytes 3145732
  123.9 11.5 %collective-permute-start.14 = (f32[32,1,128]{2,1,0:T(1,128)S(1)}, f32[32,1,128]{2,1,0:T(1,128)S(1)}, u32[]{:S(2)}, u32[]{:S(2)}) collective-permute-start(f32[32,1,128]{2,1,0:T(1,128)S(1)} %get-tuple-element.42), channel_id=1, source_target_pairs={{1,0},{2,1},{3,2},{4,3},{5,4},{6,5},{7,6},{8,7},{9,8},{10,9},{11,1... | collective-permute-start | bytes 49160 | tf_op jit(solution)/shard_map/ppermute | solution.py:24
  125.2 10.2 %collective-permute-start.15 = (f32[32,1,128]{2,1,0:T(1,128)S(1)}, f32[32,1,128]{2,1,0:T(1,128)S(1)}, u32[]{:S(2)}, u32[]{:S(2)}) collective-permute-start(f32[32,1,128]{2,1,0:T(1,128)S(1)} %get-tuple-element.43), channel_id=1, source_target_pairs={{0,1},{1,2},{2,3},{3,4},{4,5},{5,6},{6,7},{7,8},{8,9},{9,10},{10,1... | collective-permute-start | bytes 49160 | tf_op jit(solution)/shard_map/ppermute | solution.py:23
  129.8 5.7 %collective-permute-start.13 = (f32[1,64,128]{2,1,0:T(8,128)S(1)}, f32[1,64,128]{2,1,0:T(8,128)S(1)}, u32[]{:S(2)}, u32[]{:S(2)}) collective-permute-start(f32[1,64,128]{2,1,0:T(8,128)S(1)} %get-tuple-element.44), channel_id=1, source_target_pairs={{0,16},{16,32},{32,48},{48,64},{64,80},{80,96},{96,112},{1,17},{17... | collective-permute-start | bytes 98312 | tf_op jit(solution)/shard_map/ppermute | solution.py:23
  133.8 3.2 %collective-permute-start.12 = (f32[1,64,128]{2,1,0:T(8,128)S(1)}, f32[1,64,128]{2,1,0:T(8,128)S(1)}, u32[]{:S(2)}, u32[]{:S(2)}) collective-permute-start(f32[1,64,128]{2,1,0:T(8,128)S(1)} %get-tuple-element.45), channel_id=1, source_target_pairs={{16,0},{32,16},{48,32},{64,48},{80,64},{96,80},{112,96},{17,1},{33... | collective-permute-start | bytes 98312 | tf_op jit(solution)/shard_map/ppermute | solution.py:24

commit v8 on v5

--- a/solution.py
+++ b/solution.py
@@ -9,6 +9,13 @@
 GX_GY = ("gx_0", "gx_1", "gy_0", "gy_1")
 GX = ("gx_0", "gx_1")
 GY = ("gy_0", "gy_1")
+
+
+def shifted(piece, axis, pairs, dim):
+    if dim == 1:
+        flat = piece.reshape(piece.shape[0], piece.shape[2])
+        return lax.ppermute(flat, axis, pairs).reshape(piece.shape)
+    return lax.ppermute(piece, axis, pairs)
 
 
 def extended(shard, sides, width):
@@ -19,8 +26,8 @@
         last = lax.slice_in_dim(shard, length - width, length, axis=dim)
         first = lax.slice_in_dim(shard, 0, width, axis=dim)
         edges[dim] = (
-            lax.ppermute(last, axis, up),
-            lax.ppermute(first, axis, [(b, a) for a, b in up]),
+            shifted(last, axis, up, dim),
+            shifted(first, axis, [(b, a) for a, b in up], dim),
         )
     done = []
     for _, dim in sides:
@@ -42,10 +49,10 @@
         count = lax.axis_size(axis)
         forward = [(i, i + 1) for i in range(count - 1)]
         backward = [(target, source) for source, target in forward]
-        low = lax.ppermute(
-            lax.slice_in_dim(block, block.shape[dim] - width, None, axis=dim), axis, forward
+        low = shifted(
+            lax.slice_in_dim(block, block.shape[dim] - width, None, axis=dim), axis, forward, dim
         )
-        high = lax.ppermute(lax.slice_in_dim(block, 0, width, axis=dim), axis, backward)
+        high = shifted(lax.slice_in_dim(block, 0, width, axis=dim), axis, backward, dim)
         block = jnp.concatenate([low, block, high], axis=dim)
     return block
 

time: 190 us -> 190 us (level)
  starting transfers between devices: 50.2 us -> 48 us
    ppermute x16, starting transfers between devices: 38.6 us -> 36.4 us  [the longest x8 20.8 us: shifted(): return lax.ppermute(flat, axis, pairs).reshape(piece.shape)]
  transfers between devices with their start and end apart: 17 -> 17, of which waited for: 4 -> 5; matrix products, arithmetic and copies ran while one was open for 10% -> 10% of each run, Pallas kernels for 8% -> 8%
where the time goes in v8:
time: 190 us; the launch traced here: 188 us
  starting transfers between devices  48 us (25%)
  blocking collectives  38.1 us (20%)
  waiting for transfers between devices  37.9 us (20%)
  other arithmetic  20 us (11%)
  local copies, waits for them, and re-layouts  16.7 us (9%)
  Pallas kernels  14.7 us (8%)
  matrix products  6.86 us (4%)
  between operations  6.15 us (3%)
    psum x4, blocking collectives, over_axes(): shard = lax.psum(shard, axis)  38.1 us
    all_to_all x1, waiting for transfers between devices, body(): lax.all_to_all(payload.reshape(peers, capacity, payload.shape[1]), GX_GY,...  32.3 us
    ppermute x8, starting transfers between devices, shifted(): return lax.ppermute(flat, axis, pairs).reshape(piece.shape)  20.8 us
    ppermute x8, starting transfers between devices, shifted(): return lax.ppermute(piece, axis, pairs)  15.5 us
    pallas_call x1, Pallas kernels, to_grid(): pl.pallas_call(relayout_kernel, out_shape=jax.ShapeDtypeStruct((3, span_x...  14.7 us
    all_to_all x1, starting transfers between devices, body(): lax.all_to_all(payload.reshape(peers, capacity, payload.shape[1]), GX_GY,...  11.6 us
    reshape x1, local copies, waits for them, and re-layouts, body(): arrived = lax.all_to_all(payload.reshape(peers, capacity, payload.shape[1...  5.36 us
    dot_general x1, matrix products, body(): jnp.einsum('ks,kj->sj', picks.astype(jnp.bfloat16), arrived[:, :1536], pr...  4.84 us
  transfers between devices with their start and end apart: 17, of which 5 were waited for; matrix products, arithmetic and copies ran while one was open for 10% of the time, Pallas kernels for 8%

profile of v8, /device:TPU:0, one launch (start us, length us, event | category | flops | bytes accessed | tf_op | source)
XLA Modules:
  0.0 188.5 jit_solution(12097934430477853837)
XLA Ops:
  1.9 2.0 %broadcast_select_fusion = (bf16[256]{0:T(256)(128)(2,1)S(1)}, bf16[256]{0:T(256)(128)(2,1)S(1)}) fusion(pred[]{:T(512)} %compare_reduce_fusion, s32[256]{0:T(256)} %param.11, pred[]{:T(512)} %compare_reduce_fusion.1), kind=kLoop, calls=%fused_computation.105 | loop fusion | flops 5888 | bytes 2050 | tf_op jit(solution)/shard_map/select.12
  6.7 2.0 %convolution_convert_fusion = bf16[768,1664]{1,0:T(8,128)(2,1)S(1)} fusion(bf16[256,128]{1,0:T(8,128)(2,1)S(1)} %copy.18, bf16[256,1536]{1,0:T(8,128)(2,1)} %param.9, s32[256]{0:T(256)S(1)} %multiply_add_fusion.1), kind=kOutput, calls=%fused_computation | convolution fusion | flops 657489920 | bytes 3408896 | tf_op jit(solution)/shard_map/pk,kj->pj/dot_general | solution.py:71
  8.8 2.6 %reshape.141 = bf16[128,6,1664]{2,1,0:T(8,128)(2,1)} reshape(bf16[768,1664]{1,0:T(8,128)(2,1)S(1)} %convolution_convert_fusion) | data formatting | bytes 5111808 | tf_op jit(solution)/shard_map/reshape | solution.py:154
  11.4 11.6 %all-to-all-start = ((bf16[128,6,1664]{2,1,0:T(8,128)(2,1)}), bf16[128,6,1664]{2,1,0:T(8,128)(2,1)}, u32[]{:S(2)}, u32[]{:S(2)}) async-start(bf16[128,6,1664]{2,1,0:T(8,128)(2,1)} %reshape.141), calls=%async_computation | async-start | bytes 6815744 | tf_op jit(solution)/shard_map/all_to_all | solution.py:153
  24.4 3.7 %collective-permute-start.7 = (f32[32,128]{1,0:T(8,128)S(1)}, f32[32,128]{1,0:T(8,128)S(1)}, u32[]{:S(2)}, u32[]{:S(2)}) collective-permute-start(f32[32,128]{1,0:T(8,128)S(1)} %bitcast.77), channel_id=1, source_target_pairs={{0,1},{1,2},{2,3},{3,4},{4,5},{5,6},{6,7},{7,8},{8,9},{9,10},{10,1... | collective-permute-start | bytes 49160 | tf_op jit(solution)/shard_map/ppermute | solution.py:17
  33.8 32.3 %all-to-all-done = bf16[128,6,1664]{2,1,0:T(8,128)(2,1)} async-done(((bf16[128,6,1664]{2,1,0:T(8,128)(2,1)}), bf16[128,6,1664]{2,1,0:T(8,128)(2,1)}, u32[]{:S(2)}, u32[]{:S(2)}) %all-to-all-start) | async-done | bytes 2555936 | tf_op jit(solution)/shard_map/all_to_all | solution.py:153
  66.1 5.4 %reshape.142 = bf16[768,1664]{1,0:T(8,128)(2,1)} reshape(bf16[128,6,1664]{2,1,0:T(8,128)(2,1)} %all-to-all-done) | data formatting | bytes 5111808 | tf_op jit(solution)/shard_map/reshape | solution.py:155
  72.7 4.8 %fusion.blk_ref = f32[512,1536]{1,0:T(8,128)} fusion(bf16[768,1664]{1,0:T(8,128)(2,1)} %reshape.142, s32[768]{0:T(1024)S(1)} %fusion.34), kind=kOutput, calls=%fused_computation.1 | convolution fusion | flops 1208352768 | bytes 5508096 | tf_op jit(solution)/shard_map/ks,kj->sj/dot_general | solution.py:163
  77.6 14.7 %shard_map.68 = f32[3,32,64,128]{3,2,1,0:T(8,128)} custom-call(f32[512,1536]{1,0:T(8,128)} %fusion.blk_ref), custom_call_target="tpu_custom_call" | custom-call | tf_op jit(solution)/shard_map/pallas_call | solution.py:141
  92.3 2.1 %slice_bitcast_fusion.2 = (f32[32,64,128]{2,1,0:T(8,128)S(1)}, f32[32,64,128]{2,1,0:T(8,128)S(1)}, f32[32,64,128]{2,1,0:T(8,128)S(1)}) fusion(f32[3,32,64,128]{3,2,1,0:T(8,128)} %shard_map.68), kind=kLoop, calls=%fused_computation.62 | loop fusion | bytes 6291456 | tf_op jit(solution)/shard_map/squeeze | solution.py:170
  95.2 2.9 %collective-permute-start.3 = (f32[32,128]{1,0:T(8,128)S(1)}, f32[32,128]{1,0:T(8,128)S(1)}, u32[]{:S(2)}, u32[]{:S(2)}) collective-permute-start(f32[32,128]{1,0:T(8,128)S(1)} %bitcast.79), channel_id=1, source_target_pairs={{0,1},{1,2},{2,3},{3,4},{4,5},{5,6},{6,7},{7,8},{8,9},{9,10},{10,1... | collective-permute-start | bytes 49160 | tf_op jit(solution)/shard_map/ppermute | solution.py:17
  100.7 3.0 %collective-permute-start.1 = (f32[1,64,128]{2,1,0:T(8,128)S(1)}, f32[1,64,128]{2,1,0:T(8,128)S(1)}, u32[]{:S(2)}, u32[]{:S(2)}) collective-permute-start(f32[1,64,128]{2,1,0:T(8,128)S(1)} %get-tuple-element.36), channel_id=1, source_target_pairs={{0,16},{16,32},{32,48},{48,64},{64,80},{80,96},{96,112},{1,17},{17... | collective-permute-start | bytes 98312 | tf_op jit(solution)/shard_map/ppermute | solution.py:18
  104.9 3.6 %fusion.45 = (f32[32,64,128]{2,1,0:T(8,128)S(1)}, f32[32,64,128]{2,1,0:T(8,128)S(1)}) fusion(f32[32,64,128]{2,1,0:T(8,128)S(1)} %copy-done.1, f32[32,64,127]{2,1,0:T(8,128)S(1)} %get-tuple-element.70, f32[32,64,127]{2,1,0:T(8,128)S(1)} %get-tuple-element.71, f32[34,64,128]{2,1,0:T(8,128)} %constant_dynamic-update-slice_fusion, ...), kind=kLoop, calls=%fused_computation.114 | loop fusion | flops 8126464 | bytes 11763712 | tf_op jit(solution)/shard_map/mul | solution.py:179
  108.6 4.5 %collective-permute-start.11 = (f32[32,128]{1,0:T(8,128)S(1)}, f32[32,128]{1,0:T(8,128)S(1)}, u32[]{:S(2)}, u32[]{:S(2)}) collective-permute-start(f32[32,128]{1,0:T(8,128)S(1)} %bitcast.82), channel_id=1, source_target_pairs={{0,1},{1,2},{2,3},{3,4},{4,5},{5,6},{6,7},{7,8},{8,9},{9,10},{10,1... | collective-permute-start | bytes 49160 | tf_op jit(solution)/shard_map/ppermute | solution.py:17
  118.8 2.4 %collective-permute-done.8 = f32[1,64,128]{2,1,0:T(8,128)S(1)} collective-permute-done((f32[1,64,128]{2,1,0:T(8,128)S(1)}, f32[1,64,128]{2,1,0:T(8,128)S(1)}, u32[]{:S(2)}, u32[]{:S(2)}) %collective-permute-start.8) | collective-permute-done | bytes 32800 | tf_op jit(solution)/shard_map/ppermute | solution.py:18
  122.0 4.5 %collective-permute-start.15 = (f32[32,128]{1,0:T(8,128)S(1)}, f32[32,128]{1,0:T(8,128)S(1)}, u32[]{:S(2)}, u32[]{:S(2)}) collective-permute-start(f32[32,128]{1,0:T(8,128)S(1)} %bitcast.83), channel_id=1, source_target_pairs={{0,1},{1,2},{2,3},{3,4},{4,5},{5,6},{6,7},{7,8},{8,9},{9,10},{10,1... | collective-permute-start | bytes 49160 | tf_op jit(solution)/shard_map/ppermute | solution.py:17
  127.9 4.3 %collective-permute-start.13 = (f32[1,64,128]{2,1,0:T(8,128)S(1)}, f32[1,64,128]{2,1,0:T(8,128)S(1)}, u32[]{:S(2)}, u32[]{:S(2)}) collective-permute-start(f32[1,64,128]{2,1,0:T(8,128)S(1)} %get-tuple-element.44), channel_id=1, source_target_pairs={{0,16},{16,32},{32,48},{48,64},{64,80},{80,96},{96,112},{1,17},{17... | collective-permute-start | bytes 98312 | tf_op jit(solution)/shard_map/ppermute | solution.py:18
  135.2 3.3 %multiply_reduce_fusion.3 = (f32[]{:T(128)}, f32[]{:T(128)}, f32[]{:T(128)}, f32[]{:T(128)}, f32[32,64,128]{2,1,0:T(8,128)}) fusion(f32[32,64,128]{2,1,0:T(8,128)S(1)} %get-tuple-element.34, f32[32,64,128]{2,1,0:T(8,128)S(1)} %copy-done.1, f32[32,64,128]{2,1,0:T(8,128)S(1)} %get-tuple-element.32, f32[32,64,128]{2,1,0:T(8,128)S(1)} %get-tuple-element.31, ...), kind=kLoop, calls=%fused_computation.69 | loop fusion | flops 8388604 | bytes 7421968 | tf_op jit(solution)/shard_map/reduce_sum | solution.py:186
  138.5 2.6 %pad_maximum_fusion.20 = f32[4]{0:T(128)S(1)} fusion(f32[1]{0:T(128)} %bitcast.30, f32[1]{0:T(128)} %bitcast.25, f32[1]{0:T(128)} %bitcast.24, f32[1]{0:T(128)} %bitcast.19), kind=kLoop, calls=%fused_computation.108 | loop fusion | flops 12 | bytes 32 | tf_op jit(solution)/shard_map/stack | solution.py:184
  141.1 10.9 %psum.28 = f32[4]{0:T(128)S(1)} all-reduce(f32[4]{0:T(128)S(1)} %pad_maximum_fusion.20), channel_id=1, replica_groups=mesh['gx_0'=4,'gx_1'=2,'gy_0'=4,'gy_1'=4] {'gx_0'}, use_global_device_ids=true, to_apply=%region_9.10 | all-reduce | flops 4 | bytes 32 | tf_op jit(solution)/shard_map/psum | solution.py:43
  152.0 2.5 %psum.29 = f32[4]{0:T(128)S(1)} all-reduce(f32[4]{0:T(128)S(1)} %psum.28), channel_id=1, replica_groups=mesh['gx_0'=4,'gx_1'=2,'gy_0'=4,'gy_1'=4] {'gx_1'}, use_global_device_ids=true, to_apply=%region_10.11 | all-reduce | flops 4 | bytes 32 | tf_op jit(solution)/shard_map/psum | solution.py:43
  154.5 17.0 %psum.30 = f32[4]{0:T(128)S(1)} all-reduce(f32[4]{0:T(128)S(1)} %psum.29), channel_id=1, replica_groups=mesh['gx_0'=4,'gx_1'=2,'gy_0'=4,'gy_1'=4] {'gy_0'}, use_global_device_ids=true, to_apply=%region_11.12 | all-reduce | flops 4 | bytes 32 | tf_op jit(solution)/shard_map/psum | solution.py:43
  171.5 7.7 %psum.31 = f32[4]{0:T(128)S(1)} all-reduce(f32[4]{0:T(128)S(1)} %psum.30), channel_id=1, replica_groups=mesh['gx_0'=4,'gx_1'=2,'gy_0'=4,'gy_1'=4] {'gy_1'}, use_global_device_ids=true, to_apply=%region_12.13 | all-reduce | flops 4 | bytes 32 | tf_op jit(solution)/shard_map/psum | solution.py:43
  185.0 3.5 %multiply_subtract_fusion = (f32[32,64,128]{2,1,0:T(8,128)}, f32[32,64,128]{2,1,0:T(8,128)}) fusion(f32[32,64,128]{2,1,0:T(8,128)} %copy-done.2, f32[32,64,128]{2,1,0:T(8,128)} %get-tuple-element.30, f32[32,64,128]{2,1,0:T(8,128)S(1)} %get-tuple-element.34, f32[]{:T(128)S(6)} %div.34, f32[]{:T(128)S(6)} %div.35, f32[]{:T(128)S(6)} %div.33, ...), kind=kLoop, calls=%fused_computation.63 | loop fusion | flops 4718592 | bytes 7340044 | tf_op jit(solution)/shard_map/sub | solution.py:206
  (66 shorter events, 28.3 us)
Async XLA Ops:
  11.4 11.7 %copy-start = (f32[32,64,128]{2,1,0:T(8,128)S(1)}, f32[32,64,128]{2,1,0:T(8,128)}, u32[]{:S(2)}) copy-start(f32[32,64,128]{2,1,0:T(8,128)} %param.13) | copy-start | bytes 3145732
  11.4 54.7 %all-to-all-start = ((bf16[128,6,1664]{2,1,0:T(8,128)(2,1)}), bf16[128,6,1664]{2,1,0:T(8,128)(2,1)}, u32[]{:S(2)}, u32[]{:S(2)}) async-start(bf16[128,6,1664]{2,1,0:T(8,128)(2,1)} %reshape.141), calls=%async_computation | async-start | bytes 6815744 | tf_op jit(solution)/shard_map/all_to_all | solution.py:153
  23.1 7.6 %collective-permute-start.5 = (f32[1,64,128]{2,1,0:T(8,128)S(1)}, f32[1,64,128]{2,1,0:T(8,128)S(1)}, u32[]{:S(2)}, u32[]{:S(2)}) collective-permute-start(f32[1,64,128]{2,1,0:T(8,128)S(1)} %get-tuple-element.61), channel_id=1, source_target_pairs={{0,16},{16,32},{32,48},{48,64},{64,80},{80,96},{96,112},{1,17},{17... | collective-permute-start | bytes 98312 | tf_op jit(solution)/shard_map/ppermute | solution.py:18
  24.4 76.3 %collective-permute-start.7 = (f32[32,128]{1,0:T(8,128)S(1)}, f32[32,128]{1,0:T(8,128)S(1)}, u32[]{:S(2)}, u32[]{:S(2)}) collective-permute-start(f32[32,128]{1,0:T(8,128)S(1)} %bitcast.77), channel_id=1, source_target_pairs={{0,1},{1,2},{2,3},{3,4},{4,5},{5,6},{6,7},{7,8},{8,9},{9,10},{10,1... | collective-permute-start | bytes 49160 | tf_op jit(solution)/shard_map/ppermute | solution.py:17
  28.1 76.4 %collective-permute-start.6 = (f32[32,128]{1,0:T(8,128)S(1)}, f32[32,128]{1,0:T(8,128)S(1)}, u32[]{:S(2)}, u32[]{:S(2)}) collective-permute-start(f32[32,128]{1,0:T(8,128)S(1)} %bitcast.76), channel_id=1, source_target_pairs={{1,0},{2,1},{3,2},{4,3},{5,4},{6,5},{7,6},{8,7},{9,8},{10,9},{11,1... | collective-permute-start | bytes 49160 | tf_op jit(solution)/shard_map/ppermute | solution.py:17
  29.4 3.8 %collective-permute-start.4 = (f32[1,64,128]{2,1,0:T(8,128)S(1)}, f32[1,64,128]{2,1,0:T(8,128)S(1)}, u32[]{:S(2)}, u32[]{:S(2)}) collective-permute-start(f32[1,64,128]{2,1,0:T(8,128)S(1)} %get-tuple-element.60), channel_id=1, source_target_pairs={{16,0},{32,16},{48,32},{64,48},{80,64},{96,80},{112,96},{17,1},{33... | collective-permute-start | bytes 98312 | tf_op jit(solution)/shard_map/ppermute | solution.py:18
  95.2 9.3 %collective-permute-start.3 = (f32[32,128]{1,0:T(8,128)S(1)}, f32[32,128]{1,0:T(8,128)S(1)}, u32[]{:S(2)}, u32[]{:S(2)}) collective-permute-start(f32[32,128]{1,0:T(8,128)S(1)} %bitcast.79), channel_id=1, source_target_pairs={{0,1},{1,2},{2,3},{3,4},{4,5},{5,6},{6,7},{7,8},{8,9},{9,10},{10,1... | collective-permute-start | bytes 49160 | tf_op jit(solution)/shard_map/ppermute | solution.py:17
  98.1 6.4 %collective-permute-start.2 = (f32[32,128]{1,0:T(8,128)S(1)}, f32[32,128]{1,0:T(8,128)S(1)}, u32[]{:S(2)}, u32[]{:S(2)}) collective-permute-start(f32[32,128]{1,0:T(8,128)S(1)} %bitcast.78), channel_id=1, source_target_pairs={{1,0},{2,1},{3,2},{4,3},{5,4},{6,5},{7,6},{8,7},{9,8},{10,9},{11,1... | collective-permute-start | bytes 49160 | tf_op jit(solution)/shard_map/ppermute | solution.py:17
  99.4 5.1 %collective-permute-start = (f32[1,64,128]{2,1,0:T(8,128)S(1)}, f32[1,64,128]{2,1,0:T(8,128)S(1)}, u32[]{:S(2)}, u32[]{:S(2)}) collective-permute-start(f32[1,64,128]{2,1,0:T(8,128)S(1)} %get-tuple-element.35), channel_id=1, source_target_pairs={{16,0},{32,16},{48,32},{64,48},{80,64},{96,80},{112,96},{17,1},{33... | collective-permute-start | bytes 98312 | tf_op jit(solution)/shard_map/ppermute | solution.py:18
  100.7 3.9 %collective-permute-start.1 = (f32[1,64,128]{2,1,0:T(8,128)S(1)}, f32[1,64,128]{2,1,0:T(8,128)S(1)}, u32[]{:S(2)}, u32[]{:S(2)}) collective-permute-start(f32[1,64,128]{2,1,0:T(8,128)S(1)} %get-tuple-element.36), channel_id=1, source_target_pairs={{0,16},{16,32},{32,48},{48,64},{64,80},{80,96},{96,112},{1,17},{17... | collective-permute-start | bytes 98312 | tf_op jit(solution)/shard_map/ppermute | solution.py:18
  103.7 1.2 copy-start.1
  108.6 9.3 %collective-permute-start.11 = (f32[32,128]{1,0:T(8,128)S(1)}, f32[32,128]{1,0:T(8,128)S(1)}, u32[]{:S(2)}, u32[]{:S(2)}) collective-permute-start(f32[32,128]{1,0:T(8,128)S(1)} %bitcast.82), channel_id=1, source_target_pairs={{0,1},{1,2},{2,3},{3,4},{4,5},{5,6},{6,7},{7,8},{8,9},{9,10},{10,1... | collective-permute-start | bytes 49160 | tf_op jit(solution)/shard_map/ppermute | solution.py:17
  113.2 5.6 %collective-permute-start.10 = (f32[32,128]{1,0:T(8,128)S(1)}, f32[32,128]{1,0:T(8,128)S(1)}, u32[]{:S(2)}, u32[]{:S(2)}) collective-permute-start(f32[32,128]{1,0:T(8,128)S(1)} %bitcast.80), channel_id=1, source_target_pairs={{1,0},{2,1},{3,2},{4,3},{5,4},{6,5},{7,6},{8,7},{9,8},{10,9},{11,1... | collective-permute-start | bytes 49160 | tf_op jit(solution)/shard_map/ppermute | solution.py:17
  114.5 4.3 %collective-permute-start.9 = (f32[1,64,128]{2,1,0:T(8,128)S(1)}, f32[1,64,128]{2,1,0:T(8,128)S(1)}, u32[]{:S(2)}, u32[]{:S(2)}) collective-permute-start(f32[1,64,128]{2,1,0:T(8,128)S(1)} %get-tuple-element.50), channel_id=1, source_target_pairs={{0,16},{16,32},{32,48},{48,64},{64,80},{80,96},{96,112},{1,17},{17... | collective-permute-start | bytes 98312 | tf_op jit(solution)/shard_map/ppermute | solution.py:18
  116.3 5.0 %collective-permute-start.8 = (f32[1,64,128]{2,1,0:T(8,128)S(1)}, f32[1,64,128]{2,1,0:T(8,128)S(1)}, u32[]{:S(2)}, u32[]{:S(2)}) collective-permute-start(f32[1,64,128]{2,1,0:T(8,128)S(1)} %get-tuple-element.51), channel_id=1, source_target_pairs={{16,0},{32,16},{48,32},{64,48},{80,64},{96,80},{112,96},{17,1},{33... | collective-permute-start | bytes 98312 | tf_op jit(solution)/shard_map/ppermute | solution.py:18
  121.9 16.6 %copy-start.2 = (f32[32,64,128]{2,1,0:T(8,128)}, f32[32,64,128]{2,1,0:T(8,128)S(1)}, u32[]{:S(2)}) copy-start(f32[32,64,128]{2,1,0:T(8,128)S(1)} %get-tuple-element.32) | copy-start | bytes 3145732
  122.0 11.8 %collective-permute-start.15 = (f32[32,128]{1,0:T(8,128)S(1)}, f32[32,128]{1,0:T(8,128)S(1)}, u32[]{:S(2)}, u32[]{:S(2)}) collective-permute-start(f32[32,128]{1,0:T(8,128)S(1)} %bitcast.83), channel_id=1, source_target_pairs={{0,1},{1,2},{2,3},{3,4},{4,5},{5,6},{6,7},{7,8},{8,9},{9,10},{10,1... | collective-permute-start | bytes 49160 | tf_op jit(solution)/shard_map/ppermute | solution.py:17
  126.6 7.3 %collective-permute-start.14 = (f32[32,128]{1,0:T(8,128)S(1)}, f32[32,128]{1,0:T(8,128)S(1)}, u32[]{:S(2)}, u32[]{:S(2)}) collective-permute-start(f32[32,128]{1,0:T(8,128)S(1)} %bitcast.81), channel_id=1, source_target_pairs={{1,0},{2,1},{3,2},{4,3},{5,4},{6,5},{7,6},{8,7},{9,8},{10,9},{11,1... | collective-permute-start | bytes 49160 | tf_op jit(solution)/shard_map/ppermute | solution.py:17
  127.9 6.0 %collective-permute-start.13 = (f32[1,64,128]{2,1,0:T(8,128)S(1)}, f32[1,64,128]{2,1,0:T(8,128)S(1)}, u32[]{:S(2)}, u32[]{:S(2)}) collective-permute-start(f32[1,64,128]{2,1,0:T(8,128)S(1)} %get-tuple-element.44), channel_id=1, source_target_pairs={{0,16},{16,32},{32,48},{48,64},{64,80},{80,96},{96,112},{1,17},{17... | collective-permute-start | bytes 98312 | tf_op jit(solution)/shard_map/ppermute | solution.py:18
  132.1 3.1 %collective-permute-start.12 = (f32[1,64,128]{2,1,0:T(8,128)S(1)}, f32[1,64,128]{2,1,0:T(8,128)S(1)}, u32[]{:S(2)}, u32[]{:S(2)}) collective-permute-start(f32[1,64,128]{2,1,0:T(8,128)S(1)} %get-tuple-element.45), channel_id=1, source_target_pairs={{16,0},{32,16},{48,32},{64,48},{80,64},{96,80},{112,96},{17,1},{33... | collective-permute-start | bytes 98312 | tf_op jit(solution)/shard_map/ppermute | solution.py:18

commit v9 on v8

--- a/solution.py
+++ b/solution.py
@@ -150,22 +150,25 @@
     peers = lax.axis_size(GX_GY)
     capacity = max(2, 3 * bricks.shape[0] // peers)
     payload = build_send(bricks, brick_target, brick_slot, peers, capacity)
+    row = payload.shape[1]
     arrived = lax.all_to_all(
-        payload.reshape(peers, capacity, payload.shape[1]), GX_GY, split_axis=0, concat_axis=0, tiled=True
-    ).reshape(peers * capacity, payload.shape[1])
-    tag = arrived[:, 1536:1538].astype(jnp.int32)
-    landed = tag[:, 0] * 32 + tag[:, 1]
+        payload.reshape(peers, capacity * row), GX_GY, split_axis=0, concat_axis=0, tiled=True
+    )
     width_x, width_y, depth = screen.shape
     span_x = width_x // 8
     span_y = width_y // 8
     span_z = depth // 8
-    picks = landed.reshape(-1, 1) == jnp.arange(span_x * span_y * span_z, dtype=jnp.int32)[None, :]
-    blocks = jnp.einsum(
-        "ks,kj->sj",
-        picks.astype(jnp.bfloat16),
-        arrived[:, :1536],
-        preferred_element_type=jnp.float32,
-    )
+    cells = jnp.arange(span_x * span_y * span_z, dtype=jnp.int32)[None, :]
+    blocks = None
+    for slot in range(capacity):
+        part = arrived[:, slot * row:(slot + 1) * row]
+        tag = part[:, 1536:1538].astype(jnp.int32)
+        landed = tag[:, 0] * 32 + tag[:, 1]
+        picks = (landed[:, None] == cells).astype(jnp.bfloat16)
+        term = jnp.einsum(
+            "ks,kj->sj", picks, part[:, :1536], preferred_element_type=jnp.float32
+        )
+        blocks = term if blocks is None else blocks + term
     normals = to_grid(blocks, span_x, span_y, depth)
     normal_x, normal_y, normal_z = normals[0], normals[1], normals[2]
     along_x = with_halo(normal_x, ((GX, 0),), 1)

time: 190 us -> 266 us (1.40)
  other arithmetic: 20 us -> 76.4 us
  local copies, waits for them, and re-layouts: 16.7 us -> 43.7 us
  waiting for transfers between devices: 37.9 us -> 23.9 us
  starting transfers between devices: 48 us -> 51.2 us
    all_to_all x0 -> x1, other arithmetic: none -> 57 us  [body(): lax.all_to_all(payload.reshape(peers, capacity * row), GX_GY, split_axis=...]
    unnamed x9 -> x16, local copies, waits for them, and re-layouts: 2.04 us -> 24.7 us
    all_to_all x1, waiting for transfers between devices: 32.3 us -> 21.4 us  [body(): lax.all_to_all(payload.reshape(peers, capacity * row), GX_GY, split_axis=...]
    all_to_all x0 -> x2, local copies, waits for them, and re-layouts: none -> 10.8 us  [body(): lax.all_to_all(payload.reshape(peers, capacity * row), GX_GY, split_axis=...]
    reshape x2 -> x0, local copies, waits for them, and re-layouts: 7.98 us -> none  [the longest x1 5.36 us: body(): arrived = lax.all_to_all(payload.reshape(peers, capacity, payload.shape[1...]
    ppermute x8, waiting for transfers between devices: 4.79 us -> 0.45 us  [shifted(): return lax.ppermute(piece, axis, pairs)]
    ppermute x8, starting transfers between devices: 20.8 us -> 23.5 us  [shifted(): return lax.ppermute(flat, axis, pairs).reshape(piece.shape)]
    dot_general x1 -> x6, matrix products: 4.84 us -> 5.82 us  [body(): jnp.einsum('ks,kj->sj', picks, part[:, :1536], preferred_element_type=jnp...]
  transfers between devices with their start and end apart: 17 -> 17, of which waited for: 5 -> 4; matrix products, arithmetic and copies ran while one was open for 10% -> 13% of each run, Pallas kernels for 8% -> 6%
where the time goes in v9:
time: 266 us; the launch traced here: 265 us
  other arithmetic  76.4 us (29%)
  starting transfers between devices  51.2 us (19%)
  local copies, waits for them, and re-layouts  43.7 us (16%)
  blocking collectives  39 us (15%)
  waiting for transfers between devices  23.9 us (9%)
  Pallas kernels  14.7 us (6%)
  matrix products  9.36 us (4%)
  between operations  6.19 us (2%)
    all_to_all x1, other arithmetic, body(): lax.all_to_all(payload.reshape(peers, capacity * row), GX_GY, split_axis=...  57 us
    psum x4, blocking collectives, over_axes(): shard = lax.psum(shard, axis)  39 us
    unnamed x16, local copies, waits for them, and re-layouts  24.7 us
    ppermute x8, starting transfers between devices, shifted(): return lax.ppermute(flat, axis, pairs).reshape(piece.shape)  23.5 us
    all_to_all x1, waiting for transfers between devices, body(): lax.all_to_all(payload.reshape(peers, capacity * row), GX_GY, split_axis=...  21.4 us
    ppermute x8, starting transfers between devices, shifted(): return lax.ppermute(piece, axis, pairs)  16.1 us
    pallas_call x1, Pallas kernels, to_grid(): pl.pallas_call(relayout_kernel, out_shape=jax.ShapeDtypeStruct((3, span_x...  14.7 us
    all_to_all x1, starting transfers between devices, body(): lax.all_to_all(payload.reshape(peers, capacity * row), GX_GY, split_axis=...  11.6 us
  transfers between devices with their start and end apart: 17, of which 4 were waited for; matrix products, arithmetic and copies ran while one was open for 13% of the time, Pallas kernels for 6%

profile of v9, /device:TPU:0, one launch (start us, length us, event | category | flops | bytes accessed | tf_op | source)
XLA Modules:
  0.0 264.5 jit_solution(15595209769604957823)
XLA Ops:
  6.7 3.5 %convolution_convert_fusion = bf16[768,1664]{1,0:T(8,128)(2,1)} fusion(bf16[256,128]{1,0:T(8,128)(2,1)S(1)} %copy.43, bf16[256,1536]{1,0:T(8,128)(2,1)} %param.9, s32[256]{0:T(256)S(1)} %multiply_add_fusion.1), kind=kOutput, calls=%fused_computation.5 | convolution fusion | flops 657489920 | bytes 3408896 | tf_op jit(solution)/shard_map/pk,kj->pj/dot_general | solution.py:71
  10.3 10.3 %all_to_all.11 = bf16[128,1,9984]{2,1,0:T(2,128)(2,1)} reshape(bf16[768,1664]{1,0:T(8,128)(2,1)} %convolution_convert_fusion) | data formatting | bytes 5111808 | tf_op jit(solution)/shard_map/all_to_all | solution.py:154
  21.1 57.0 %reduce.28 = bf16[128,9984]{1,0:T(8,128)(2,1)} reduce(bf16[128,1,9984]{2,1,0:T(2,128)(2,1)} %all_to_all.11, bf16[]{:T(256)} %broadcast.245), dimensions={1}, to_apply=%all_to_all.11.reduce_sub_computation | reduce | bytes 5111810 | tf_op jit(solution)/shard_map/all_to_all | solution.py:154
  78.1 4.2 %reshape.160 = bf16[128,2,4992]{2,1,0:T(2,128)(2,1)} reshape(bf16[128,9984]{1,0:T(8,128)(2,1)} %reduce.28) | data formatting | bytes 5111808
  82.3 11.6 %all-to-all-start = ((bf16[128,2,4992]{2,1,0:T(2,128)(2,1)}), bf16[128,2,4992]{2,1,0:T(2,128)(2,1)}, u32[]{:S(2)}, u32[]{:S(2)}) async-start(bf16[128,2,4992]{2,1,0:T(2,128)(2,1)} %reshape.160), calls=%async_computation | async-start | bytes 5111808 | tf_op jit(solution)/shard_map/all_to_all | solution.py:154
  97.9 4.7 %collective-permute-start.7 = (f32[32,128]{1,0:T(8,128)S(1)}, f32[32,128]{1,0:T(8,128)S(1)}, u32[]{:S(2)}, u32[]{:S(2)}) collective-permute-start(f32[32,128]{1,0:T(8,128)S(1)} %bitcast.86), channel_id=1, source_target_pairs={{0,1},{1,2},{2,3},{3,4},{4,5},{5,6},{6,7},{7,8},{8,9},{9,10},{10,1... | collective-permute-start | bytes 49160 | tf_op jit(solution)/shard_map/ppermute | solution.py:17
  106.7 21.4 %all-to-all-done = bf16[128,2,4992]{2,1,0:T(2,128)(2,1)} async-done(((bf16[128,2,4992]{2,1,0:T(2,128)(2,1)}), bf16[128,2,4992]{2,1,0:T(2,128)(2,1)}, u32[]{:S(2)}, u32[]{:S(2)}) %all-to-all-start) | async-done | bytes 2555936 | tf_op jit(solution)/shard_map/all_to_all | solution.py:154
  128.0 16.0 %reshape.161 = bf16[128,1,9984]{2,1,0:T(2,128)(2,1)} reshape(bf16[128,2,4992]{2,1,0:T(2,128)(2,1)} %all-to-all-done) | data formatting | bytes 5111808
  144.0 2.7 %copy.62 = bf16[128,1,9984]{2,0,1:T(8,128)(2,1)S(1)} copy(bf16[128,1,9984]{2,1,0:T(2,128)(2,1)} %reshape.161) | data formatting | bytes 5111808
  153.2 14.7 %shard_map.68 = f32[3,32,64,128]{3,2,1,0:T(8,128)} custom-call(f32[512,1536]{1,0:T(8,128)} %convolution_add_fusion.blk_ref), custom_call_target="tpu_custom_call" | custom-call | tf_op jit(solution)/shard_map/pallas_call | solution.py:141
  172.3 4.5 %collective-permute-start.3 = (f32[32,128]{1,0:T(8,128)S(1)}, f32[32,128]{1,0:T(8,128)S(1)}, u32[]{:S(2)}, u32[]{:S(2)}) collective-permute-start(f32[32,128]{1,0:T(8,128)S(1)} %bitcast.88), channel_id=1, source_target_pairs={{0,1},{1,2},{2,3},{3,4},{4,5},{5,6},{6,7},{7,8},{8,9},{9,10},{10,1... | collective-permute-start | bytes 49160 | tf_op jit(solution)/shard_map/ppermute | solution.py:17
  178.2 3.0 %collective-permute-start.1 = (f32[1,64,128]{2,1,0:T(8,128)S(1)}, f32[1,64,128]{2,1,0:T(8,128)S(1)}, u32[]{:S(2)}, u32[]{:S(2)}) collective-permute-start(f32[1,64,128]{2,1,0:T(8,128)S(1)} %get-tuple-element.36), channel_id=1, source_target_pairs={{0,16},{16,32},{32,48},{48,64},{64,80},{80,96},{96,112},{1,17},{17... | collective-permute-start | bytes 98312 | tf_op jit(solution)/shard_map/ppermute | solution.py:18
  182.1 3.6 %fusion.60 = (f32[32,64,128]{2,1,0:T(8,128)S(1)}, f32[32,64,128]{2,1,0:T(8,128)S(1)}) fusion(f32[32,64,128]{2,1,0:T(8,128)S(1)} %copy-done.1, f32[32,64,127]{2,1,0:T(8,128)S(1)} %copy-done.4, f32[32,64,127]{2,1,0:T(8,128)S(1)} %copy-done.3, f32[34,64,128]{2,1,0:T(8,128)} %constant_dynamic-update-slice_fusion, f32[32,1,128]{2,1,0:T(1,128)S(1)} %bitcast.78, ...), kind=kLoop, calls=%fused_computation.155 | loop fusion | flops 8126464 | bytes 11763712 | tf_op jit(solution)/shard_map/mul | solution.py:182
  187.0 3.0 %collective-permute-start.9 = (f32[1,64,128]{2,1,0:T(8,128)S(1)}, f32[1,64,128]{2,1,0:T(8,128)S(1)}, u32[]{:S(2)}, u32[]{:S(2)}) collective-permute-start(f32[1,64,128]{2,1,0:T(8,128)S(1)} %get-tuple-element.56), channel_id=1, source_target_pairs={{0,16},{16,32},{32,48},{48,64},{64,80},{80,96},{96,112},{1,17},{17... | collective-permute-start | bytes 98312 | tf_op jit(solution)/shard_map/ppermute | solution.py:18
  191.3 4.5 %collective-permute-start.11 = (f32[32,128]{1,0:T(8,128)S(1)}, f32[32,128]{1,0:T(8,128)S(1)}, u32[]{:S(2)}, u32[]{:S(2)}) collective-permute-start(f32[32,128]{1,0:T(8,128)S(1)} %bitcast.90), channel_id=1, source_target_pairs={{0,1},{1,2},{2,3},{3,4},{4,5},{5,6},{6,7},{7,8},{8,9},{9,10},{10,1... | collective-permute-start | bytes 49160 | tf_op jit(solution)/shard_map/ppermute | solution.py:17
  199.3 3.6 %collective-permute-start.13 = (f32[1,64,128]{2,1,0:T(8,128)S(1)}, f32[1,64,128]{2,1,0:T(8,128)S(1)}, u32[]{:S(2)}, u32[]{:S(2)}) collective-permute-start(f32[1,64,128]{2,1,0:T(8,128)S(1)} %get-tuple-element.50), channel_id=1, source_target_pairs={{0,16},{16,32},{32,48},{48,64},{64,80},{80,96},{96,112},{1,17},{17... | collective-permute-start | bytes 98312 | tf_op jit(solution)/shard_map/ppermute | solution.py:18
  204.2 4.5 %collective-permute-start.15 = (f32[32,128]{1,0:T(8,128)S(1)}, f32[32,128]{1,0:T(8,128)S(1)}, u32[]{:S(2)}, u32[]{:S(2)}) collective-permute-start(f32[32,128]{1,0:T(8,128)S(1)} %bitcast.91), channel_id=1, source_target_pairs={{0,1},{1,2},{2,3},{3,4},{4,5},{5,6},{6,7},{7,8},{8,9},{9,10},{10,1... | collective-permute-start | bytes 49160 | tf_op jit(solution)/shard_map/ppermute | solution.py:17
  210.2 3.3 %multiply_reduce_fusion.3 = (f32[]{:T(128)}, f32[]{:T(128)}, f32[]{:T(128)}, f32[]{:T(128)}, f32[32,64,128]{2,1,0:T(8,128)}) fusion(f32[32,64,128]{2,1,0:T(8,128)S(1)} %get-tuple-element.34, f32[32,64,128]{2,1,0:T(8,128)S(1)} %copy-done.1, f32[32,64,128]{2,1,0:T(8,128)S(1)} %get-tuple-element.32, f32[32,64,128]{2,1,0:T(8,128)S(1)} %get-tuple-element.31, ...), kind=kLoop, calls=%fused_computation.72 | loop fusion | flops 8388604 | bytes 7421968 | tf_op jit(solution)/shard_map/reduce_sum | solution.py:189
  213.5 2.6 pad_maximum_fusion.20
  216.1 10.8 %psum.28 = f32[4]{0:T(128)S(1)} all-reduce(f32[4]{0:T(128)S(1)} %pad_maximum_fusion.20), channel_id=1, replica_groups=mesh['gx_0'=4,'gx_1'=2,'gy_0'=4,'gy_1'=4] {'gx_0'}, use_global_device_ids=true, to_apply=%region_9.10 | all-reduce | flops 4 | bytes 32 | tf_op jit(solution)/shard_map/psum | solution.py:43
  226.9 2.5 psum.29
  229.4 18.1 %psum.30 = f32[4]{0:T(128)S(1)} all-reduce(f32[4]{0:T(128)S(1)} %psum.29), channel_id=1, replica_groups=mesh['gx_0'=4,'gx_1'=2,'gy_0'=4,'gy_1'=4] {'gy_0'}, use_global_device_ids=true, to_apply=%region_11.12 | all-reduce | flops 4 | bytes 32 | tf_op jit(solution)/shard_map/psum | solution.py:43
  247.4 7.7 %psum.31 = f32[4]{0:T(128)S(1)} all-reduce(f32[4]{0:T(128)S(1)} %psum.30), channel_id=1, replica_groups=mesh['gx_0'=4,'gx_1'=2,'gy_0'=4,'gy_1'=4] {'gy_1'}, use_global_device_ids=true, to_apply=%region_12.13 | all-reduce | flops 4 | bytes 32 | tf_op jit(solution)/shard_map/psum | solution.py:43
  260.9 3.6 %multiply_subtract_fusion = (f32[32,64,128]{2,1,0:T(8,128)}, f32[32,64,128]{2,1,0:T(8,128)}) fusion(f32[32,64,128]{2,1,0:T(8,128)} %copy-done.2, f32[32,64,128]{2,1,0:T(8,128)} %get-tuple-element.30, f32[32,64,128]{2,1,0:T(8,128)S(1)} %get-tuple-element.34, f32[]{:T(128)S(6)} %div.34, f32[]{:T(128)S(6)} %div.35, f32[]{:T(128)S(6)} %div.33, ...), kind=kLoop, calls=%fused_computation.66 | loop fusion | flops 4718592 | bytes 7340044 | tf_op jit(solution)/shard_map/sub | solution.py:209
  (82 shorter events, 36.8 us)
Async XLA Ops:
  82.3 11.7 %copy-start = (f32[32,64,128]{2,1,0:T(8,128)S(1)}, f32[32,64,128]{2,1,0:T(8,128)}, u32[]{:S(2)}) copy-start(f32[32,64,128]{2,1,0:T(8,128)} %param.13) | copy-start | bytes 3145732
  82.3 45.8 %all-to-all-start = ((bf16[128,2,4992]{2,1,0:T(2,128)(2,1)}), bf16[128,2,4992]{2,1,0:T(2,128)(2,1)}, u32[]{:S(2)}, u32[]{:S(2)}) async-start(bf16[128,2,4992]{2,1,0:T(2,128)(2,1)} %reshape.160), calls=%async_computation | async-start | bytes 5111808 | tf_op jit(solution)/shard_map/all_to_all | solution.py:154
  93.9 10.3 %collective-permute-start.5 = (f32[1,64,128]{2,1,0:T(8,128)S(1)}, f32[1,64,128]{2,1,0:T(8,128)S(1)}, u32[]{:S(2)}, u32[]{:S(2)}) collective-permute-start(f32[1,64,128]{2,1,0:T(8,128)S(1)} %get-tuple-element.67), channel_id=1, source_target_pairs={{0,16},{16,32},{32,48},{48,64},{64,80},{80,96},{96,112},{1,17},{17... | collective-permute-start | bytes 98312 | tf_op jit(solution)/shard_map/ppermute | solution.py:18
  95.2 10.8 %collective-permute-start.4 = (f32[1,64,128]{2,1,0:T(8,128)S(1)}, f32[1,64,128]{2,1,0:T(8,128)S(1)}, u32[]{:S(2)}, u32[]{:S(2)}) collective-permute-start(f32[1,64,128]{2,1,0:T(8,128)S(1)} %get-tuple-element.66), channel_id=1, source_target_pairs={{16,0},{32,16},{48,32},{64,48},{80,64},{96,80},{112,96},{17,1},{33... | collective-permute-start | bytes 98312 | tf_op jit(solution)/shard_map/ppermute | solution.py:18
  96.6 81.6 %collective-permute-start.6 = (f32[32,128]{1,0:T(8,128)S(1)}, f32[32,128]{1,0:T(8,128)S(1)}, u32[]{:S(2)}, u32[]{:S(2)}) collective-permute-start(f32[32,128]{1,0:T(8,128)S(1)} %bitcast.87), channel_id=1, source_target_pairs={{1,0},{2,1},{3,2},{4,3},{5,4},{6,5},{7,6},{8,7},{9,8},{10,9},{11,1... | collective-permute-start | bytes 49160 | tf_op jit(solution)/shard_map/ppermute | solution.py:17
  97.9 83.7 %collective-permute-start.7 = (f32[32,128]{1,0:T(8,128)S(1)}, f32[32,128]{1,0:T(8,128)S(1)}, u32[]{:S(2)}, u32[]{:S(2)}) collective-permute-start(f32[32,128]{1,0:T(8,128)S(1)} %bitcast.86), channel_id=1, source_target_pairs={{0,1},{1,2},{2,3},{3,4},{4,5},{5,6},{6,7},{7,8},{8,9},{9,10},{10,1... | collective-permute-start | bytes 49160 | tf_op jit(solution)/shard_map/ppermute | solution.py:17
  170.0 12.0 %copy-start.1 = (f32[32,64,128]{2,1,0:T(8,128)S(1)}, f32[32,64,128]{2,1,0:T(8,128)}, u32[]{:S(2)}) copy-start(f32[32,64,128]{2,1,0:T(8,128)} %param.12) | copy-start | bytes 3145732
  170.0 12.0 %copy-start.3 = (f32[32,64,127]{2,1,0:T(8,128)S(1)}, f32[32,64,127]{2,1,0:T(8,128)}, u32[]{:S(2)}) copy-start(f32[32,64,127]{2,1,0:T(8,128)} %get-tuple-element.68) | copy-start | bytes 3121156
  170.0 12.0 %copy-start.4 = (f32[32,64,127]{2,1,0:T(8,128)S(1)}, f32[32,64,127]{2,1,0:T(8,128)}, u32[]{:S(2)}) copy-start(f32[32,64,127]{2,1,0:T(8,128)} %get-tuple-element.69) | copy-start | bytes 3121156
  171.0 10.6 %collective-permute-start.2 = (f32[32,128]{1,0:T(8,128)S(1)}, f32[32,128]{1,0:T(8,128)S(1)}, u32[]{:S(2)}, u32[]{:S(2)}) collective-permute-start(f32[32,128]{1,0:T(8,128)S(1)} %bitcast.89), channel_id=1, source_target_pairs={{1,0},{2,1},{3,2},{4,3},{5,4},{6,5},{7,6},{8,7},{9,8},{10,9},{11,1... | collective-permute-start | bytes 49160 | tf_op jit(solution)/shard_map/ppermute | solution.py:17
  172.3 9.3 %collective-permute-start.3 = (f32[32,128]{1,0:T(8,128)S(1)}, f32[32,128]{1,0:T(8,128)S(1)}, u32[]{:S(2)}, u32[]{:S(2)}) collective-permute-start(f32[32,128]{1,0:T(8,128)S(1)} %bitcast.88), channel_id=1, source_target_pairs={{0,1},{1,2},{2,3},{3,4},{4,5},{5,6},{6,7},{7,8},{8,9},{9,10},{10,1... | collective-permute-start | bytes 49160 | tf_op jit(solution)/shard_map/ppermute | solution.py:17
  176.9 4.7 %collective-permute-start = (f32[1,64,128]{2,1,0:T(8,128)S(1)}, f32[1,64,128]{2,1,0:T(8,128)S(1)}, u32[]{:S(2)}, u32[]{:S(2)}) collective-permute-start(f32[1,64,128]{2,1,0:T(8,128)S(1)} %get-tuple-element.35), channel_id=1, source_target_pairs={{16,0},{32,16},{48,32},{64,48},{80,64},{96,80},{112,96},{17,1},{33... | collective-permute-start | bytes 98312 | tf_op jit(solution)/shard_map/ppermute | solution.py:18
  178.2 3.9 %collective-permute-start.1 = (f32[1,64,128]{2,1,0:T(8,128)S(1)}, f32[1,64,128]{2,1,0:T(8,128)S(1)}, u32[]{:S(2)}, u32[]{:S(2)}) collective-permute-start(f32[1,64,128]{2,1,0:T(8,128)S(1)} %get-tuple-element.36), channel_id=1, source_target_pairs={{0,16},{16,32},{32,48},{48,64},{64,80},{80,96},{96,112},{1,17},{17... | collective-permute-start | bytes 98312 | tf_op jit(solution)/shard_map/ppermute | solution.py:18
  185.7 11.6 %collective-permute-start.8 = (f32[1,64,128]{2,1,0:T(8,128)S(1)}, f32[1,64,128]{2,1,0:T(8,128)S(1)}, u32[]{:S(2)}, u32[]{:S(2)}) collective-permute-start(f32[1,64,128]{2,1,0:T(8,128)S(1)} %get-tuple-element.57), channel_id=1, source_target_pairs={{16,0},{32,16},{48,32},{64,48},{80,64},{96,80},{112,96},{17,1},{33... | collective-permute-start | bytes 98312 | tf_op jit(solution)/shard_map/ppermute | solution.py:18
  187.0 10.3 %collective-permute-start.9 = (f32[1,64,128]{2,1,0:T(8,128)S(1)}, f32[1,64,128]{2,1,0:T(8,128)S(1)}, u32[]{:S(2)}, u32[]{:S(2)}) collective-permute-start(f32[1,64,128]{2,1,0:T(8,128)S(1)} %get-tuple-element.56), channel_id=1, source_target_pairs={{0,16},{16,32},{32,48},{48,64},{64,80},{80,96},{96,112},{1,17},{17... | collective-permute-start | bytes 98312 | tf_op jit(solution)/shard_map/ppermute | solution.py:18
  190.0 6.2 %collective-permute-start.10 = (f32[32,128]{1,0:T(8,128)S(1)}, f32[32,128]{1,0:T(8,128)S(1)}, u32[]{:S(2)}, u32[]{:S(2)}) collective-permute-start(f32[32,128]{1,0:T(8,128)S(1)} %bitcast.92), channel_id=1, source_target_pairs={{1,0},{2,1},{3,2},{4,3},{5,4},{6,5},{7,6},{8,7},{9,8},{10,9},{11,1... | collective-permute-start | bytes 49160 | tf_op jit(solution)/shard_map/ppermute | solution.py:17
  191.3 6.0 %collective-permute-start.11 = (f32[32,128]{1,0:T(8,128)S(1)}, f32[32,128]{1,0:T(8,128)S(1)}, u32[]{:S(2)}, u32[]{:S(2)}) collective-permute-start(f32[32,128]{1,0:T(8,128)S(1)} %bitcast.90), channel_id=1, source_target_pairs={{0,1},{1,2},{2,3},{3,4},{4,5},{5,6},{6,7},{7,8},{8,9},{9,10},{10,1... | collective-permute-start | bytes 49160 | tf_op jit(solution)/shard_map/ppermute | solution.py:17
  198.0 15.6 %copy-start.2 = (f32[32,64,128]{2,1,0:T(8,128)}, f32[32,64,128]{2,1,0:T(8,128)S(1)}, u32[]{:S(2)}) copy-start(f32[32,64,128]{2,1,0:T(8,128)S(1)} %get-tuple-element.32) | copy-start | bytes 3145732
  198.0 12.1 %collective-permute-start.12 = (f32[1,64,128]{2,1,0:T(8,128)S(1)}, f32[1,64,128]{2,1,0:T(8,128)S(1)}, u32[]{:S(2)}, u32[]{:S(2)}) collective-permute-start(f32[1,64,128]{2,1,0:T(8,128)S(1)} %get-tuple-element.51), channel_id=1, source_target_pairs={{16,0},{32,16},{48,32},{64,48},{80,64},{96,80},{112,96},{17,1},{33... | collective-permute-start | bytes 98312 | tf_op jit(solution)/shard_map/ppermute | solution.py:18
  199.3 10.9 %collective-permute-start.13 = (f32[1,64,128]{2,1,0:T(8,128)S(1)}, f32[1,64,128]{2,1,0:T(8,128)S(1)}, u32[]{:S(2)}, u32[]{:S(2)}) collective-permute-start(f32[1,64,128]{2,1,0:T(8,128)S(1)} %get-tuple-element.50), channel_id=1, source_target_pairs={{0,16},{16,32},{32,48},{48,64},{64,80},{80,96},{96,112},{1,17},{17... | collective-permute-start | bytes 98312 | tf_op jit(solution)/shard_map/ppermute | solution.py:18
  202.9 6.2 %collective-permute-start.14 = (f32[32,128]{1,0:T(8,128)S(1)}, f32[32,128]{1,0:T(8,128)S(1)}, u32[]{:S(2)}, u32[]{:S(2)}) collective-permute-start(f32[32,128]{1,0:T(8,128)S(1)} %bitcast.93), channel_id=1, source_target_pairs={{1,0},{2,1},{3,2},{4,3},{5,4},{6,5},{7,6},{8,7},{9,8},{10,9},{11,1... | collective-permute-start | bytes 49160 | tf_op jit(solution)/shard_map/ppermute | solution.py:17
  204.2 6.0 %collective-permute-start.15 = (f32[32,128]{1,0:T(8,128)S(1)}, f32[32,128]{1,0:T(8,128)S(1)}, u32[]{:S(2)}, u32[]{:S(2)}) collective-permute-start(f32[32,128]{1,0:T(8,128)S(1)} %bitcast.91), channel_id=1, source_target_pairs={{0,1},{1,2},{2,3},{3,4},{4,5},{5,6},{6,7},{7,8},{8,9},{9,10},{10,1... | collective-permute-start | bytes 49160 | tf_op jit(solution)/shard_map/ppermute | solution.py:17

commit v10 on v8

--- a/solution.py
+++ b/solution.py
@@ -67,9 +67,12 @@
     low = (brick_slot % 32).astype(jnp.bfloat16)
     tag = jnp.zeros((bricks.shape[0], 128), jnp.bfloat16).at[:, 0].set(high).at[:, 1].set(low)
     rows = jnp.concatenate([bricks, tag], axis=1)
-    chosen = place[None, :] == jnp.arange(peers * capacity, dtype=jnp.int32)[:, None]
+    chosen = place[None, None, :] == (
+        jnp.arange(peers, dtype=jnp.int32)[:, None, None] * capacity
+        + jnp.arange(capacity, dtype=jnp.int32)[None, :, None]
+    )
     payload = jnp.einsum(
-        "pk,kj->pj", chosen.astype(jnp.bfloat16), rows, preferred_element_type=jnp.float32
+        "pck,kj->pcj", chosen.astype(jnp.bfloat16), rows, preferred_element_type=jnp.float32
     )
     return payload.astype(jnp.bfloat16)
 
@@ -150,20 +153,18 @@
     peers = lax.axis_size(GX_GY)
     capacity = max(2, 3 * bricks.shape[0] // peers)
     payload = build_send(bricks, brick_target, brick_slot, peers, capacity)
-    arrived = lax.all_to_all(
-        payload.reshape(peers, capacity, payload.shape[1]), GX_GY, split_axis=0, concat_axis=0, tiled=True
-    ).reshape(peers * capacity, payload.shape[1])
-    tag = arrived[:, 1536:1538].astype(jnp.int32)
-    landed = tag[:, 0] * 32 + tag[:, 1]
+    arrived = lax.all_to_all(payload, GX_GY, split_axis=0, concat_axis=0, tiled=True)
+    tag = arrived[:, :, 1536:1538].astype(jnp.int32)
+    landed = tag[:, :, 0] * 32 + tag[:, :, 1]
     width_x, width_y, depth = screen.shape
     span_x = width_x // 8
     span_y = width_y // 8
     span_z = depth // 8
-    picks = landed.reshape(-1, 1) == jnp.arange(span_x * span_y * span_z, dtype=jnp.int32)[None, :]
+    picks = landed[:, :, None] == jnp.arange(span_x * span_y * span_z, dtype=jnp.int32)[None, None, :]
     blocks = jnp.einsum(
-        "ks,kj->sj",
+        "pcs,pcj->sj",
         picks.astype(jnp.bfloat16),
-        arrived[:, :1536],
+        arrived[:, :, :1536],
         preferred_element_type=jnp.float32,
     )
     normals = to_grid(blocks, span_x, span_y, depth)

time: 190 us -> 186 us (0.979)
    reshape x2 -> x0, local copies, waits for them, and re-layouts: 7.98 us -> none  [the longest x1 5.36 us: body(): arrived = lax.all_to_all(payload.reshape(peers, capacity, payload.shape[1...]
    convert_element_type x0 -> x1, local copies, waits for them, and re-layouts: none -> 3.21 us  [build_send(): return payload.astype(jnp.bfloat16)]
    slice x0 -> x2, local copies, waits for them, and re-layouts: none -> 3.09 us  [the longest x1 2.1 us: body(): arrived[:, :, :1536]]
  transfers between devices with their start and end apart: 17 -> 17, of which waited for: 5 -> 5; matrix products, arithmetic and copies ran while one was open for 10% -> 7% of each run, Pallas kernels for 8% -> 8%
where the time goes in v10:
time: 186 us; the launch traced here: 185 us
  starting transfers between devices  48.2 us (26%)
  blocking collectives  38.1 us (20%)
  waiting for transfers between devices  37.7 us (20%)
  other arithmetic  18.6 us (10%)
  local copies, waits for them, and re-layouts  15.6 us (8%)
  Pallas kernels  14.7 us (8%)
  between operations  6.09 us (3%)
  matrix products  5.6 us (3%)
    psum x4, blocking collectives, over_axes(): shard = lax.psum(shard, axis)  38.1 us
    all_to_all x1, waiting for transfers between devices, body(): lax.all_to_all(payload, GX_GY, split_axis=0, concat_axis=0, tiled=True)  32.3 us
    ppermute x8, starting transfers between devices, shifted(): return lax.ppermute(flat, axis, pairs).reshape(piece.shape)  20.8 us
    ppermute x8, starting transfers between devices, shifted(): return lax.ppermute(piece, axis, pairs)  15.7 us
    pallas_call x1, Pallas kernels, to_grid(): pl.pallas_call(relayout_kernel, out_shape=jax.ShapeDtypeStruct((3, span_x...  14.7 us
    all_to_all x1, starting transfers between devices, body(): lax.all_to_all(payload, GX_GY, split_axis=0, concat_axis=0, tiled=True)  11.6 us
    ppermute x8, waiting for transfers between devices, shifted(): return lax.ppermute(piece, axis, pairs)  4.54 us
  transfers between devices with their start and end apart: 17, of which 5 were waited for; matrix products, arithmetic and copies ran while one was open for 7% of the time, Pallas kernels for 8%

profile of v10, /device:TPU:0, one launch (start us, length us, event | category | flops | bytes accessed | tf_op | source)
XLA Modules:
  0.0 184.6 jit_solution(499246678459685880)
XLA Ops:
  1.9 2.0 %broadcast_select_fusion = (bf16[256]{0:T(256)(128)(2,1)S(1)}, bf16[256]{0:T(256)(128)(2,1)S(1)}) fusion(pred[]{:T(512)} %compare_reduce_fusion, s32[256]{0:T(256)} %param.11, pred[]{:T(512)} %compare_reduce_fusion.1), kind=kLoop, calls=%fused_computation.106 | loop fusion | flops 5888 | bytes 2050 | tf_op jit(solution)/shard_map/select.12
  7.0 2.1 %convolution_convert_fusion = bf16[128,6,1664]{2,0,1:T(8,128)(2,1)S(1)} fusion(bf16[256,128]{1,0:T(8,128)(2,1)S(1)} %scatter.9, bf16[256,1536]{1,0:T(8,128)(2,1)} %param.9, s32[128,6]{0,1:T(8,128)S(1)} %iota_add_fusion, s32[256]{0:T(256)S(1)} %multiply_add_fusion.1), kind=kOutput, calls=%fused_computation | convolution fusion | flops 657489920 | bytes 3411968 | tf_op jit(solution)/shard_map/pck,kj->pcj/dot_general | solution.py:74
  9.1 3.2 %copy.32 = bf16[128,6,1664]{2,1,0:T(8,128)(2,1)} copy(bf16[128,6,1664]{2,0,1:T(8,128)(2,1)S(1)} %convolution_convert_fusion) | data formatting | bytes 5111808 | tf_op jit(solution)/shard_map/convert_element_type | solution.py:77
  12.3 11.6 %all-to-all-start = ((bf16[128,6,1664]{2,1,0:T(8,128)(2,1)}), bf16[128,6,1664]{2,1,0:T(8,128)(2,1)}, u32[]{:S(2)}, u32[]{:S(2)}) async-start(bf16[128,6,1664]{2,1,0:T(8,128)(2,1)} %copy.32), calls=%async_computation | async-start | bytes 6815744 | tf_op jit(solution)/shard_map/all_to_all | solution.py:156
  25.3 3.7 %collective-permute-start.7 = (f32[32,128]{1,0:T(8,128)S(1)}, f32[32,128]{1,0:T(8,128)S(1)}, u32[]{:S(2)}, u32[]{:S(2)}) collective-permute-start(f32[32,128]{1,0:T(8,128)S(1)} %bitcast.84), channel_id=1, source_target_pairs={{0,1},{1,2},{2,3},{3,4},{4,5},{5,6},{6,7},{7,8},{8,9},{9,10},{10,1... | collective-permute-start | bytes 49160 | tf_op jit(solution)/shard_map/ppermute | solution.py:17
  34.7 32.3 %all-to-all-done = bf16[128,6,1664]{2,1,0:T(8,128)(2,1)} async-done(((bf16[128,6,1664]{2,1,0:T(8,128)(2,1)}), bf16[128,6,1664]{2,1,0:T(8,128)(2,1)}, u32[]{:S(2)}, u32[]{:S(2)}) %all-to-all-start) | async-done | bytes 2555936 | tf_op jit(solution)/shard_map/all_to_all | solution.py:156
  68.3 2.1 %slice.271 = bf16[128,6,1536]{2,1,0:T(8,128)(2,1)S(1)} slice(bf16[128,6,1664]{2,1,0:T(8,128)(2,1)} %all-to-all-done), slice={[0:128], [0:6], [0:1536]} | slice | bytes 4718592 | tf_op jit(solution)/shard_map/slice | solution.py:167
  70.3 3.5 %convolution_bitcast_fusion.blk_ref = f32[512,1536]{1,0:T(8,128)} fusion(bf16[128,6,1536]{2,1,0:T(8,128)(2,1)S(1)} %slice.271, s32[128,6]{0,1:T(8,128)S(1)} %fusion.40), kind=kOutput, calls=%fused_computation.1 | convolution fusion | flops 1208352768 | bytes 5508096 | tf_op jit(solution)/shard_map/pcs,pcj->sj/dot_general | solution.py:164
  73.9 14.7 %shard_map.68 = f32[3,32,64,128]{3,2,1,0:T(8,128)} custom-call(f32[512,1536]{1,0:T(8,128)} %convolution_bitcast_fusion.blk_ref), custom_call_target="tpu_custom_call" | custom-call | tf_op jit(solution)/shard_map/pallas_call | solution.py:144
  88.6 2.1 %slice_bitcast_fusion.2 = (f32[32,64,128]{2,1,0:T(8,128)S(1)}, f32[32,64,128]{2,1,0:T(8,128)S(1)}, f32[32,64,128]{2,1,0:T(8,128)S(1)}) fusion(f32[3,32,64,128]{3,2,1,0:T(8,128)} %shard_map.68), kind=kLoop, calls=%fused_computation.62 | loop fusion | bytes 6291456 | tf_op jit(solution)/shard_map/squeeze | solution.py:171
  91.5 2.9 %collective-permute-start.3 = (f32[32,128]{1,0:T(8,128)S(1)}, f32[32,128]{1,0:T(8,128)S(1)}, u32[]{:S(2)}, u32[]{:S(2)}) collective-permute-start(f32[32,128]{1,0:T(8,128)S(1)} %bitcast.86), channel_id=1, source_target_pairs={{0,1},{1,2},{2,3},{3,4},{4,5},{5,6},{6,7},{7,8},{8,9},{9,10},{10,1... | collective-permute-start | bytes 49160 | tf_op jit(solution)/shard_map/ppermute | solution.py:17
  97.0 3.0 %collective-permute-start.1 = (f32[1,64,128]{2,1,0:T(8,128)S(1)}, f32[1,64,128]{2,1,0:T(8,128)S(1)}, u32[]{:S(2)}, u32[]{:S(2)}) collective-permute-start(f32[1,64,128]{2,1,0:T(8,128)S(1)} %get-tuple-element.36), channel_id=1, source_target_pairs={{0,16},{16,32},{32,48},{48,64},{64,80},{80,96},{96,112},{1,17},{17... | collective-permute-start | bytes 98312 | tf_op jit(solution)/shard_map/ppermute | solution.py:18
  101.3 3.6 %fusion.45 = (f32[32,64,128]{2,1,0:T(8,128)S(1)}, f32[32,64,128]{2,1,0:T(8,128)S(1)}) fusion(f32[32,64,128]{2,1,0:T(8,128)S(1)} %copy-done.1, f32[32,64,127]{2,1,0:T(8,128)S(1)} %get-tuple-element.70, f32[32,64,127]{2,1,0:T(8,128)S(1)} %get-tuple-element.71, f32[34,64,128]{2,1,0:T(8,128)} %constant_dynamic-update-slice_fusion, ...), kind=kLoop, calls=%fused_computation.116 | loop fusion | flops 8126464 | bytes 11763712 | tf_op jit(solution)/shard_map/mul | solution.py:180
  104.9 4.5 %collective-permute-start.11 = (f32[32,128]{1,0:T(8,128)S(1)}, f32[32,128]{1,0:T(8,128)S(1)}, u32[]{:S(2)}, u32[]{:S(2)}) collective-permute-start(f32[32,128]{1,0:T(8,128)S(1)} %bitcast.89), channel_id=1, source_target_pairs={{0,1},{1,2},{2,3},{3,4},{4,5},{5,6},{6,7},{7,8},{8,9},{9,10},{10,1... | collective-permute-start | bytes 49160 | tf_op jit(solution)/shard_map/ppermute | solution.py:17
  115.1 2.4 %collective-permute-done.8 = f32[1,64,128]{2,1,0:T(8,128)S(1)} collective-permute-done((f32[1,64,128]{2,1,0:T(8,128)S(1)}, f32[1,64,128]{2,1,0:T(8,128)S(1)}, u32[]{:S(2)}, u32[]{:S(2)}) %collective-permute-start.8) | collective-permute-done | bytes 32800 | tf_op jit(solution)/shard_map/ppermute | solution.py:18
  118.3 4.5 %collective-permute-start.15 = (f32[32,128]{1,0:T(8,128)S(1)}, f32[32,128]{1,0:T(8,128)S(1)}, u32[]{:S(2)}, u32[]{:S(2)}) collective-permute-start(f32[32,128]{1,0:T(8,128)S(1)} %bitcast.90), channel_id=1, source_target_pairs={{0,1},{1,2},{2,3},{3,4},{4,5},{5,6},{6,7},{7,8},{8,9},{9,10},{10,1... | collective-permute-start | bytes 49160 | tf_op jit(solution)/shard_map/ppermute | solution.py:17
  124.1 4.3 %collective-permute-start.13 = (f32[1,64,128]{2,1,0:T(8,128)S(1)}, f32[1,64,128]{2,1,0:T(8,128)S(1)}, u32[]{:S(2)}, u32[]{:S(2)}) collective-permute-start(f32[1,64,128]{2,1,0:T(8,128)S(1)} %get-tuple-element.44), channel_id=1, source_target_pairs={{0,16},{16,32},{32,48},{48,64},{64,80},{80,96},{96,112},{1,17},{17... | collective-permute-start | bytes 98312 | tf_op jit(solution)/shard_map/ppermute | solution.py:18
  131.5 3.3 %multiply_reduce_fusion.3 = (f32[]{:T(128)}, f32[]{:T(128)}, f32[]{:T(128)}, f32[]{:T(128)}, f32[32,64,128]{2,1,0:T(8,128)}) fusion(f32[32,64,128]{2,1,0:T(8,128)S(1)} %get-tuple-element.34, f32[32,64,128]{2,1,0:T(8,128)S(1)} %copy-done.1, f32[32,64,128]{2,1,0:T(8,128)S(1)} %get-tuple-element.32, f32[32,64,128]{2,1,0:T(8,128)S(1)} %get-tuple-element.31, ...), kind=kLoop, calls=%fused_computation.69 | loop fusion | flops 8388604 | bytes 7421968 | tf_op jit(solution)/shard_map/reduce_sum | solution.py:187
  134.8 2.5 %pad_maximum_fusion.20 = f32[4]{0:T(128)S(1)} fusion(f32[1]{0:T(128)} %bitcast.33, f32[1]{0:T(128)} %bitcast.28, f32[1]{0:T(128)} %bitcast.27, f32[1]{0:T(128)} %bitcast.22), kind=kLoop, calls=%fused_computation.109 | loop fusion | flops 12 | bytes 32 | tf_op jit(solution)/shard_map/stack | solution.py:185
  137.3 10.9 %psum.28 = f32[4]{0:T(128)S(1)} all-reduce(f32[4]{0:T(128)S(1)} %pad_maximum_fusion.20), channel_id=1, replica_groups=mesh['gx_0'=4,'gx_1'=2,'gy_0'=4,'gy_1'=4] {'gx_0'}, use_global_device_ids=true, to_apply=%region_9.10 | all-reduce | flops 4 | bytes 32 | tf_op jit(solution)/shard_map/psum | solution.py:43
  148.2 2.5 %psum.29 = f32[4]{0:T(128)S(1)} all-reduce(f32[4]{0:T(128)S(1)} %psum.28), channel_id=1, replica_groups=mesh['gx_0'=4,'gx_1'=2,'gy_0'=4,'gy_1'=4] {'gx_1'}, use_global_device_ids=true, to_apply=%region_10.11 | all-reduce | flops 4 | bytes 32 | tf_op jit(solution)/shard_map/psum | solution.py:43
  150.7 17.0 %psum.30 = f32[4]{0:T(128)S(1)} all-reduce(f32[4]{0:T(128)S(1)} %psum.29), channel_id=1, replica_groups=mesh['gx_0'=4,'gx_1'=2,'gy_0'=4,'gy_1'=4] {'gy_0'}, use_global_device_ids=true, to_apply=%region_11.12 | all-reduce | flops 4 | bytes 32 | tf_op jit(solution)/shard_map/psum | solution.py:43
  167.6 7.7 %psum.31 = f32[4]{0:T(128)S(1)} all-reduce(f32[4]{0:T(128)S(1)} %psum.30), channel_id=1, replica_groups=mesh['gx_0'=4,'gx_1'=2,'gy_0'=4,'gy_1'=4] {'gy_1'}, use_global_device_ids=true, to_apply=%region_12.13 | all-reduce | flops 4 | bytes 32 | tf_op jit(solution)/shard_map/psum | solution.py:43
  181.1 3.5 %multiply_subtract_fusion = (f32[32,64,128]{2,1,0:T(8,128)}, f32[32,64,128]{2,1,0:T(8,128)}) fusion(f32[32,64,128]{2,1,0:T(8,128)} %copy-done.2, f32[32,64,128]{2,1,0:T(8,128)} %get-tuple-element.30, f32[32,64,128]{2,1,0:T(8,128)S(1)} %get-tuple-element.34, f32[]{:T(128)S(6)} %div.34, f32[]{:T(128)S(6)} %div.35, f32[]{:T(128)S(6)} %div.33, ...), kind=kLoop, calls=%fused_computation.63 | loop fusion | flops 4718592 | bytes 7340044 | tf_op jit(solution)/shard_map/sub | solution.py:207
  (69 shorter events, 28.6 us)
Async XLA Ops:
  12.3 11.7 %copy-start = (f32[32,64,128]{2,1,0:T(8,128)S(1)}, f32[32,64,128]{2,1,0:T(8,128)}, u32[]{:S(2)}) copy-start(f32[32,64,128]{2,1,0:T(8,128)} %param.13) | copy-start | bytes 3145732
  12.3 54.7 %all-to-all-start = ((bf16[128,6,1664]{2,1,0:T(8,128)(2,1)}), bf16[128,6,1664]{2,1,0:T(8,128)(2,1)}, u32[]{:S(2)}, u32[]{:S(2)}) async-start(bf16[128,6,1664]{2,1,0:T(8,128)(2,1)} %copy.32), calls=%async_computation | async-start | bytes 6815744 | tf_op jit(solution)/shard_map/all_to_all | solution.py:156
  24.0 7.6 %collective-permute-start.5 = (f32[1,64,128]{2,1,0:T(8,128)S(1)}, f32[1,64,128]{2,1,0:T(8,128)S(1)}, u32[]{:S(2)}, u32[]{:S(2)}) collective-permute-start(f32[1,64,128]{2,1,0:T(8,128)S(1)} %get-tuple-element.61), channel_id=1, source_target_pairs={{0,16},{16,32},{32,48},{48,64},{64,80},{80,96},{96,112},{1,17},{17... | collective-permute-start | bytes 98312 | tf_op jit(solution)/shard_map/ppermute | solution.py:18
  25.3 71.7 %collective-permute-start.7 = (f32[32,128]{1,0:T(8,128)S(1)}, f32[32,128]{1,0:T(8,128)S(1)}, u32[]{:S(2)}, u32[]{:S(2)}) collective-permute-start(f32[32,128]{1,0:T(8,128)S(1)} %bitcast.84), channel_id=1, source_target_pairs={{0,1},{1,2},{2,3},{3,4},{4,5},{5,6},{6,7},{7,8},{8,9},{9,10},{10,1... | collective-permute-start | bytes 49160 | tf_op jit(solution)/shard_map/ppermute | solution.py:17
  29.0 71.8 %collective-permute-start.6 = (f32[32,128]{1,0:T(8,128)S(1)}, f32[32,128]{1,0:T(8,128)S(1)}, u32[]{:S(2)}, u32[]{:S(2)}) collective-permute-start(f32[32,128]{1,0:T(8,128)S(1)} %bitcast.83), channel_id=1, source_target_pairs={{1,0},{2,1},{3,2},{4,3},{5,4},{6,5},{7,6},{8,7},{9,8},{10,9},{11,1... | collective-permute-start | bytes 49160 | tf_op jit(solution)/shard_map/ppermute | solution.py:17
  30.3 3.8 %collective-permute-start.4 = (f32[1,64,128]{2,1,0:T(8,128)S(1)}, f32[1,64,128]{2,1,0:T(8,128)S(1)}, u32[]{:S(2)}, u32[]{:S(2)}) collective-permute-start(f32[1,64,128]{2,1,0:T(8,128)S(1)} %get-tuple-element.60), channel_id=1, source_target_pairs={{16,0},{32,16},{48,32},{64,48},{80,64},{96,80},{112,96},{17,1},{33... | collective-permute-start | bytes 98312 | tf_op jit(solution)/shard_map/ppermute | solution.py:18
  91.5 9.4 %collective-permute-start.3 = (f32[32,128]{1,0:T(8,128)S(1)}, f32[32,128]{1,0:T(8,128)S(1)}, u32[]{:S(2)}, u32[]{:S(2)}) collective-permute-start(f32[32,128]{1,0:T(8,128)S(1)} %bitcast.86), channel_id=1, source_target_pairs={{0,1},{1,2},{2,3},{3,4},{4,5},{5,6},{6,7},{7,8},{8,9},{9,10},{10,1... | collective-permute-start | bytes 49160 | tf_op jit(solution)/shard_map/ppermute | solution.py:17
  94.4 6.5 %collective-permute-start.2 = (f32[32,128]{1,0:T(8,128)S(1)}, f32[32,128]{1,0:T(8,128)S(1)}, u32[]{:S(2)}, u32[]{:S(2)}) collective-permute-start(f32[32,128]{1,0:T(8,128)S(1)} %bitcast.85), channel_id=1, source_target_pairs={{1,0},{2,1},{3,2},{4,3},{5,4},{6,5},{7,6},{8,7},{9,8},{10,9},{11,1... | collective-permute-start | bytes 49160 | tf_op jit(solution)/shard_map/ppermute | solution.py:17
  95.7 5.2 %collective-permute-start = (f32[1,64,128]{2,1,0:T(8,128)S(1)}, f32[1,64,128]{2,1,0:T(8,128)S(1)}, u32[]{:S(2)}, u32[]{:S(2)}) collective-permute-start(f32[1,64,128]{2,1,0:T(8,128)S(1)} %get-tuple-element.35), channel_id=1, source_target_pairs={{16,0},{32,16},{48,32},{64,48},{80,64},{96,80},{112,96},{17,1},{33... | collective-permute-start | bytes 98312 | tf_op jit(solution)/shard_map/ppermute | solution.py:18
  97.0 3.9 %collective-permute-start.1 = (f32[1,64,128]{2,1,0:T(8,128)S(1)}, f32[1,64,128]{2,1,0:T(8,128)S(1)}, u32[]{:S(2)}, u32[]{:S(2)}) collective-permute-start(f32[1,64,128]{2,1,0:T(8,128)S(1)} %get-tuple-element.36), channel_id=1, source_target_pairs={{0,16},{16,32},{32,48},{48,64},{64,80},{80,96},{96,112},{1,17},{17... | collective-permute-start | bytes 98312 | tf_op jit(solution)/shard_map/ppermute | solution.py:18
  100.0 1.2 copy-start.1
  104.9 9.3 %collective-permute-start.11 = (f32[32,128]{1,0:T(8,128)S(1)}, f32[32,128]{1,0:T(8,128)S(1)}, u32[]{:S(2)}, u32[]{:S(2)}) collective-permute-start(f32[32,128]{1,0:T(8,128)S(1)} %bitcast.89), channel_id=1, source_target_pairs={{0,1},{1,2},{2,3},{3,4},{4,5},{5,6},{6,7},{7,8},{8,9},{9,10},{10,1... | collective-permute-start | bytes 49160 | tf_op jit(solution)/shard_map/ppermute | solution.py:17
  109.4 5.6 %collective-permute-start.10 = (f32[32,128]{1,0:T(8,128)S(1)}, f32[32,128]{1,0:T(8,128)S(1)}, u32[]{:S(2)}, u32[]{:S(2)}) collective-permute-start(f32[32,128]{1,0:T(8,128)S(1)} %bitcast.87), channel_id=1, source_target_pairs={{1,0},{2,1},{3,2},{4,3},{5,4},{6,5},{7,6},{8,7},{9,8},{10,9},{11,1... | collective-permute-start | bytes 49160 | tf_op jit(solution)/shard_map/ppermute | solution.py:17
  110.7 4.3 %collective-permute-start.9 = (f32[1,64,128]{2,1,0:T(8,128)S(1)}, f32[1,64,128]{2,1,0:T(8,128)S(1)}, u32[]{:S(2)}, u32[]{:S(2)}) collective-permute-start(f32[1,64,128]{2,1,0:T(8,128)S(1)} %get-tuple-element.50), channel_id=1, source_target_pairs={{0,16},{16,32},{32,48},{48,64},{64,80},{80,96},{96,112},{1,17},{17... | collective-permute-start | bytes 98312 | tf_op jit(solution)/shard_map/ppermute | solution.py:18
  112.5 5.0 %collective-permute-start.8 = (f32[1,64,128]{2,1,0:T(8,128)S(1)}, f32[1,64,128]{2,1,0:T(8,128)S(1)}, u32[]{:S(2)}, u32[]{:S(2)}) collective-permute-start(f32[1,64,128]{2,1,0:T(8,128)S(1)} %get-tuple-element.51), channel_id=1, source_target_pairs={{16,0},{32,16},{48,32},{64,48},{80,64},{96,80},{112,96},{17,1},{33... | collective-permute-start | bytes 98312 | tf_op jit(solution)/shard_map/ppermute | solution.py:18
  118.2 16.6 %copy-start.2 = (f32[32,64,128]{2,1,0:T(8,128)}, f32[32,64,128]{2,1,0:T(8,128)S(1)}, u32[]{:S(2)}) copy-start(f32[32,64,128]{2,1,0:T(8,128)S(1)} %get-tuple-element.32) | copy-start | bytes 3145732
  118.3 12.0 %collective-permute-start.15 = (f32[32,128]{1,0:T(8,128)S(1)}, f32[32,128]{1,0:T(8,128)S(1)}, u32[]{:S(2)}, u32[]{:S(2)}) collective-permute-start(f32[32,128]{1,0:T(8,128)S(1)} %bitcast.90), channel_id=1, source_target_pairs={{0,1},{1,2},{2,3},{3,4},{4,5},{5,6},{6,7},{7,8},{8,9},{9,10},{10,1... | collective-permute-start | bytes 49160 | tf_op jit(solution)/shard_map/ppermute | solution.py:17
  122.8 7.4 %collective-permute-start.14 = (f32[32,128]{1,0:T(8,128)S(1)}, f32[32,128]{1,0:T(8,128)S(1)}, u32[]{:S(2)}, u32[]{:S(2)}) collective-permute-start(f32[32,128]{1,0:T(8,128)S(1)} %bitcast.88), channel_id=1, source_target_pairs={{1,0},{2,1},{3,2},{4,3},{5,4},{6,5},{7,6},{8,7},{9,8},{10,9},{11,1... | collective-permute-start | bytes 49160 | tf_op jit(solution)/shard_map/ppermute | solution.py:17
  124.1 6.1 %collective-permute-start.13 = (f32[1,64,128]{2,1,0:T(8,128)S(1)}, f32[1,64,128]{2,1,0:T(8,128)S(1)}, u32[]{:S(2)}, u32[]{:S(2)}) collective-permute-start(f32[1,64,128]{2,1,0:T(8,128)S(1)} %get-tuple-element.44), channel_id=1, source_target_pairs={{0,16},{16,32},{32,48},{48,64},{64,80},{80,96},{96,112},{1,17},{17... | collective-permute-start | bytes 98312 | tf_op jit(solution)/shard_map/ppermute | solution.py:18
  128.4 3.1 %collective-permute-start.12 = (f32[1,64,128]{2,1,0:T(8,128)S(1)}, f32[1,64,128]{2,1,0:T(8,128)S(1)}, u32[]{:S(2)}, u32[]{:S(2)}) collective-permute-start(f32[1,64,128]{2,1,0:T(8,128)S(1)} %get-tuple-element.45), channel_id=1, source_target_pairs={{16,0},{32,16},{48,32},{64,48},{80,64},{96,80},{112,96},{17,1},{33... | collective-permute-start | bytes 98312 | tf_op jit(solution)/shard_map/ppermute | solution.py:18

commit v11 on v10

--- a/solution.py
+++ b/solution.py
@@ -6,9 +6,10 @@
 from jax.experimental import pallas as pl
 from jax.experimental.pallas import tpu as pltpu
 
-GX_GY = ("gx_0", "gx_1", "gy_0", "gy_1")
-GX = ("gx_0", "gx_1")
-GY = ("gy_0", "gy_1")
+GX = ("y", "core")
+GY = ("x_hi", "x_lo", "z")
+GX_GY = GX + GY
+ORDER = ("y", "core", "z", "x_lo", "x_hi")
 
 
 def shifted(piece, axis, pairs, dim):
@@ -164,7 +165,7 @@
     blocks = jnp.einsum(
         "pcs,pcj->sj",
         picks.astype(jnp.bfloat16),
-        arrived[:, :, :1536],
+        arrived,
         preferred_element_type=jnp.float32,
     )
     normals = to_grid(blocks, span_x, span_y, depth)
@@ -190,7 +191,7 @@
                 jnp.sum(scaled * scaled_image),
             ]
         ),
-        GX_GY,
+        ORDER,
     )
     gamma, delta, energy, curvature = sums[0], sums[1], sums[2], sums[3]
     alpha = gamma / delta
@@ -209,7 +210,7 @@
 
 
 def solution(mesh):
-    split = Mesh(mesh.devices.reshape(4, 2, 4, 4), ("gx_0", "gx_1", "gy_0", "gy_1"))
+    split = Mesh(mesh.devices.reshape(4, 2, 2, 2, 4), GX_GY)
     placed = (P(GX_GY, None), P(GX_GY, None), P(GX_GY), P(GX, GY, None), P(GX, GY, None))
     return jax.shard_map(
         body,

time: 186 us -> 187 us (level)
  local copies, waits for them, and re-layouts: 15.6 us -> 13.5 us
  matrix products: 5.6 us -> 7.52 us
    slice x1 -> x0, local copies, waits for them, and re-layouts: 2.1 us -> none  [body(): arrived[:, :, :1536]]
    dot_general x1, matrix products: 3.53 us -> 5.46 us  [body(): jnp.einsum('pcs,pcj->sj', picks.astype(jnp.bfloat16), arrived, preferred_...]
    psum x4 -> x5, blocking collectives: 38.1 us -> 39.5 us  [over_axes(): shard = lax.psum(shard, axis)]
where the time goes in v11:
time: 187 us; the launch traced here: 186 us
  starting transfers between devices  48 us (26%)
  blocking collectives  39.5 us (21%)
  waiting for transfers between devices  37.9 us (20%)
  other arithmetic  18.7 us (10%)
  Pallas kernels  14.7 us (8%)
  local copies, waits for them, and re-layouts  13.5 us (7%)
  matrix products  7.52 us (4%)
  between operations  6.15 us (3%)
    psum x5, blocking collectives, over_axes(): shard = lax.psum(shard, axis)  39.5 us
    all_to_all x1, waiting for transfers between devices, body(): lax.all_to_all(payload, GX_GY, split_axis=0, concat_axis=0, tiled=True)  32.3 us
    ppermute x8, starting transfers between devices, shifted(): return lax.ppermute(flat, axis, pairs).reshape(piece.shape)  20.8 us
    ppermute x8, starting transfers between devices, shifted(): return lax.ppermute(piece, axis, pairs)  15.5 us
    pallas_call x1, Pallas kernels, to_grid(): pl.pallas_call(relayout_kernel, out_shape=jax.ShapeDtypeStruct((3, span_x...  14.7 us
    all_to_all x1, starting transfers between devices, body(): lax.all_to_all(payload, GX_GY, split_axis=0, concat_axis=0, tiled=True)  11.6 us
    dot_general x1, matrix products, body(): jnp.einsum('pcs,pcj->sj', picks.astype(jnp.bfloat16), arrived, preferred_...  5.46 us
    ppermute x8, waiting for transfers between devices, shifted(): return lax.ppermute(piece, axis, pairs)  4.71 us
  transfers between devices with their start and end apart: 17, of which 5 were waited for; matrix products, arithmetic and copies ran while one was open for 7% of the time, Pallas kernels for 8%

profile of v11, /device:TPU:0, one launch (start us, length us, event | category | flops | bytes accessed | tf_op | source)
XLA Modules:
  0.0 186.0 jit_solution(15830134974952757334)
XLA Ops:
  1.9 2.0 %broadcast_select_fusion = (bf16[256]{0:T(256)(128)(2,1)S(1)}, bf16[256]{0:T(256)(128)(2,1)S(1)}) fusion(pred[]{:T(512)} %compare_reduce_fusion, s32[256]{0:T(256)} %param.11, pred[]{:T(512)} %compare_reduce_fusion.1), kind=kLoop, calls=%fused_computation.106 | loop fusion | flops 5888 | bytes 2050 | tf_op jit(solution)/shard_map/select.12
  7.0 2.1 %convolution_convert_fusion = bf16[128,6,1664]{2,0,1:T(8,128)(2,1)S(1)} fusion(bf16[256,128]{1,0:T(8,128)(2,1)S(1)} %scatter.9, bf16[256,1536]{1,0:T(8,128)(2,1)} %param.9, s32[128,6]{0,1:T(8,128)S(1)} %iota_add_fusion, s32[256]{0:T(256)S(1)} %multiply_add_fusion.1), kind=kOutput, calls=%fused_computation | convolution fusion | flops 657489920 | bytes 3411968 | tf_op jit(solution)/shard_map/pck,kj->pcj/dot_general | solution.py:75
  9.1 3.2 %copy.32 = bf16[128,6,1664]{2,1,0:T(8,128)(2,1)} copy(bf16[128,6,1664]{2,0,1:T(8,128)(2,1)S(1)} %convolution_convert_fusion) | data formatting | bytes 5111808 | tf_op jit(solution)/shard_map/convert_element_type | solution.py:78
  12.3 11.6 %all-to-all-start = ((bf16[128,6,1664]{2,1,0:T(8,128)(2,1)}), bf16[128,6,1664]{2,1,0:T(8,128)(2,1)}, u32[]{:S(2)}, u32[]{:S(2)}) async-start(bf16[128,6,1664]{2,1,0:T(8,128)(2,1)} %copy.32), calls=%async_computation | async-start | bytes 6815744 | tf_op jit(solution)/shard_map/all_to_all | solution.py:157
  25.3 3.7 %collective-permute-start.7 = (f32[32,128]{1,0:T(8,128)S(1)}, f32[32,128]{1,0:T(8,128)S(1)}, u32[]{:S(2)}, u32[]{:S(2)}) collective-permute-start(f32[32,128]{1,0:T(8,128)S(1)} %bitcast.84), channel_id=1, source_target_pairs={{0,1},{1,2},{2,3},{3,4},{4,5},{5,6},{6,7},{7,8},{8,9},{9,10},{10,1... | collective-permute-start | bytes 49160 | tf_op jit(solution)/shard_map/ppermute | solution.py:18
  34.8 32.3 %all-to-all-done = bf16[128,6,1664]{2,1,0:T(8,128)(2,1)} async-done(((bf16[128,6,1664]{2,1,0:T(8,128)(2,1)}), bf16[128,6,1664]{2,1,0:T(8,128)(2,1)}, u32[]{:S(2)}, u32[]{:S(2)}) %all-to-all-start) | async-done | bytes 2555936 | tf_op jit(solution)/shard_map/all_to_all | solution.py:157
  68.3 5.5 %convolution_bitcast_fusion.blk_ref = f32[512,1664]{1,0:T(8,128)} fusion(bf16[128,6,1664]{2,1,0:T(8,128)(2,1)} %all-to-all-done, s32[128,6]{0,1:T(8,128)S(1)} %fusion.40), kind=kOutput, calls=%fused_computation.1 | convolution fusion | flops 1309016064 | bytes 5966848 | tf_op jit(solution)/shard_map/pcs,pcj->sj/dot_general | solution.py:165
  73.7 14.7 %shard_map.68 = f32[3,32,64,128]{3,2,1,0:T(8,128)} custom-call(f32[512,1664]{1,0:T(8,128)} %convolution_bitcast_fusion.blk_ref), custom_call_target="tpu_custom_call" | custom-call | tf_op jit(solution)/shard_map/pallas_call | solution.py:145
  88.5 2.1 %slice_bitcast_fusion.2 = (f32[32,64,128]{2,1,0:T(8,128)S(1)}, f32[32,64,128]{2,1,0:T(8,128)S(1)}, f32[32,64,128]{2,1,0:T(8,128)S(1)}) fusion(f32[3,32,64,128]{3,2,1,0:T(8,128)} %shard_map.68), kind=kLoop, calls=%fused_computation.62 | loop fusion | bytes 6291456 | tf_op jit(solution)/shard_map/squeeze | solution.py:172
  91.4 2.9 %collective-permute-start.3 = (f32[32,128]{1,0:T(8,128)S(1)}, f32[32,128]{1,0:T(8,128)S(1)}, u32[]{:S(2)}, u32[]{:S(2)}) collective-permute-start(f32[32,128]{1,0:T(8,128)S(1)} %bitcast.86), channel_id=1, source_target_pairs={{0,1},{1,2},{2,3},{3,4},{4,5},{5,6},{6,7},{7,8},{8,9},{9,10},{10,1... | collective-permute-start | bytes 49160 | tf_op jit(solution)/shard_map/ppermute | solution.py:18
  96.9 3.0 %collective-permute-start.1 = (f32[1,64,128]{2,1,0:T(8,128)S(1)}, f32[1,64,128]{2,1,0:T(8,128)S(1)}, u32[]{:S(2)}, u32[]{:S(2)}) collective-permute-start(f32[1,64,128]{2,1,0:T(8,128)S(1)} %get-tuple-element.36), channel_id=1, source_target_pairs={{0,16},{16,32},{32,48},{48,64},{64,80},{80,96},{96,112},{1,17},{17... | collective-permute-start | bytes 98312 | tf_op jit(solution)/shard_map/ppermute | solution.py:19
  101.1 3.6 %fusion.45 = (f32[32,64,128]{2,1,0:T(8,128)S(1)}, f32[32,64,128]{2,1,0:T(8,128)S(1)}) fusion(f32[32,64,128]{2,1,0:T(8,128)S(1)} %copy-done.1, f32[32,64,127]{2,1,0:T(8,128)S(1)} %get-tuple-element.70, f32[32,64,127]{2,1,0:T(8,128)S(1)} %get-tuple-element.71, f32[34,64,128]{2,1,0:T(8,128)} %constant_dynamic-update-slice_fusion, ...), kind=kLoop, calls=%fused_computation.116 | loop fusion | flops 8126464 | bytes 11763712 | tf_op jit(solution)/shard_map/mul | solution.py:181
  104.8 4.5 %collective-permute-start.11 = (f32[32,128]{1,0:T(8,128)S(1)}, f32[32,128]{1,0:T(8,128)S(1)}, u32[]{:S(2)}, u32[]{:S(2)}) collective-permute-start(f32[32,128]{1,0:T(8,128)S(1)} %bitcast.89), channel_id=1, source_target_pairs={{0,1},{1,2},{2,3},{3,4},{4,5},{5,6},{6,7},{7,8},{8,9},{9,10},{10,1... | collective-permute-start | bytes 49160 | tf_op jit(solution)/shard_map/ppermute | solution.py:18
  115.0 2.4 %collective-permute-done.8 = f32[1,64,128]{2,1,0:T(8,128)S(1)} collective-permute-done((f32[1,64,128]{2,1,0:T(8,128)S(1)}, f32[1,64,128]{2,1,0:T(8,128)S(1)}, u32[]{:S(2)}, u32[]{:S(2)}) %collective-permute-start.8) | collective-permute-done | bytes 32800 | tf_op jit(solution)/shard_map/ppermute | solution.py:19
  118.1 4.5 %collective-permute-start.15 = (f32[32,128]{1,0:T(8,128)S(1)}, f32[32,128]{1,0:T(8,128)S(1)}, u32[]{:S(2)}, u32[]{:S(2)}) collective-permute-start(f32[32,128]{1,0:T(8,128)S(1)} %bitcast.90), channel_id=1, source_target_pairs={{0,1},{1,2},{2,3},{3,4},{4,5},{5,6},{6,7},{7,8},{8,9},{9,10},{10,1... | collective-permute-start | bytes 49160 | tf_op jit(solution)/shard_map/ppermute | solution.py:18
  124.0 4.3 %collective-permute-start.13 = (f32[1,64,128]{2,1,0:T(8,128)S(1)}, f32[1,64,128]{2,1,0:T(8,128)S(1)}, u32[]{:S(2)}, u32[]{:S(2)}) collective-permute-start(f32[1,64,128]{2,1,0:T(8,128)S(1)} %get-tuple-element.44), channel_id=1, source_target_pairs={{0,16},{16,32},{32,48},{48,64},{64,80},{80,96},{96,112},{1,17},{17... | collective-permute-start | bytes 98312 | tf_op jit(solution)/shard_map/ppermute | solution.py:19
  131.4 3.3 %multiply_reduce_fusion.3 = (f32[]{:T(128)}, f32[]{:T(128)}, f32[]{:T(128)}, f32[]{:T(128)}, f32[32,64,128]{2,1,0:T(8,128)}) fusion(f32[32,64,128]{2,1,0:T(8,128)S(1)} %get-tuple-element.34, f32[32,64,128]{2,1,0:T(8,128)S(1)} %copy-done.1, f32[32,64,128]{2,1,0:T(8,128)S(1)} %get-tuple-element.32, f32[32,64,128]{2,1,0:T(8,128)S(1)} %get-tuple-element.31, ...), kind=kLoop, calls=%fused_computation.69 | loop fusion | flops 8388604 | bytes 7421968 | tf_op jit(solution)/shard_map/reduce_sum | solution.py:188
  134.7 2.6 %pad_maximum_fusion.20 = f32[4]{0:T(128)S(1)} fusion(f32[1]{0:T(128)} %bitcast.33, f32[1]{0:T(128)} %bitcast.28, f32[1]{0:T(128)} %bitcast.27, f32[1]{0:T(128)} %bitcast.22), kind=kLoop, calls=%fused_computation.109 | loop fusion | flops 12 | bytes 32 | tf_op jit(solution)/shard_map/stack | solution.py:186
  137.3 10.9 %psum.35 = f32[4]{0:T(128)S(1)} all-reduce(f32[4]{0:T(128)S(1)} %pad_maximum_fusion.20), channel_id=1, replica_groups=mesh['y'=4,'core'=2,'x_hi'=2,'x_lo'=2,'z'=4] {'y'}, use_global_device_ids=true, to_apply=%region_9.10 | all-reduce | flops 4 | bytes 32 | tf_op jit(solution)/shard_map/psum | solution.py:44
  148.2 2.5 %psum.36 = f32[4]{0:T(128)S(1)} all-reduce(f32[4]{0:T(128)S(1)} %psum.35), channel_id=1, replica_groups=mesh['y'=4,'core'=2,'x_hi'=2,'x_lo'=2,'z'=4] {'core'}, use_global_device_ids=true, to_apply=%region_10.11 | all-reduce | flops 4 | bytes 32 | tf_op jit(solution)/shard_map/psum | solution.py:44
  150.6 14.8 %psum.37 = f32[4]{0:T(128)S(1)} all-reduce(f32[4]{0:T(128)S(1)} %psum.36), channel_id=1, replica_groups=mesh['y'=4,'core'=2,'x_hi'=2,'x_lo'=2,'z'=4] {'z'}, use_global_device_ids=true, to_apply=%region_11.12 | all-reduce | flops 4 | bytes 32 | tf_op jit(solution)/shard_map/psum | solution.py:44
  165.4 4.9 %psum.38 = f32[4]{0:T(128)S(1)} all-reduce(f32[4]{0:T(128)S(1)} %psum.37), channel_id=1, replica_groups=mesh['y'=4,'core'=2,'x_hi'=2,'x_lo'=2,'z'=4] {'x_lo'}, use_global_device_ids=true, to_apply=%region_12.13 | all-reduce | flops 4 | bytes 32 | tf_op jit(solution)/shard_map/psum | solution.py:44
  170.4 6.4 %psum.39 = f32[4]{0:T(128)S(1)} all-reduce(f32[4]{0:T(128)S(1)} %psum.38), channel_id=1, replica_groups=mesh['y'=4,'core'=2,'x_hi'=2,'x_lo'=2,'z'=4] {'x_hi'}, use_global_device_ids=true, to_apply=%region_13.14 | all-reduce | flops 4 | bytes 32 | tf_op jit(solution)/shard_map/psum | solution.py:44
  182.5 3.5 %multiply_subtract_fusion = (f32[32,64,128]{2,1,0:T(8,128)}, f32[32,64,128]{2,1,0:T(8,128)}) fusion(f32[32,64,128]{2,1,0:T(8,128)} %copy-done.2, f32[32,64,128]{2,1,0:T(8,128)} %get-tuple-element.30, f32[32,64,128]{2,1,0:T(8,128)S(1)} %get-tuple-element.34, f32[]{:T(128)S(6)} %div.34, f32[]{:T(128)S(6)} %div.35, f32[]{:T(128)S(6)} %div.33, ...), kind=kLoop, calls=%fused_computation.63 | loop fusion | flops 4718592 | bytes 7340044 | tf_op jit(solution)/shard_map/sub | solution.py:208
  (69 shorter events, 28.6 us)
Async XLA Ops:
  12.3 11.7 %copy-start = (f32[32,64,128]{2,1,0:T(8,128)S(1)}, f32[32,64,128]{2,1,0:T(8,128)}, u32[]{:S(2)}) copy-start(f32[32,64,128]{2,1,0:T(8,128)} %param.13) | copy-start | bytes 3145732
  12.3 54.7 %all-to-all-start = ((bf16[128,6,1664]{2,1,0:T(8,128)(2,1)}), bf16[128,6,1664]{2,1,0:T(8,128)(2,1)}, u32[]{:S(2)}, u32[]{:S(2)}) async-start(bf16[128,6,1664]{2,1,0:T(8,128)(2,1)} %copy.32), calls=%async_computation | async-start | bytes 6815744 | tf_op jit(solution)/shard_map/all_to_all | solution.py:157
  24.0 7.6 %collective-permute-start.5 = (f32[1,64,128]{2,1,0:T(8,128)S(1)}, f32[1,64,128]{2,1,0:T(8,128)S(1)}, u32[]{:S(2)}, u32[]{:S(2)}) collective-permute-start(f32[1,64,128]{2,1,0:T(8,128)S(1)} %get-tuple-element.61), channel_id=1, source_target_pairs={{0,16},{16,32},{32,48},{48,64},{64,80},{80,96},{96,112},{1,17},{17... | collective-permute-start | bytes 98312 | tf_op jit(solution)/shard_map/ppermute | solution.py:19
  25.3 71.5 %collective-permute-start.7 = (f32[32,128]{1,0:T(8,128)S(1)}, f32[32,128]{1,0:T(8,128)S(1)}, u32[]{:S(2)}, u32[]{:S(2)}) collective-permute-start(f32[32,128]{1,0:T(8,128)S(1)} %bitcast.84), channel_id=1, source_target_pairs={{0,1},{1,2},{2,3},{3,4},{4,5},{5,6},{6,7},{7,8},{8,9},{9,10},{10,1... | collective-permute-start | bytes 49160 | tf_op jit(solution)/shard_map/ppermute | solution.py:18
  29.0 71.7 %collective-permute-start.6 = (f32[32,128]{1,0:T(8,128)S(1)}, f32[32,128]{1,0:T(8,128)S(1)}, u32[]{:S(2)}, u32[]{:S(2)}) collective-permute-start(f32[32,128]{1,0:T(8,128)S(1)} %bitcast.83), channel_id=1, source_target_pairs={{1,0},{2,1},{3,2},{4,3},{5,4},{6,5},{7,6},{8,7},{9,8},{10,9},{11,1... | collective-permute-start | bytes 49160 | tf_op jit(solution)/shard_map/ppermute | solution.py:18
  30.3 3.8 %collective-permute-start.4 = (f32[1,64,128]{2,1,0:T(8,128)S(1)}, f32[1,64,128]{2,1,0:T(8,128)S(1)}, u32[]{:S(2)}, u32[]{:S(2)}) collective-permute-start(f32[1,64,128]{2,1,0:T(8,128)S(1)} %get-tuple-element.60), channel_id=1, source_target_pairs={{16,0},{32,16},{48,32},{64,48},{80,64},{96,80},{112,96},{17,1},{33... | collective-permute-start | bytes 98312 | tf_op jit(solution)/shard_map/ppermute | solution.py:19
  91.4 9.4 %collective-permute-start.3 = (f32[32,128]{1,0:T(8,128)S(1)}, f32[32,128]{1,0:T(8,128)S(1)}, u32[]{:S(2)}, u32[]{:S(2)}) collective-permute-start(f32[32,128]{1,0:T(8,128)S(1)} %bitcast.86), channel_id=1, source_target_pairs={{0,1},{1,2},{2,3},{3,4},{4,5},{5,6},{6,7},{7,8},{8,9},{9,10},{10,1... | collective-permute-start | bytes 49160 | tf_op jit(solution)/shard_map/ppermute | solution.py:18
  94.3 6.5 %collective-permute-start.2 = (f32[32,128]{1,0:T(8,128)S(1)}, f32[32,128]{1,0:T(8,128)S(1)}, u32[]{:S(2)}, u32[]{:S(2)}) collective-permute-start(f32[32,128]{1,0:T(8,128)S(1)} %bitcast.85), channel_id=1, source_target_pairs={{1,0},{2,1},{3,2},{4,3},{5,4},{6,5},{7,6},{8,7},{9,8},{10,9},{11,1... | collective-permute-start | bytes 49160 | tf_op jit(solution)/shard_map/ppermute | solution.py:18
  95.6 5.2 %collective-permute-start = (f32[1,64,128]{2,1,0:T(8,128)S(1)}, f32[1,64,128]{2,1,0:T(8,128)S(1)}, u32[]{:S(2)}, u32[]{:S(2)}) collective-permute-start(f32[1,64,128]{2,1,0:T(8,128)S(1)} %get-tuple-element.35), channel_id=1, source_target_pairs={{16,0},{32,16},{48,32},{64,48},{80,64},{96,80},{112,96},{17,1},{33... | collective-permute-start | bytes 98312 | tf_op jit(solution)/shard_map/ppermute | solution.py:19
  96.9 3.9 %collective-permute-start.1 = (f32[1,64,128]{2,1,0:T(8,128)S(1)}, f32[1,64,128]{2,1,0:T(8,128)S(1)}, u32[]{:S(2)}, u32[]{:S(2)}) collective-permute-start(f32[1,64,128]{2,1,0:T(8,128)S(1)} %get-tuple-element.36), channel_id=1, source_target_pairs={{0,16},{16,32},{32,48},{48,64},{64,80},{80,96},{96,112},{1,17},{17... | collective-permute-start | bytes 98312 | tf_op jit(solution)/shard_map/ppermute | solution.py:19
  99.9 1.2 copy-start.1
  104.8 9.3 %collective-permute-start.11 = (f32[32,128]{1,0:T(8,128)S(1)}, f32[32,128]{1,0:T(8,128)S(1)}, u32[]{:S(2)}, u32[]{:S(2)}) collective-permute-start(f32[32,128]{1,0:T(8,128)S(1)} %bitcast.89), channel_id=1, source_target_pairs={{0,1},{1,2},{2,3},{3,4},{4,5},{5,6},{6,7},{7,8},{8,9},{9,10},{10,1... | collective-permute-start | bytes 49160 | tf_op jit(solution)/shard_map/ppermute | solution.py:18
  109.3 5.6 %collective-permute-start.10 = (f32[32,128]{1,0:T(8,128)S(1)}, f32[32,128]{1,0:T(8,128)S(1)}, u32[]{:S(2)}, u32[]{:S(2)}) collective-permute-start(f32[32,128]{1,0:T(8,128)S(1)} %bitcast.87), channel_id=1, source_target_pairs={{1,0},{2,1},{3,2},{4,3},{5,4},{6,5},{7,6},{8,7},{9,8},{10,9},{11,1... | collective-permute-start | bytes 49160 | tf_op jit(solution)/shard_map/ppermute | solution.py:18
  110.6 4.3 %collective-permute-start.9 = (f32[1,64,128]{2,1,0:T(8,128)S(1)}, f32[1,64,128]{2,1,0:T(8,128)S(1)}, u32[]{:S(2)}, u32[]{:S(2)}) collective-permute-start(f32[1,64,128]{2,1,0:T(8,128)S(1)} %get-tuple-element.50), channel_id=1, source_target_pairs={{0,16},{16,32},{32,48},{48,64},{64,80},{80,96},{96,112},{1,17},{17... | collective-permute-start | bytes 98312 | tf_op jit(solution)/shard_map/ppermute | solution.py:19
  112.4 5.0 %collective-permute-start.8 = (f32[1,64,128]{2,1,0:T(8,128)S(1)}, f32[1,64,128]{2,1,0:T(8,128)S(1)}, u32[]{:S(2)}, u32[]{:S(2)}) collective-permute-start(f32[1,64,128]{2,1,0:T(8,128)S(1)} %get-tuple-element.51), channel_id=1, source_target_pairs={{16,0},{32,16},{48,32},{64,48},{80,64},{96,80},{112,96},{17,1},{33... | collective-permute-start | bytes 98312 | tf_op jit(solution)/shard_map/ppermute | solution.py:19
  118.1 13.3 %copy-start.2 = (f32[32,64,128]{2,1,0:T(8,128)}, f32[32,64,128]{2,1,0:T(8,128)S(1)}, u32[]{:S(2)}) copy-start(f32[32,64,128]{2,1,0:T(8,128)S(1)} %get-tuple-element.32) | copy-start | bytes 3145732
  118.1 11.8 %collective-permute-start.15 = (f32[32,128]{1,0:T(8,128)S(1)}, f32[32,128]{1,0:T(8,128)S(1)}, u32[]{:S(2)}, u32[]{:S(2)}) collective-permute-start(f32[32,128]{1,0:T(8,128)S(1)} %bitcast.90), channel_id=1, source_target_pairs={{0,1},{1,2},{2,3},{3,4},{4,5},{5,6},{6,7},{7,8},{8,9},{9,10},{10,1... | collective-permute-start | bytes 49160 | tf_op jit(solution)/shard_map/ppermute | solution.py:18
  122.7 7.3 %collective-permute-start.14 = (f32[32,128]{1,0:T(8,128)S(1)}, f32[32,128]{1,0:T(8,128)S(1)}, u32[]{:S(2)}, u32[]{:S(2)}) collective-permute-start(f32[32,128]{1,0:T(8,128)S(1)} %bitcast.88), channel_id=1, source_target_pairs={{1,0},{2,1},{3,2},{4,3},{5,4},{6,5},{7,6},{8,7},{9,8},{10,9},{11,1... | collective-permute-start | bytes 49160 | tf_op jit(solution)/shard_map/ppermute | solution.py:18
  124.0 6.0 %collective-permute-start.13 = (f32[1,64,128]{2,1,0:T(8,128)S(1)}, f32[1,64,128]{2,1,0:T(8,128)S(1)}, u32[]{:S(2)}, u32[]{:S(2)}) collective-permute-start(f32[1,64,128]{2,1,0:T(8,128)S(1)} %get-tuple-element.44), channel_id=1, source_target_pairs={{0,16},{16,32},{32,48},{48,64},{64,80},{80,96},{96,112},{1,17},{17... | collective-permute-start | bytes 98312 | tf_op jit(solution)/shard_map/ppermute | solution.py:19
  128.3 3.1 %collective-permute-start.12 = (f32[1,64,128]{2,1,0:T(8,128)S(1)}, f32[1,64,128]{2,1,0:T(8,128)S(1)}, u32[]{:S(2)}, u32[]{:S(2)}) collective-permute-start(f32[1,64,128]{2,1,0:T(8,128)S(1)} %get-tuple-element.45), channel_id=1, source_target_pairs={{16,0},{32,16},{48,32},{64,48},{80,64},{96,80},{112,96},{17,1},{33... | collective-permute-start | bytes 98312 | tf_op jit(solution)/shard_map/ppermute | solution.py:19

commit v12 on v10

--- a/solution.py
+++ b/solution.py
@@ -1,3 +1,5 @@
+import functools
+
 import jax
 import jax.numpy as jnp
 from jax import lax
@@ -101,7 +103,7 @@
     return grid.reshape(span_x * 8, span_y * 8, span_z * 8)
 
 
-def relayout_kernel(blk_ref, out_ref):
+def relayout_kernel(comp, blk_ref, out_ref):
     sub = lax.broadcasted_iota(jnp.int32, (8, 128), 0)
     lane = lax.broadcasted_iota(jnp.int32, (8, 128), 1)
     grp = (lane // 8) % 8
@@ -126,26 +128,27 @@
         y = pl.multiple_of(ly * 8, 8)
         top = blk_ref[pl.ds(row, 8), :]
         bottom = blk_ref[pl.ds(row + 8, 8), :]
-        for c in range(3):
-            for uh in range(4):
-                col = (c * 4 + uh) * 128
-                s0 = top[:, col:col + 128]
-                s1 = bottom[:, col:col + 128]
-                u0 = jnp.where(low_half, s0, pltpu.roll(s1, 64, 1))
-                u1 = jnp.where(low_half, pltpu.roll(s0, 64, 1), s1)
-                out_ref[c, lx * 8 + uh * 2, pl.ds(y, 8), :] = transpose_groups(u0)
-                out_ref[c, lx * 8 + uh * 2 + 1, pl.ds(y, 8), :] = transpose_groups(u1)
+        for uh in range(4):
+            col = (comp * 4 + uh) * 128
+            s0 = top[:, col:col + 128]
+            s1 = bottom[:, col:col + 128]
+            u0 = jnp.where(low_half, s0, pltpu.roll(s1, 64, 1))
+            u1 = jnp.where(low_half, pltpu.roll(s0, 64, 1), s1)
+            out_ref[lx * 8 + uh * 2, pl.ds(y, 8), :] = transpose_groups(u0)
+            out_ref[lx * 8 + uh * 2 + 1, pl.ds(y, 8), :] = transpose_groups(u1)
         return carry
 
     lax.fori_loop(0, 32, step, 0)
 
 
-def to_grid(blocks, span_x, span_y, depth):
+def to_grid(blocks, comp, span_x, span_y, depth):
+    cells = span_x * span_y * 8 * depth
     return pl.pallas_call(
-        relayout_kernel,
-        out_shape=jax.ShapeDtypeStruct((3, span_x * 8, span_y * 8, depth), jnp.float32),
+        functools.partial(relayout_kernel, comp),
+        out_shape=jax.ShapeDtypeStruct((span_x * 8, span_y * 8, depth), jnp.float32),
         in_specs=[pl.BlockSpec(memory_space=pltpu.VMEM)],
         out_specs=pl.BlockSpec(memory_space=pltpu.VMEM),
+        cost_estimate=pl.CostEstimate(flops=20 * cells, bytes_accessed=8 * cells, transcendentals=0),
     )(blocks)
 
 
@@ -167,8 +170,9 @@
         arrived[:, :, :1536],
         preferred_element_type=jnp.float32,
     )
-    normals = to_grid(blocks, span_x, span_y, depth)
-    normal_x, normal_y, normal_z = normals[0], normals[1], normals[2]
+    normal_x = to_grid(blocks, 0, span_x, span_y, depth)
+    normal_y = to_grid(blocks, 1, span_x, span_y, depth)
+    normal_z = to_grid(blocks, 2, span_x, span_y, depth)
     along_x = with_halo(normal_x, ((GX, 0),), 1)
     along_y = with_halo(normal_y, ((GY, 1),), 1)
     total = along_x[2:] - along_x[:-2]

time: 186 us -> 211 us (1.13)
  Pallas kernels: 14.7 us -> 38.6 us
  waiting for transfers between devices: 37.7 us -> 34.9 us
    pallas_call x1 -> x3, Pallas kernels: 14.7 us -> 38.6 us  [to_grid(): pl.pallas_call(functools.partial(relayout_kernel, comp), out_shape=jax.Sh...]
    ppermute x8, waiting for transfers between devices: 4.54 us -> 0.02 us  [shifted(): return lax.ppermute(piece, axis, pairs)]
    ppermute x8, waiting for transfers between devices: 0.86 us -> 4.28 us  [shifted(): return lax.ppermute(flat, axis, pairs).reshape(piece.shape)]
    slice x3 -> x4, local copies, waits for them, and re-layouts: 1.51 us -> 4.35 us  [next_along_z(): return jnp.concatenate([field[..., 1:], edge], axis=-1)]
  transfers between devices with their start and end apart: 17 -> 17, of which waited for: 5 -> 4; matrix products, arithmetic and copies ran while one was open for 7% -> 7% of each run, Pallas kernels for 8% -> 18%
where the time goes in v12:
time: 211 us; the launch traced here: 209 us
  starting transfers between devices  49.6 us (24%)
  Pallas kernels  38.6 us (18%)
  blocking collectives  38.5 us (18%)
  waiting for transfers between devices  34.9 us (17%)
  other arithmetic  19 us (9%)
  local copies, waits for them, and re-layouts  16.9 us (8%)
  between operations  6.2 us (3%)
  matrix products  5.58 us (3%)
    pallas_call x3, Pallas kernels, to_grid(): pl.pallas_call(functools.partial(relayout_kernel, comp), out_shape=jax.Sh...  38.6 us
    psum x4, blocking collectives, over_axes(): shard = lax.psum(shard, axis)  38.5 us
    all_to_all x1, waiting for transfers between devices, body(): lax.all_to_all(payload, GX_GY, split_axis=0, concat_axis=0, tiled=True)  30.6 us
    ppermute x8, starting transfers between devices, shifted(): return lax.ppermute(flat, axis, pairs).reshape(piece.shape)  22.4 us
    ppermute x8, starting transfers between devices, shifted(): return lax.ppermute(piece, axis, pairs)  15.5 us
    all_to_all x1, starting transfers between devices, body(): lax.all_to_all(payload, GX_GY, split_axis=0, concat_axis=0, tiled=True)  11.6 us
    slice x4, local copies, waits for them, and re-layouts, next_along_z(): return jnp.concatenate([field[..., 1:], edge], axis=-1)  4.35 us
    ppermute x8, waiting for transfers between devices, shifted(): return lax.ppermute(flat, axis, pairs).reshape(piece.shape)  4.28 us
  transfers between devices with their start and end apart: 17, of which 4 were waited for; matrix products, arithmetic and copies ran while one was open for 7% of the time, Pallas kernels for 18%

profile of v12, /device:TPU:0, one launch (start us, length us, event | category | flops | bytes accessed | tf_op | source)
XLA Modules:
  0.0 209.3 jit_solution(3157252226572606445)
XLA Ops:
  9.1 3.2 %copy.32 = bf16[128,6,1664]{2,1,0:T(8,128)(2,1)} copy(bf16[128,6,1664]{2,0,1:T(8,128)(2,1)S(1)} %convolution_convert_fusion) | data formatting | bytes 5111808 | tf_op jit(solution)/shard_map/convert_element_type | solution.py:79
  12.3 11.6 %all-to-all-start = ((bf16[128,6,1664]{2,1,0:T(8,128)(2,1)}), bf16[128,6,1664]{2,1,0:T(8,128)(2,1)}, u32[]{:S(2)}, u32[]{:S(2)}) async-start(bf16[128,6,1664]{2,1,0:T(8,128)(2,1)} %copy.32), calls=%async_computation | async-start | bytes 6815744 | tf_op jit(solution)/shard_map/all_to_all | solution.py:159
  27.9 4.5 %collective-permute-start.7 = (f32[32,128]{1,0:T(8,128)S(1)}, f32[32,128]{1,0:T(8,128)S(1)}, u32[]{:S(2)}, u32[]{:S(2)}) collective-permute-start(f32[32,128]{1,0:T(8,128)S(1)} %bitcast.73), channel_id=1, source_target_pairs={{0,1},{1,2},{2,3},{3,4},{4,5},{5,6},{6,7},{7,8},{8,9},{9,10},{10,1... | collective-permute-start | bytes 49160 | tf_op jit(solution)/shard_map/ppermute | solution.py:19
  36.5 30.6 %all-to-all-done = bf16[128,6,1664]{2,1,0:T(8,128)(2,1)} async-done(((bf16[128,6,1664]{2,1,0:T(8,128)(2,1)}), bf16[128,6,1664]{2,1,0:T(8,128)(2,1)}, u32[]{:S(2)}, u32[]{:S(2)}) %all-to-all-start) | async-done | bytes 2555936 | tf_op jit(solution)/shard_map/all_to_all | solution.py:159
  68.3 2.1 %slice.249 = bf16[128,6,1536]{2,1,0:T(8,128)(2,1)S(1)} slice(bf16[128,6,1664]{2,1,0:T(8,128)(2,1)} %all-to-all-done), slice={[0:128], [0:6], [0:1536]} | slice | bytes 4718592 | tf_op jit(solution)/shard_map/slice | solution.py:170
  70.4 3.5 %convolution_bitcast_fusion.blk_ref = f32[512,1536]{1,0:T(8,128)} fusion(bf16[128,6,1536]{2,1,0:T(8,128)(2,1)S(1)} %slice.249, s32[128,6]{0,1:T(8,128)S(1)} %fusion.40), kind=kOutput, calls=%fused_computation.1 | convolution fusion | flops 1208352768 | bytes 5508096 | tf_op jit(solution)/shard_map/pcs,pcj->sj/dot_general | solution.py:167
  73.9 12.9 %shard_map.68 = f32[32,64,128]{2,1,0:T(8,128)} custom-call(f32[512,1536]{1,0:T(8,128)} %convolution_bitcast_fusion.blk_ref), custom_call_target="tpu_custom_call" | custom-call | flops 655360 | bytes 262144 | tf_op jit(solution)/shard_map/pallas_call | solution.py:146
  86.7 12.9 %shard_map.69 = f32[32,64,128]{2,1,0:T(8,128)} custom-call(f32[512,1536]{1,0:T(8,128)} %convolution_bitcast_fusion.blk_ref), custom_call_target="tpu_custom_call" | custom-call | flops 655360 | bytes 262144 | tf_op jit(solution)/shard_map/pallas_call | solution.py:146
  101.7 3.0 %collective-permute-start.1 = (f32[1,64,128]{2,1,0:T(8,128)S(1)}, f32[1,64,128]{2,1,0:T(8,128)S(1)}, u32[]{:S(2)}, u32[]{:S(2)}) collective-permute-start(f32[1,64,128]{2,1,0:T(8,128)S(1)} %get-tuple-element.50), channel_id=1, source_target_pairs={{0,16},{16,32},{32,48},{48,64},{64,80},{80,96},{96,112},{1,17},{17... | collective-permute-start | bytes 98312 | tf_op jit(solution)/shard_map/ppermute | solution.py:20
  105.7 2.9 %collective-permute-start.3 = (f32[32,128]{1,0:T(8,128)S(1)}, f32[32,128]{1,0:T(8,128)S(1)}, u32[]{:S(2)}, u32[]{:S(2)}) collective-permute-start(f32[32,128]{1,0:T(8,128)S(1)} %bitcast.78), channel_id=1, source_target_pairs={{0,1},{1,2},{2,3},{3,4},{4,5},{5,6},{6,7},{7,8},{8,9},{9,10},{10,1... | collective-permute-start | bytes 49160 | tf_op jit(solution)/shard_map/ppermute | solution.py:19
  108.6 12.9 %shard_map.70 = f32[32,64,128]{2,1,0:T(8,128)} custom-call(f32[512,1536]{1,0:T(8,128)} %convolution_bitcast_fusion.blk_ref), custom_call_target="tpu_custom_call" | custom-call | flops 655360 | bytes 262144 | tf_op jit(solution)/shard_map/pallas_call | solution.py:146
  125.1 2.4 %collective-permute-done.2 = f32[32,128]{1,0:T(8,128)S(1)} collective-permute-done((f32[32,128]{1,0:T(8,128)S(1)}, f32[32,128]{1,0:T(8,128)S(1)}, u32[]{:S(2)}, u32[]{:S(2)}) %collective-permute-start.2) | collective-permute-done | bytes 16416 | tf_op jit(solution)/shard_map/ppermute | solution.py:19
  127.5 3.8 %fusion.45 = (f32[32,64,128]{2,1,0:T(8,128)S(1)}, f32[32,64,128]{2,1,0:T(8,128)S(1)}) fusion(f32[32,64,128]{2,1,0:T(8,128)S(1)} %copy-done.1, f32[32,64,127]{2,1,0:T(8,128)} %get-tuple-element.60, f32[32,64,127]{2,1,0:T(8,128)S(1)} %copy-done.5, f32[34,64,128]{2,1,0:T(8,128)} %constant_dynamic-update-slice_fusion, f32[32,1,128]{2,1,0:T(1,128)S(1)} %bitcast.65, ...), kind=kLoop, calls=%fused_computation.111 | loop fusion | flops 8126464 | bytes 11763712 | tf_op jit(solution)/shard_map/mul | solution.py:184
  132.7 3.0 %collective-permute-start.9 = (f32[1,64,128]{2,1,0:T(8,128)S(1)}, f32[1,64,128]{2,1,0:T(8,128)S(1)}, u32[]{:S(2)}, u32[]{:S(2)}) collective-permute-start(f32[1,64,128]{2,1,0:T(8,128)S(1)} %get-tuple-element.45), channel_id=1, source_target_pairs={{0,16},{16,32},{32,48},{48,64},{64,80},{80,96},{96,112},{1,17},{17... | collective-permute-start | bytes 98312 | tf_op jit(solution)/shard_map/ppermute | solution.py:20
  137.0 4.5 %collective-permute-start.11 = (f32[32,128]{1,0:T(8,128)S(1)}, f32[32,128]{1,0:T(8,128)S(1)}, u32[]{:S(2)}, u32[]{:S(2)}) collective-permute-start(f32[32,128]{1,0:T(8,128)S(1)} %bitcast.76), channel_id=1, source_target_pairs={{0,1},{1,2},{2,3},{3,4},{4,5},{5,6},{6,7},{7,8},{8,9},{9,10},{10,1... | collective-permute-start | bytes 49160 | tf_op jit(solution)/shard_map/ppermute | solution.py:19
  145.1 3.0 %collective-permute-start.13 = (f32[1,64,128]{2,1,0:T(8,128)S(1)}, f32[1,64,128]{2,1,0:T(8,128)S(1)}, u32[]{:S(2)}, u32[]{:S(2)}) collective-permute-start(f32[1,64,128]{2,1,0:T(8,128)S(1)} %get-tuple-element.39), channel_id=1, source_target_pairs={{0,16},{16,32},{32,48},{48,64},{64,80},{80,96},{96,112},{1,17},{17... | collective-permute-start | bytes 98312 | tf_op jit(solution)/shard_map/ppermute | solution.py:20
  149.4 5.0 %collective-permute-start.15 = (f32[32,128]{1,0:T(8,128)S(1)}, f32[32,128]{1,0:T(8,128)S(1)}, u32[]{:S(2)}, u32[]{:S(2)}) collective-permute-start(f32[32,128]{1,0:T(8,128)S(1)} %bitcast.77), channel_id=1, source_target_pairs={{0,1},{1,2},{2,3},{3,4},{4,5},{5,6},{6,7},{7,8},{8,9},{9,10},{10,1... | collective-permute-start | bytes 49160 | tf_op jit(solution)/shard_map/ppermute | solution.py:19
  155.7 3.4 %multiply_reduce_fusion.3 = (f32[]{:T(128)}, f32[]{:T(128)}, f32[]{:T(128)}, f32[]{:T(128)}, f32[32,64,128]{2,1,0:T(8,128)}) fusion(f32[32,64,128]{2,1,0:T(8,128)S(1)} %get-tuple-element.34, f32[32,64,128]{2,1,0:T(8,128)S(1)} %copy-done.1, f32[32,64,128]{2,1,0:T(8,128)S(1)} %get-tuple-element.32, f32[32,64,128]{2,1,0:T(8,128)S(1)} %get-tuple-element.31, ...), kind=kLoop, calls=%fused_computation.66 | loop fusion | flops 8388604 | bytes 7421968 | tf_op jit(solution)/shard_map/reduce_sum | solution.py:191
  159.0 2.5 %pad_maximum_fusion.20 = f32[4]{0:T(128)S(1)} fusion(f32[1]{0:T(128)} %bitcast.27, f32[1]{0:T(128)} %bitcast.22, f32[1]{0:T(128)} %bitcast.21, f32[1]{0:T(128)} %bitcast.16), kind=kLoop, calls=%fused_computation.104 | loop fusion | flops 12 | bytes 32 | tf_op jit(solution)/shard_map/stack | solution.py:189
  161.6 9.1 %psum.28 = f32[4]{0:T(128)S(1)} all-reduce(f32[4]{0:T(128)S(1)} %pad_maximum_fusion.20), channel_id=1, replica_groups=mesh['gx_0'=4,'gx_1'=2,'gy_0'=4,'gy_1'=4] {'gx_0'}, use_global_device_ids=true, to_apply=%region_9.10 | all-reduce | flops 4 | bytes 32 | tf_op jit(solution)/shard_map/psum | solution.py:45
  170.7 2.5 %psum.29 = f32[4]{0:T(128)S(1)} all-reduce(f32[4]{0:T(128)S(1)} %psum.28), channel_id=1, replica_groups=mesh['gx_0'=4,'gx_1'=2,'gy_0'=4,'gy_1'=4] {'gx_1'}, use_global_device_ids=true, to_apply=%region_10.11 | all-reduce | flops 4 | bytes 32 | tf_op jit(solution)/shard_map/psum | solution.py:45
  173.2 19.2 %psum.30 = f32[4]{0:T(128)S(1)} all-reduce(f32[4]{0:T(128)S(1)} %psum.29), channel_id=1, replica_groups=mesh['gx_0'=4,'gx_1'=2,'gy_0'=4,'gy_1'=4] {'gy_0'}, use_global_device_ids=true, to_apply=%region_11.12 | all-reduce | flops 4 | bytes 32 | tf_op jit(solution)/shard_map/psum | solution.py:45
  192.3 7.7 %psum.31 = f32[4]{0:T(128)S(1)} all-reduce(f32[4]{0:T(128)S(1)} %psum.30), channel_id=1, replica_groups=mesh['gx_0'=4,'gx_1'=2,'gy_0'=4,'gy_1'=4] {'gy_1'}, use_global_device_ids=true, to_apply=%region_12.13 | all-reduce | flops 4 | bytes 32 | tf_op jit(solution)/shard_map/psum | solution.py:45
  205.8 3.5 %multiply_subtract_fusion = (f32[32,64,128]{2,1,0:T(8,128)}, f32[32,64,128]{2,1,0:T(8,128)}) fusion(f32[32,64,128]{2,1,0:T(8,128)} %copy-done.2, f32[32,64,128]{2,1,0:T(8,128)} %get-tuple-element.30, f32[32,64,128]{2,1,0:T(8,128)S(1)} %get-tuple-element.34, f32[]{:T(128)S(6)} %div.34, f32[]{:T(128)S(6)} %div.35, f32[]{:T(128)S(6)} %div.33, ...), kind=kLoop, calls=%fused_computation.60 | loop fusion | flops 4718592 | bytes 7340044 | tf_op jit(solution)/shard_map/sub | solution.py:211
  (77 shorter events, 33.3 us)
Async XLA Ops:
  12.3 11.7 %copy-start = (f32[32,64,128]{2,1,0:T(8,128)S(1)}, f32[32,64,128]{2,1,0:T(8,128)}, u32[]{:S(2)}) copy-start(f32[32,64,128]{2,1,0:T(8,128)} %param.13) | copy-start | bytes 3145732
  12.3 54.7 %all-to-all-start = ((bf16[128,6,1664]{2,1,0:T(8,128)(2,1)}), bf16[128,6,1664]{2,1,0:T(8,128)(2,1)}, u32[]{:S(2)}, u32[]{:S(2)}) async-start(bf16[128,6,1664]{2,1,0:T(8,128)(2,1)} %copy.32), calls=%async_computation | async-start | bytes 6815744 | tf_op jit(solution)/shard_map/all_to_all | solution.py:159
  24.0 10.2 %collective-permute-start.5 = (f32[1,64,128]{2,1,0:T(8,128)S(1)}, f32[1,64,128]{2,1,0:T(8,128)S(1)}, u32[]{:S(2)}, u32[]{:S(2)}) collective-permute-start(f32[1,64,128]{2,1,0:T(8,128)S(1)} %get-tuple-element.58), channel_id=1, source_target_pairs={{0,16},{16,32},{32,48},{48,64},{64,80},{80,96},{96,112},{1,17},{17... | collective-permute-start | bytes 98312 | tf_op jit(solution)/shard_map/ppermute | solution.py:20
  25.3 10.5 %collective-permute-start.4 = (f32[1,64,128]{2,1,0:T(8,128)S(1)}, f32[1,64,128]{2,1,0:T(8,128)S(1)}, u32[]{:S(2)}, u32[]{:S(2)}) collective-permute-start(f32[1,64,128]{2,1,0:T(8,128)S(1)} %get-tuple-element.57), channel_id=1, source_target_pairs={{16,0},{32,16},{48,32},{64,48},{80,64},{96,80},{112,96},{17,1},{33... | collective-permute-start | bytes 98312 | tf_op jit(solution)/shard_map/ppermute | solution.py:20
  26.6 94.9 %collective-permute-start.6 = (f32[32,128]{1,0:T(8,128)S(1)}, f32[32,128]{1,0:T(8,128)S(1)}, u32[]{:S(2)}, u32[]{:S(2)}) collective-permute-start(f32[32,128]{1,0:T(8,128)S(1)} %bitcast.74), channel_id=1, source_target_pairs={{1,0},{2,1},{3,2},{4,3},{5,4},{6,5},{7,6},{8,7},{9,8},{10,9},{11,1... | collective-permute-start | bytes 49160 | tf_op jit(solution)/shard_map/ppermute | solution.py:19
  27.9 97.1 %collective-permute-start.7 = (f32[32,128]{1,0:T(8,128)S(1)}, f32[32,128]{1,0:T(8,128)S(1)}, u32[]{:S(2)}, u32[]{:S(2)}) collective-permute-start(f32[32,128]{1,0:T(8,128)S(1)} %bitcast.73), channel_id=1, source_target_pairs={{0,1},{1,2},{2,3},{3,4},{4,5},{5,6},{6,7},{7,8},{8,9},{9,10},{10,1... | collective-permute-start | bytes 49160 | tf_op jit(solution)/shard_map/ppermute | solution.py:19
  100.4 27.1 %collective-permute-start = (f32[1,64,128]{2,1,0:T(8,128)S(1)}, f32[1,64,128]{2,1,0:T(8,128)S(1)}, u32[]{:S(2)}, u32[]{:S(2)}) collective-permute-start(f32[1,64,128]{2,1,0:T(8,128)S(1)} %get-tuple-element.49), channel_id=1, source_target_pairs={{16,0},{32,16},{48,32},{64,48},{80,64},{96,80},{112,96},{17,1},{33... | collective-permute-start | bytes 98312 | tf_op jit(solution)/shard_map/ppermute | solution.py:20
  101.7 25.8 %collective-permute-start.1 = (f32[1,64,128]{2,1,0:T(8,128)S(1)}, f32[1,64,128]{2,1,0:T(8,128)S(1)}, u32[]{:S(2)}, u32[]{:S(2)}) collective-permute-start(f32[1,64,128]{2,1,0:T(8,128)S(1)} %get-tuple-element.50), channel_id=1, source_target_pairs={{0,16},{16,32},{32,48},{48,64},{64,80},{80,96},{96,112},{1,17},{17... | collective-permute-start | bytes 98312 | tf_op jit(solution)/shard_map/ppermute | solution.py:20
  105.7 19.4 %collective-permute-start.3 = (f32[32,128]{1,0:T(8,128)S(1)}, f32[32,128]{1,0:T(8,128)S(1)}, u32[]{:S(2)}, u32[]{:S(2)}) collective-permute-start(f32[32,128]{1,0:T(8,128)S(1)} %bitcast.78), channel_id=1, source_target_pairs={{0,1},{1,2},{2,3},{3,4},{4,5},{5,6},{6,7},{7,8},{8,9},{9,10},{10,1... | collective-permute-start | bytes 49160 | tf_op jit(solution)/shard_map/ppermute | solution.py:19
  121.5 5.9 %copy-start.1 = (f32[32,64,128]{2,1,0:T(8,128)S(1)}, f32[32,64,128]{2,1,0:T(8,128)}, u32[]{:S(2)}) copy-start(f32[32,64,128]{2,1,0:T(8,128)} %param.12) | copy-start | bytes 3145732
  121.5 5.9 %copy-start.3 = (f32[32,64,128]{2,1,0:T(8,128)S(1)}, f32[32,64,128]{2,1,0:T(8,128)}, u32[]{:S(2)}) copy-start(f32[32,64,128]{2,1,0:T(8,128)} %shard_map.68) | copy-start | bytes 3145732
  121.5 5.9 %copy-start.4 = (f32[32,64,128]{2,1,0:T(8,128)S(1)}, f32[32,64,128]{2,1,0:T(8,128)}, u32[]{:S(2)}) copy-start(f32[32,64,128]{2,1,0:T(8,128)} %shard_map.69) | copy-start | bytes 3145732
  121.5 5.9 %copy-start.5 = (f32[32,64,127]{2,1,0:T(8,128)S(1)}, f32[32,64,127]{2,1,0:T(8,128)}, u32[]{:S(2)}) copy-start(f32[32,64,127]{2,1,0:T(8,128)} %get-tuple-element.59) | copy-start | bytes 3121156
  121.6 5.9 %collective-permute-start.2 = (f32[32,128]{1,0:T(8,128)S(1)}, f32[32,128]{1,0:T(8,128)S(1)}, u32[]{:S(2)}, u32[]{:S(2)}) collective-permute-start(f32[32,128]{1,0:T(8,128)S(1)} %bitcast.75), channel_id=1, source_target_pairs={{1,0},{2,1},{3,2},{4,3},{5,4},{6,5},{7,6},{8,7},{9,8},{10,9},{11,1... | collective-permute-start | bytes 49160 | tf_op jit(solution)/shard_map/ppermute | solution.py:19
  131.4 11.6 %collective-permute-start.8 = (f32[1,64,128]{2,1,0:T(8,128)S(1)}, f32[1,64,128]{2,1,0:T(8,128)S(1)}, u32[]{:S(2)}, u32[]{:S(2)}) collective-permute-start(f32[1,64,128]{2,1,0:T(8,128)S(1)} %get-tuple-element.46), channel_id=1, source_target_pairs={{16,0},{32,16},{48,32},{64,48},{80,64},{96,80},{112,96},{17,1},{33... | collective-permute-start | bytes 98312 | tf_op jit(solution)/shard_map/ppermute | solution.py:20
  132.7 10.3 %collective-permute-start.9 = (f32[1,64,128]{2,1,0:T(8,128)S(1)}, f32[1,64,128]{2,1,0:T(8,128)S(1)}, u32[]{:S(2)}, u32[]{:S(2)}) collective-permute-start(f32[1,64,128]{2,1,0:T(8,128)S(1)} %get-tuple-element.45), channel_id=1, source_target_pairs={{0,16},{16,32},{32,48},{48,64},{64,80},{80,96},{96,112},{1,17},{17... | collective-permute-start | bytes 98312 | tf_op jit(solution)/shard_map/ppermute | solution.py:20
  135.7 6.2 %collective-permute-start.10 = (f32[32,128]{1,0:T(8,128)S(1)}, f32[32,128]{1,0:T(8,128)S(1)}, u32[]{:S(2)}, u32[]{:S(2)}) collective-permute-start(f32[32,128]{1,0:T(8,128)S(1)} %bitcast.79), channel_id=1, source_target_pairs={{1,0},{2,1},{3,2},{4,3},{5,4},{6,5},{7,6},{8,7},{9,8},{10,9},{11,1... | collective-permute-start | bytes 49160 | tf_op jit(solution)/shard_map/ppermute | solution.py:19
  137.0 6.0 %collective-permute-start.11 = (f32[32,128]{1,0:T(8,128)S(1)}, f32[32,128]{1,0:T(8,128)S(1)}, u32[]{:S(2)}, u32[]{:S(2)}) collective-permute-start(f32[32,128]{1,0:T(8,128)S(1)} %bitcast.76), channel_id=1, source_target_pairs={{0,1},{1,2},{2,3},{3,4},{4,5},{5,6},{6,7},{7,8},{8,9},{9,10},{10,1... | collective-permute-start | bytes 49160 | tf_op jit(solution)/shard_map/ppermute | solution.py:19
  143.7 12.0 %copy-start.2 = (f32[32,64,128]{2,1,0:T(8,128)}, f32[32,64,128]{2,1,0:T(8,128)S(1)}, u32[]{:S(2)}) copy-start(f32[32,64,128]{2,1,0:T(8,128)S(1)} %get-tuple-element.32) | copy-start | bytes 3145732
  143.8 11.9 %collective-permute-start.12 = (f32[1,64,128]{2,1,0:T(8,128)S(1)}, f32[1,64,128]{2,1,0:T(8,128)S(1)}, u32[]{:S(2)}, u32[]{:S(2)}) collective-permute-start(f32[1,64,128]{2,1,0:T(8,128)S(1)} %get-tuple-element.40), channel_id=1, source_target_pairs={{16,0},{32,16},{48,32},{64,48},{80,64},{96,80},{112,96},{17,1},{33... | collective-permute-start | bytes 98312 | tf_op jit(solution)/shard_map/ppermute | solution.py:20
  145.1 10.6 %collective-permute-start.13 = (f32[1,64,128]{2,1,0:T(8,128)S(1)}, f32[1,64,128]{2,1,0:T(8,128)S(1)}, u32[]{:S(2)}, u32[]{:S(2)}) collective-permute-start(f32[1,64,128]{2,1,0:T(8,128)S(1)} %get-tuple-element.39), channel_id=1, source_target_pairs={{0,16},{16,32},{32,48},{48,64},{64,80},{80,96},{96,112},{1,17},{17... | collective-permute-start | bytes 98312 | tf_op jit(solution)/shard_map/ppermute | solution.py:20
  148.1 6.7 %collective-permute-start.14 = (f32[32,128]{1,0:T(8,128)S(1)}, f32[32,128]{1,0:T(8,128)S(1)}, u32[]{:S(2)}, u32[]{:S(2)}) collective-permute-start(f32[32,128]{1,0:T(8,128)S(1)} %bitcast.80), channel_id=1, source_target_pairs={{1,0},{2,1},{3,2},{4,3},{5,4},{6,5},{7,6},{8,7},{9,8},{10,9},{11,1... | collective-permute-start | bytes 49160 | tf_op jit(solution)/shard_map/ppermute | solution.py:19
  149.4 6.3 %collective-permute-start.15 = (f32[32,128]{1,0:T(8,128)S(1)}, f32[32,128]{1,0:T(8,128)S(1)}, u32[]{:S(2)}, u32[]{:S(2)}) collective-permute-start(f32[32,128]{1,0:T(8,128)S(1)} %bitcast.77), channel_id=1, source_target_pairs={{0,1},{1,2},{2,3},{3,4},{4,5},{5,6},{6,7},{7,8},{8,9},{9,10},{10,1... | collective-permute-start | bytes 49160 | tf_op jit(solution)/shard_map/ppermute | solution.py:19

commit v13 on v10

--- a/solution.py
+++ b/solution.py
@@ -119,33 +119,28 @@
             x = jnp.where(first, a, jnp.where(second, b, x))
         return x
 
-    def step(i, carry):
-        ly = i % 8
-        lx = i // 8
-        row = pl.multiple_of(i * 16, 16)
-        y = pl.multiple_of(ly * 8, 8)
-        top = blk_ref[pl.ds(row, 8), :]
-        bottom = blk_ref[pl.ds(row + 8, 8), :]
-        for c in range(3):
-            for uh in range(4):
-                col = (c * 4 + uh) * 128
-                s0 = top[:, col:col + 128]
-                s1 = bottom[:, col:col + 128]
-                u0 = jnp.where(low_half, s0, pltpu.roll(s1, 64, 1))
-                u1 = jnp.where(low_half, pltpu.roll(s0, 64, 1), s1)
-                out_ref[c, lx * 8 + uh * 2, pl.ds(y, 8), :] = transpose_groups(u0)
-                out_ref[c, lx * 8 + uh * 2 + 1, pl.ds(y, 8), :] = transpose_groups(u1)
-        return carry
-
-    lax.fori_loop(0, 32, step, 0)
+    top = blk_ref[0:8, :]
+    bottom = blk_ref[8:16, :]
+    for c in range(3):
+        for uh in range(4):
+            col = (c * 4 + uh) * 128
+            s0 = top[:, col:col + 128]
+            s1 = bottom[:, col:col + 128]
+            u0 = jnp.where(low_half, s0, pltpu.roll(s1, 64, 1))
+            u1 = jnp.where(low_half, pltpu.roll(s0, 64, 1), s1)
+            out_ref[c, uh * 2] = transpose_groups(u0)
+            out_ref[c, uh * 2 + 1] = transpose_groups(u1)
 
 
 def to_grid(blocks, span_x, span_y, depth):
+    cells = 3 * span_x * span_y * 64 * depth
     return pl.pallas_call(
         relayout_kernel,
         out_shape=jax.ShapeDtypeStruct((3, span_x * 8, span_y * 8, depth), jnp.float32),
-        in_specs=[pl.BlockSpec(memory_space=pltpu.VMEM)],
-        out_specs=pl.BlockSpec(memory_space=pltpu.VMEM),
+        grid=(span_x, span_y),
+        in_specs=[pl.BlockSpec((16, blocks.shape[1]), lambda i, j: (i * span_y + j, 0))],
+        out_specs=pl.BlockSpec((3, 8, 8, depth), lambda i, j: (0, i, j, 0)),
+        cost_estimate=pl.CostEstimate(flops=20 * cells, bytes_accessed=8 * cells, transcendentals=0),
     )(blocks)
 
 

time: 186 us -> 194 us (1.043)
  Pallas kernels: 14.7 us -> 22.3 us
    pallas_call x1, Pallas kernels: 14.7 us -> 22.3 us  [to_grid(): pl.pallas_call(relayout_kernel, out_shape=jax.ShapeDtypeStruct((3, span_x...]
  transfers between devices with their start and end apart: 17 -> 17, of which waited for: 5 -> 5; matrix products, arithmetic and copies ran while one was open for 7% -> 7% of each run, Pallas kernels for 8% -> 12%
where the time goes in v13:
time: 194 us; the launch traced here: 192 us
  starting transfers between devices  48.2 us (25%)
  blocking collectives  38.1 us (20%)
  waiting for transfers between devices  37.7 us (19%)
  Pallas kernels  22.3 us (11%)
  other arithmetic  18.6 us (10%)
  local copies, waits for them, and re-layouts  15.6 us (8%)
  between operations  6.09 us (3%)
  matrix products  5.6 us (3%)
    psum x4, blocking collectives, over_axes(): shard = lax.psum(shard, axis)  38.1 us
    all_to_all x1, waiting for transfers between devices, body(): lax.all_to_all(payload, GX_GY, split_axis=0, concat_axis=0, tiled=True)  32.3 us
    pallas_call x1, Pallas kernels, to_grid(): pl.pallas_call(relayout_kernel, out_shape=jax.ShapeDtypeStruct((3, span_x...  22.3 us
    ppermute x8, starting transfers between devices, shifted(): return lax.ppermute(flat, axis, pairs).reshape(piece.shape)  20.8 us
    ppermute x8, starting transfers between devices, shifted(): return lax.ppermute(piece, axis, pairs)  15.7 us
    all_to_all x1, starting transfers between devices, body(): lax.all_to_all(payload, GX_GY, split_axis=0, concat_axis=0, tiled=True)  11.6 us
    ppermute x8, waiting for transfers between devices, shifted(): return lax.ppermute(piece, axis, pairs)  4.54 us
  transfers between devices with their start and end apart: 17, of which 5 were waited for; matrix products, arithmetic and copies ran while one was open for 7% of the time, Pallas kernels for 12%

profile of v13, /device:TPU:0, one launch (start us, length us, event | category | flops | bytes accessed | tf_op | source)
XLA Modules:
  0.0 192.1 jit_solution(10850581505075555378)
XLA Ops:
  1.9 2.0 %broadcast_select_fusion = (bf16[256]{0:T(256)(128)(2,1)S(1)}, bf16[256]{0:T(256)(128)(2,1)S(1)}) fusion(pred[]{:T(512)} %compare_reduce_fusion, s32[256]{0:T(256)} %param.11, pred[]{:T(512)} %compare_reduce_fusion.1), kind=kLoop, calls=%fused_computation.106 | loop fusion | flops 5888 | bytes 2050 | tf_op jit(solution)/shard_map/select.12
  7.0 2.1 %convolution_convert_fusion = bf16[128,6,1664]{2,0,1:T(8,128)(2,1)S(1)} fusion(bf16[256,128]{1,0:T(8,128)(2,1)S(1)} %scatter.9, bf16[256,1536]{1,0:T(8,128)(2,1)} %param.9, s32[128,6]{0,1:T(8,128)S(1)} %iota_add_fusion, s32[256]{0:T(256)S(1)} %multiply_add_fusion.1), kind=kOutput, calls=%fused_computation | convolution fusion | flops 657489920 | bytes 3411968 | tf_op jit(solution)/shard_map/pck,kj->pcj/dot_general | solution.py:74
  9.1 3.2 %copy.32 = bf16[128,6,1664]{2,1,0:T(8,128)(2,1)} copy(bf16[128,6,1664]{2,0,1:T(8,128)(2,1)S(1)} %convolution_convert_fusion) | data formatting | bytes 5111808 | tf_op jit(solution)/shard_map/convert_element_type | solution.py:77
  12.3 11.6 %all-to-all-start = ((bf16[128,6,1664]{2,1,0:T(8,128)(2,1)}), bf16[128,6,1664]{2,1,0:T(8,128)(2,1)}, u32[]{:S(2)}, u32[]{:S(2)}) async-start(bf16[128,6,1664]{2,1,0:T(8,128)(2,1)} %copy.32), calls=%async_computation | async-start | bytes 6815744 | tf_op jit(solution)/shard_map/all_to_all | solution.py:151
  25.3 3.7 %collective-permute-start.7 = (f32[32,128]{1,0:T(8,128)S(1)}, f32[32,128]{1,0:T(8,128)S(1)}, u32[]{:S(2)}, u32[]{:S(2)}) collective-permute-start(f32[32,128]{1,0:T(8,128)S(1)} %bitcast.84), channel_id=1, source_target_pairs={{0,1},{1,2},{2,3},{3,4},{4,5},{5,6},{6,7},{7,8},{8,9},{9,10},{10,1... | collective-permute-start | bytes 49160 | tf_op jit(solution)/shard_map/ppermute | solution.py:17
  34.7 32.3 %all-to-all-done = bf16[128,6,1664]{2,1,0:T(8,128)(2,1)} async-done(((bf16[128,6,1664]{2,1,0:T(8,128)(2,1)}), bf16[128,6,1664]{2,1,0:T(8,128)(2,1)}, u32[]{:S(2)}, u32[]{:S(2)}) %all-to-all-start) | async-done | bytes 2555936 | tf_op jit(solution)/shard_map/all_to_all | solution.py:151
  68.3 2.1 %slice.271 = bf16[128,6,1536]{2,1,0:T(8,128)(2,1)S(1)} slice(bf16[128,6,1664]{2,1,0:T(8,128)(2,1)} %all-to-all-done), slice={[0:128], [0:6], [0:1536]} | slice | bytes 4718592 | tf_op jit(solution)/shard_map/slice | solution.py:162
  70.3 3.5 %convolution_bitcast_fusion.blk_ref = f32[512,1536]{1,0:T(8,128)} fusion(bf16[128,6,1536]{2,1,0:T(8,128)(2,1)S(1)} %slice.271, s32[128,6]{0,1:T(8,128)S(1)} %fusion.40), kind=kOutput, calls=%fused_computation.1 | convolution fusion | flops 1208352768 | bytes 5508096 | tf_op jit(solution)/shard_map/pcs,pcj->sj/dot_general | solution.py:159
  73.9 22.3 %shard_map.68 = f32[3,32,64,128]{3,2,1,0:T(8,128)} custom-call(f32[512,1536]{1,0:T(8,128)} %convolution_bitcast_fusion.blk_ref), custom_call_target="tpu_custom_call" | custom-call | flops 15728640 | bytes 6291456 | tf_op jit(solution)/shard_map/pallas_call | solution.py:137
  96.2 2.1 %slice_bitcast_fusion.2 = (f32[32,64,128]{2,1,0:T(8,128)S(1)}, f32[32,64,128]{2,1,0:T(8,128)S(1)}, f32[32,64,128]{2,1,0:T(8,128)S(1)}) fusion(f32[3,32,64,128]{3,2,1,0:T(8,128)} %shard_map.68), kind=kLoop, calls=%fused_computation.62 | loop fusion | bytes 6291456 | tf_op jit(solution)/shard_map/squeeze | solution.py:166
  99.1 2.9 %collective-permute-start.3 = (f32[32,128]{1,0:T(8,128)S(1)}, f32[32,128]{1,0:T(8,128)S(1)}, u32[]{:S(2)}, u32[]{:S(2)}) collective-permute-start(f32[32,128]{1,0:T(8,128)S(1)} %bitcast.86), channel_id=1, source_target_pairs={{0,1},{1,2},{2,3},{3,4},{4,5},{5,6},{6,7},{7,8},{8,9},{9,10},{10,1... | collective-permute-start | bytes 49160 | tf_op jit(solution)/shard_map/ppermute | solution.py:17
  104.6 3.0 %collective-permute-start.1 = (f32[1,64,128]{2,1,0:T(8,128)S(1)}, f32[1,64,128]{2,1,0:T(8,128)S(1)}, u32[]{:S(2)}, u32[]{:S(2)}) collective-permute-start(f32[1,64,128]{2,1,0:T(8,128)S(1)} %get-tuple-element.36), channel_id=1, source_target_pairs={{0,16},{16,32},{32,48},{48,64},{64,80},{80,96},{96,112},{1,17},{17... | collective-permute-start | bytes 98312 | tf_op jit(solution)/shard_map/ppermute | solution.py:18
  108.8 3.6 %fusion.45 = (f32[32,64,128]{2,1,0:T(8,128)S(1)}, f32[32,64,128]{2,1,0:T(8,128)S(1)}) fusion(f32[32,64,128]{2,1,0:T(8,128)S(1)} %copy-done.1, f32[32,64,127]{2,1,0:T(8,128)S(1)} %get-tuple-element.70, f32[32,64,127]{2,1,0:T(8,128)S(1)} %get-tuple-element.71, f32[34,64,128]{2,1,0:T(8,128)} %constant_dynamic-update-slice_fusion, ...), kind=kLoop, calls=%fused_computation.116 | loop fusion | flops 8126464 | bytes 11763712 | tf_op jit(solution)/shard_map/mul | solution.py:175
  112.5 4.5 %collective-permute-start.11 = (f32[32,128]{1,0:T(8,128)S(1)}, f32[32,128]{1,0:T(8,128)S(1)}, u32[]{:S(2)}, u32[]{:S(2)}) collective-permute-start(f32[32,128]{1,0:T(8,128)S(1)} %bitcast.89), channel_id=1, source_target_pairs={{0,1},{1,2},{2,3},{3,4},{4,5},{5,6},{6,7},{7,8},{8,9},{9,10},{10,1... | collective-permute-start | bytes 49160 | tf_op jit(solution)/shard_map/ppermute | solution.py:17
  122.7 2.4 %collective-permute-done.8 = f32[1,64,128]{2,1,0:T(8,128)S(1)} collective-permute-done((f32[1,64,128]{2,1,0:T(8,128)S(1)}, f32[1,64,128]{2,1,0:T(8,128)S(1)}, u32[]{:S(2)}, u32[]{:S(2)}) %collective-permute-start.8) | collective-permute-done | bytes 32800 | tf_op jit(solution)/shard_map/ppermute | solution.py:18
  125.9 4.5 %collective-permute-start.15 = (f32[32,128]{1,0:T(8,128)S(1)}, f32[32,128]{1,0:T(8,128)S(1)}, u32[]{:S(2)}, u32[]{:S(2)}) collective-permute-start(f32[32,128]{1,0:T(8,128)S(1)} %bitcast.90), channel_id=1, source_target_pairs={{0,1},{1,2},{2,3},{3,4},{4,5},{5,6},{6,7},{7,8},{8,9},{9,10},{10,1... | collective-permute-start | bytes 49160 | tf_op jit(solution)/shard_map/ppermute | solution.py:17
  131.7 4.3 %collective-permute-start.13 = (f32[1,64,128]{2,1,0:T(8,128)S(1)}, f32[1,64,128]{2,1,0:T(8,128)S(1)}, u32[]{:S(2)}, u32[]{:S(2)}) collective-permute-start(f32[1,64,128]{2,1,0:T(8,128)S(1)} %get-tuple-element.44), channel_id=1, source_target_pairs={{0,16},{16,32},{32,48},{48,64},{64,80},{80,96},{96,112},{1,17},{17... | collective-permute-start | bytes 98312 | tf_op jit(solution)/shard_map/ppermute | solution.py:18
  139.1 3.3 %multiply_reduce_fusion.3 = (f32[]{:T(128)}, f32[]{:T(128)}, f32[]{:T(128)}, f32[]{:T(128)}, f32[32,64,128]{2,1,0:T(8,128)}) fusion(f32[32,64,128]{2,1,0:T(8,128)S(1)} %get-tuple-element.34, f32[32,64,128]{2,1,0:T(8,128)S(1)} %copy-done.1, f32[32,64,128]{2,1,0:T(8,128)S(1)} %get-tuple-element.32, f32[32,64,128]{2,1,0:T(8,128)S(1)} %get-tuple-element.31, ...), kind=kLoop, calls=%fused_computation.69 | loop fusion | flops 8388604 | bytes 7421968 | tf_op jit(solution)/shard_map/reduce_sum | solution.py:182
  142.4 2.5 %pad_maximum_fusion.20 = f32[4]{0:T(128)S(1)} fusion(f32[1]{0:T(128)} %bitcast.33, f32[1]{0:T(128)} %bitcast.28, f32[1]{0:T(128)} %bitcast.27, f32[1]{0:T(128)} %bitcast.22), kind=kLoop, calls=%fused_computation.109 | loop fusion | flops 12 | bytes 32 | tf_op jit(solution)/shard_map/stack | solution.py:180
  144.9 10.9 %psum.28 = f32[4]{0:T(128)S(1)} all-reduce(f32[4]{0:T(128)S(1)} %pad_maximum_fusion.20), channel_id=1, replica_groups=mesh['gx_0'=4,'gx_1'=2,'gy_0'=4,'gy_1'=4] {'gx_0'}, use_global_device_ids=true, to_apply=%region_9.10 | all-reduce | flops 4 | bytes 32 | tf_op jit(solution)/shard_map/psum | solution.py:43
  155.8 2.5 %psum.29 = f32[4]{0:T(128)S(1)} all-reduce(f32[4]{0:T(128)S(1)} %psum.28), channel_id=1, replica_groups=mesh['gx_0'=4,'gx_1'=2,'gy_0'=4,'gy_1'=4] {'gx_1'}, use_global_device_ids=true, to_apply=%region_10.11 | all-reduce | flops 4 | bytes 32 | tf_op jit(solution)/shard_map/psum | solution.py:43
  158.2 17.0 %psum.30 = f32[4]{0:T(128)S(1)} all-reduce(f32[4]{0:T(128)S(1)} %psum.29), channel_id=1, replica_groups=mesh['gx_0'=4,'gx_1'=2,'gy_0'=4,'gy_1'=4] {'gy_0'}, use_global_device_ids=true, to_apply=%region_11.12 | all-reduce | flops 4 | bytes 32 | tf_op jit(solution)/shard_map/psum | solution.py:43
  175.2 7.7 %psum.31 = f32[4]{0:T(128)S(1)} all-reduce(f32[4]{0:T(128)S(1)} %psum.30), channel_id=1, replica_groups=mesh['gx_0'=4,'gx_1'=2,'gy_0'=4,'gy_1'=4] {'gy_1'}, use_global_device_ids=true, to_apply=%region_12.13 | all-reduce | flops 4 | bytes 32 | tf_op jit(solution)/shard_map/psum | solution.py:43
  188.6 3.5 %multiply_subtract_fusion = (f32[32,64,128]{2,1,0:T(8,128)}, f32[32,64,128]{2,1,0:T(8,128)}) fusion(f32[32,64,128]{2,1,0:T(8,128)} %copy-done.2, f32[32,64,128]{2,1,0:T(8,128)} %get-tuple-element.30, f32[32,64,128]{2,1,0:T(8,128)S(1)} %get-tuple-element.34, f32[]{:T(128)S(6)} %div.34, f32[]{:T(128)S(6)} %div.35, f32[]{:T(128)S(6)} %div.33, ...), kind=kLoop, calls=%fused_computation.63 | loop fusion | flops 4718592 | bytes 7340044 | tf_op jit(solution)/shard_map/sub | solution.py:202
  (69 shorter events, 28.6 us)
Async XLA Ops:
  12.3 11.7 %copy-start = (f32[32,64,128]{2,1,0:T(8,128)S(1)}, f32[32,64,128]{2,1,0:T(8,128)}, u32[]{:S(2)}) copy-start(f32[32,64,128]{2,1,0:T(8,128)} %param.13) | copy-start | bytes 3145732
  12.3 54.7 %all-to-all-start = ((bf16[128,6,1664]{2,1,0:T(8,128)(2,1)}), bf16[128,6,1664]{2,1,0:T(8,128)(2,1)}, u32[]{:S(2)}, u32[]{:S(2)}) async-start(bf16[128,6,1664]{2,1,0:T(8,128)(2,1)} %copy.32), calls=%async_computation | async-start | bytes 6815744 | tf_op jit(solution)/shard_map/all_to_all | solution.py:151
  24.0 7.6 %collective-permute-start.5 = (f32[1,64,128]{2,1,0:T(8,128)S(1)}, f32[1,64,128]{2,1,0:T(8,128)S(1)}, u32[]{:S(2)}, u32[]{:S(2)}) collective-permute-start(f32[1,64,128]{2,1,0:T(8,128)S(1)} %get-tuple-element.61), channel_id=1, source_target_pairs={{0,16},{16,32},{32,48},{48,64},{64,80},{80,96},{96,112},{1,17},{17... | collective-permute-start | bytes 98312 | tf_op jit(solution)/shard_map/ppermute | solution.py:18
  25.3 79.2 %collective-permute-start.7 = (f32[32,128]{1,0:T(8,128)S(1)}, f32[32,128]{1,0:T(8,128)S(1)}, u32[]{:S(2)}, u32[]{:S(2)}) collective-permute-start(f32[32,128]{1,0:T(8,128)S(1)} %bitcast.84), channel_id=1, source_target_pairs={{0,1},{1,2},{2,3},{3,4},{4,5},{5,6},{6,7},{7,8},{8,9},{9,10},{10,1... | collective-permute-start | bytes 49160 | tf_op jit(solution)/shard_map/ppermute | solution.py:17
  29.0 79.4 %collective-permute-start.6 = (f32[32,128]{1,0:T(8,128)S(1)}, f32[32,128]{1,0:T(8,128)S(1)}, u32[]{:S(2)}, u32[]{:S(2)}) collective-permute-start(f32[32,128]{1,0:T(8,128)S(1)} %bitcast.83), channel_id=1, source_target_pairs={{1,0},{2,1},{3,2},{4,3},{5,4},{6,5},{7,6},{8,7},{9,8},{10,9},{11,1... | collective-permute-start | bytes 49160 | tf_op jit(solution)/shard_map/ppermute | solution.py:17
  30.3 3.8 %collective-permute-start.4 = (f32[1,64,128]{2,1,0:T(8,128)S(1)}, f32[1,64,128]{2,1,0:T(8,128)S(1)}, u32[]{:S(2)}, u32[]{:S(2)}) collective-permute-start(f32[1,64,128]{2,1,0:T(8,128)S(1)} %get-tuple-element.60), channel_id=1, source_target_pairs={{16,0},{32,16},{48,32},{64,48},{80,64},{96,80},{112,96},{17,1},{33... | collective-permute-start | bytes 98312 | tf_op jit(solution)/shard_map/ppermute | solution.py:18
  99.1 9.4 %collective-permute-start.3 = (f32[32,128]{1,0:T(8,128)S(1)}, f32[32,128]{1,0:T(8,128)S(1)}, u32[]{:S(2)}, u32[]{:S(2)}) collective-permute-start(f32[32,128]{1,0:T(8,128)S(1)} %bitcast.86), channel_id=1, source_target_pairs={{0,1},{1,2},{2,3},{3,4},{4,5},{5,6},{6,7},{7,8},{8,9},{9,10},{10,1... | collective-permute-start | bytes 49160 | tf_op jit(solution)/shard_map/ppermute | solution.py:17
  102.0 6.5 %collective-permute-start.2 = (f32[32,128]{1,0:T(8,128)S(1)}, f32[32,128]{1,0:T(8,128)S(1)}, u32[]{:S(2)}, u32[]{:S(2)}) collective-permute-start(f32[32,128]{1,0:T(8,128)S(1)} %bitcast.85), channel_id=1, source_target_pairs={{1,0},{2,1},{3,2},{4,3},{5,4},{6,5},{7,6},{8,7},{9,8},{10,9},{11,1... | collective-permute-start | bytes 49160 | tf_op jit(solution)/shard_map/ppermute | solution.py:17
  103.3 5.2 %collective-permute-start = (f32[1,64,128]{2,1,0:T(8,128)S(1)}, f32[1,64,128]{2,1,0:T(8,128)S(1)}, u32[]{:S(2)}, u32[]{:S(2)}) collective-permute-start(f32[1,64,128]{2,1,0:T(8,128)S(1)} %get-tuple-element.35), channel_id=1, source_target_pairs={{16,0},{32,16},{48,32},{64,48},{80,64},{96,80},{112,96},{17,1},{33... | collective-permute-start | bytes 98312 | tf_op jit(solution)/shard_map/ppermute | solution.py:18
  104.6 3.9 %collective-permute-start.1 = (f32[1,64,128]{2,1,0:T(8,128)S(1)}, f32[1,64,128]{2,1,0:T(8,128)S(1)}, u32[]{:S(2)}, u32[]{:S(2)}) collective-permute-start(f32[1,64,128]{2,1,0:T(8,128)S(1)} %get-tuple-element.36), channel_id=1, source_target_pairs={{0,16},{16,32},{32,48},{48,64},{64,80},{80,96},{96,112},{1,17},{17... | collective-permute-start | bytes 98312 | tf_op jit(solution)/shard_map/ppermute | solution.py:18
  107.6 1.2 copy-start.1
  112.5 9.3 %collective-permute-start.11 = (f32[32,128]{1,0:T(8,128)S(1)}, f32[32,128]{1,0:T(8,128)S(1)}, u32[]{:S(2)}, u32[]{:S(2)}) collective-permute-start(f32[32,128]{1,0:T(8,128)S(1)} %bitcast.89), channel_id=1, source_target_pairs={{0,1},{1,2},{2,3},{3,4},{4,5},{5,6},{6,7},{7,8},{8,9},{9,10},{10,1... | collective-permute-start | bytes 49160 | tf_op jit(solution)/shard_map/ppermute | solution.py:17
  117.0 5.6 %collective-permute-start.10 = (f32[32,128]{1,0:T(8,128)S(1)}, f32[32,128]{1,0:T(8,128)S(1)}, u32[]{:S(2)}, u32[]{:S(2)}) collective-permute-start(f32[32,128]{1,0:T(8,128)S(1)} %bitcast.87), channel_id=1, source_target_pairs={{1,0},{2,1},{3,2},{4,3},{5,4},{6,5},{7,6},{8,7},{9,8},{10,9},{11,1... | collective-permute-start | bytes 49160 | tf_op jit(solution)/shard_map/ppermute | solution.py:17
  118.3 4.3 %collective-permute-start.9 = (f32[1,64,128]{2,1,0:T(8,128)S(1)}, f32[1,64,128]{2,1,0:T(8,128)S(1)}, u32[]{:S(2)}, u32[]{:S(2)}) collective-permute-start(f32[1,64,128]{2,1,0:T(8,128)S(1)} %get-tuple-element.50), channel_id=1, source_target_pairs={{0,16},{16,32},{32,48},{48,64},{64,80},{80,96},{96,112},{1,17},{17... | collective-permute-start | bytes 98312 | tf_op jit(solution)/shard_map/ppermute | solution.py:18
  120.1 5.0 %collective-permute-start.8 = (f32[1,64,128]{2,1,0:T(8,128)S(1)}, f32[1,64,128]{2,1,0:T(8,128)S(1)}, u32[]{:S(2)}, u32[]{:S(2)}) collective-permute-start(f32[1,64,128]{2,1,0:T(8,128)S(1)} %get-tuple-element.51), channel_id=1, source_target_pairs={{16,0},{32,16},{48,32},{64,48},{80,64},{96,80},{112,96},{17,1},{33... | collective-permute-start | bytes 98312 | tf_op jit(solution)/shard_map/ppermute | solution.py:18
  125.8 16.6 %copy-start.2 = (f32[32,64,128]{2,1,0:T(8,128)}, f32[32,64,128]{2,1,0:T(8,128)S(1)}, u32[]{:S(2)}) copy-start(f32[32,64,128]{2,1,0:T(8,128)S(1)} %get-tuple-element.32) | copy-start | bytes 3145732
  125.9 12.0 %collective-permute-start.15 = (f32[32,128]{1,0:T(8,128)S(1)}, f32[32,128]{1,0:T(8,128)S(1)}, u32[]{:S(2)}, u32[]{:S(2)}) collective-permute-start(f32[32,128]{1,0:T(8,128)S(1)} %bitcast.90), channel_id=1, source_target_pairs={{0,1},{1,2},{2,3},{3,4},{4,5},{5,6},{6,7},{7,8},{8,9},{9,10},{10,1... | collective-permute-start | bytes 49160 | tf_op jit(solution)/shard_map/ppermute | solution.py:17
  130.4 7.4 %collective-permute-start.14 = (f32[32,128]{1,0:T(8,128)S(1)}, f32[32,128]{1,0:T(8,128)S(1)}, u32[]{:S(2)}, u32[]{:S(2)}) collective-permute-start(f32[32,128]{1,0:T(8,128)S(1)} %bitcast.88), channel_id=1, source_target_pairs={{1,0},{2,1},{3,2},{4,3},{5,4},{6,5},{7,6},{8,7},{9,8},{10,9},{11,1... | collective-permute-start | bytes 49160 | tf_op jit(solution)/shard_map/ppermute | solution.py:17
  131.7 6.1 %collective-permute-start.13 = (f32[1,64,128]{2,1,0:T(8,128)S(1)}, f32[1,64,128]{2,1,0:T(8,128)S(1)}, u32[]{:S(2)}, u32[]{:S(2)}) collective-permute-start(f32[1,64,128]{2,1,0:T(8,128)S(1)} %get-tuple-element.44), channel_id=1, source_target_pairs={{0,16},{16,32},{32,48},{48,64},{64,80},{80,96},{96,112},{1,17},{17... | collective-permute-start | bytes 98312 | tf_op jit(solution)/shard_map/ppermute | solution.py:18
  136.0 3.1 %collective-permute-start.12 = (f32[1,64,128]{2,1,0:T(8,128)S(1)}, f32[1,64,128]{2,1,0:T(8,128)S(1)}, u32[]{:S(2)}, u32[]{:S(2)}) collective-permute-start(f32[1,64,128]{2,1,0:T(8,128)S(1)} %get-tuple-element.45), channel_id=1, source_target_pairs={{16,0},{32,16},{48,32},{64,48},{80,64},{96,80},{112,96},{17,1},{33... | collective-permute-start | bytes 98312 | tf_op jit(solution)/shard_map/ppermute | solution.py:18

commit v14 on v10

--- a/solution.py
+++ b/solution.py
@@ -119,10 +119,8 @@
             x = jnp.where(first, a, jnp.where(second, b, x))
         return x
 
-    def step(i, carry):
-        ly = i % 8
-        lx = i // 8
-        row = pl.multiple_of(i * 16, 16)
+    def step(ly, carry):
+        row = pl.multiple_of(ly * 16, 16)
         y = pl.multiple_of(ly * 8, 8)
         top = blk_ref[pl.ds(row, 8), :]
         bottom = blk_ref[pl.ds(row + 8, 8), :]
@@ -133,19 +131,22 @@
                 s1 = bottom[:, col:col + 128]
                 u0 = jnp.where(low_half, s0, pltpu.roll(s1, 64, 1))
                 u1 = jnp.where(low_half, pltpu.roll(s0, 64, 1), s1)
-                out_ref[c, lx * 8 + uh * 2, pl.ds(y, 8), :] = transpose_groups(u0)
-                out_ref[c, lx * 8 + uh * 2 + 1, pl.ds(y, 8), :] = transpose_groups(u1)
+                out_ref[c, uh * 2, pl.ds(y, 8), :] = transpose_groups(u0)
+                out_ref[c, uh * 2 + 1, pl.ds(y, 8), :] = transpose_groups(u1)
         return carry
 
-    lax.fori_loop(0, 32, step, 0)
+    lax.fori_loop(0, 8, step, 0)
 
 
 def to_grid(blocks, span_x, span_y, depth):
+    cells = 3 * span_x * span_y * 64 * depth
     return pl.pallas_call(
         relayout_kernel,
         out_shape=jax.ShapeDtypeStruct((3, span_x * 8, span_y * 8, depth), jnp.float32),
-        in_specs=[pl.BlockSpec(memory_space=pltpu.VMEM)],
-        out_specs=pl.BlockSpec(memory_space=pltpu.VMEM),
+        grid=(span_x,),
+        in_specs=[pl.BlockSpec((span_y * 16, blocks.shape[1]), lambda i: (i, 0))],
+        out_specs=pl.BlockSpec((3, 8, span_y * 8, depth), lambda i: (0, i, 0, 0)),
+        cost_estimate=pl.CostEstimate(flops=20 * cells, bytes_accessed=8 * cells, transcendentals=0),
     )(blocks)
 
 

time: 186 us -> 184 us (0.989)
  transfers between devices with their start and end apart: 17 -> 17, of which waited for: 5 -> 5; matrix products, arithmetic and copies ran while one was open for 7% -> 7% of each run, Pallas kernels for 8% -> 7%
where the time goes in v14:
time: 184 us; the launch traced here: 183 us
  starting transfers between devices  48.2 us (26%)
  blocking collectives  38.1 us (21%)
  waiting for transfers between devices  37.7 us (20%)
  other arithmetic  18.6 us (10%)
  local copies, waits for them, and re-layouts  15.6 us (8%)
  Pallas kernels  13.3 us (7%)
  between operations  6.09 us (3%)
  matrix products  5.6 us (3%)
    psum x4, blocking collectives, over_axes(): shard = lax.psum(shard, axis)  38.1 us
    all_to_all x1, waiting for transfers between devices, body(): lax.all_to_all(payload, GX_GY, split_axis=0, concat_axis=0, tiled=True)  32.3 us
    ppermute x8, starting transfers between devices, shifted(): return lax.ppermute(flat, axis, pairs).reshape(piece.shape)  20.8 us
    ppermute x8, starting transfers between devices, shifted(): return lax.ppermute(piece, axis, pairs)  15.7 us
    pallas_call x1, Pallas kernels, to_grid(): pl.pallas_call(relayout_kernel, out_shape=jax.ShapeDtypeStruct((3, span_x...  13.3 us
    all_to_all x1, starting transfers between devices, body(): lax.all_to_all(payload, GX_GY, split_axis=0, concat_axis=0, tiled=True)  11.6 us
    ppermute x8, waiting for transfers between devices, shifted(): return lax.ppermute(piece, axis, pairs)  4.54 us
  transfers between devices with their start and end apart: 17, of which 5 were waited for; matrix products, arithmetic and copies ran while one was open for 7% of the time, Pallas kernels for 7%

profile of v14, /device:TPU:0, one launch (start us, length us, event | category | flops | bytes accessed | tf_op | source)
XLA Modules:
  0.0 183.1 jit_solution(17759947731608869111)
XLA Ops:
  1.9 2.0 %broadcast_select_fusion = (bf16[256]{0:T(256)(128)(2,1)S(1)}, bf16[256]{0:T(256)(128)(2,1)S(1)}) fusion(pred[]{:T(512)} %compare_reduce_fusion, s32[256]{0:T(256)} %param.11, pred[]{:T(512)} %compare_reduce_fusion.1), kind=kLoop, calls=%fused_computation.106 | loop fusion | flops 5888 | bytes 2050 | tf_op jit(solution)/shard_map/select.12
  7.0 2.1 %convolution_convert_fusion = bf16[128,6,1664]{2,0,1:T(8,128)(2,1)S(1)} fusion(bf16[256,128]{1,0:T(8,128)(2,1)S(1)} %scatter.9, bf16[256,1536]{1,0:T(8,128)(2,1)} %param.9, s32[128,6]{0,1:T(8,128)S(1)} %iota_add_fusion, s32[256]{0:T(256)S(1)} %multiply_add_fusion.1), kind=kOutput, calls=%fused_computation | convolution fusion | flops 657489920 | bytes 3411968 | tf_op jit(solution)/shard_map/pck,kj->pcj/dot_general | solution.py:74
  9.1 3.2 %copy.32 = bf16[128,6,1664]{2,1,0:T(8,128)(2,1)} copy(bf16[128,6,1664]{2,0,1:T(8,128)(2,1)S(1)} %convolution_convert_fusion) | data formatting | bytes 5111808 | tf_op jit(solution)/shard_map/convert_element_type | solution.py:77
  12.3 11.6 %all-to-all-start = ((bf16[128,6,1664]{2,1,0:T(8,128)(2,1)}), bf16[128,6,1664]{2,1,0:T(8,128)(2,1)}, u32[]{:S(2)}, u32[]{:S(2)}) async-start(bf16[128,6,1664]{2,1,0:T(8,128)(2,1)} %copy.32), calls=%async_computation | async-start | bytes 6815744 | tf_op jit(solution)/shard_map/all_to_all | solution.py:157
  25.3 3.7 %collective-permute-start.7 = (f32[32,128]{1,0:T(8,128)S(1)}, f32[32,128]{1,0:T(8,128)S(1)}, u32[]{:S(2)}, u32[]{:S(2)}) collective-permute-start(f32[32,128]{1,0:T(8,128)S(1)} %bitcast.84), channel_id=1, source_target_pairs={{0,1},{1,2},{2,3},{3,4},{4,5},{5,6},{6,7},{7,8},{8,9},{9,10},{10,1... | collective-permute-start | bytes 49160 | tf_op jit(solution)/shard_map/ppermute | solution.py:17
  34.7 32.3 %all-to-all-done = bf16[128,6,1664]{2,1,0:T(8,128)(2,1)} async-done(((bf16[128,6,1664]{2,1,0:T(8,128)(2,1)}), bf16[128,6,1664]{2,1,0:T(8,128)(2,1)}, u32[]{:S(2)}, u32[]{:S(2)}) %all-to-all-start) | async-done | bytes 2555936 | tf_op jit(solution)/shard_map/all_to_all | solution.py:157
  68.3 2.1 %slice.271 = bf16[128,6,1536]{2,1,0:T(8,128)(2,1)S(1)} slice(bf16[128,6,1664]{2,1,0:T(8,128)(2,1)} %all-to-all-done), slice={[0:128], [0:6], [0:1536]} | slice | bytes 4718592 | tf_op jit(solution)/shard_map/slice | solution.py:168
  70.3 3.5 %convolution_bitcast_fusion.blk_ref = f32[512,1536]{1,0:T(8,128)} fusion(bf16[128,6,1536]{2,1,0:T(8,128)(2,1)S(1)} %slice.271, s32[128,6]{0,1:T(8,128)S(1)} %fusion.40), kind=kOutput, calls=%fused_computation.1 | convolution fusion | flops 1208352768 | bytes 5508096 | tf_op jit(solution)/shard_map/pcs,pcj->sj/dot_general | solution.py:165
  73.9 13.3 %shard_map.68 = f32[3,32,64,128]{3,2,1,0:T(8,128)} custom-call(f32[512,1536]{1,0:T(8,128)} %convolution_bitcast_fusion.blk_ref), custom_call_target="tpu_custom_call" | custom-call | flops 15728640 | bytes 6291456 | tf_op jit(solution)/shard_map/pallas_call | solution.py:143
  87.1 2.1 %slice_bitcast_fusion.2 = (f32[32,64,128]{2,1,0:T(8,128)S(1)}, f32[32,64,128]{2,1,0:T(8,128)S(1)}, f32[32,64,128]{2,1,0:T(8,128)S(1)}) fusion(f32[3,32,64,128]{3,2,1,0:T(8,128)} %shard_map.68), kind=kLoop, calls=%fused_computation.62 | loop fusion | bytes 6291456 | tf_op jit(solution)/shard_map/squeeze | solution.py:172
  90.0 2.9 %collective-permute-start.3 = (f32[32,128]{1,0:T(8,128)S(1)}, f32[32,128]{1,0:T(8,128)S(1)}, u32[]{:S(2)}, u32[]{:S(2)}) collective-permute-start(f32[32,128]{1,0:T(8,128)S(1)} %bitcast.86), channel_id=1, source_target_pairs={{0,1},{1,2},{2,3},{3,4},{4,5},{5,6},{6,7},{7,8},{8,9},{9,10},{10,1... | collective-permute-start | bytes 49160 | tf_op jit(solution)/shard_map/ppermute | solution.py:17
  95.6 3.0 %collective-permute-start.1 = (f32[1,64,128]{2,1,0:T(8,128)S(1)}, f32[1,64,128]{2,1,0:T(8,128)S(1)}, u32[]{:S(2)}, u32[]{:S(2)}) collective-permute-start(f32[1,64,128]{2,1,0:T(8,128)S(1)} %get-tuple-element.36), channel_id=1, source_target_pairs={{0,16},{16,32},{32,48},{48,64},{64,80},{80,96},{96,112},{1,17},{17... | collective-permute-start | bytes 98312 | tf_op jit(solution)/shard_map/ppermute | solution.py:18
  99.8 3.6 %fusion.45 = (f32[32,64,128]{2,1,0:T(8,128)S(1)}, f32[32,64,128]{2,1,0:T(8,128)S(1)}) fusion(f32[32,64,128]{2,1,0:T(8,128)S(1)} %copy-done.1, f32[32,64,127]{2,1,0:T(8,128)S(1)} %get-tuple-element.70, f32[32,64,127]{2,1,0:T(8,128)S(1)} %get-tuple-element.71, f32[34,64,128]{2,1,0:T(8,128)} %constant_dynamic-update-slice_fusion, ...), kind=kLoop, calls=%fused_computation.116 | loop fusion | flops 8126464 | bytes 11763712 | tf_op jit(solution)/shard_map/mul | solution.py:181
  103.4 4.5 %collective-permute-start.11 = (f32[32,128]{1,0:T(8,128)S(1)}, f32[32,128]{1,0:T(8,128)S(1)}, u32[]{:S(2)}, u32[]{:S(2)}) collective-permute-start(f32[32,128]{1,0:T(8,128)S(1)} %bitcast.89), channel_id=1, source_target_pairs={{0,1},{1,2},{2,3},{3,4},{4,5},{5,6},{6,7},{7,8},{8,9},{9,10},{10,1... | collective-permute-start | bytes 49160 | tf_op jit(solution)/shard_map/ppermute | solution.py:17
  113.6 2.4 %collective-permute-done.8 = f32[1,64,128]{2,1,0:T(8,128)S(1)} collective-permute-done((f32[1,64,128]{2,1,0:T(8,128)S(1)}, f32[1,64,128]{2,1,0:T(8,128)S(1)}, u32[]{:S(2)}, u32[]{:S(2)}) %collective-permute-start.8) | collective-permute-done | bytes 32800 | tf_op jit(solution)/shard_map/ppermute | solution.py:18
  116.8 4.5 %collective-permute-start.15 = (f32[32,128]{1,0:T(8,128)S(1)}, f32[32,128]{1,0:T(8,128)S(1)}, u32[]{:S(2)}, u32[]{:S(2)}) collective-permute-start(f32[32,128]{1,0:T(8,128)S(1)} %bitcast.90), channel_id=1, source_target_pairs={{0,1},{1,2},{2,3},{3,4},{4,5},{5,6},{6,7},{7,8},{8,9},{9,10},{10,1... | collective-permute-start | bytes 49160 | tf_op jit(solution)/shard_map/ppermute | solution.py:17
  122.7 4.3 %collective-permute-start.13 = (f32[1,64,128]{2,1,0:T(8,128)S(1)}, f32[1,64,128]{2,1,0:T(8,128)S(1)}, u32[]{:S(2)}, u32[]{:S(2)}) collective-permute-start(f32[1,64,128]{2,1,0:T(8,128)S(1)} %get-tuple-element.44), channel_id=1, source_target_pairs={{0,16},{16,32},{32,48},{48,64},{64,80},{80,96},{96,112},{1,17},{17... | collective-permute-start | bytes 98312 | tf_op jit(solution)/shard_map/ppermute | solution.py:18
  130.0 3.3 %multiply_reduce_fusion.3 = (f32[]{:T(128)}, f32[]{:T(128)}, f32[]{:T(128)}, f32[]{:T(128)}, f32[32,64,128]{2,1,0:T(8,128)}) fusion(f32[32,64,128]{2,1,0:T(8,128)S(1)} %get-tuple-element.34, f32[32,64,128]{2,1,0:T(8,128)S(1)} %copy-done.1, f32[32,64,128]{2,1,0:T(8,128)S(1)} %get-tuple-element.32, f32[32,64,128]{2,1,0:T(8,128)S(1)} %get-tuple-element.31, ...), kind=kLoop, calls=%fused_computation.69 | loop fusion | flops 8388604 | bytes 7421968 | tf_op jit(solution)/shard_map/reduce_sum | solution.py:188
  133.4 2.5 %pad_maximum_fusion.20 = f32[4]{0:T(128)S(1)} fusion(f32[1]{0:T(128)} %bitcast.33, f32[1]{0:T(128)} %bitcast.28, f32[1]{0:T(128)} %bitcast.27, f32[1]{0:T(128)} %bitcast.22), kind=kLoop, calls=%fused_computation.109 | loop fusion | flops 12 | bytes 32 | tf_op jit(solution)/shard_map/stack | solution.py:186
  135.9 10.9 %psum.28 = f32[4]{0:T(128)S(1)} all-reduce(f32[4]{0:T(128)S(1)} %pad_maximum_fusion.20), channel_id=1, replica_groups=mesh['gx_0'=4,'gx_1'=2,'gy_0'=4,'gy_1'=4] {'gx_0'}, use_global_device_ids=true, to_apply=%region_9.10 | all-reduce | flops 4 | bytes 32 | tf_op jit(solution)/shard_map/psum | solution.py:43
  146.8 2.5 %psum.29 = f32[4]{0:T(128)S(1)} all-reduce(f32[4]{0:T(128)S(1)} %psum.28), channel_id=1, replica_groups=mesh['gx_0'=4,'gx_1'=2,'gy_0'=4,'gy_1'=4] {'gx_1'}, use_global_device_ids=true, to_apply=%region_10.11 | all-reduce | flops 4 | bytes 32 | tf_op jit(solution)/shard_map/psum | solution.py:43
  149.2 17.0 %psum.30 = f32[4]{0:T(128)S(1)} all-reduce(f32[4]{0:T(128)S(1)} %psum.29), channel_id=1, replica_groups=mesh['gx_0'=4,'gx_1'=2,'gy_0'=4,'gy_1'=4] {'gy_0'}, use_global_device_ids=true, to_apply=%region_11.12 | all-reduce | flops 4 | bytes 32 | tf_op jit(solution)/shard_map/psum | solution.py:43
  166.2 7.7 %psum.31 = f32[4]{0:T(128)S(1)} all-reduce(f32[4]{0:T(128)S(1)} %psum.30), channel_id=1, replica_groups=mesh['gx_0'=4,'gx_1'=2,'gy_0'=4,'gy_1'=4] {'gy_1'}, use_global_device_ids=true, to_apply=%region_12.13 | all-reduce | flops 4 | bytes 32 | tf_op jit(solution)/shard_map/psum | solution.py:43
  179.6 3.5 %multiply_subtract_fusion = (f32[32,64,128]{2,1,0:T(8,128)}, f32[32,64,128]{2,1,0:T(8,128)}) fusion(f32[32,64,128]{2,1,0:T(8,128)} %copy-done.2, f32[32,64,128]{2,1,0:T(8,128)} %get-tuple-element.30, f32[32,64,128]{2,1,0:T(8,128)S(1)} %get-tuple-element.34, f32[]{:T(128)S(6)} %div.34, f32[]{:T(128)S(6)} %div.35, f32[]{:T(128)S(6)} %div.33, ...), kind=kLoop, calls=%fused_computation.63 | loop fusion | flops 4718592 | bytes 7340044 | tf_op jit(solution)/shard_map/sub | solution.py:208
  (69 shorter events, 28.6 us)
Async XLA Ops:
  12.3 11.7 %copy-start = (f32[32,64,128]{2,1,0:T(8,128)S(1)}, f32[32,64,128]{2,1,0:T(8,128)}, u32[]{:S(2)}) copy-start(f32[32,64,128]{2,1,0:T(8,128)} %param.13) | copy-start | bytes 3145732
  12.3 54.7 %all-to-all-start = ((bf16[128,6,1664]{2,1,0:T(8,128)(2,1)}), bf16[128,6,1664]{2,1,0:T(8,128)(2,1)}, u32[]{:S(2)}, u32[]{:S(2)}) async-start(bf16[128,6,1664]{2,1,0:T(8,128)(2,1)} %copy.32), calls=%async_computation | async-start | bytes 6815744 | tf_op jit(solution)/shard_map/all_to_all | solution.py:157
  24.0 7.6 %collective-permute-start.5 = (f32[1,64,128]{2,1,0:T(8,128)S(1)}, f32[1,64,128]{2,1,0:T(8,128)S(1)}, u32[]{:S(2)}, u32[]{:S(2)}) collective-permute-start(f32[1,64,128]{2,1,0:T(8,128)S(1)} %get-tuple-element.61), channel_id=1, source_target_pairs={{0,16},{16,32},{32,48},{48,64},{64,80},{80,96},{96,112},{1,17},{17... | collective-permute-start | bytes 98312 | tf_op jit(solution)/shard_map/ppermute | solution.py:18
  25.3 70.2 %collective-permute-start.7 = (f32[32,128]{1,0:T(8,128)S(1)}, f32[32,128]{1,0:T(8,128)S(1)}, u32[]{:S(2)}, u32[]{:S(2)}) collective-permute-start(f32[32,128]{1,0:T(8,128)S(1)} %bitcast.84), channel_id=1, source_target_pairs={{0,1},{1,2},{2,3},{3,4},{4,5},{5,6},{6,7},{7,8},{8,9},{9,10},{10,1... | collective-permute-start | bytes 49160 | tf_op jit(solution)/shard_map/ppermute | solution.py:17
  29.0 70.4 %collective-permute-start.6 = (f32[32,128]{1,0:T(8,128)S(1)}, f32[32,128]{1,0:T(8,128)S(1)}, u32[]{:S(2)}, u32[]{:S(2)}) collective-permute-start(f32[32,128]{1,0:T(8,128)S(1)} %bitcast.83), channel_id=1, source_target_pairs={{1,0},{2,1},{3,2},{4,3},{5,4},{6,5},{7,6},{8,7},{9,8},{10,9},{11,1... | collective-permute-start | bytes 49160 | tf_op jit(solution)/shard_map/ppermute | solution.py:17
  30.3 3.8 %collective-permute-start.4 = (f32[1,64,128]{2,1,0:T(8,128)S(1)}, f32[1,64,128]{2,1,0:T(8,128)S(1)}, u32[]{:S(2)}, u32[]{:S(2)}) collective-permute-start(f32[1,64,128]{2,1,0:T(8,128)S(1)} %get-tuple-element.60), channel_id=1, source_target_pairs={{16,0},{32,16},{48,32},{64,48},{80,64},{96,80},{112,96},{17,1},{33... | collective-permute-start | bytes 98312 | tf_op jit(solution)/shard_map/ppermute | solution.py:18
  90.0 9.4 %collective-permute-start.3 = (f32[32,128]{1,0:T(8,128)S(1)}, f32[32,128]{1,0:T(8,128)S(1)}, u32[]{:S(2)}, u32[]{:S(2)}) collective-permute-start(f32[32,128]{1,0:T(8,128)S(1)} %bitcast.86), channel_id=1, source_target_pairs={{0,1},{1,2},{2,3},{3,4},{4,5},{5,6},{6,7},{7,8},{8,9},{9,10},{10,1... | collective-permute-start | bytes 49160 | tf_op jit(solution)/shard_map/ppermute | solution.py:17
  92.9 6.5 %collective-permute-start.2 = (f32[32,128]{1,0:T(8,128)S(1)}, f32[32,128]{1,0:T(8,128)S(1)}, u32[]{:S(2)}, u32[]{:S(2)}) collective-permute-start(f32[32,128]{1,0:T(8,128)S(1)} %bitcast.85), channel_id=1, source_target_pairs={{1,0},{2,1},{3,2},{4,3},{5,4},{6,5},{7,6},{8,7},{9,8},{10,9},{11,1... | collective-permute-start | bytes 49160 | tf_op jit(solution)/shard_map/ppermute | solution.py:17
  94.2 5.2 %collective-permute-start = (f32[1,64,128]{2,1,0:T(8,128)S(1)}, f32[1,64,128]{2,1,0:T(8,128)S(1)}, u32[]{:S(2)}, u32[]{:S(2)}) collective-permute-start(f32[1,64,128]{2,1,0:T(8,128)S(1)} %get-tuple-element.35), channel_id=1, source_target_pairs={{16,0},{32,16},{48,32},{64,48},{80,64},{96,80},{112,96},{17,1},{33... | collective-permute-start | bytes 98312 | tf_op jit(solution)/shard_map/ppermute | solution.py:18
  95.6 3.9 %collective-permute-start.1 = (f32[1,64,128]{2,1,0:T(8,128)S(1)}, f32[1,64,128]{2,1,0:T(8,128)S(1)}, u32[]{:S(2)}, u32[]{:S(2)}) collective-permute-start(f32[1,64,128]{2,1,0:T(8,128)S(1)} %get-tuple-element.36), channel_id=1, source_target_pairs={{0,16},{16,32},{32,48},{48,64},{64,80},{80,96},{96,112},{1,17},{17... | collective-permute-start | bytes 98312 | tf_op jit(solution)/shard_map/ppermute | solution.py:18
  98.6 1.2 copy-start.1
  103.4 9.3 %collective-permute-start.11 = (f32[32,128]{1,0:T(8,128)S(1)}, f32[32,128]{1,0:T(8,128)S(1)}, u32[]{:S(2)}, u32[]{:S(2)}) collective-permute-start(f32[32,128]{1,0:T(8,128)S(1)} %bitcast.89), channel_id=1, source_target_pairs={{0,1},{1,2},{2,3},{3,4},{4,5},{5,6},{6,7},{7,8},{8,9},{9,10},{10,1... | collective-permute-start | bytes 49160 | tf_op jit(solution)/shard_map/ppermute | solution.py:17
  108.0 5.6 %collective-permute-start.10 = (f32[32,128]{1,0:T(8,128)S(1)}, f32[32,128]{1,0:T(8,128)S(1)}, u32[]{:S(2)}, u32[]{:S(2)}) collective-permute-start(f32[32,128]{1,0:T(8,128)S(1)} %bitcast.87), channel_id=1, source_target_pairs={{1,0},{2,1},{3,2},{4,3},{5,4},{6,5},{7,6},{8,7},{9,8},{10,9},{11,1... | collective-permute-start | bytes 49160 | tf_op jit(solution)/shard_map/ppermute | solution.py:17
  109.3 4.3 %collective-permute-start.9 = (f32[1,64,128]{2,1,0:T(8,128)S(1)}, f32[1,64,128]{2,1,0:T(8,128)S(1)}, u32[]{:S(2)}, u32[]{:S(2)}) collective-permute-start(f32[1,64,128]{2,1,0:T(8,128)S(1)} %get-tuple-element.50), channel_id=1, source_target_pairs={{0,16},{16,32},{32,48},{48,64},{64,80},{80,96},{96,112},{1,17},{17... | collective-permute-start | bytes 98312 | tf_op jit(solution)/shard_map/ppermute | solution.py:18
  111.1 5.0 %collective-permute-start.8 = (f32[1,64,128]{2,1,0:T(8,128)S(1)}, f32[1,64,128]{2,1,0:T(8,128)S(1)}, u32[]{:S(2)}, u32[]{:S(2)}) collective-permute-start(f32[1,64,128]{2,1,0:T(8,128)S(1)} %get-tuple-element.51), channel_id=1, source_target_pairs={{16,0},{32,16},{48,32},{64,48},{80,64},{96,80},{112,96},{17,1},{33... | collective-permute-start | bytes 98312 | tf_op jit(solution)/shard_map/ppermute | solution.py:18
  116.8 16.6 %copy-start.2 = (f32[32,64,128]{2,1,0:T(8,128)}, f32[32,64,128]{2,1,0:T(8,128)S(1)}, u32[]{:S(2)}) copy-start(f32[32,64,128]{2,1,0:T(8,128)S(1)} %get-tuple-element.32) | copy-start | bytes 3145732
  116.8 12.0 %collective-permute-start.15 = (f32[32,128]{1,0:T(8,128)S(1)}, f32[32,128]{1,0:T(8,128)S(1)}, u32[]{:S(2)}, u32[]{:S(2)}) collective-permute-start(f32[32,128]{1,0:T(8,128)S(1)} %bitcast.90), channel_id=1, source_target_pairs={{0,1},{1,2},{2,3},{3,4},{4,5},{5,6},{6,7},{7,8},{8,9},{9,10},{10,1... | collective-permute-start | bytes 49160 | tf_op jit(solution)/shard_map/ppermute | solution.py:17
  121.4 7.4 %collective-permute-start.14 = (f32[32,128]{1,0:T(8,128)S(1)}, f32[32,128]{1,0:T(8,128)S(1)}, u32[]{:S(2)}, u32[]{:S(2)}) collective-permute-start(f32[32,128]{1,0:T(8,128)S(1)} %bitcast.88), channel_id=1, source_target_pairs={{1,0},{2,1},{3,2},{4,3},{5,4},{6,5},{7,6},{8,7},{9,8},{10,9},{11,1... | collective-permute-start | bytes 49160 | tf_op jit(solution)/shard_map/ppermute | solution.py:17
  122.7 6.1 %collective-permute-start.13 = (f32[1,64,128]{2,1,0:T(8,128)S(1)}, f32[1,64,128]{2,1,0:T(8,128)S(1)}, u32[]{:S(2)}, u32[]{:S(2)}) collective-permute-start(f32[1,64,128]{2,1,0:T(8,128)S(1)} %get-tuple-element.44), channel_id=1, source_target_pairs={{0,16},{16,32},{32,48},{48,64},{64,80},{80,96},{96,112},{1,17},{17... | collective-permute-start | bytes 98312 | tf_op jit(solution)/shard_map/ppermute | solution.py:18
  126.9 3.1 %collective-permute-start.12 = (f32[1,64,128]{2,1,0:T(8,128)S(1)}, f32[1,64,128]{2,1,0:T(8,128)S(1)}, u32[]{:S(2)}, u32[]{:S(2)}) collective-permute-start(f32[1,64,128]{2,1,0:T(8,128)S(1)} %get-tuple-element.45), channel_id=1, source_target_pairs={{16,0},{32,16},{48,32},{64,48},{80,64},{96,80},{112,96},{17,1},{33... | collective-permute-start | bytes 98312 | tf_op jit(solution)/shard_map/ppermute | solution.py:18

commit v15 on v14

--- a/solution.py
+++ b/solution.py
@@ -182,18 +182,15 @@
     image = operate(precond, screen)
     scaled = image * inverse
     scaled_image = operate(scaled, screen)
-    sums = over_axes(
-        jnp.stack(
-            [
-                jnp.sum(residual * precond),
-                jnp.sum(precond * image),
-                jnp.sum(image * scaled),
-                jnp.sum(scaled * scaled_image),
-            ]
+    gamma, delta, energy, curvature = over_axes(
+        (
+            jnp.sum(residual * precond),
+            jnp.sum(precond * image),
+            jnp.sum(image * scaled),
+            jnp.sum(scaled * scaled_image),
         ),
         GX_GY,
     )
-    gamma, delta, energy, curvature = sums[0], sums[1], sums[2], sums[3]
     alpha = gamma / delta
     gamma_next = alpha * alpha * energy - gamma
     ratio = gamma_next / gamma

time: 184 us -> 184 us (level)
  blocking collectives: 38.1 us -> 40.9 us
  other arithmetic: 18.6 us -> 16.2 us
    psum x4, blocking collectives: 38.1 us -> 40.9 us  [over_axes(): shard = lax.psum(shard, axis)]
    another operation x7 -> x6, other arithmetic: 6.02 us -> 3.51 us
where the time goes in v15:
time: 184 us; the launch traced here: 183 us
  starting transfers between devices  48.2 us (26%)
  blocking collectives  40.9 us (22%)
  waiting for transfers between devices  37.7 us (20%)
  other arithmetic  16.2 us (9%)
  local copies, waits for them, and re-layouts  15 us (8%)
  Pallas kernels  13.2 us (7%)
  between operations  6.1 us (3%)
  matrix products  5.58 us (3%)
    psum x4, blocking collectives, over_axes(): shard = lax.psum(shard, axis)  40.9 us
    all_to_all x1, waiting for transfers between devices, body(): lax.all_to_all(payload, GX_GY, split_axis=0, concat_axis=0, tiled=True)  32.3 us
    ppermute x8, starting transfers between devices, shifted(): return lax.ppermute(flat, axis, pairs).reshape(piece.shape)  20.8 us
    ppermute x8, starting transfers between devices, shifted(): return lax.ppermute(piece, axis, pairs)  15.7 us
    pallas_call x1, Pallas kernels, to_grid(): pl.pallas_call(relayout_kernel, out_shape=jax.ShapeDtypeStruct((3, span_x...  13.2 us
    all_to_all x1, starting transfers between devices, body(): lax.all_to_all(payload, GX_GY, split_axis=0, concat_axis=0, tiled=True)  11.6 us
    ppermute x8, waiting for transfers between devices, shifted(): return lax.ppermute(piece, axis, pairs)  4.54 us
  transfers between devices with their start and end apart: 17, of which 5 were waited for; matrix products, arithmetic and copies ran while one was open for 7% of the time, Pallas kernels for 7%

profile of v15, /device:TPU:0, one launch (start us, length us, event | category | flops | bytes accessed | tf_op | source)
XLA Modules:
  0.0 182.8 jit_solution(16147611793061522872)
XLA Ops:
  1.9 2.0 %broadcast_select_fusion = (bf16[256]{0:T(256)(128)(2,1)S(1)}, bf16[256]{0:T(256)(128)(2,1)S(1)}) fusion(pred[]{:T(512)} %compare_reduce_fusion, s32[256]{0:T(256)} %param.11, pred[]{:T(512)} %compare_reduce_fusion.1), kind=kLoop, calls=%fused_computation.106 | loop fusion | flops 5888 | bytes 2050 | tf_op jit(solution)/shard_map/select.12
  7.0 2.1 %convolution_convert_fusion = bf16[128,6,1664]{2,0,1:T(8,128)(2,1)S(1)} fusion(bf16[256,128]{1,0:T(8,128)(2,1)S(1)} %scatter.9, bf16[256,1536]{1,0:T(8,128)(2,1)} %param.9, s32[128,6]{0,1:T(8,128)S(1)} %iota_add_fusion, s32[256]{0:T(256)S(1)} %multiply_add_fusion.1), kind=kOutput, calls=%fused_computation | convolution fusion | flops 657489920 | bytes 3411968 | tf_op jit(solution)/shard_map/pck,kj->pcj/dot_general | solution.py:74
  9.1 3.2 %copy.32 = bf16[128,6,1664]{2,1,0:T(8,128)(2,1)} copy(bf16[128,6,1664]{2,0,1:T(8,128)(2,1)S(1)} %convolution_convert_fusion) | data formatting | bytes 5111808 | tf_op jit(solution)/shard_map/convert_element_type | solution.py:77
  12.3 11.6 %all-to-all-start = ((bf16[128,6,1664]{2,1,0:T(8,128)(2,1)}), bf16[128,6,1664]{2,1,0:T(8,128)(2,1)}, u32[]{:S(2)}, u32[]{:S(2)}) async-start(bf16[128,6,1664]{2,1,0:T(8,128)(2,1)} %copy.32), calls=%async_computation | async-start | bytes 6815744 | tf_op jit(solution)/shard_map/all_to_all | solution.py:157
  25.3 3.7 %collective-permute-start.7 = (f32[32,128]{1,0:T(8,128)S(1)}, f32[32,128]{1,0:T(8,128)S(1)}, u32[]{:S(2)}, u32[]{:S(2)}) collective-permute-start(f32[32,128]{1,0:T(8,128)S(1)} %bitcast.76), channel_id=1, source_target_pairs={{0,1},{1,2},{2,3},{3,4},{4,5},{5,6},{6,7},{7,8},{8,9},{9,10},{10,1... | collective-permute-start | bytes 49160 | tf_op jit(solution)/shard_map/ppermute | solution.py:17
  34.8 32.3 %all-to-all-done = bf16[128,6,1664]{2,1,0:T(8,128)(2,1)} async-done(((bf16[128,6,1664]{2,1,0:T(8,128)(2,1)}), bf16[128,6,1664]{2,1,0:T(8,128)(2,1)}, u32[]{:S(2)}, u32[]{:S(2)}) %all-to-all-start) | async-done | bytes 2555936 | tf_op jit(solution)/shard_map/all_to_all | solution.py:157
  68.3 2.1 %slice.255 = bf16[128,6,1536]{2,1,0:T(8,128)(2,1)S(1)} slice(bf16[128,6,1664]{2,1,0:T(8,128)(2,1)} %all-to-all-done), slice={[0:128], [0:6], [0:1536]} | slice | bytes 4718592 | tf_op jit(solution)/shard_map/slice | solution.py:168
  70.4 3.5 %convolution_bitcast_fusion.blk_ref = f32[512,1536]{1,0:T(8,128)} fusion(bf16[128,6,1536]{2,1,0:T(8,128)(2,1)S(1)} %slice.255, s32[128,6]{0,1:T(8,128)S(1)} %fusion.40), kind=kOutput, calls=%fused_computation.1 | convolution fusion | flops 1208352768 | bytes 5508096 | tf_op jit(solution)/shard_map/pcs,pcj->sj/dot_general | solution.py:165
  73.9 13.2 %shard_map.68 = f32[3,32,64,128]{3,2,1,0:T(8,128)} custom-call(f32[512,1536]{1,0:T(8,128)} %convolution_bitcast_fusion.blk_ref), custom_call_target="tpu_custom_call" | custom-call | flops 15728640 | bytes 6291456 | tf_op jit(solution)/shard_map/pallas_call | solution.py:143
  87.1 2.1 %slice_bitcast_fusion.2 = (f32[32,64,128]{2,1,0:T(8,128)S(1)}, f32[32,64,128]{2,1,0:T(8,128)S(1)}, f32[32,64,128]{2,1,0:T(8,128)S(1)}) fusion(f32[3,32,64,128]{3,2,1,0:T(8,128)} %shard_map.68), kind=kLoop, calls=%fused_computation.62 | loop fusion | bytes 6291456 | tf_op jit(solution)/shard_map/squeeze | solution.py:172
  90.0 2.9 %collective-permute-start.3 = (f32[32,128]{1,0:T(8,128)S(1)}, f32[32,128]{1,0:T(8,128)S(1)}, u32[]{:S(2)}, u32[]{:S(2)}) collective-permute-start(f32[32,128]{1,0:T(8,128)S(1)} %bitcast.78), channel_id=1, source_target_pairs={{0,1},{1,2},{2,3},{3,4},{4,5},{5,6},{6,7},{7,8},{8,9},{9,10},{10,1... | collective-permute-start | bytes 49160 | tf_op jit(solution)/shard_map/ppermute | solution.py:17
  95.5 3.0 %collective-permute-start.1 = (f32[1,64,128]{2,1,0:T(8,128)S(1)}, f32[1,64,128]{2,1,0:T(8,128)S(1)}, u32[]{:S(2)}, u32[]{:S(2)}) collective-permute-start(f32[1,64,128]{2,1,0:T(8,128)S(1)} %get-tuple-element.54), channel_id=1, source_target_pairs={{0,16},{16,32},{32,48},{48,64},{64,80},{80,96},{96,112},{1,17},{17... | collective-permute-start | bytes 98312 | tf_op jit(solution)/shard_map/ppermute | solution.py:18
  99.8 3.6 %fusion.45 = (f32[32,64,128]{2,1,0:T(8,128)S(1)}, f32[32,64,128]{2,1,0:T(8,128)S(1)}) fusion(f32[32,64,128]{2,1,0:T(8,128)S(1)} %copy-done.1, f32[32,64,127]{2,1,0:T(8,128)S(1)} %get-tuple-element.84, f32[32,64,127]{2,1,0:T(8,128)S(1)} %get-tuple-element.85, f32[34,64,128]{2,1,0:T(8,128)} %constant_dynamic-update-slice_fusion, ...), kind=kLoop, calls=%fused_computation.115 | loop fusion | flops 8126464 | bytes 11763712 | tf_op jit(solution)/shard_map/mul | solution.py:181
  103.4 4.5 %collective-permute-start.11 = (f32[32,128]{1,0:T(8,128)S(1)}, f32[32,128]{1,0:T(8,128)S(1)}, u32[]{:S(2)}, u32[]{:S(2)}) collective-permute-start(f32[32,128]{1,0:T(8,128)S(1)} %bitcast.81), channel_id=1, source_target_pairs={{0,1},{1,2},{2,3},{3,4},{4,5},{5,6},{6,7},{7,8},{8,9},{9,10},{10,1... | collective-permute-start | bytes 49160 | tf_op jit(solution)/shard_map/ppermute | solution.py:17
  109.3 1.8 collective-permute-start.9
  113.6 2.4 %collective-permute-done.8 = f32[1,64,128]{2,1,0:T(8,128)S(1)} collective-permute-done((f32[1,64,128]{2,1,0:T(8,128)S(1)}, f32[1,64,128]{2,1,0:T(8,128)S(1)}, u32[]{:S(2)}, u32[]{:S(2)}) %collective-permute-start.8) | collective-permute-done | bytes 32800 | tf_op jit(solution)/shard_map/ppermute | solution.py:18
  116.8 4.5 %collective-permute-start.15 = (f32[32,128]{1,0:T(8,128)S(1)}, f32[32,128]{1,0:T(8,128)S(1)}, u32[]{:S(2)}, u32[]{:S(2)}) collective-permute-start(f32[32,128]{1,0:T(8,128)S(1)} %bitcast.82), channel_id=1, source_target_pairs={{0,1},{1,2},{2,3},{3,4},{4,5},{5,6},{6,7},{7,8},{8,9},{9,10},{10,1... | collective-permute-start | bytes 49160 | tf_op jit(solution)/shard_map/ppermute | solution.py:17
  122.7 4.3 %collective-permute-start.13 = (f32[1,64,128]{2,1,0:T(8,128)S(1)}, f32[1,64,128]{2,1,0:T(8,128)S(1)}, u32[]{:S(2)}, u32[]{:S(2)}) collective-permute-start(f32[1,64,128]{2,1,0:T(8,128)S(1)} %get-tuple-element.62), channel_id=1, source_target_pairs={{0,16},{16,32},{32,48},{48,64},{64,80},{80,96},{96,112},{1,17},{17... | collective-permute-start | bytes 98312 | tf_op jit(solution)/shard_map/ppermute | solution.py:18
  130.0 3.3 %multiply_reduce_fusion = (f32[]{:T(128)}, f32[]{:T(128)}, f32[]{:T(128)}, f32[]{:T(128)}, f32[32,64,128]{2,1,0:T(8,128)}) fusion(f32[32,64,128]{2,1,0:T(8,128)S(1)} %get-tuple-element.49, f32[32,64,128]{2,1,0:T(8,128)S(1)} %get-tuple-element.50, f32[32,64,128]{2,1,0:T(8,128)S(1)} %get-tuple-element.52, f32[32,64,128]{2,1,0:T(8,128)S(1)} %copy-done.1, ...), kind=kLoop, calls=%fused_computation.66 | loop fusion | flops 8388604 | bytes 7421968 | tf_op jit(solution)/shard_map/reduce_sum | solution.py:190
  133.3 11.6 %all-reduce.17 = (f32[]{:T(128)}, f32[]{:T(128)}, f32[]{:T(128)}, f32[]{:T(128)}) all-reduce(f32[]{:T(128)} %get-tuple-element.30, f32[]{:T(128)} %get-tuple-element.31, f32[]{:T(128)} %get-tuple-element.29, f32[]{:T(128)} %get-tuple-element.28), channel_id=1, replica_groups=mesh['gx_0'=4,'gx_1'=2,'gy_0'=4,'gy_1'=4] {'gx_0'}, use_global_device_ids=true, to_apply=%region_6.7 | all-reduce | flops 4 | bytes 32 | tf_op jit(solution)/shard_map/psum | solution.py:43
  145.0 3.2 %all-reduce.18 = (f32[]{:T(128)}, f32[]{:T(128)}, f32[]{:T(128)}, f32[]{:T(128)}) all-reduce(f32[]{:T(128)} %get-tuple-element.40, f32[]{:T(128)} %get-tuple-element.41, f32[]{:T(128)} %get-tuple-element.42, f32[]{:T(128)} %get-tuple-element.43), channel_id=1, replica_groups=mesh['gx_0'=4,'gx_1'=2,'gy_0'=4,'gy_1'=4] {'gx_1'}, use_global_device_ids=true, to_apply=%region_7.8 | all-reduce | flops 4 | bytes 32 | tf_op jit(solution)/shard_map/psum | solution.py:43
  148.1 17.7 %all-reduce.16 = (f32[]{:T(128)}, f32[]{:T(128)}, f32[]{:T(128)}, f32[]{:T(128)}) all-reduce(f32[]{:T(128)} %get-tuple-element.44, f32[]{:T(128)} %get-tuple-element.45, f32[]{:T(128)} %get-tuple-element.46, f32[]{:T(128)} %get-tuple-element.47), channel_id=1, replica_groups=mesh['gx_0'=4,'gx_1'=2,'gy_0'=4,'gy_1'=4] {'gy_0'}, use_global_device_ids=true, to_apply=%region_8.9 | all-reduce | flops 4 | bytes 32 | tf_op jit(solution)/shard_map/psum | solution.py:43
  165.8 8.4 %all-reduce.15 = (f32[]{:T(128)}, f32[]{:T(128)}, f32[]{:T(128)}, f32[]{:T(128)}) all-reduce(f32[]{:T(128)} %get-tuple-element.36, f32[]{:T(128)} %get-tuple-element.37, f32[]{:T(128)} %get-tuple-element.38, f32[]{:T(128)} %get-tuple-element.39), channel_id=1, replica_groups=mesh['gx_0'=4,'gx_1'=2,'gy_0'=4,'gy_1'=4] {'gy_1'}, use_global_device_ids=true, to_apply=%region_9.10 | all-reduce | flops 4 | bytes 32 | tf_op jit(solution)/shard_map/psum | solution.py:43
  179.3 3.5 %multiply_subtract_fusion = (f32[32,64,128]{2,1,0:T(8,128)}, f32[32,64,128]{2,1,0:T(8,128)}) fusion(f32[32,64,128]{2,1,0:T(8,128)} %copy-done.2, f32[32,64,128]{2,1,0:T(8,128)} %get-tuple-element.48, f32[32,64,128]{2,1,0:T(8,128)S(1)} %get-tuple-element.52, f32[]{:T(128)S(6)} %div.34, f32[]{:T(128)S(6)} %div.35, f32[]{:T(128)S(6)} %div.33, ...), kind=kLoop, calls=%fused_computation.63 | loop fusion | flops 4718592 | bytes 7340044 | tf_op jit(solution)/shard_map/sub | solution.py:205
  (67 shorter events, 26.1 us)
Async XLA Ops:
  12.3 11.7 %copy-start = (f32[32,64,128]{2,1,0:T(8,128)S(1)}, f32[32,64,128]{2,1,0:T(8,128)}, u32[]{:S(2)}) copy-start(f32[32,64,128]{2,1,0:T(8,128)} %param.13) | copy-start | bytes 3145732
  12.3 54.7 %all-to-all-start = ((bf16[128,6,1664]{2,1,0:T(8,128)(2,1)}), bf16[128,6,1664]{2,1,0:T(8,128)(2,1)}, u32[]{:S(2)}, u32[]{:S(2)}) async-start(bf16[128,6,1664]{2,1,0:T(8,128)(2,1)} %copy.32), calls=%async_computation | async-start | bytes 6815744 | tf_op jit(solution)/shard_map/all_to_all | solution.py:157
  24.0 7.6 %collective-permute-start.5 = (f32[1,64,128]{2,1,0:T(8,128)S(1)}, f32[1,64,128]{2,1,0:T(8,128)S(1)}, u32[]{:S(2)}, u32[]{:S(2)}) collective-permute-start(f32[1,64,128]{2,1,0:T(8,128)S(1)} %get-tuple-element.79), channel_id=1, source_target_pairs={{0,16},{16,32},{32,48},{48,64},{64,80},{80,96},{96,112},{1,17},{17... | collective-permute-start | bytes 98312 | tf_op jit(solution)/shard_map/ppermute | solution.py:18
  25.3 70.2 %collective-permute-start.7 = (f32[32,128]{1,0:T(8,128)S(1)}, f32[32,128]{1,0:T(8,128)S(1)}, u32[]{:S(2)}, u32[]{:S(2)}) collective-permute-start(f32[32,128]{1,0:T(8,128)S(1)} %bitcast.76), channel_id=1, source_target_pairs={{0,1},{1,2},{2,3},{3,4},{4,5},{5,6},{6,7},{7,8},{8,9},{9,10},{10,1... | collective-permute-start | bytes 49160 | tf_op jit(solution)/shard_map/ppermute | solution.py:17
  29.0 70.4 %collective-permute-start.6 = (f32[32,128]{1,0:T(8,128)S(1)}, f32[32,128]{1,0:T(8,128)S(1)}, u32[]{:S(2)}, u32[]{:S(2)}) collective-permute-start(f32[32,128]{1,0:T(8,128)S(1)} %bitcast.75), channel_id=1, source_target_pairs={{1,0},{2,1},{3,2},{4,3},{5,4},{6,5},{7,6},{8,7},{9,8},{10,9},{11,1... | collective-permute-start | bytes 49160 | tf_op jit(solution)/shard_map/ppermute | solution.py:17
  30.3 3.8 %collective-permute-start.4 = (f32[1,64,128]{2,1,0:T(8,128)S(1)}, f32[1,64,128]{2,1,0:T(8,128)S(1)}, u32[]{:S(2)}, u32[]{:S(2)}) collective-permute-start(f32[1,64,128]{2,1,0:T(8,128)S(1)} %get-tuple-element.78), channel_id=1, source_target_pairs={{16,0},{32,16},{48,32},{64,48},{80,64},{96,80},{112,96},{17,1},{33... | collective-permute-start | bytes 98312 | tf_op jit(solution)/shard_map/ppermute | solution.py:18
  90.0 9.4 %collective-permute-start.3 = (f32[32,128]{1,0:T(8,128)S(1)}, f32[32,128]{1,0:T(8,128)S(1)}, u32[]{:S(2)}, u32[]{:S(2)}) collective-permute-start(f32[32,128]{1,0:T(8,128)S(1)} %bitcast.78), channel_id=1, source_target_pairs={{0,1},{1,2},{2,3},{3,4},{4,5},{5,6},{6,7},{7,8},{8,9},{9,10},{10,1... | collective-permute-start | bytes 49160 | tf_op jit(solution)/shard_map/ppermute | solution.py:17
  92.9 6.5 %collective-permute-start.2 = (f32[32,128]{1,0:T(8,128)S(1)}, f32[32,128]{1,0:T(8,128)S(1)}, u32[]{:S(2)}, u32[]{:S(2)}) collective-permute-start(f32[32,128]{1,0:T(8,128)S(1)} %bitcast.77), channel_id=1, source_target_pairs={{1,0},{2,1},{3,2},{4,3},{5,4},{6,5},{7,6},{8,7},{9,8},{10,9},{11,1... | collective-permute-start | bytes 49160 | tf_op jit(solution)/shard_map/ppermute | solution.py:17
  94.2 5.2 %collective-permute-start = (f32[1,64,128]{2,1,0:T(8,128)S(1)}, f32[1,64,128]{2,1,0:T(8,128)S(1)}, u32[]{:S(2)}, u32[]{:S(2)}) collective-permute-start(f32[1,64,128]{2,1,0:T(8,128)S(1)} %get-tuple-element.53), channel_id=1, source_target_pairs={{16,0},{32,16},{48,32},{64,48},{80,64},{96,80},{112,96},{17,1},{33... | collective-permute-start | bytes 98312 | tf_op jit(solution)/shard_map/ppermute | solution.py:18
  95.5 3.9 %collective-permute-start.1 = (f32[1,64,128]{2,1,0:T(8,128)S(1)}, f32[1,64,128]{2,1,0:T(8,128)S(1)}, u32[]{:S(2)}, u32[]{:S(2)}) collective-permute-start(f32[1,64,128]{2,1,0:T(8,128)S(1)} %get-tuple-element.54), channel_id=1, source_target_pairs={{0,16},{16,32},{32,48},{48,64},{64,80},{80,96},{96,112},{1,17},{17... | collective-permute-start | bytes 98312 | tf_op jit(solution)/shard_map/ppermute | solution.py:18
  98.6 1.2 copy-start.1
  103.4 9.3 %collective-permute-start.11 = (f32[32,128]{1,0:T(8,128)S(1)}, f32[32,128]{1,0:T(8,128)S(1)}, u32[]{:S(2)}, u32[]{:S(2)}) collective-permute-start(f32[32,128]{1,0:T(8,128)S(1)} %bitcast.81), channel_id=1, source_target_pairs={{0,1},{1,2},{2,3},{3,4},{4,5},{5,6},{6,7},{7,8},{8,9},{9,10},{10,1... | collective-permute-start | bytes 49160 | tf_op jit(solution)/shard_map/ppermute | solution.py:17
  108.0 5.6 %collective-permute-start.10 = (f32[32,128]{1,0:T(8,128)S(1)}, f32[32,128]{1,0:T(8,128)S(1)}, u32[]{:S(2)}, u32[]{:S(2)}) collective-permute-start(f32[32,128]{1,0:T(8,128)S(1)} %bitcast.79), channel_id=1, source_target_pairs={{1,0},{2,1},{3,2},{4,3},{5,4},{6,5},{7,6},{8,7},{9,8},{10,9},{11,1... | collective-permute-start | bytes 49160 | tf_op jit(solution)/shard_map/ppermute | solution.py:17
  109.3 4.3 %collective-permute-start.9 = (f32[1,64,128]{2,1,0:T(8,128)S(1)}, f32[1,64,128]{2,1,0:T(8,128)S(1)}, u32[]{:S(2)}, u32[]{:S(2)}) collective-permute-start(f32[1,64,128]{2,1,0:T(8,128)S(1)} %get-tuple-element.68), channel_id=1, source_target_pairs={{0,16},{16,32},{32,48},{48,64},{64,80},{80,96},{96,112},{1,17},{17... | collective-permute-start | bytes 98312 | tf_op jit(solution)/shard_map/ppermute | solution.py:18
  111.1 5.0 %collective-permute-start.8 = (f32[1,64,128]{2,1,0:T(8,128)S(1)}, f32[1,64,128]{2,1,0:T(8,128)S(1)}, u32[]{:S(2)}, u32[]{:S(2)}) collective-permute-start(f32[1,64,128]{2,1,0:T(8,128)S(1)} %get-tuple-element.69), channel_id=1, source_target_pairs={{16,0},{32,16},{48,32},{64,48},{80,64},{96,80},{112,96},{17,1},{33... | collective-permute-start | bytes 98312 | tf_op jit(solution)/shard_map/ppermute | solution.py:18
  116.7 16.6 %copy-start.2 = (f32[32,64,128]{2,1,0:T(8,128)}, f32[32,64,128]{2,1,0:T(8,128)S(1)}, u32[]{:S(2)}) copy-start(f32[32,64,128]{2,1,0:T(8,128)S(1)} %get-tuple-element.50) | copy-start | bytes 3145732
  116.8 12.0 %collective-permute-start.15 = (f32[32,128]{1,0:T(8,128)S(1)}, f32[32,128]{1,0:T(8,128)S(1)}, u32[]{:S(2)}, u32[]{:S(2)}) collective-permute-start(f32[32,128]{1,0:T(8,128)S(1)} %bitcast.82), channel_id=1, source_target_pairs={{0,1},{1,2},{2,3},{3,4},{4,5},{5,6},{6,7},{7,8},{8,9},{9,10},{10,1... | collective-permute-start | bytes 49160 | tf_op jit(solution)/shard_map/ppermute | solution.py:17
  121.4 7.4 %collective-permute-start.14 = (f32[32,128]{1,0:T(8,128)S(1)}, f32[32,128]{1,0:T(8,128)S(1)}, u32[]{:S(2)}, u32[]{:S(2)}) collective-permute-start(f32[32,128]{1,0:T(8,128)S(1)} %bitcast.80), channel_id=1, source_target_pairs={{1,0},{2,1},{3,2},{4,3},{5,4},{6,5},{7,6},{8,7},{9,8},{10,9},{11,1... | collective-permute-start | bytes 49160 | tf_op jit(solution)/shard_map/ppermute | solution.py:17
  122.7 6.1 %collective-permute-start.13 = (f32[1,64,128]{2,1,0:T(8,128)S(1)}, f32[1,64,128]{2,1,0:T(8,128)S(1)}, u32[]{:S(2)}, u32[]{:S(2)}) collective-permute-start(f32[1,64,128]{2,1,0:T(8,128)S(1)} %get-tuple-element.62), channel_id=1, source_target_pairs={{0,16},{16,32},{32,48},{48,64},{64,80},{80,96},{96,112},{1,17},{17... | collective-permute-start | bytes 98312 | tf_op jit(solution)/shard_map/ppermute | solution.py:18
  126.9 3.1 %collective-permute-start.12 = (f32[1,64,128]{2,1,0:T(8,128)S(1)}, f32[1,64,128]{2,1,0:T(8,128)S(1)}, u32[]{:S(2)}, u32[]{:S(2)}) collective-permute-start(f32[1,64,128]{2,1,0:T(8,128)S(1)} %get-tuple-element.63), channel_id=1, source_target_pairs={{16,0},{32,16},{48,32},{64,48},{80,64},{96,80},{112,96},{17,1},{33... | collective-permute-start | bytes 98312 | tf_op jit(solution)/shard_map/ppermute | solution.py:18

commit v16 on v14

--- a/solution.py
+++ b/solution.py
@@ -114,8 +114,10 @@
 
     def transpose_groups(x):
         for m, first, second in swaps:
-            a = pltpu.roll(pltpu.roll(x, 8 - m, 0), 8 * m, 1)
-            b = pltpu.roll(pltpu.roll(x, m, 0), 128 - 8 * m, 1)
+            down = pltpu.roll(x, 8 - m, 0)
+            up = down if m == 4 else pltpu.roll(x, m, 0)
+            a = pltpu.roll(down, 8 * m, 1)
+            b = pltpu.roll(up, 128 - 8 * m, 1)
             x = jnp.where(first, a, jnp.where(second, b, x))
         return x
 

time: 184 us -> 184 us (level)
  no operation moved by 1% of the time
where the time goes in v16:
time: 184 us; the launch traced here: 183 us
  starting transfers between devices  48.2 us (26%)
  blocking collectives  38.1 us (21%)
  waiting for transfers between devices  37.7 us (20%)
  other arithmetic  18.6 us (10%)
  local copies, waits for them, and re-layouts  15.6 us (8%)
  Pallas kernels  13.3 us (7%)
  between operations  6.09 us (3%)
  matrix products  5.6 us (3%)
    psum x4, blocking collectives, over_axes(): shard = lax.psum(shard, axis)  38.1 us
    all_to_all x1, waiting for transfers between devices, body(): lax.all_to_all(payload, GX_GY, split_axis=0, concat_axis=0, tiled=True)  32.3 us
    ppermute x8, starting transfers between devices, shifted(): return lax.ppermute(flat, axis, pairs).reshape(piece.shape)  20.8 us
    ppermute x8, starting transfers between devices, shifted(): return lax.ppermute(piece, axis, pairs)  15.7 us
    pallas_call x1, Pallas kernels, to_grid(): pl.pallas_call(relayout_kernel, out_shape=jax.ShapeDtypeStruct((3, span_x...  13.3 us
    all_to_all x1, starting transfers between devices, body(): lax.all_to_all(payload, GX_GY, split_axis=0, concat_axis=0, tiled=True)  11.6 us
    ppermute x8, waiting for transfers between devices, shifted(): return lax.ppermute(piece, axis, pairs)  4.54 us
  transfers between devices with their start and end apart: 17, of which 5 were waited for; matrix products, arithmetic and copies ran while one was open for 7% of the time, Pallas kernels for 7%

profile of v16, /device:TPU:0, one launch (start us, length us, event | category | flops | bytes accessed | tf_op | source)
XLA Modules:
  0.0 183.1 jit_solution(17759947731608869111)
XLA Ops:
  1.9 2.0 %broadcast_select_fusion = (bf16[256]{0:T(256)(128)(2,1)S(1)}, bf16[256]{0:T(256)(128)(2,1)S(1)}) fusion(pred[]{:T(512)} %compare_reduce_fusion, s32[256]{0:T(256)} %param.11, pred[]{:T(512)} %compare_reduce_fusion.1), kind=kLoop, calls=%fused_computation.106 | loop fusion | flops 5888 | bytes 2050 | tf_op jit(solution)/shard_map/select.12
  7.0 2.1 %convolution_convert_fusion = bf16[128,6,1664]{2,0,1:T(8,128)(2,1)S(1)} fusion(bf16[256,128]{1,0:T(8,128)(2,1)S(1)} %scatter.9, bf16[256,1536]{1,0:T(8,128)(2,1)} %param.9, s32[128,6]{0,1:T(8,128)S(1)} %iota_add_fusion, s32[256]{0:T(256)S(1)} %multiply_add_fusion.1), kind=kOutput, calls=%fused_computation | convolution fusion | flops 657489920 | bytes 3411968 | tf_op jit(solution)/shard_map/pck,kj->pcj/dot_general | solution.py:74
  9.1 3.2 %copy.32 = bf16[128,6,1664]{2,1,0:T(8,128)(2,1)} copy(bf16[128,6,1664]{2,0,1:T(8,128)(2,1)S(1)} %convolution_convert_fusion) | data formatting | bytes 5111808 | tf_op jit(solution)/shard_map/convert_element_type | solution.py:77
  12.3 11.6 %all-to-all-start = ((bf16[128,6,1664]{2,1,0:T(8,128)(2,1)}), bf16[128,6,1664]{2,1,0:T(8,128)(2,1)}, u32[]{:S(2)}, u32[]{:S(2)}) async-start(bf16[128,6,1664]{2,1,0:T(8,128)(2,1)} %copy.32), calls=%async_computation | async-start | bytes 6815744 | tf_op jit(solution)/shard_map/all_to_all | solution.py:159
  25.3 3.7 %collective-permute-start.7 = (f32[32,128]{1,0:T(8,128)S(1)}, f32[32,128]{1,0:T(8,128)S(1)}, u32[]{:S(2)}, u32[]{:S(2)}) collective-permute-start(f32[32,128]{1,0:T(8,128)S(1)} %bitcast.84), channel_id=1, source_target_pairs={{0,1},{1,2},{2,3},{3,4},{4,5},{5,6},{6,7},{7,8},{8,9},{9,10},{10,1... | collective-permute-start | bytes 49160 | tf_op jit(solution)/shard_map/ppermute | solution.py:17
  34.7 32.3 %all-to-all-done = bf16[128,6,1664]{2,1,0:T(8,128)(2,1)} async-done(((bf16[128,6,1664]{2,1,0:T(8,128)(2,1)}), bf16[128,6,1664]{2,1,0:T(8,128)(2,1)}, u32[]{:S(2)}, u32[]{:S(2)}) %all-to-all-start) | async-done | bytes 2555936 | tf_op jit(solution)/shard_map/all_to_all | solution.py:159
  68.3 2.1 %slice.271 = bf16[128,6,1536]{2,1,0:T(8,128)(2,1)S(1)} slice(bf16[128,6,1664]{2,1,0:T(8,128)(2,1)} %all-to-all-done), slice={[0:128], [0:6], [0:1536]} | slice | bytes 4718592 | tf_op jit(solution)/shard_map/slice | solution.py:170
  70.3 3.5 %convolution_bitcast_fusion.blk_ref = f32[512,1536]{1,0:T(8,128)} fusion(bf16[128,6,1536]{2,1,0:T(8,128)(2,1)S(1)} %slice.271, s32[128,6]{0,1:T(8,128)S(1)} %fusion.40), kind=kOutput, calls=%fused_computation.1 | convolution fusion | flops 1208352768 | bytes 5508096 | tf_op jit(solution)/shard_map/pcs,pcj->sj/dot_general | solution.py:167
  73.9 13.3 %shard_map.68 = f32[3,32,64,128]{3,2,1,0:T(8,128)} custom-call(f32[512,1536]{1,0:T(8,128)} %convolution_bitcast_fusion.blk_ref), custom_call_target="tpu_custom_call" | custom-call | flops 15728640 | bytes 6291456 | tf_op jit(solution)/shard_map/pallas_call | solution.py:145
  87.1 2.1 %slice_bitcast_fusion.2 = (f32[32,64,128]{2,1,0:T(8,128)S(1)}, f32[32,64,128]{2,1,0:T(8,128)S(1)}, f32[32,64,128]{2,1,0:T(8,128)S(1)}) fusion(f32[3,32,64,128]{3,2,1,0:T(8,128)} %shard_map.68), kind=kLoop, calls=%fused_computation.62 | loop fusion | bytes 6291456 | tf_op jit(solution)/shard_map/squeeze | solution.py:174
  90.0 2.9 %collective-permute-start.3 = (f32[32,128]{1,0:T(8,128)S(1)}, f32[32,128]{1,0:T(8,128)S(1)}, u32[]{:S(2)}, u32[]{:S(2)}) collective-permute-start(f32[32,128]{1,0:T(8,128)S(1)} %bitcast.86), channel_id=1, source_target_pairs={{0,1},{1,2},{2,3},{3,4},{4,5},{5,6},{6,7},{7,8},{8,9},{9,10},{10,1... | collective-permute-start | bytes 49160 | tf_op jit(solution)/shard_map/ppermute | solution.py:17
  95.6 3.0 %collective-permute-start.1 = (f32[1,64,128]{2,1,0:T(8,128)S(1)}, f32[1,64,128]{2,1,0:T(8,128)S(1)}, u32[]{:S(2)}, u32[]{:S(2)}) collective-permute-start(f32[1,64,128]{2,1,0:T(8,128)S(1)} %get-tuple-element.36), channel_id=1, source_target_pairs={{0,16},{16,32},{32,48},{48,64},{64,80},{80,96},{96,112},{1,17},{17... | collective-permute-start | bytes 98312 | tf_op jit(solution)/shard_map/ppermute | solution.py:18
  99.8 3.6 %fusion.45 = (f32[32,64,128]{2,1,0:T(8,128)S(1)}, f32[32,64,128]{2,1,0:T(8,128)S(1)}) fusion(f32[32,64,128]{2,1,0:T(8,128)S(1)} %copy-done.1, f32[32,64,127]{2,1,0:T(8,128)S(1)} %get-tuple-element.70, f32[32,64,127]{2,1,0:T(8,128)S(1)} %get-tuple-element.71, f32[34,64,128]{2,1,0:T(8,128)} %constant_dynamic-update-slice_fusion, ...), kind=kLoop, calls=%fused_computation.116 | loop fusion | flops 8126464 | bytes 11763712 | tf_op jit(solution)/shard_map/mul | solution.py:183
  103.4 4.5 %collective-permute-start.11 = (f32[32,128]{1,0:T(8,128)S(1)}, f32[32,128]{1,0:T(8,128)S(1)}, u32[]{:S(2)}, u32[]{:S(2)}) collective-permute-start(f32[32,128]{1,0:T(8,128)S(1)} %bitcast.89), channel_id=1, source_target_pairs={{0,1},{1,2},{2,3},{3,4},{4,5},{5,6},{6,7},{7,8},{8,9},{9,10},{10,1... | collective-permute-start | bytes 49160 | tf_op jit(solution)/shard_map/ppermute | solution.py:17
  113.6 2.4 %collective-permute-done.8 = f32[1,64,128]{2,1,0:T(8,128)S(1)} collective-permute-done((f32[1,64,128]{2,1,0:T(8,128)S(1)}, f32[1,64,128]{2,1,0:T(8,128)S(1)}, u32[]{:S(2)}, u32[]{:S(2)}) %collective-permute-start.8) | collective-permute-done | bytes 32800 | tf_op jit(solution)/shard_map/ppermute | solution.py:18
  116.8 4.5 %collective-permute-start.15 = (f32[32,128]{1,0:T(8,128)S(1)}, f32[32,128]{1,0:T(8,128)S(1)}, u32[]{:S(2)}, u32[]{:S(2)}) collective-permute-start(f32[32,128]{1,0:T(8,128)S(1)} %bitcast.90), channel_id=1, source_target_pairs={{0,1},{1,2},{2,3},{3,4},{4,5},{5,6},{6,7},{7,8},{8,9},{9,10},{10,1... | collective-permute-start | bytes 49160 | tf_op jit(solution)/shard_map/ppermute | solution.py:17
  122.7 4.3 %collective-permute-start.13 = (f32[1,64,128]{2,1,0:T(8,128)S(1)}, f32[1,64,128]{2,1,0:T(8,128)S(1)}, u32[]{:S(2)}, u32[]{:S(2)}) collective-permute-start(f32[1,64,128]{2,1,0:T(8,128)S(1)} %get-tuple-element.44), channel_id=1, source_target_pairs={{0,16},{16,32},{32,48},{48,64},{64,80},{80,96},{96,112},{1,17},{17... | collective-permute-start | bytes 98312 | tf_op jit(solution)/shard_map/ppermute | solution.py:18
  130.0 3.3 %multiply_reduce_fusion.3 = (f32[]{:T(128)}, f32[]{:T(128)}, f32[]{:T(128)}, f32[]{:T(128)}, f32[32,64,128]{2,1,0:T(8,128)}) fusion(f32[32,64,128]{2,1,0:T(8,128)S(1)} %get-tuple-element.34, f32[32,64,128]{2,1,0:T(8,128)S(1)} %copy-done.1, f32[32,64,128]{2,1,0:T(8,128)S(1)} %get-tuple-element.32, f32[32,64,128]{2,1,0:T(8,128)S(1)} %get-tuple-element.31, ...), kind=kLoop, calls=%fused_computation.69 | loop fusion | flops 8388604 | bytes 7421968 | tf_op jit(solution)/shard_map/reduce_sum | solution.py:190
  133.4 2.5 %pad_maximum_fusion.20 = f32[4]{0:T(128)S(1)} fusion(f32[1]{0:T(128)} %bitcast.33, f32[1]{0:T(128)} %bitcast.28, f32[1]{0:T(128)} %bitcast.27, f32[1]{0:T(128)} %bitcast.22), kind=kLoop, calls=%fused_computation.109 | loop fusion | flops 12 | bytes 32 | tf_op jit(solution)/shard_map/stack | solution.py:188
  135.9 10.9 %psum.28 = f32[4]{0:T(128)S(1)} all-reduce(f32[4]{0:T(128)S(1)} %pad_maximum_fusion.20), channel_id=1, replica_groups=mesh['gx_0'=4,'gx_1'=2,'gy_0'=4,'gy_1'=4] {'gx_0'}, use_global_device_ids=true, to_apply=%region_9.10 | all-reduce | flops 4 | bytes 32 | tf_op jit(solution)/shard_map/psum | solution.py:43
  146.8 2.5 %psum.29 = f32[4]{0:T(128)S(1)} all-reduce(f32[4]{0:T(128)S(1)} %psum.28), channel_id=1, replica_groups=mesh['gx_0'=4,'gx_1'=2,'gy_0'=4,'gy_1'=4] {'gx_1'}, use_global_device_ids=true, to_apply=%region_10.11 | all-reduce | flops 4 | bytes 32 | tf_op jit(solution)/shard_map/psum | solution.py:43
  149.2 17.0 %psum.30 = f32[4]{0:T(128)S(1)} all-reduce(f32[4]{0:T(128)S(1)} %psum.29), channel_id=1, replica_groups=mesh['gx_0'=4,'gx_1'=2,'gy_0'=4,'gy_1'=4] {'gy_0'}, use_global_device_ids=true, to_apply=%region_11.12 | all-reduce | flops 4 | bytes 32 | tf_op jit(solution)/shard_map/psum | solution.py:43
  166.2 7.7 %psum.31 = f32[4]{0:T(128)S(1)} all-reduce(f32[4]{0:T(128)S(1)} %psum.30), channel_id=1, replica_groups=mesh['gx_0'=4,'gx_1'=2,'gy_0'=4,'gy_1'=4] {'gy_1'}, use_global_device_ids=true, to_apply=%region_12.13 | all-reduce | flops 4 | bytes 32 | tf_op jit(solution)/shard_map/psum | solution.py:43
  179.6 3.5 %multiply_subtract_fusion = (f32[32,64,128]{2,1,0:T(8,128)}, f32[32,64,128]{2,1,0:T(8,128)}) fusion(f32[32,64,128]{2,1,0:T(8,128)} %copy-done.2, f32[32,64,128]{2,1,0:T(8,128)} %get-tuple-element.30, f32[32,64,128]{2,1,0:T(8,128)S(1)} %get-tuple-element.34, f32[]{:T(128)S(6)} %div.34, f32[]{:T(128)S(6)} %div.35, f32[]{:T(128)S(6)} %div.33, ...), kind=kLoop, calls=%fused_computation.63 | loop fusion | flops 4718592 | bytes 7340044 | tf_op jit(solution)/shard_map/sub | solution.py:210
  (69 shorter events, 28.6 us)
Async XLA Ops:
  12.3 11.7 %copy-start = (f32[32,64,128]{2,1,0:T(8,128)S(1)}, f32[32,64,128]{2,1,0:T(8,128)}, u32[]{:S(2)}) copy-start(f32[32,64,128]{2,1,0:T(8,128)} %param.13) | copy-start | bytes 3145732
  12.3 54.7 %all-to-all-start = ((bf16[128,6,1664]{2,1,0:T(8,128)(2,1)}), bf16[128,6,1664]{2,1,0:T(8,128)(2,1)}, u32[]{:S(2)}, u32[]{:S(2)}) async-start(bf16[128,6,1664]{2,1,0:T(8,128)(2,1)} %copy.32), calls=%async_computation | async-start | bytes 6815744 | tf_op jit(solution)/shard_map/all_to_all | solution.py:159
  24.0 7.6 %collective-permute-start.5 = (f32[1,64,128]{2,1,0:T(8,128)S(1)}, f32[1,64,128]{2,1,0:T(8,128)S(1)}, u32[]{:S(2)}, u32[]{:S(2)}) collective-permute-start(f32[1,64,128]{2,1,0:T(8,128)S(1)} %get-tuple-element.61), channel_id=1, source_target_pairs={{0,16},{16,32},{32,48},{48,64},{64,80},{80,96},{96,112},{1,17},{17... | collective-permute-start | bytes 98312 | tf_op jit(solution)/shard_map/ppermute | solution.py:18
  25.3 70.2 %collective-permute-start.7 = (f32[32,128]{1,0:T(8,128)S(1)}, f32[32,128]{1,0:T(8,128)S(1)}, u32[]{:S(2)}, u32[]{:S(2)}) collective-permute-start(f32[32,128]{1,0:T(8,128)S(1)} %bitcast.84), channel_id=1, source_target_pairs={{0,1},{1,2},{2,3},{3,4},{4,5},{5,6},{6,7},{7,8},{8,9},{9,10},{10,1... | collective-permute-start | bytes 49160 | tf_op jit(solution)/shard_map/ppermute | solution.py:17
  29.0 70.4 %collective-permute-start.6 = (f32[32,128]{1,0:T(8,128)S(1)}, f32[32,128]{1,0:T(8,128)S(1)}, u32[]{:S(2)}, u32[]{:S(2)}) collective-permute-start(f32[32,128]{1,0:T(8,128)S(1)} %bitcast.83), channel_id=1, source_target_pairs={{1,0},{2,1},{3,2},{4,3},{5,4},{6,5},{7,6},{8,7},{9,8},{10,9},{11,1... | collective-permute-start | bytes 49160 | tf_op jit(solution)/shard_map/ppermute | solution.py:17
  30.3 3.8 %collective-permute-start.4 = (f32[1,64,128]{2,1,0:T(8,128)S(1)}, f32[1,64,128]{2,1,0:T(8,128)S(1)}, u32[]{:S(2)}, u32[]{:S(2)}) collective-permute-start(f32[1,64,128]{2,1,0:T(8,128)S(1)} %get-tuple-element.60), channel_id=1, source_target_pairs={{16,0},{32,16},{48,32},{64,48},{80,64},{96,80},{112,96},{17,1},{33... | collective-permute-start | bytes 98312 | tf_op jit(solution)/shard_map/ppermute | solution.py:18
  90.0 9.4 %collective-permute-start.3 = (f32[32,128]{1,0:T(8,128)S(1)}, f32[32,128]{1,0:T(8,128)S(1)}, u32[]{:S(2)}, u32[]{:S(2)}) collective-permute-start(f32[32,128]{1,0:T(8,128)S(1)} %bitcast.86), channel_id=1, source_target_pairs={{0,1},{1,2},{2,3},{3,4},{4,5},{5,6},{6,7},{7,8},{8,9},{9,10},{10,1... | collective-permute-start | bytes 49160 | tf_op jit(solution)/shard_map/ppermute | solution.py:17
  92.9 6.5 %collective-permute-start.2 = (f32[32,128]{1,0:T(8,128)S(1)}, f32[32,128]{1,0:T(8,128)S(1)}, u32[]{:S(2)}, u32[]{:S(2)}) collective-permute-start(f32[32,128]{1,0:T(8,128)S(1)} %bitcast.85), channel_id=1, source_target_pairs={{1,0},{2,1},{3,2},{4,3},{5,4},{6,5},{7,6},{8,7},{9,8},{10,9},{11,1... | collective-permute-start | bytes 49160 | tf_op jit(solution)/shard_map/ppermute | solution.py:17
  94.2 5.2 %collective-permute-start = (f32[1,64,128]{2,1,0:T(8,128)S(1)}, f32[1,64,128]{2,1,0:T(8,128)S(1)}, u32[]{:S(2)}, u32[]{:S(2)}) collective-permute-start(f32[1,64,128]{2,1,0:T(8,128)S(1)} %get-tuple-element.35), channel_id=1, source_target_pairs={{16,0},{32,16},{48,32},{64,48},{80,64},{96,80},{112,96},{17,1},{33... | collective-permute-start | bytes 98312 | tf_op jit(solution)/shard_map/ppermute | solution.py:18
  95.6 3.9 %collective-permute-start.1 = (f32[1,64,128]{2,1,0:T(8,128)S(1)}, f32[1,64,128]{2,1,0:T(8,128)S(1)}, u32[]{:S(2)}, u32[]{:S(2)}) collective-permute-start(f32[1,64,128]{2,1,0:T(8,128)S(1)} %get-tuple-element.36), channel_id=1, source_target_pairs={{0,16},{16,32},{32,48},{48,64},{64,80},{80,96},{96,112},{1,17},{17... | collective-permute-start | bytes 98312 | tf_op jit(solution)/shard_map/ppermute | solution.py:18
  98.6 1.2 copy-start.1
  103.4 9.3 %collective-permute-start.11 = (f32[32,128]{1,0:T(8,128)S(1)}, f32[32,128]{1,0:T(8,128)S(1)}, u32[]{:S(2)}, u32[]{:S(2)}) collective-permute-start(f32[32,128]{1,0:T(8,128)S(1)} %bitcast.89), channel_id=1, source_target_pairs={{0,1},{1,2},{2,3},{3,4},{4,5},{5,6},{6,7},{7,8},{8,9},{9,10},{10,1... | collective-permute-start | bytes 49160 | tf_op jit(solution)/shard_map/ppermute | solution.py:17
  108.0 5.6 %collective-permute-start.10 = (f32[32,128]{1,0:T(8,128)S(1)}, f32[32,128]{1,0:T(8,128)S(1)}, u32[]{:S(2)}, u32[]{:S(2)}) collective-permute-start(f32[32,128]{1,0:T(8,128)S(1)} %bitcast.87), channel_id=1, source_target_pairs={{1,0},{2,1},{3,2},{4,3},{5,4},{6,5},{7,6},{8,7},{9,8},{10,9},{11,1... | collective-permute-start | bytes 49160 | tf_op jit(solution)/shard_map/ppermute | solution.py:17
  109.3 4.3 %collective-permute-start.9 = (f32[1,64,128]{2,1,0:T(8,128)S(1)}, f32[1,64,128]{2,1,0:T(8,128)S(1)}, u32[]{:S(2)}, u32[]{:S(2)}) collective-permute-start(f32[1,64,128]{2,1,0:T(8,128)S(1)} %get-tuple-element.50), channel_id=1, source_target_pairs={{0,16},{16,32},{32,48},{48,64},{64,80},{80,96},{96,112},{1,17},{17... | collective-permute-start | bytes 98312 | tf_op jit(solution)/shard_map/ppermute | solution.py:18
  111.1 5.0 %collective-permute-start.8 = (f32[1,64,128]{2,1,0:T(8,128)S(1)}, f32[1,64,128]{2,1,0:T(8,128)S(1)}, u32[]{:S(2)}, u32[]{:S(2)}) collective-permute-start(f32[1,64,128]{2,1,0:T(8,128)S(1)} %get-tuple-element.51), channel_id=1, source_target_pairs={{16,0},{32,16},{48,32},{64,48},{80,64},{96,80},{112,96},{17,1},{33... | collective-permute-start | bytes 98312 | tf_op jit(solution)/shard_map/ppermute | solution.py:18
  116.8 16.6 %copy-start.2 = (f32[32,64,128]{2,1,0:T(8,128)}, f32[32,64,128]{2,1,0:T(8,128)S(1)}, u32[]{:S(2)}) copy-start(f32[32,64,128]{2,1,0:T(8,128)S(1)} %get-tuple-element.32) | copy-start | bytes 3145732
  116.8 12.0 %collective-permute-start.15 = (f32[32,128]{1,0:T(8,128)S(1)}, f32[32,128]{1,0:T(8,128)S(1)}, u32[]{:S(2)}, u32[]{:S(2)}) collective-permute-start(f32[32,128]{1,0:T(8,128)S(1)} %bitcast.90), channel_id=1, source_target_pairs={{0,1},{1,2},{2,3},{3,4},{4,5},{5,6},{6,7},{7,8},{8,9},{9,10},{10,1... | collective-permute-start | bytes 49160 | tf_op jit(solution)/shard_map/ppermute | solution.py:17
  121.4 7.4 %collective-permute-start.14 = (f32[32,128]{1,0:T(8,128)S(1)}, f32[32,128]{1,0:T(8,128)S(1)}, u32[]{:S(2)}, u32[]{:S(2)}) collective-permute-start(f32[32,128]{1,0:T(8,128)S(1)} %bitcast.88), channel_id=1, source_target_pairs={{1,0},{2,1},{3,2},{4,3},{5,4},{6,5},{7,6},{8,7},{9,8},{10,9},{11,1... | collective-permute-start | bytes 49160 | tf_op jit(solution)/shard_map/ppermute | solution.py:17
  122.7 6.1 %collective-permute-start.13 = (f32[1,64,128]{2,1,0:T(8,128)S(1)}, f32[1,64,128]{2,1,0:T(8,128)S(1)}, u32[]{:S(2)}, u32[]{:S(2)}) collective-permute-start(f32[1,64,128]{2,1,0:T(8,128)S(1)} %get-tuple-element.44), channel_id=1, source_target_pairs={{0,16},{16,32},{32,48},{48,64},{64,80},{80,96},{96,112},{1,17},{17... | collective-permute-start | bytes 98312 | tf_op jit(solution)/shard_map/ppermute | solution.py:18
  126.9 3.1 %collective-permute-start.12 = (f32[1,64,128]{2,1,0:T(8,128)S(1)}, f32[1,64,128]{2,1,0:T(8,128)S(1)}, u32[]{:S(2)}, u32[]{:S(2)}) collective-permute-start(f32[1,64,128]{2,1,0:T(8,128)S(1)} %get-tuple-element.45), channel_id=1, source_target_pairs={{16,0},{32,16},{48,32},{64,48},{80,64},{96,80},{112,96},{17,1},{33... | collective-permute-start | bytes 98312 | tf_op jit(solution)/shard_map/ppermute | solution.py:18

commit v17 on v16

--- a/solution.py
+++ b/solution.py
@@ -121,23 +121,24 @@
             x = jnp.where(first, a, jnp.where(second, b, x))
         return x
 
-    def step(ly, carry):
+    def step(i, carry):
+        ly = i // 3
+        c = i % 3
         row = pl.multiple_of(ly * 16, 16)
         y = pl.multiple_of(ly * 8, 8)
-        top = blk_ref[pl.ds(row, 8), :]
-        bottom = blk_ref[pl.ds(row + 8, 8), :]
-        for c in range(3):
-            for uh in range(4):
-                col = (c * 4 + uh) * 128
-                s0 = top[:, col:col + 128]
-                s1 = bottom[:, col:col + 128]
-                u0 = jnp.where(low_half, s0, pltpu.roll(s1, 64, 1))
-                u1 = jnp.where(low_half, pltpu.roll(s0, 64, 1), s1)
-                out_ref[c, uh * 2, pl.ds(y, 8), :] = transpose_groups(u0)
-                out_ref[c, uh * 2 + 1, pl.ds(y, 8), :] = transpose_groups(u1)
+        col = pl.multiple_of(c * 512, 512)
+        top = blk_ref[pl.ds(row, 8), pl.ds(col, 512)]
+        bottom = blk_ref[pl.ds(row + 8, 8), pl.ds(col, 512)]
+        for uh in range(4):
+            s0 = top[:, uh * 128:(uh + 1) * 128]
+            s1 = bottom[:, uh * 128:(uh + 1) * 128]
+            u0 = jnp.where(low_half, s0, pltpu.roll(s1, 64, 1))
+            u1 = jnp.where(low_half, pltpu.roll(s0, 64, 1), s1)
+            out_ref[c, uh * 2, pl.ds(y, 8), :] = transpose_groups(u0)
+            out_ref[c, uh * 2 + 1, pl.ds(y, 8), :] = transpose_groups(u1)
         return carry
 
-    lax.fori_loop(0, 8, step, 0)
+    lax.fori_loop(0, 24, step, 0)
 
 
 def to_grid(blocks, span_x, span_y, depth):

time: 184 us -> 204 us (1.11)
  Pallas kernels: 13.3 us -> 32.5 us
    pallas_call x1, Pallas kernels: 13.3 us -> 32.5 us  [to_grid(): pl.pallas_call(relayout_kernel, out_shape=jax.ShapeDtypeStruct((3, span_x...]
  transfers between devices with their start and end apart: 17 -> 17, of which waited for: 5 -> 5; matrix products, arithmetic and copies ran while one was open for 7% -> 7% of each run, Pallas kernels for 7% -> 16%
where the time goes in v17:
time: 204 us; the launch traced here: 202 us
  starting transfers between devices  48.2 us (24%)
  blocking collectives  38.1 us (19%)
  waiting for transfers between devices  37.7 us (18%)
  Pallas kernels  32.5 us (16%)
  other arithmetic  18.6 us (9%)
  local copies, waits for them, and re-layouts  15.6 us (8%)
  between operations  6.09 us (3%)
  matrix products  5.6 us (3%)
    psum x4, blocking collectives, over_axes(): shard = lax.psum(shard, axis)  38.1 us
    pallas_call x1, Pallas kernels, to_grid(): pl.pallas_call(relayout_kernel, out_shape=jax.ShapeDtypeStruct((3, span_x...  32.5 us
    all_to_all x1, waiting for transfers between devices, body(): lax.all_to_all(payload, GX_GY, split_axis=0, concat_axis=0, tiled=True)  32.3 us
    ppermute x8, starting transfers between devices, shifted(): return lax.ppermute(flat, axis, pairs).reshape(piece.shape)  20.8 us
    ppermute x8, starting transfers between devices, shifted(): return lax.ppermute(piece, axis, pairs)  15.7 us
    all_to_all x1, starting transfers between devices, body(): lax.all_to_all(payload, GX_GY, split_axis=0, concat_axis=0, tiled=True)  11.6 us
    ppermute x8, waiting for transfers between devices, shifted(): return lax.ppermute(piece, axis, pairs)  4.54 us
  transfers between devices with their start and end apart: 17, of which 5 were waited for; matrix products, arithmetic and copies ran while one was open for 7% of the time, Pallas kernels for 16%

profile of v17, /device:TPU:0, one launch (start us, length us, event | category | flops | bytes accessed | tf_op | source)
XLA Modules:
  0.0 202.4 jit_solution(8568604943021918128)
XLA Ops:
  1.9 2.0 broadcast_select_fusion
  7.0 2.1 %convolution_convert_fusion = bf16[128,6,1664]{2,0,1:T(8,128)(2,1)S(1)} fusion(bf16[256,128]{1,0:T(8,128)(2,1)S(1)} %scatter.9, bf16[256,1536]{1,0:T(8,128)(2,1)} %param.9, s32[128,6]{0,1:T(8,128)S(1)} %iota_add_fusion, s32[256]{0:T(256)S(1)} %multiply_add_fusion.1), kind=kOutput, calls=%fused_computation | convolution fusion | flops 657489920 | bytes 3411968 | tf_op jit(solution)/shard_map/pck,kj->pcj/dot_general | solution.py:74
  9.1 3.2 %copy.32 = bf16[128,6,1664]{2,1,0:T(8,128)(2,1)} copy(bf16[128,6,1664]{2,0,1:T(8,128)(2,1)S(1)} %convolution_convert_fusion) | data formatting | bytes 5111808 | tf_op jit(solution)/shard_map/convert_element_type | solution.py:77
  12.3 11.6 %all-to-all-start = ((bf16[128,6,1664]{2,1,0:T(8,128)(2,1)}), bf16[128,6,1664]{2,1,0:T(8,128)(2,1)}, u32[]{:S(2)}, u32[]{:S(2)}) async-start(bf16[128,6,1664]{2,1,0:T(8,128)(2,1)} %copy.32), calls=%async_computation | async-start | bytes 6815744 | tf_op jit(solution)/shard_map/all_to_all | solution.py:160
  25.3 3.7 %collective-permute-start.7 = (f32[32,128]{1,0:T(8,128)S(1)}, f32[32,128]{1,0:T(8,128)S(1)}, u32[]{:S(2)}, u32[]{:S(2)}) collective-permute-start(f32[32,128]{1,0:T(8,128)S(1)} %bitcast.84), channel_id=1, source_target_pairs={{0,1},{1,2},{2,3},{3,4},{4,5},{5,6},{6,7},{7,8},{8,9},{9,10},{10,1... | collective-permute-start | bytes 49160 | tf_op jit(solution)/shard_map/ppermute | solution.py:17
  34.7 32.3 %all-to-all-done = bf16[128,6,1664]{2,1,0:T(8,128)(2,1)} async-done(((bf16[128,6,1664]{2,1,0:T(8,128)(2,1)}), bf16[128,6,1664]{2,1,0:T(8,128)(2,1)}, u32[]{:S(2)}, u32[]{:S(2)}) %all-to-all-start) | async-done | bytes 2555936 | tf_op jit(solution)/shard_map/all_to_all | solution.py:160
  68.3 2.1 %slice.271 = bf16[128,6,1536]{2,1,0:T(8,128)(2,1)S(1)} slice(bf16[128,6,1664]{2,1,0:T(8,128)(2,1)} %all-to-all-done), slice={[0:128], [0:6], [0:1536]} | slice | bytes 4718592 | tf_op jit(solution)/shard_map/slice | solution.py:171
  70.3 3.5 %convolution_bitcast_fusion.blk_ref = f32[512,1536]{1,0:T(8,128)} fusion(bf16[128,6,1536]{2,1,0:T(8,128)(2,1)S(1)} %slice.271, s32[128,6]{0,1:T(8,128)S(1)} %fusion.40), kind=kOutput, calls=%fused_computation.1 | convolution fusion | flops 1208352768 | bytes 5508096 | tf_op jit(solution)/shard_map/pcs,pcj->sj/dot_general | solution.py:168
  73.9 32.5 %shard_map.68 = f32[3,32,64,128]{3,2,1,0:T(8,128)} custom-call(f32[512,1536]{1,0:T(8,128)} %convolution_bitcast_fusion.blk_ref), custom_call_target="tpu_custom_call" | custom-call | flops 15728640 | bytes 6291456 | tf_op jit(solution)/shard_map/pallas_call | solution.py:146
  106.4 2.1 %slice_bitcast_fusion.2 = (f32[32,64,128]{2,1,0:T(8,128)S(1)}, f32[32,64,128]{2,1,0:T(8,128)S(1)}, f32[32,64,128]{2,1,0:T(8,128)S(1)}) fusion(f32[3,32,64,128]{3,2,1,0:T(8,128)} %shard_map.68), kind=kLoop, calls=%fused_computation.62 | loop fusion | bytes 6291456 | tf_op jit(solution)/shard_map/squeeze | solution.py:175
  109.3 2.9 %collective-permute-start.3 = (f32[32,128]{1,0:T(8,128)S(1)}, f32[32,128]{1,0:T(8,128)S(1)}, u32[]{:S(2)}, u32[]{:S(2)}) collective-permute-start(f32[32,128]{1,0:T(8,128)S(1)} %bitcast.86), channel_id=1, source_target_pairs={{0,1},{1,2},{2,3},{3,4},{4,5},{5,6},{6,7},{7,8},{8,9},{9,10},{10,1... | collective-permute-start | bytes 49160 | tf_op jit(solution)/shard_map/ppermute | solution.py:17
  114.8 3.0 %collective-permute-start.1 = (f32[1,64,128]{2,1,0:T(8,128)S(1)}, f32[1,64,128]{2,1,0:T(8,128)S(1)}, u32[]{:S(2)}, u32[]{:S(2)}) collective-permute-start(f32[1,64,128]{2,1,0:T(8,128)S(1)} %get-tuple-element.36), channel_id=1, source_target_pairs={{0,16},{16,32},{32,48},{48,64},{64,80},{80,96},{96,112},{1,17},{17... | collective-permute-start | bytes 98312 | tf_op jit(solution)/shard_map/ppermute | solution.py:18
  119.1 3.6 %fusion.45 = (f32[32,64,128]{2,1,0:T(8,128)S(1)}, f32[32,64,128]{2,1,0:T(8,128)S(1)}) fusion(f32[32,64,128]{2,1,0:T(8,128)S(1)} %copy-done.1, f32[32,64,127]{2,1,0:T(8,128)S(1)} %get-tuple-element.70, f32[32,64,127]{2,1,0:T(8,128)S(1)} %get-tuple-element.71, f32[34,64,128]{2,1,0:T(8,128)} %constant_dynamic-update-slice_fusion, ...), kind=kLoop, calls=%fused_computation.116 | loop fusion | flops 8126464 | bytes 11763712 | tf_op jit(solution)/shard_map/mul | solution.py:184
  122.7 4.5 %collective-permute-start.11 = (f32[32,128]{1,0:T(8,128)S(1)}, f32[32,128]{1,0:T(8,128)S(1)}, u32[]{:S(2)}, u32[]{:S(2)}) collective-permute-start(f32[32,128]{1,0:T(8,128)S(1)} %bitcast.89), channel_id=1, source_target_pairs={{0,1},{1,2},{2,3},{3,4},{4,5},{5,6},{6,7},{7,8},{8,9},{9,10},{10,1... | collective-permute-start | bytes 49160 | tf_op jit(solution)/shard_map/ppermute | solution.py:17
  132.9 2.4 %collective-permute-done.8 = f32[1,64,128]{2,1,0:T(8,128)S(1)} collective-permute-done((f32[1,64,128]{2,1,0:T(8,128)S(1)}, f32[1,64,128]{2,1,0:T(8,128)S(1)}, u32[]{:S(2)}, u32[]{:S(2)}) %collective-permute-start.8) | collective-permute-done | bytes 32800 | tf_op jit(solution)/shard_map/ppermute | solution.py:18
  136.1 4.5 %collective-permute-start.15 = (f32[32,128]{1,0:T(8,128)S(1)}, f32[32,128]{1,0:T(8,128)S(1)}, u32[]{:S(2)}, u32[]{:S(2)}) collective-permute-start(f32[32,128]{1,0:T(8,128)S(1)} %bitcast.90), channel_id=1, source_target_pairs={{0,1},{1,2},{2,3},{3,4},{4,5},{5,6},{6,7},{7,8},{8,9},{9,10},{10,1... | collective-permute-start | bytes 49160 | tf_op jit(solution)/shard_map/ppermute | solution.py:17
  142.0 4.3 %collective-permute-start.13 = (f32[1,64,128]{2,1,0:T(8,128)S(1)}, f32[1,64,128]{2,1,0:T(8,128)S(1)}, u32[]{:S(2)}, u32[]{:S(2)}) collective-permute-start(f32[1,64,128]{2,1,0:T(8,128)S(1)} %get-tuple-element.44), channel_id=1, source_target_pairs={{0,16},{16,32},{32,48},{48,64},{64,80},{80,96},{96,112},{1,17},{17... | collective-permute-start | bytes 98312 | tf_op jit(solution)/shard_map/ppermute | solution.py:18
  149.3 3.3 %multiply_reduce_fusion.3 = (f32[]{:T(128)}, f32[]{:T(128)}, f32[]{:T(128)}, f32[]{:T(128)}, f32[32,64,128]{2,1,0:T(8,128)}) fusion(f32[32,64,128]{2,1,0:T(8,128)S(1)} %get-tuple-element.34, f32[32,64,128]{2,1,0:T(8,128)S(1)} %copy-done.1, f32[32,64,128]{2,1,0:T(8,128)S(1)} %get-tuple-element.32, f32[32,64,128]{2,1,0:T(8,128)S(1)} %get-tuple-element.31, ...), kind=kLoop, calls=%fused_computation.69 | loop fusion | flops 8388604 | bytes 7421968 | tf_op jit(solution)/shard_map/reduce_sum | solution.py:191
  152.6 2.5 %pad_maximum_fusion.20 = f32[4]{0:T(128)S(1)} fusion(f32[1]{0:T(128)} %bitcast.33, f32[1]{0:T(128)} %bitcast.28, f32[1]{0:T(128)} %bitcast.27, f32[1]{0:T(128)} %bitcast.22), kind=kLoop, calls=%fused_computation.109 | loop fusion | flops 12 | bytes 32 | tf_op jit(solution)/shard_map/stack | solution.py:189
  155.1 10.9 %psum.28 = f32[4]{0:T(128)S(1)} all-reduce(f32[4]{0:T(128)S(1)} %pad_maximum_fusion.20), channel_id=1, replica_groups=mesh['gx_0'=4,'gx_1'=2,'gy_0'=4,'gy_1'=4] {'gx_0'}, use_global_device_ids=true, to_apply=%region_9.10 | all-reduce | flops 4 | bytes 32 | tf_op jit(solution)/shard_map/psum | solution.py:43
  166.0 2.5 %psum.29 = f32[4]{0:T(128)S(1)} all-reduce(f32[4]{0:T(128)S(1)} %psum.28), channel_id=1, replica_groups=mesh['gx_0'=4,'gx_1'=2,'gy_0'=4,'gy_1'=4] {'gx_1'}, use_global_device_ids=true, to_apply=%region_10.11 | all-reduce | flops 4 | bytes 32 | tf_op jit(solution)/shard_map/psum | solution.py:43
  168.5 17.0 %psum.30 = f32[4]{0:T(128)S(1)} all-reduce(f32[4]{0:T(128)S(1)} %psum.29), channel_id=1, replica_groups=mesh['gx_0'=4,'gx_1'=2,'gy_0'=4,'gy_1'=4] {'gy_0'}, use_global_device_ids=true, to_apply=%region_11.12 | all-reduce | flops 4 | bytes 32 | tf_op jit(solution)/shard_map/psum | solution.py:43
  185.5 7.7 %psum.31 = f32[4]{0:T(128)S(1)} all-reduce(f32[4]{0:T(128)S(1)} %psum.30), channel_id=1, replica_groups=mesh['gx_0'=4,'gx_1'=2,'gy_0'=4,'gy_1'=4] {'gy_1'}, use_global_device_ids=true, to_apply=%region_12.13 | all-reduce | flops 4 | bytes 32 | tf_op jit(solution)/shard_map/psum | solution.py:43
  198.9 3.5 %multiply_subtract_fusion = (f32[32,64,128]{2,1,0:T(8,128)}, f32[32,64,128]{2,1,0:T(8,128)}) fusion(f32[32,64,128]{2,1,0:T(8,128)} %copy-done.2, f32[32,64,128]{2,1,0:T(8,128)} %get-tuple-element.30, f32[32,64,128]{2,1,0:T(8,128)S(1)} %get-tuple-element.34, f32[]{:T(128)S(6)} %div.34, f32[]{:T(128)S(6)} %div.35, f32[]{:T(128)S(6)} %div.33, ...), kind=kLoop, calls=%fused_computation.63 | loop fusion | flops 4718592 | bytes 7340044 | tf_op jit(solution)/shard_map/sub | solution.py:211
  (69 shorter events, 28.6 us)
Async XLA Ops:
  12.3 11.7 %copy-start = (f32[32,64,128]{2,1,0:T(8,128)S(1)}, f32[32,64,128]{2,1,0:T(8,128)}, u32[]{:S(2)}) copy-start(f32[32,64,128]{2,1,0:T(8,128)} %param.13) | copy-start | bytes 3145732
  12.3 54.7 %all-to-all-start = ((bf16[128,6,1664]{2,1,0:T(8,128)(2,1)}), bf16[128,6,1664]{2,1,0:T(8,128)(2,1)}, u32[]{:S(2)}, u32[]{:S(2)}) async-start(bf16[128,6,1664]{2,1,0:T(8,128)(2,1)} %copy.32), calls=%async_computation | async-start | bytes 6815744 | tf_op jit(solution)/shard_map/all_to_all | solution.py:160
  24.0 7.6 %collective-permute-start.5 = (f32[1,64,128]{2,1,0:T(8,128)S(1)}, f32[1,64,128]{2,1,0:T(8,128)S(1)}, u32[]{:S(2)}, u32[]{:S(2)}) collective-permute-start(f32[1,64,128]{2,1,0:T(8,128)S(1)} %get-tuple-element.61), channel_id=1, source_target_pairs={{0,16},{16,32},{32,48},{48,64},{64,80},{80,96},{96,112},{1,17},{17... | collective-permute-start | bytes 98312 | tf_op jit(solution)/shard_map/ppermute | solution.py:18
  25.3 89.5 %collective-permute-start.7 = (f32[32,128]{1,0:T(8,128)S(1)}, f32[32,128]{1,0:T(8,128)S(1)}, u32[]{:S(2)}, u32[]{:S(2)}) collective-permute-start(f32[32,128]{1,0:T(8,128)S(1)} %bitcast.84), channel_id=1, source_target_pairs={{0,1},{1,2},{2,3},{3,4},{4,5},{5,6},{6,7},{7,8},{8,9},{9,10},{10,1... | collective-permute-start | bytes 49160 | tf_op jit(solution)/shard_map/ppermute | solution.py:17
  29.0 89.7 %collective-permute-start.6 = (f32[32,128]{1,0:T(8,128)S(1)}, f32[32,128]{1,0:T(8,128)S(1)}, u32[]{:S(2)}, u32[]{:S(2)}) collective-permute-start(f32[32,128]{1,0:T(8,128)S(1)} %bitcast.83), channel_id=1, source_target_pairs={{1,0},{2,1},{3,2},{4,3},{5,4},{6,5},{7,6},{8,7},{9,8},{10,9},{11,1... | collective-permute-start | bytes 49160 | tf_op jit(solution)/shard_map/ppermute | solution.py:17
  30.3 3.8 %collective-permute-start.4 = (f32[1,64,128]{2,1,0:T(8,128)S(1)}, f32[1,64,128]{2,1,0:T(8,128)S(1)}, u32[]{:S(2)}, u32[]{:S(2)}) collective-permute-start(f32[1,64,128]{2,1,0:T(8,128)S(1)} %get-tuple-element.60), channel_id=1, source_target_pairs={{16,0},{32,16},{48,32},{64,48},{80,64},{96,80},{112,96},{17,1},{33... | collective-permute-start | bytes 98312 | tf_op jit(solution)/shard_map/ppermute | solution.py:18
  109.3 9.4 %collective-permute-start.3 = (f32[32,128]{1,0:T(8,128)S(1)}, f32[32,128]{1,0:T(8,128)S(1)}, u32[]{:S(2)}, u32[]{:S(2)}) collective-permute-start(f32[32,128]{1,0:T(8,128)S(1)} %bitcast.86), channel_id=1, source_target_pairs={{0,1},{1,2},{2,3},{3,4},{4,5},{5,6},{6,7},{7,8},{8,9},{9,10},{10,1... | collective-permute-start | bytes 49160 | tf_op jit(solution)/shard_map/ppermute | solution.py:17
  112.2 6.5 %collective-permute-start.2 = (f32[32,128]{1,0:T(8,128)S(1)}, f32[32,128]{1,0:T(8,128)S(1)}, u32[]{:S(2)}, u32[]{:S(2)}) collective-permute-start(f32[32,128]{1,0:T(8,128)S(1)} %bitcast.85), channel_id=1, source_target_pairs={{1,0},{2,1},{3,2},{4,3},{5,4},{6,5},{7,6},{8,7},{9,8},{10,9},{11,1... | collective-permute-start | bytes 49160 | tf_op jit(solution)/shard_map/ppermute | solution.py:17
  113.5 5.2 %collective-permute-start = (f32[1,64,128]{2,1,0:T(8,128)S(1)}, f32[1,64,128]{2,1,0:T(8,128)S(1)}, u32[]{:S(2)}, u32[]{:S(2)}) collective-permute-start(f32[1,64,128]{2,1,0:T(8,128)S(1)} %get-tuple-element.35), channel_id=1, source_target_pairs={{16,0},{32,16},{48,32},{64,48},{80,64},{96,80},{112,96},{17,1},{33... | collective-permute-start | bytes 98312 | tf_op jit(solution)/shard_map/ppermute | solution.py:18
  114.8 3.9 %collective-permute-start.1 = (f32[1,64,128]{2,1,0:T(8,128)S(1)}, f32[1,64,128]{2,1,0:T(8,128)S(1)}, u32[]{:S(2)}, u32[]{:S(2)}) collective-permute-start(f32[1,64,128]{2,1,0:T(8,128)S(1)} %get-tuple-element.36), channel_id=1, source_target_pairs={{0,16},{16,32},{32,48},{48,64},{64,80},{80,96},{96,112},{1,17},{17... | collective-permute-start | bytes 98312 | tf_op jit(solution)/shard_map/ppermute | solution.py:18
  117.9 1.2 copy-start.1
  122.7 9.3 %collective-permute-start.11 = (f32[32,128]{1,0:T(8,128)S(1)}, f32[32,128]{1,0:T(8,128)S(1)}, u32[]{:S(2)}, u32[]{:S(2)}) collective-permute-start(f32[32,128]{1,0:T(8,128)S(1)} %bitcast.89), channel_id=1, source_target_pairs={{0,1},{1,2},{2,3},{3,4},{4,5},{5,6},{6,7},{7,8},{8,9},{9,10},{10,1... | collective-permute-start | bytes 49160 | tf_op jit(solution)/shard_map/ppermute | solution.py:17
  127.3 5.6 %collective-permute-start.10 = (f32[32,128]{1,0:T(8,128)S(1)}, f32[32,128]{1,0:T(8,128)S(1)}, u32[]{:S(2)}, u32[]{:S(2)}) collective-permute-start(f32[32,128]{1,0:T(8,128)S(1)} %bitcast.87), channel_id=1, source_target_pairs={{1,0},{2,1},{3,2},{4,3},{5,4},{6,5},{7,6},{8,7},{9,8},{10,9},{11,1... | collective-permute-start | bytes 49160 | tf_op jit(solution)/shard_map/ppermute | solution.py:17
  128.6 4.3 %collective-permute-start.9 = (f32[1,64,128]{2,1,0:T(8,128)S(1)}, f32[1,64,128]{2,1,0:T(8,128)S(1)}, u32[]{:S(2)}, u32[]{:S(2)}) collective-permute-start(f32[1,64,128]{2,1,0:T(8,128)S(1)} %get-tuple-element.50), channel_id=1, source_target_pairs={{0,16},{16,32},{32,48},{48,64},{64,80},{80,96},{96,112},{1,17},{17... | collective-permute-start | bytes 98312 | tf_op jit(solution)/shard_map/ppermute | solution.py:18
  130.4 5.0 %collective-permute-start.8 = (f32[1,64,128]{2,1,0:T(8,128)S(1)}, f32[1,64,128]{2,1,0:T(8,128)S(1)}, u32[]{:S(2)}, u32[]{:S(2)}) collective-permute-start(f32[1,64,128]{2,1,0:T(8,128)S(1)} %get-tuple-element.51), channel_id=1, source_target_pairs={{16,0},{32,16},{48,32},{64,48},{80,64},{96,80},{112,96},{17,1},{33... | collective-permute-start | bytes 98312 | tf_op jit(solution)/shard_map/ppermute | solution.py:18
  136.0 16.6 %copy-start.2 = (f32[32,64,128]{2,1,0:T(8,128)}, f32[32,64,128]{2,1,0:T(8,128)S(1)}, u32[]{:S(2)}) copy-start(f32[32,64,128]{2,1,0:T(8,128)S(1)} %get-tuple-element.32) | copy-start | bytes 3145732
  136.1 12.0 %collective-permute-start.15 = (f32[32,128]{1,0:T(8,128)S(1)}, f32[32,128]{1,0:T(8,128)S(1)}, u32[]{:S(2)}, u32[]{:S(2)}) collective-permute-start(f32[32,128]{1,0:T(8,128)S(1)} %bitcast.90), channel_id=1, source_target_pairs={{0,1},{1,2},{2,3},{3,4},{4,5},{5,6},{6,7},{7,8},{8,9},{9,10},{10,1... | collective-permute-start | bytes 49160 | tf_op jit(solution)/shard_map/ppermute | solution.py:17
  140.7 7.4 %collective-permute-start.14 = (f32[32,128]{1,0:T(8,128)S(1)}, f32[32,128]{1,0:T(8,128)S(1)}, u32[]{:S(2)}, u32[]{:S(2)}) collective-permute-start(f32[32,128]{1,0:T(8,128)S(1)} %bitcast.88), channel_id=1, source_target_pairs={{1,0},{2,1},{3,2},{4,3},{5,4},{6,5},{7,6},{8,7},{9,8},{10,9},{11,1... | collective-permute-start | bytes 49160 | tf_op jit(solution)/shard_map/ppermute | solution.py:17
  142.0 6.1 %collective-permute-start.13 = (f32[1,64,128]{2,1,0:T(8,128)S(1)}, f32[1,64,128]{2,1,0:T(8,128)S(1)}, u32[]{:S(2)}, u32[]{:S(2)}) collective-permute-start(f32[1,64,128]{2,1,0:T(8,128)S(1)} %get-tuple-element.44), channel_id=1, source_target_pairs={{0,16},{16,32},{32,48},{48,64},{64,80},{80,96},{96,112},{1,17},{17... | collective-permute-start | bytes 98312 | tf_op jit(solution)/shard_map/ppermute | solution.py:18
  146.2 3.1 %collective-permute-start.12 = (f32[1,64,128]{2,1,0:T(8,128)S(1)}, f32[1,64,128]{2,1,0:T(8,128)S(1)}, u32[]{:S(2)}, u32[]{:S(2)}) collective-permute-start(f32[1,64,128]{2,1,0:T(8,128)S(1)} %get-tuple-element.45), channel_id=1, source_target_pairs={{16,0},{32,16},{48,32},{64,48},{80,64},{96,80},{112,96},{17,1},{33... | collective-permute-start | bytes 98312 | tf_op jit(solution)/shard_map/ppermute | solution.py:18

commit v18 on v16

--- a/solution.py
+++ b/solution.py
@@ -137,7 +137,7 @@
                 out_ref[c, uh * 2 + 1, pl.ds(y, 8), :] = transpose_groups(u1)
         return carry
 
-    lax.fori_loop(0, 8, step, 0)
+    lax.fori_loop(0, 8, step, 0, unroll=2)
 
 
 def to_grid(blocks, span_x, span_y, depth):

time: 184 us -> 191 us (1.038)
  Pallas kernels: 13.3 us -> 20 us
    pallas_call x1, Pallas kernels: 13.3 us -> 20 us  [to_grid(): pl.pallas_call(relayout_kernel, out_shape=jax.ShapeDtypeStruct((3, span_x...]
  transfers between devices with their start and end apart: 17 -> 17, of which waited for: 5 -> 5; matrix products, arithmetic and copies ran while one was open for 7% -> 7% of each run, Pallas kernels for 7% -> 11%
where the time goes in v18:
time: 191 us; the launch traced here: 190 us
  starting transfers between devices  48.2 us (25%)
  blocking collectives  38.1 us (20%)
  waiting for transfers between devices  37.7 us (20%)
  Pallas kernels  20 us (10%)
  other arithmetic  18.6 us (10%)
  local copies, waits for them, and re-layouts  15.6 us (8%)
  between operations  6.09 us (3%)
  matrix products  5.6 us (3%)
    psum x4, blocking collectives, over_axes(): shard = lax.psum(shard, axis)  38.1 us
    all_to_all x1, waiting for transfers between devices, body(): lax.all_to_all(payload, GX_GY, split_axis=0, concat_axis=0, tiled=True)  32.3 us
    ppermute x8, starting transfers between devices, shifted(): return lax.ppermute(flat, axis, pairs).reshape(piece.shape)  20.8 us
    pallas_call x1, Pallas kernels, to_grid(): pl.pallas_call(relayout_kernel, out_shape=jax.ShapeDtypeStruct((3, span_x...  20 us
    ppermute x8, starting transfers between devices, shifted(): return lax.ppermute(piece, axis, pairs)  15.7 us
    all_to_all x1, starting transfers between devices, body(): lax.all_to_all(payload, GX_GY, split_axis=0, concat_axis=0, tiled=True)  11.6 us
    ppermute x8, waiting for transfers between devices, shifted(): return lax.ppermute(piece, axis, pairs)  4.54 us
  transfers between devices with their start and end apart: 17, of which 5 were waited for; matrix products, arithmetic and copies ran while one was open for 7% of the time, Pallas kernels for 11%

profile of v18, /device:TPU:0, one launch (start us, length us, event | category | flops | bytes accessed | tf_op | source)
XLA Modules:
  0.0 189.9 jit_solution(6528367584238945788)
XLA Ops:
  1.9 2.0 %broadcast_select_fusion = (bf16[256]{0:T(256)(128)(2,1)S(1)}, bf16[256]{0:T(256)(128)(2,1)S(1)}) fusion(pred[]{:T(512)} %compare_reduce_fusion, s32[256]{0:T(256)} %param.11, pred[]{:T(512)} %compare_reduce_fusion.1), kind=kLoop, calls=%fused_computation.106 | loop fusion | flops 5888 | bytes 2050 | tf_op jit(solution)/shard_map/select.12
  7.0 2.1 %convolution_convert_fusion = bf16[128,6,1664]{2,0,1:T(8,128)(2,1)S(1)} fusion(bf16[256,128]{1,0:T(8,128)(2,1)S(1)} %scatter.9, bf16[256,1536]{1,0:T(8,128)(2,1)} %param.9, s32[128,6]{0,1:T(8,128)S(1)} %iota_add_fusion, s32[256]{0:T(256)S(1)} %multiply_add_fusion.1), kind=kOutput, calls=%fused_computation | convolution fusion | flops 657489920 | bytes 3411968 | tf_op jit(solution)/shard_map/pck,kj->pcj/dot_general | solution.py:74
  9.1 3.2 %copy.32 = bf16[128,6,1664]{2,1,0:T(8,128)(2,1)} copy(bf16[128,6,1664]{2,0,1:T(8,128)(2,1)S(1)} %convolution_convert_fusion) | data formatting | bytes 5111808 | tf_op jit(solution)/shard_map/convert_element_type | solution.py:77
  12.3 11.6 %all-to-all-start = ((bf16[128,6,1664]{2,1,0:T(8,128)(2,1)}), bf16[128,6,1664]{2,1,0:T(8,128)(2,1)}, u32[]{:S(2)}, u32[]{:S(2)}) async-start(bf16[128,6,1664]{2,1,0:T(8,128)(2,1)} %copy.32), calls=%async_computation | async-start | bytes 6815744 | tf_op jit(solution)/shard_map/all_to_all | solution.py:159
  25.3 3.7 %collective-permute-start.7 = (f32[32,128]{1,0:T(8,128)S(1)}, f32[32,128]{1,0:T(8,128)S(1)}, u32[]{:S(2)}, u32[]{:S(2)}) collective-permute-start(f32[32,128]{1,0:T(8,128)S(1)} %bitcast.84), channel_id=1, source_target_pairs={{0,1},{1,2},{2,3},{3,4},{4,5},{5,6},{6,7},{7,8},{8,9},{9,10},{10,1... | collective-permute-start | bytes 49160 | tf_op jit(solution)/shard_map/ppermute | solution.py:17
  34.7 32.3 %all-to-all-done = bf16[128,6,1664]{2,1,0:T(8,128)(2,1)} async-done(((bf16[128,6,1664]{2,1,0:T(8,128)(2,1)}), bf16[128,6,1664]{2,1,0:T(8,128)(2,1)}, u32[]{:S(2)}, u32[]{:S(2)}) %all-to-all-start) | async-done | bytes 2555936 | tf_op jit(solution)/shard_map/all_to_all | solution.py:159
  68.3 2.1 %slice.271 = bf16[128,6,1536]{2,1,0:T(8,128)(2,1)S(1)} slice(bf16[128,6,1664]{2,1,0:T(8,128)(2,1)} %all-to-all-done), slice={[0:128], [0:6], [0:1536]} | slice | bytes 4718592 | tf_op jit(solution)/shard_map/slice | solution.py:170
  70.3 3.5 %convolution_bitcast_fusion.blk_ref = f32[512,1536]{1,0:T(8,128)} fusion(bf16[128,6,1536]{2,1,0:T(8,128)(2,1)S(1)} %slice.271, s32[128,6]{0,1:T(8,128)S(1)} %fusion.40), kind=kOutput, calls=%fused_computation.1 | convolution fusion | flops 1208352768 | bytes 5508096 | tf_op jit(solution)/shard_map/pcs,pcj->sj/dot_general | solution.py:167
  73.9 20.0 %shard_map.68 = f32[3,32,64,128]{3,2,1,0:T(8,128)} custom-call(f32[512,1536]{1,0:T(8,128)} %convolution_bitcast_fusion.blk_ref), custom_call_target="tpu_custom_call" | custom-call | flops 15728640 | bytes 6291456 | tf_op jit(solution)/shard_map/pallas_call | solution.py:145
  93.9 2.1 %slice_bitcast_fusion.2 = (f32[32,64,128]{2,1,0:T(8,128)S(1)}, f32[32,64,128]{2,1,0:T(8,128)S(1)}, f32[32,64,128]{2,1,0:T(8,128)S(1)}) fusion(f32[3,32,64,128]{3,2,1,0:T(8,128)} %shard_map.68), kind=kLoop, calls=%fused_computation.62 | loop fusion | bytes 6291456 | tf_op jit(solution)/shard_map/squeeze | solution.py:174
  96.8 2.9 %collective-permute-start.3 = (f32[32,128]{1,0:T(8,128)S(1)}, f32[32,128]{1,0:T(8,128)S(1)}, u32[]{:S(2)}, u32[]{:S(2)}) collective-permute-start(f32[32,128]{1,0:T(8,128)S(1)} %bitcast.86), channel_id=1, source_target_pairs={{0,1},{1,2},{2,3},{3,4},{4,5},{5,6},{6,7},{7,8},{8,9},{9,10},{10,1... | collective-permute-start | bytes 49160 | tf_op jit(solution)/shard_map/ppermute | solution.py:17
  102.3 3.0 %collective-permute-start.1 = (f32[1,64,128]{2,1,0:T(8,128)S(1)}, f32[1,64,128]{2,1,0:T(8,128)S(1)}, u32[]{:S(2)}, u32[]{:S(2)}) collective-permute-start(f32[1,64,128]{2,1,0:T(8,128)S(1)} %get-tuple-element.36), channel_id=1, source_target_pairs={{0,16},{16,32},{32,48},{48,64},{64,80},{80,96},{96,112},{1,17},{17... | collective-permute-start | bytes 98312 | tf_op jit(solution)/shard_map/ppermute | solution.py:18
  106.6 3.6 %fusion.45 = (f32[32,64,128]{2,1,0:T(8,128)S(1)}, f32[32,64,128]{2,1,0:T(8,128)S(1)}) fusion(f32[32,64,128]{2,1,0:T(8,128)S(1)} %copy-done.1, f32[32,64,127]{2,1,0:T(8,128)S(1)} %get-tuple-element.70, f32[32,64,127]{2,1,0:T(8,128)S(1)} %get-tuple-element.71, f32[34,64,128]{2,1,0:T(8,128)} %constant_dynamic-update-slice_fusion, ...), kind=kLoop, calls=%fused_computation.116 | loop fusion | flops 8126464 | bytes 11763712 | tf_op jit(solution)/shard_map/mul | solution.py:183
  110.2 4.5 %collective-permute-start.11 = (f32[32,128]{1,0:T(8,128)S(1)}, f32[32,128]{1,0:T(8,128)S(1)}, u32[]{:S(2)}, u32[]{:S(2)}) collective-permute-start(f32[32,128]{1,0:T(8,128)S(1)} %bitcast.89), channel_id=1, source_target_pairs={{0,1},{1,2},{2,3},{3,4},{4,5},{5,6},{6,7},{7,8},{8,9},{9,10},{10,1... | collective-permute-start | bytes 49160 | tf_op jit(solution)/shard_map/ppermute | solution.py:17
  120.4 2.4 %collective-permute-done.8 = f32[1,64,128]{2,1,0:T(8,128)S(1)} collective-permute-done((f32[1,64,128]{2,1,0:T(8,128)S(1)}, f32[1,64,128]{2,1,0:T(8,128)S(1)}, u32[]{:S(2)}, u32[]{:S(2)}) %collective-permute-start.8) | collective-permute-done | bytes 32800 | tf_op jit(solution)/shard_map/ppermute | solution.py:18
  123.6 4.5 %collective-permute-start.15 = (f32[32,128]{1,0:T(8,128)S(1)}, f32[32,128]{1,0:T(8,128)S(1)}, u32[]{:S(2)}, u32[]{:S(2)}) collective-permute-start(f32[32,128]{1,0:T(8,128)S(1)} %bitcast.90), channel_id=1, source_target_pairs={{0,1},{1,2},{2,3},{3,4},{4,5},{5,6},{6,7},{7,8},{8,9},{9,10},{10,1... | collective-permute-start | bytes 49160 | tf_op jit(solution)/shard_map/ppermute | solution.py:17
  129.4 4.3 %collective-permute-start.13 = (f32[1,64,128]{2,1,0:T(8,128)S(1)}, f32[1,64,128]{2,1,0:T(8,128)S(1)}, u32[]{:S(2)}, u32[]{:S(2)}) collective-permute-start(f32[1,64,128]{2,1,0:T(8,128)S(1)} %get-tuple-element.44), channel_id=1, source_target_pairs={{0,16},{16,32},{32,48},{48,64},{64,80},{80,96},{96,112},{1,17},{17... | collective-permute-start | bytes 98312 | tf_op jit(solution)/shard_map/ppermute | solution.py:18
  136.8 3.3 %multiply_reduce_fusion.3 = (f32[]{:T(128)}, f32[]{:T(128)}, f32[]{:T(128)}, f32[]{:T(128)}, f32[32,64,128]{2,1,0:T(8,128)}) fusion(f32[32,64,128]{2,1,0:T(8,128)S(1)} %get-tuple-element.34, f32[32,64,128]{2,1,0:T(8,128)S(1)} %copy-done.1, f32[32,64,128]{2,1,0:T(8,128)S(1)} %get-tuple-element.32, f32[32,64,128]{2,1,0:T(8,128)S(1)} %get-tuple-element.31, ...), kind=kLoop, calls=%fused_computation.69 | loop fusion | flops 8388604 | bytes 7421968 | tf_op jit(solution)/shard_map/reduce_sum | solution.py:190
  140.1 2.5 %pad_maximum_fusion.20 = f32[4]{0:T(128)S(1)} fusion(f32[1]{0:T(128)} %bitcast.33, f32[1]{0:T(128)} %bitcast.28, f32[1]{0:T(128)} %bitcast.27, f32[1]{0:T(128)} %bitcast.22), kind=kLoop, calls=%fused_computation.109 | loop fusion | flops 12 | bytes 32 | tf_op jit(solution)/shard_map/stack | solution.py:188
  142.6 10.9 %psum.28 = f32[4]{0:T(128)S(1)} all-reduce(f32[4]{0:T(128)S(1)} %pad_maximum_fusion.20), channel_id=1, replica_groups=mesh['gx_0'=4,'gx_1'=2,'gy_0'=4,'gy_1'=4] {'gx_0'}, use_global_device_ids=true, to_apply=%region_9.10 | all-reduce | flops 4 | bytes 32 | tf_op jit(solution)/shard_map/psum | solution.py:43
  153.5 2.5 %psum.29 = f32[4]{0:T(128)S(1)} all-reduce(f32[4]{0:T(128)S(1)} %psum.28), channel_id=1, replica_groups=mesh['gx_0'=4,'gx_1'=2,'gy_0'=4,'gy_1'=4] {'gx_1'}, use_global_device_ids=true, to_apply=%region_10.11 | all-reduce | flops 4 | bytes 32 | tf_op jit(solution)/shard_map/psum | solution.py:43
  156.0 17.0 %psum.30 = f32[4]{0:T(128)S(1)} all-reduce(f32[4]{0:T(128)S(1)} %psum.29), channel_id=1, replica_groups=mesh['gx_0'=4,'gx_1'=2,'gy_0'=4,'gy_1'=4] {'gy_0'}, use_global_device_ids=true, to_apply=%region_11.12 | all-reduce | flops 4 | bytes 32 | tf_op jit(solution)/shard_map/psum | solution.py:43
  173.0 7.7 %psum.31 = f32[4]{0:T(128)S(1)} all-reduce(f32[4]{0:T(128)S(1)} %psum.30), channel_id=1, replica_groups=mesh['gx_0'=4,'gx_1'=2,'gy_0'=4,'gy_1'=4] {'gy_1'}, use_global_device_ids=true, to_apply=%region_12.13 | all-reduce | flops 4 | bytes 32 | tf_op jit(solution)/shard_map/psum | solution.py:43
  186.4 3.5 %multiply_subtract_fusion = (f32[32,64,128]{2,1,0:T(8,128)}, f32[32,64,128]{2,1,0:T(8,128)}) fusion(f32[32,64,128]{2,1,0:T(8,128)} %copy-done.2, f32[32,64,128]{2,1,0:T(8,128)} %get-tuple-element.30, f32[32,64,128]{2,1,0:T(8,128)S(1)} %get-tuple-element.34, f32[]{:T(128)S(6)} %div.34, f32[]{:T(128)S(6)} %div.35, f32[]{:T(128)S(6)} %div.33, ...), kind=kLoop, calls=%fused_computation.63 | loop fusion | flops 4718592 | bytes 7340044 | tf_op jit(solution)/shard_map/sub | solution.py:210
  (69 shorter events, 28.6 us)
Async XLA Ops:
  12.3 11.7 %copy-start = (f32[32,64,128]{2,1,0:T(8,128)S(1)}, f32[32,64,128]{2,1,0:T(8,128)}, u32[]{:S(2)}) copy-start(f32[32,64,128]{2,1,0:T(8,128)} %param.13) | copy-start | bytes 3145732
  12.3 54.7 %all-to-all-start = ((bf16[128,6,1664]{2,1,0:T(8,128)(2,1)}), bf16[128,6,1664]{2,1,0:T(8,128)(2,1)}, u32[]{:S(2)}, u32[]{:S(2)}) async-start(bf16[128,6,1664]{2,1,0:T(8,128)(2,1)} %copy.32), calls=%async_computation | async-start | bytes 6815744 | tf_op jit(solution)/shard_map/all_to_all | solution.py:159
  24.0 7.6 %collective-permute-start.5 = (f32[1,64,128]{2,1,0:T(8,128)S(1)}, f32[1,64,128]{2,1,0:T(8,128)S(1)}, u32[]{:S(2)}, u32[]{:S(2)}) collective-permute-start(f32[1,64,128]{2,1,0:T(8,128)S(1)} %get-tuple-element.61), channel_id=1, source_target_pairs={{0,16},{16,32},{32,48},{48,64},{64,80},{80,96},{96,112},{1,17},{17... | collective-permute-start | bytes 98312 | tf_op jit(solution)/shard_map/ppermute | solution.py:18
  25.3 77.0 %collective-permute-start.7 = (f32[32,128]{1,0:T(8,128)S(1)}, f32[32,128]{1,0:T(8,128)S(1)}, u32[]{:S(2)}, u32[]{:S(2)}) collective-permute-start(f32[32,128]{1,0:T(8,128)S(1)} %bitcast.84), channel_id=1, source_target_pairs={{0,1},{1,2},{2,3},{3,4},{4,5},{5,6},{6,7},{7,8},{8,9},{9,10},{10,1... | collective-permute-start | bytes 49160 | tf_op jit(solution)/shard_map/ppermute | solution.py:17
  29.0 77.2 %collective-permute-start.6 = (f32[32,128]{1,0:T(8,128)S(1)}, f32[32,128]{1,0:T(8,128)S(1)}, u32[]{:S(2)}, u32[]{:S(2)}) collective-permute-start(f32[32,128]{1,0:T(8,128)S(1)} %bitcast.83), channel_id=1, source_target_pairs={{1,0},{2,1},{3,2},{4,3},{5,4},{6,5},{7,6},{8,7},{9,8},{10,9},{11,1... | collective-permute-start | bytes 49160 | tf_op jit(solution)/shard_map/ppermute | solution.py:17
  30.3 3.8 %collective-permute-start.4 = (f32[1,64,128]{2,1,0:T(8,128)S(1)}, f32[1,64,128]{2,1,0:T(8,128)S(1)}, u32[]{:S(2)}, u32[]{:S(2)}) collective-permute-start(f32[1,64,128]{2,1,0:T(8,128)S(1)} %get-tuple-element.60), channel_id=1, source_target_pairs={{16,0},{32,16},{48,32},{64,48},{80,64},{96,80},{112,96},{17,1},{33... | collective-permute-start | bytes 98312 | tf_op jit(solution)/shard_map/ppermute | solution.py:18
  96.8 9.4 %collective-permute-start.3 = (f32[32,128]{1,0:T(8,128)S(1)}, f32[32,128]{1,0:T(8,128)S(1)}, u32[]{:S(2)}, u32[]{:S(2)}) collective-permute-start(f32[32,128]{1,0:T(8,128)S(1)} %bitcast.86), channel_id=1, source_target_pairs={{0,1},{1,2},{2,3},{3,4},{4,5},{5,6},{6,7},{7,8},{8,9},{9,10},{10,1... | collective-permute-start | bytes 49160 | tf_op jit(solution)/shard_map/ppermute | solution.py:17
  99.7 6.5 %collective-permute-start.2 = (f32[32,128]{1,0:T(8,128)S(1)}, f32[32,128]{1,0:T(8,128)S(1)}, u32[]{:S(2)}, u32[]{:S(2)}) collective-permute-start(f32[32,128]{1,0:T(8,128)S(1)} %bitcast.85), channel_id=1, source_target_pairs={{1,0},{2,1},{3,2},{4,3},{5,4},{6,5},{7,6},{8,7},{9,8},{10,9},{11,1... | collective-permute-start | bytes 49160 | tf_op jit(solution)/shard_map/ppermute | solution.py:17
  101.0 5.2 %collective-permute-start = (f32[1,64,128]{2,1,0:T(8,128)S(1)}, f32[1,64,128]{2,1,0:T(8,128)S(1)}, u32[]{:S(2)}, u32[]{:S(2)}) collective-permute-start(f32[1,64,128]{2,1,0:T(8,128)S(1)} %get-tuple-element.35), channel_id=1, source_target_pairs={{16,0},{32,16},{48,32},{64,48},{80,64},{96,80},{112,96},{17,1},{33... | collective-permute-start | bytes 98312 | tf_op jit(solution)/shard_map/ppermute | solution.py:18
  102.3 3.9 %collective-permute-start.1 = (f32[1,64,128]{2,1,0:T(8,128)S(1)}, f32[1,64,128]{2,1,0:T(8,128)S(1)}, u32[]{:S(2)}, u32[]{:S(2)}) collective-permute-start(f32[1,64,128]{2,1,0:T(8,128)S(1)} %get-tuple-element.36), channel_id=1, source_target_pairs={{0,16},{16,32},{32,48},{48,64},{64,80},{80,96},{96,112},{1,17},{17... | collective-permute-start | bytes 98312 | tf_op jit(solution)/shard_map/ppermute | solution.py:18
  105.4 1.2 copy-start.1
  110.2 9.3 %collective-permute-start.11 = (f32[32,128]{1,0:T(8,128)S(1)}, f32[32,128]{1,0:T(8,128)S(1)}, u32[]{:S(2)}, u32[]{:S(2)}) collective-permute-start(f32[32,128]{1,0:T(8,128)S(1)} %bitcast.89), channel_id=1, source_target_pairs={{0,1},{1,2},{2,3},{3,4},{4,5},{5,6},{6,7},{7,8},{8,9},{9,10},{10,1... | collective-permute-start | bytes 49160 | tf_op jit(solution)/shard_map/ppermute | solution.py:17
  114.8 5.6 %collective-permute-start.10 = (f32[32,128]{1,0:T(8,128)S(1)}, f32[32,128]{1,0:T(8,128)S(1)}, u32[]{:S(2)}, u32[]{:S(2)}) collective-permute-start(f32[32,128]{1,0:T(8,128)S(1)} %bitcast.87), channel_id=1, source_target_pairs={{1,0},{2,1},{3,2},{4,3},{5,4},{6,5},{7,6},{8,7},{9,8},{10,9},{11,1... | collective-permute-start | bytes 49160 | tf_op jit(solution)/shard_map/ppermute | solution.py:17
  116.1 4.3 %collective-permute-start.9 = (f32[1,64,128]{2,1,0:T(8,128)S(1)}, f32[1,64,128]{2,1,0:T(8,128)S(1)}, u32[]{:S(2)}, u32[]{:S(2)}) collective-permute-start(f32[1,64,128]{2,1,0:T(8,128)S(1)} %get-tuple-element.50), channel_id=1, source_target_pairs={{0,16},{16,32},{32,48},{48,64},{64,80},{80,96},{96,112},{1,17},{17... | collective-permute-start | bytes 98312 | tf_op jit(solution)/shard_map/ppermute | solution.py:18
  117.9 5.0 %collective-permute-start.8 = (f32[1,64,128]{2,1,0:T(8,128)S(1)}, f32[1,64,128]{2,1,0:T(8,128)S(1)}, u32[]{:S(2)}, u32[]{:S(2)}) collective-permute-start(f32[1,64,128]{2,1,0:T(8,128)S(1)} %get-tuple-element.51), channel_id=1, source_target_pairs={{16,0},{32,16},{48,32},{64,48},{80,64},{96,80},{112,96},{17,1},{33... | collective-permute-start | bytes 98312 | tf_op jit(solution)/shard_map/ppermute | solution.py:18
  123.5 16.6 %copy-start.2 = (f32[32,64,128]{2,1,0:T(8,128)}, f32[32,64,128]{2,1,0:T(8,128)S(1)}, u32[]{:S(2)}) copy-start(f32[32,64,128]{2,1,0:T(8,128)S(1)} %get-tuple-element.32) | copy-start | bytes 3145732
  123.6 12.0 %collective-permute-start.15 = (f32[32,128]{1,0:T(8,128)S(1)}, f32[32,128]{1,0:T(8,128)S(1)}, u32[]{:S(2)}, u32[]{:S(2)}) collective-permute-start(f32[32,128]{1,0:T(8,128)S(1)} %bitcast.90), channel_id=1, source_target_pairs={{0,1},{1,2},{2,3},{3,4},{4,5},{5,6},{6,7},{7,8},{8,9},{9,10},{10,1... | collective-permute-start | bytes 49160 | tf_op jit(solution)/shard_map/ppermute | solution.py:17
  128.1 7.4 %collective-permute-start.14 = (f32[32,128]{1,0:T(8,128)S(1)}, f32[32,128]{1,0:T(8,128)S(1)}, u32[]{:S(2)}, u32[]{:S(2)}) collective-permute-start(f32[32,128]{1,0:T(8,128)S(1)} %bitcast.88), channel_id=1, source_target_pairs={{1,0},{2,1},{3,2},{4,3},{5,4},{6,5},{7,6},{8,7},{9,8},{10,9},{11,1... | collective-permute-start | bytes 49160 | tf_op jit(solution)/shard_map/ppermute | solution.py:17
  129.4 6.1 %collective-permute-start.13 = (f32[1,64,128]{2,1,0:T(8,128)S(1)}, f32[1,64,128]{2,1,0:T(8,128)S(1)}, u32[]{:S(2)}, u32[]{:S(2)}) collective-permute-start(f32[1,64,128]{2,1,0:T(8,128)S(1)} %get-tuple-element.44), channel_id=1, source_target_pairs={{0,16},{16,32},{32,48},{48,64},{64,80},{80,96},{96,112},{1,17},{17... | collective-permute-start | bytes 98312 | tf_op jit(solution)/shard_map/ppermute | solution.py:18
  133.7 3.1 %collective-permute-start.12 = (f32[1,64,128]{2,1,0:T(8,128)S(1)}, f32[1,64,128]{2,1,0:T(8,128)S(1)}, u32[]{:S(2)}, u32[]{:S(2)}) collective-permute-start(f32[1,64,128]{2,1,0:T(8,128)S(1)} %get-tuple-element.45), channel_id=1, source_target_pairs={{16,0},{32,16},{48,32},{64,48},{80,64},{96,80},{112,96},{17,1},{33... | collective-permute-start | bytes 98312 | tf_op jit(solution)/shard_map/ppermute | solution.py:18

commit v19 on v14

--- a/solution.py
+++ b/solution.py
@@ -63,8 +63,8 @@
     earlier = jnp.cumsum(onehot, axis=0) - onehot
     order = jnp.sum(earlier * onehot, axis=1)
     place = target * capacity + order
-    high = (brick_slot // 32).astype(jnp.bfloat16)
-    low = (brick_slot % 32).astype(jnp.bfloat16)
+    high = lax.shift_right_logical(brick_slot, 5).astype(jnp.bfloat16)
+    low = (brick_slot & 31).astype(jnp.bfloat16)
     tag = jnp.zeros((bricks.shape[0], 128), jnp.bfloat16).at[:, 0].set(high).at[:, 1].set(low)
     rows = jnp.concatenate([bricks, tag], axis=1)
     chosen = place[None, None, :] == (

time: 184 us -> 184 us (level)
  no operation moved by 1% of the time
where the time goes in v19:
time: 184 us; the launch traced here: 183 us
  starting transfers between devices  48.2 us (26%)
  blocking collectives  38.1 us (21%)
  waiting for transfers between devices  37.7 us (20%)
  other arithmetic  18.6 us (10%)
  local copies, waits for them, and re-layouts  15.6 us (8%)
  Pallas kernels  13.3 us (7%)
  between operations  6.09 us (3%)
  matrix products  5.59 us (3%)
    psum x4, blocking collectives, over_axes(): shard = lax.psum(shard, axis)  38.1 us
    all_to_all x1, waiting for transfers between devices, body(): lax.all_to_all(payload, GX_GY, split_axis=0, concat_axis=0, tiled=True)  32.3 us
    ppermute x8, starting transfers between devices, shifted(): return lax.ppermute(flat, axis, pairs).reshape(piece.shape)  20.8 us
    ppermute x8, starting transfers between devices, shifted(): return lax.ppermute(piece, axis, pairs)  15.7 us
    pallas_call x1, Pallas kernels, to_grid(): pl.pallas_call(relayout_kernel, out_shape=jax.ShapeDtypeStruct((3, span_x...  13.3 us
    all_to_all x1, starting transfers between devices, body(): lax.all_to_all(payload, GX_GY, split_axis=0, concat_axis=0, tiled=True)  11.6 us
    ppermute x8, waiting for transfers between devices, shifted(): return lax.ppermute(piece, axis, pairs)  4.53 us
  transfers between devices with their start and end apart: 17, of which 5 were waited for; matrix products, arithmetic and copies ran while one was open for 7% of the time, Pallas kernels for 7%

profile of v19, /device:TPU:0, one launch (start us, length us, event | category | flops | bytes accessed | tf_op | source)
XLA Modules:
  0.0 183.1 jit_solution(6207339853471620951)
XLA Ops:
  1.9 2.0 %broadcast_select_fusion = (bf16[256]{0:T(256)(128)(2,1)S(1)}, bf16[256]{0:T(256)(128)(2,1)S(1)}) fusion(pred[]{:T(512)} %compare_reduce_fusion, s32[256]{0:T(256)} %param.11, pred[]{:T(512)} %compare_reduce_fusion.1), kind=kLoop, calls=%fused_computation.102 | loop fusion | flops 1536 | bytes 2050 | tf_op jit(solution)/shard_map/select.6
  7.0 2.1 %convolution_convert_fusion = bf16[128,6,1664]{2,0,1:T(8,128)(2,1)S(1)} fusion(bf16[256,128]{1,0:T(8,128)(2,1)S(1)} %scatter.9, bf16[256,1536]{1,0:T(8,128)(2,1)} %param.9, s32[128,6]{0,1:T(8,128)S(1)} %iota_add_fusion, s32[256]{0:T(256)S(1)} %multiply_add_fusion.1), kind=kOutput, calls=%fused_computation | convolution fusion | flops 657489920 | bytes 3411968 | tf_op jit(solution)/shard_map/pck,kj->pcj/dot_general | solution.py:74
  9.1 3.2 %copy.32 = bf16[128,6,1664]{2,1,0:T(8,128)(2,1)} copy(bf16[128,6,1664]{2,0,1:T(8,128)(2,1)S(1)} %convolution_convert_fusion) | data formatting | bytes 5111808 | tf_op jit(solution)/shard_map/convert_element_type | solution.py:77
  12.3 11.6 %all-to-all-start = ((bf16[128,6,1664]{2,1,0:T(8,128)(2,1)}), bf16[128,6,1664]{2,1,0:T(8,128)(2,1)}, u32[]{:S(2)}, u32[]{:S(2)}) async-start(bf16[128,6,1664]{2,1,0:T(8,128)(2,1)} %copy.32), calls=%async_computation | async-start | bytes 6815744 | tf_op jit(solution)/shard_map/all_to_all | solution.py:157
  25.3 3.7 %collective-permute-start.7 = (f32[32,128]{1,0:T(8,128)S(1)}, f32[32,128]{1,0:T(8,128)S(1)}, u32[]{:S(2)}, u32[]{:S(2)}) collective-permute-start(f32[32,128]{1,0:T(8,128)S(1)} %bitcast.84), channel_id=1, source_target_pairs={{0,1},{1,2},{2,3},{3,4},{4,5},{5,6},{6,7},{7,8},{8,9},{9,10},{10,1... | collective-permute-start | bytes 49160 | tf_op jit(solution)/shard_map/ppermute | solution.py:17
  34.7 32.3 %all-to-all-done = bf16[128,6,1664]{2,1,0:T(8,128)(2,1)} async-done(((bf16[128,6,1664]{2,1,0:T(8,128)(2,1)}), bf16[128,6,1664]{2,1,0:T(8,128)(2,1)}, u32[]{:S(2)}, u32[]{:S(2)}) %all-to-all-start) | async-done | bytes 2555936 | tf_op jit(solution)/shard_map/all_to_all | solution.py:157
  68.2 2.1 %slice.271 = bf16[128,6,1536]{2,1,0:T(8,128)(2,1)S(1)} slice(bf16[128,6,1664]{2,1,0:T(8,128)(2,1)} %all-to-all-done), slice={[0:128], [0:6], [0:1536]} | slice | bytes 4718592 | tf_op jit(solution)/shard_map/slice | solution.py:168
  70.3 3.5 %convolution_bitcast_fusion.blk_ref = f32[512,1536]{1,0:T(8,128)} fusion(bf16[128,6,1536]{2,1,0:T(8,128)(2,1)S(1)} %slice.271, s32[128,6]{0,1:T(8,128)S(1)} %fusion.40), kind=kOutput, calls=%fused_computation.1 | convolution fusion | flops 1208352768 | bytes 5508096 | tf_op jit(solution)/shard_map/pcs,pcj->sj/dot_general | solution.py:165
  73.9 13.3 %shard_map.68 = f32[3,32,64,128]{3,2,1,0:T(8,128)} custom-call(f32[512,1536]{1,0:T(8,128)} %convolution_bitcast_fusion.blk_ref), custom_call_target="tpu_custom_call" | custom-call | flops 15728640 | bytes 6291456 | tf_op jit(solution)/shard_map/pallas_call | solution.py:143
  87.1 2.1 %slice_bitcast_fusion.2 = (f32[32,64,128]{2,1,0:T(8,128)S(1)}, f32[32,64,128]{2,1,0:T(8,128)S(1)}, f32[32,64,128]{2,1,0:T(8,128)S(1)}) fusion(f32[3,32,64,128]{3,2,1,0:T(8,128)} %shard_map.68), kind=kLoop, calls=%fused_computation.62 | loop fusion | bytes 6291456 | tf_op jit(solution)/shard_map/squeeze | solution.py:172
  90.0 2.9 %collective-permute-start.3 = (f32[32,128]{1,0:T(8,128)S(1)}, f32[32,128]{1,0:T(8,128)S(1)}, u32[]{:S(2)}, u32[]{:S(2)}) collective-permute-start(f32[32,128]{1,0:T(8,128)S(1)} %bitcast.86), channel_id=1, source_target_pairs={{0,1},{1,2},{2,3},{3,4},{4,5},{5,6},{6,7},{7,8},{8,9},{9,10},{10,1... | collective-permute-start | bytes 49160 | tf_op jit(solution)/shard_map/ppermute | solution.py:17
  95.5 3.0 %collective-permute-start.1 = (f32[1,64,128]{2,1,0:T(8,128)S(1)}, f32[1,64,128]{2,1,0:T(8,128)S(1)}, u32[]{:S(2)}, u32[]{:S(2)}) collective-permute-start(f32[1,64,128]{2,1,0:T(8,128)S(1)} %get-tuple-element.36), channel_id=1, source_target_pairs={{0,16},{16,32},{32,48},{48,64},{64,80},{80,96},{96,112},{1,17},{17... | collective-permute-start | bytes 98312 | tf_op jit(solution)/shard_map/ppermute | solution.py:18
  99.8 3.6 %fusion.43 = (f32[32,64,128]{2,1,0:T(8,128)S(1)}, f32[32,64,128]{2,1,0:T(8,128)S(1)}) fusion(f32[32,64,128]{2,1,0:T(8,128)S(1)} %copy-done.1, f32[32,64,127]{2,1,0:T(8,128)S(1)} %get-tuple-element.70, f32[32,64,127]{2,1,0:T(8,128)S(1)} %get-tuple-element.71, f32[34,64,128]{2,1,0:T(8,128)} %constant_dynamic-update-slice_fusion, ...), kind=kLoop, calls=%fused_computation.109 | loop fusion | flops 8126464 | bytes 11763712 | tf_op jit(solution)/shard_map/mul | solution.py:181
  103.4 4.5 %collective-permute-start.11 = (f32[32,128]{1,0:T(8,128)S(1)}, f32[32,128]{1,0:T(8,128)S(1)}, u32[]{:S(2)}, u32[]{:S(2)}) collective-permute-start(f32[32,128]{1,0:T(8,128)S(1)} %bitcast.89), channel_id=1, source_target_pairs={{0,1},{1,2},{2,3},{3,4},{4,5},{5,6},{6,7},{7,8},{8,9},{9,10},{10,1... | collective-permute-start | bytes 49160 | tf_op jit(solution)/shard_map/ppermute | solution.py:17
  113.6 2.4 %collective-permute-done.8 = f32[1,64,128]{2,1,0:T(8,128)S(1)} collective-permute-done((f32[1,64,128]{2,1,0:T(8,128)S(1)}, f32[1,64,128]{2,1,0:T(8,128)S(1)}, u32[]{:S(2)}, u32[]{:S(2)}) %collective-permute-start.8) | collective-permute-done | bytes 32800 | tf_op jit(solution)/shard_map/ppermute | solution.py:18
  116.8 4.5 %collective-permute-start.15 = (f32[32,128]{1,0:T(8,128)S(1)}, f32[32,128]{1,0:T(8,128)S(1)}, u32[]{:S(2)}, u32[]{:S(2)}) collective-permute-start(f32[32,128]{1,0:T(8,128)S(1)} %bitcast.90), channel_id=1, source_target_pairs={{0,1},{1,2},{2,3},{3,4},{4,5},{5,6},{6,7},{7,8},{8,9},{9,10},{10,1... | collective-permute-start | bytes 49160 | tf_op jit(solution)/shard_map/ppermute | solution.py:17
  122.7 4.3 %collective-permute-start.13 = (f32[1,64,128]{2,1,0:T(8,128)S(1)}, f32[1,64,128]{2,1,0:T(8,128)S(1)}, u32[]{:S(2)}, u32[]{:S(2)}) collective-permute-start(f32[1,64,128]{2,1,0:T(8,128)S(1)} %get-tuple-element.44), channel_id=1, source_target_pairs={{0,16},{16,32},{32,48},{48,64},{64,80},{80,96},{96,112},{1,17},{17... | collective-permute-start | bytes 98312 | tf_op jit(solution)/shard_map/ppermute | solution.py:18
  130.0 3.3 %multiply_reduce_fusion.3 = (f32[]{:T(128)}, f32[]{:T(128)}, f32[]{:T(128)}, f32[]{:T(128)}, f32[32,64,128]{2,1,0:T(8,128)}) fusion(f32[32,64,128]{2,1,0:T(8,128)S(1)} %get-tuple-element.34, f32[32,64,128]{2,1,0:T(8,128)S(1)} %copy-done.1, f32[32,64,128]{2,1,0:T(8,128)S(1)} %get-tuple-element.32, f32[32,64,128]{2,1,0:T(8,128)S(1)} %get-tuple-element.31, ...), kind=kLoop, calls=%fused_computation.69 | loop fusion | flops 8388604 | bytes 7421968 | tf_op jit(solution)/shard_map/reduce_sum | solution.py:188
  133.3 2.5 %pad_maximum_fusion.20 = f32[4]{0:T(128)S(1)} fusion(f32[1]{0:T(128)} %bitcast.33, f32[1]{0:T(128)} %bitcast.28, f32[1]{0:T(128)} %bitcast.27, f32[1]{0:T(128)} %bitcast.22), kind=kLoop, calls=%fused_computation.104 | loop fusion | flops 12 | bytes 32 | tf_op jit(solution)/shard_map/stack | solution.py:186
  135.8 10.9 %psum.28 = f32[4]{0:T(128)S(1)} all-reduce(f32[4]{0:T(128)S(1)} %pad_maximum_fusion.20), channel_id=1, replica_groups=mesh['gx_0'=4,'gx_1'=2,'gy_0'=4,'gy_1'=4] {'gx_0'}, use_global_device_ids=true, to_apply=%region_9.10 | all-reduce | flops 4 | bytes 32 | tf_op jit(solution)/shard_map/psum | solution.py:43
  146.8 2.5 %psum.29 = f32[4]{0:T(128)S(1)} all-reduce(f32[4]{0:T(128)S(1)} %psum.28), channel_id=1, replica_groups=mesh['gx_0'=4,'gx_1'=2,'gy_0'=4,'gy_1'=4] {'gx_1'}, use_global_device_ids=true, to_apply=%region_10.11 | all-reduce | flops 4 | bytes 32 | tf_op jit(solution)/shard_map/psum | solution.py:43
  149.2 17.0 %psum.30 = f32[4]{0:T(128)S(1)} all-reduce(f32[4]{0:T(128)S(1)} %psum.29), channel_id=1, replica_groups=mesh['gx_0'=4,'gx_1'=2,'gy_0'=4,'gy_1'=4] {'gy_0'}, use_global_device_ids=true, to_apply=%region_11.12 | all-reduce | flops 4 | bytes 32 | tf_op jit(solution)/shard_map/psum | solution.py:43
  166.2 7.7 %psum.31 = f32[4]{0:T(128)S(1)} all-reduce(f32[4]{0:T(128)S(1)} %psum.30), channel_id=1, replica_groups=mesh['gx_0'=4,'gx_1'=2,'gy_0'=4,'gy_1'=4] {'gy_1'}, use_global_device_ids=true, to_apply=%region_12.13 | all-reduce | flops 4 | bytes 32 | tf_op jit(solution)/shard_map/psum | solution.py:43
  179.6 3.5 %multiply_subtract_fusion = (f32[32,64,128]{2,1,0:T(8,128)}, f32[32,64,128]{2,1,0:T(8,128)}) fusion(f32[32,64,128]{2,1,0:T(8,128)} %copy-done.2, f32[32,64,128]{2,1,0:T(8,128)} %get-tuple-element.30, f32[32,64,128]{2,1,0:T(8,128)S(1)} %get-tuple-element.34, f32[]{:T(128)S(6)} %div.18, f32[]{:T(128)S(6)} %div.19, f32[]{:T(128)S(6)} %div.17, ...), kind=kLoop, calls=%fused_computation.63 | loop fusion | flops 4718592 | bytes 7340044 | tf_op jit(solution)/shard_map/sub | solution.py:208
  (69 shorter events, 28.6 us)
Async XLA Ops:
  12.3 11.7 %copy-start = (f32[32,64,128]{2,1,0:T(8,128)S(1)}, f32[32,64,128]{2,1,0:T(8,128)}, u32[]{:S(2)}) copy-start(f32[32,64,128]{2,1,0:T(8,128)} %param.13) | copy-start | bytes 3145732
  12.3 54.7 %all-to-all-start = ((bf16[128,6,1664]{2,1,0:T(8,128)(2,1)}), bf16[128,6,1664]{2,1,0:T(8,128)(2,1)}, u32[]{:S(2)}, u32[]{:S(2)}) async-start(bf16[128,6,1664]{2,1,0:T(8,128)(2,1)} %copy.32), calls=%async_computation | async-start | bytes 6815744 | tf_op jit(solution)/shard_map/all_to_all | solution.py:157
  24.0 7.6 %collective-permute-start.5 = (f32[1,64,128]{2,1,0:T(8,128)S(1)}, f32[1,64,128]{2,1,0:T(8,128)S(1)}, u32[]{:S(2)}, u32[]{:S(2)}) collective-permute-start(f32[1,64,128]{2,1,0:T(8,128)S(1)} %get-tuple-element.61), channel_id=1, source_target_pairs={{0,16},{16,32},{32,48},{48,64},{64,80},{80,96},{96,112},{1,17},{17... | collective-permute-start | bytes 98312 | tf_op jit(solution)/shard_map/ppermute | solution.py:18
  25.3 70.2 %collective-permute-start.7 = (f32[32,128]{1,0:T(8,128)S(1)}, f32[32,128]{1,0:T(8,128)S(1)}, u32[]{:S(2)}, u32[]{:S(2)}) collective-permute-start(f32[32,128]{1,0:T(8,128)S(1)} %bitcast.84), channel_id=1, source_target_pairs={{0,1},{1,2},{2,3},{3,4},{4,5},{5,6},{6,7},{7,8},{8,9},{9,10},{10,1... | collective-permute-start | bytes 49160 | tf_op jit(solution)/shard_map/ppermute | solution.py:17
  29.0 70.4 %collective-permute-start.6 = (f32[32,128]{1,0:T(8,128)S(1)}, f32[32,128]{1,0:T(8,128)S(1)}, u32[]{:S(2)}, u32[]{:S(2)}) collective-permute-start(f32[32,128]{1,0:T(8,128)S(1)} %bitcast.83), channel_id=1, source_target_pairs={{1,0},{2,1},{3,2},{4,3},{5,4},{6,5},{7,6},{8,7},{9,8},{10,9},{11,1... | collective-permute-start | bytes 49160 | tf_op jit(solution)/shard_map/ppermute | solution.py:17
  30.3 3.8 %collective-permute-start.4 = (f32[1,64,128]{2,1,0:T(8,128)S(1)}, f32[1,64,128]{2,1,0:T(8,128)S(1)}, u32[]{:S(2)}, u32[]{:S(2)}) collective-permute-start(f32[1,64,128]{2,1,0:T(8,128)S(1)} %get-tuple-element.60), channel_id=1, source_target_pairs={{16,0},{32,16},{48,32},{64,48},{80,64},{96,80},{112,96},{17,1},{33... | collective-permute-start | bytes 98312 | tf_op jit(solution)/shard_map/ppermute | solution.py:18
  90.0 9.4 %collective-permute-start.3 = (f32[32,128]{1,0:T(8,128)S(1)}, f32[32,128]{1,0:T(8,128)S(1)}, u32[]{:S(2)}, u32[]{:S(2)}) collective-permute-start(f32[32,128]{1,0:T(8,128)S(1)} %bitcast.86), channel_id=1, source_target_pairs={{0,1},{1,2},{2,3},{3,4},{4,5},{5,6},{6,7},{7,8},{8,9},{9,10},{10,1... | collective-permute-start | bytes 49160 | tf_op jit(solution)/shard_map/ppermute | solution.py:17
  92.9 6.5 %collective-permute-start.2 = (f32[32,128]{1,0:T(8,128)S(1)}, f32[32,128]{1,0:T(8,128)S(1)}, u32[]{:S(2)}, u32[]{:S(2)}) collective-permute-start(f32[32,128]{1,0:T(8,128)S(1)} %bitcast.85), channel_id=1, source_target_pairs={{1,0},{2,1},{3,2},{4,3},{5,4},{6,5},{7,6},{8,7},{9,8},{10,9},{11,1... | collective-permute-start | bytes 49160 | tf_op jit(solution)/shard_map/ppermute | solution.py:17
  94.2 5.2 %collective-permute-start = (f32[1,64,128]{2,1,0:T(8,128)S(1)}, f32[1,64,128]{2,1,0:T(8,128)S(1)}, u32[]{:S(2)}, u32[]{:S(2)}) collective-permute-start(f32[1,64,128]{2,1,0:T(8,128)S(1)} %get-tuple-element.35), channel_id=1, source_target_pairs={{16,0},{32,16},{48,32},{64,48},{80,64},{96,80},{112,96},{17,1},{33... | collective-permute-start | bytes 98312 | tf_op jit(solution)/shard_map/ppermute | solution.py:18
  95.5 3.9 %collective-permute-start.1 = (f32[1,64,128]{2,1,0:T(8,128)S(1)}, f32[1,64,128]{2,1,0:T(8,128)S(1)}, u32[]{:S(2)}, u32[]{:S(2)}) collective-permute-start(f32[1,64,128]{2,1,0:T(8,128)S(1)} %get-tuple-element.36), channel_id=1, source_target_pairs={{0,16},{16,32},{32,48},{48,64},{64,80},{80,96},{96,112},{1,17},{17... | collective-permute-start | bytes 98312 | tf_op jit(solution)/shard_map/ppermute | solution.py:18
  98.6 1.2 copy-start.1
  103.4 9.3 %collective-permute-start.11 = (f32[32,128]{1,0:T(8,128)S(1)}, f32[32,128]{1,0:T(8,128)S(1)}, u32[]{:S(2)}, u32[]{:S(2)}) collective-permute-start(f32[32,128]{1,0:T(8,128)S(1)} %bitcast.89), channel_id=1, source_target_pairs={{0,1},{1,2},{2,3},{3,4},{4,5},{5,6},{6,7},{7,8},{8,9},{9,10},{10,1... | collective-permute-start | bytes 49160 | tf_op jit(solution)/shard_map/ppermute | solution.py:17
  108.0 5.6 %collective-permute-start.10 = (f32[32,128]{1,0:T(8,128)S(1)}, f32[32,128]{1,0:T(8,128)S(1)}, u32[]{:S(2)}, u32[]{:S(2)}) collective-permute-start(f32[32,128]{1,0:T(8,128)S(1)} %bitcast.87), channel_id=1, source_target_pairs={{1,0},{2,1},{3,2},{4,3},{5,4},{6,5},{7,6},{8,7},{9,8},{10,9},{11,1... | collective-permute-start | bytes 49160 | tf_op jit(solution)/shard_map/ppermute | solution.py:17
  109.3 4.3 %collective-permute-start.9 = (f32[1,64,128]{2,1,0:T(8,128)S(1)}, f32[1,64,128]{2,1,0:T(8,128)S(1)}, u32[]{:S(2)}, u32[]{:S(2)}) collective-permute-start(f32[1,64,128]{2,1,0:T(8,128)S(1)} %get-tuple-element.50), channel_id=1, source_target_pairs={{0,16},{16,32},{32,48},{48,64},{64,80},{80,96},{96,112},{1,17},{17... | collective-permute-start | bytes 98312 | tf_op jit(solution)/shard_map/ppermute | solution.py:18
  111.1 5.0 %collective-permute-start.8 = (f32[1,64,128]{2,1,0:T(8,128)S(1)}, f32[1,64,128]{2,1,0:T(8,128)S(1)}, u32[]{:S(2)}, u32[]{:S(2)}) collective-permute-start(f32[1,64,128]{2,1,0:T(8,128)S(1)} %get-tuple-element.51), channel_id=1, source_target_pairs={{16,0},{32,16},{48,32},{64,48},{80,64},{96,80},{112,96},{17,1},{33... | collective-permute-start | bytes 98312 | tf_op jit(solution)/shard_map/ppermute | solution.py:18
  116.8 16.6 %copy-start.2 = (f32[32,64,128]{2,1,0:T(8,128)}, f32[32,64,128]{2,1,0:T(8,128)S(1)}, u32[]{:S(2)}) copy-start(f32[32,64,128]{2,1,0:T(8,128)S(1)} %get-tuple-element.32) | copy-start | bytes 3145732
  116.8 12.0 %collective-permute-start.15 = (f32[32,128]{1,0:T(8,128)S(1)}, f32[32,128]{1,0:T(8,128)S(1)}, u32[]{:S(2)}, u32[]{:S(2)}) collective-permute-start(f32[32,128]{1,0:T(8,128)S(1)} %bitcast.90), channel_id=1, source_target_pairs={{0,1},{1,2},{2,3},{3,4},{4,5},{5,6},{6,7},{7,8},{8,9},{9,10},{10,1... | collective-permute-start | bytes 49160 | tf_op jit(solution)/shard_map/ppermute | solution.py:17
  121.4 7.4 %collective-permute-start.14 = (f32[32,128]{1,0:T(8,128)S(1)}, f32[32,128]{1,0:T(8,128)S(1)}, u32[]{:S(2)}, u32[]{:S(2)}) collective-permute-start(f32[32,128]{1,0:T(8,128)S(1)} %bitcast.88), channel_id=1, source_target_pairs={{1,0},{2,1},{3,2},{4,3},{5,4},{6,5},{7,6},{8,7},{9,8},{10,9},{11,1... | collective-permute-start | bytes 49160 | tf_op jit(solution)/shard_map/ppermute | solution.py:17
  122.7 6.1 %collective-permute-start.13 = (f32[1,64,128]{2,1,0:T(8,128)S(1)}, f32[1,64,128]{2,1,0:T(8,128)S(1)}, u32[]{:S(2)}, u32[]{:S(2)}) collective-permute-start(f32[1,64,128]{2,1,0:T(8,128)S(1)} %get-tuple-element.44), channel_id=1, source_target_pairs={{0,16},{16,32},{32,48},{48,64},{64,80},{80,96},{96,112},{1,17},{17... | collective-permute-start | bytes 98312 | tf_op jit(solution)/shard_map/ppermute | solution.py:18
  126.9 3.1 %collective-permute-start.12 = (f32[1,64,128]{2,1,0:T(8,128)S(1)}, f32[1,64,128]{2,1,0:T(8,128)S(1)}, u32[]{:S(2)}, u32[]{:S(2)}) collective-permute-start(f32[1,64,128]{2,1,0:T(8,128)S(1)} %get-tuple-element.45), channel_id=1, source_target_pairs={{16,0},{32,16},{48,32},{64,48},{80,64},{96,80},{112,96},{17,1},{33... | collective-permute-start | bytes 98312 | tf_op jit(solution)/shard_map/ppermute | solution.py:18

commit v20 on v19

--- a/solution.py
+++ b/solution.py
@@ -65,7 +65,9 @@
     place = target * capacity + order
     high = lax.shift_right_logical(brick_slot, 5).astype(jnp.bfloat16)
     low = (brick_slot & 31).astype(jnp.bfloat16)
-    tag = jnp.zeros((bricks.shape[0], 128), jnp.bfloat16).at[:, 0].set(high).at[:, 1].set(low)
+    lanes = jnp.arange(128, dtype=jnp.int32)[None, :]
+    zero = jnp.zeros((), jnp.bfloat16)
+    tag = jnp.where(lanes == 0, high[:, None], jnp.where(lanes == 1, low[:, None], zero))
     rows = jnp.concatenate([bricks, tag], axis=1)
     chosen = place[None, None, :] == (
         jnp.arange(peers, dtype=jnp.int32)[:, None, None] * capacity

time: 184 us -> 181 us (0.984)
  waiting for transfers between devices: 37.7 us -> 33.1 us
  starting transfers between devices: 48.2 us -> 51.3 us
  other arithmetic: 18.6 us -> 16.2 us
    ppermute x8, waiting for transfers between devices: 4.53 us -> 0.43 us  [shifted(): return lax.ppermute(piece, axis, pairs)]
    another operation x6 -> x3, other arithmetic: 3.51 us -> 0.25 us
    ppermute x8, starting transfers between devices: 20.8 us -> 23.3 us  [shifted(): return lax.ppermute(flat, axis, pairs).reshape(piece.shape)]
  transfers between devices with their start and end apart: 17 -> 17, of which waited for: 5 -> 4; matrix products, arithmetic and copies ran while one was open for 7% -> 8% of each run, Pallas kernels for 7% -> 7%
where the time goes in v20:
time: 181 us; the launch traced here: 180 us
  starting transfers between devices  51.3 us (28%)
  blocking collectives  38.7 us (21%)
  waiting for transfers between devices  33.1 us (18%)
  other arithmetic  16.2 us (9%)
  local copies, waits for them, and re-layouts  16.2 us (9%)
  Pallas kernels  13.2 us (7%)
  between operations  6 us (3%)
  matrix products  5.56 us (3%)
    psum x4, blocking collectives, over_axes(): shard = lax.psum(shard, axis)  38.7 us
    all_to_all x1, waiting for transfers between devices, body(): lax.all_to_all(payload, GX_GY, split_axis=0, concat_axis=0, tiled=True)  30.6 us
    ppermute x8, starting transfers between devices, shifted(): return lax.ppermute(flat, axis, pairs).reshape(piece.shape)  23.3 us
    ppermute x8, starting transfers between devices, shifted(): return lax.ppermute(piece, axis, pairs)  16.4 us
    pallas_call x1, Pallas kernels, to_grid(): pl.pallas_call(relayout_kernel, out_shape=jax.ShapeDtypeStruct((3, span_x...  13.2 us
    all_to_all x1, starting transfers between devices, body(): lax.all_to_all(payload, GX_GY, split_axis=0, concat_axis=0, tiled=True)  11.6 us
  transfers between devices with their start and end apart: 17, of which 4 were waited for; matrix products, arithmetic and copies ran while one was open for 8% of the time, Pallas kernels for 7%

profile of v20, /device:TPU:0, one launch (start us, length us, event | category | flops | bytes accessed | tf_op | source)
XLA Modules:
  0.0 180.4 jit_solution(15855725329594608527)
XLA Ops:
  4.1 2.1 %convolution_convert_fusion = bf16[128,6,1664]{2,0,1:T(8,128)(2,1)S(1)} fusion(bf16[256,128]{1,0:T(8,128)(2,1)S(1)} %select_select_fusion, bf16[256,1536]{1,0:T(8,128)(2,1)} %param.5, s32[128,6]{0,1:T(8,128)S(1)} %iota_add_fusion, s32[256]{0:T(256)S(1)} %multiply_add_fusion.1), kind=kOutput, calls=%fused_computation | convolution fusion | flops 657489920 | bytes 3411968 | tf_op jit(solution)/shard_map/pck,kj->pcj/dot_general | solution.py:76
  6.2 3.2 %copy.28 = bf16[128,6,1664]{2,1,0:T(8,128)(2,1)} copy(bf16[128,6,1664]{2,0,1:T(8,128)(2,1)S(1)} %convolution_convert_fusion) | data formatting | bytes 5111808 | tf_op jit(solution)/shard_map/convert_element_type | solution.py:79
  9.4 11.6 %all-to-all-start = ((bf16[128,6,1664]{2,1,0:T(8,128)(2,1)}), bf16[128,6,1664]{2,1,0:T(8,128)(2,1)}, u32[]{:S(2)}, u32[]{:S(2)}) async-start(bf16[128,6,1664]{2,1,0:T(8,128)(2,1)} %copy.28), calls=%async_computation | async-start | bytes 6815744 | tf_op jit(solution)/shard_map/all_to_all | solution.py:159
  25.0 4.5 %collective-permute-start.7 = (f32[32,128]{1,0:T(8,128)S(1)}, f32[32,128]{1,0:T(8,128)S(1)}, u32[]{:S(2)}, u32[]{:S(2)}) collective-permute-start(f32[32,128]{1,0:T(8,128)S(1)} %bitcast.83), channel_id=1, source_target_pairs={{0,1},{1,2},{2,3},{3,4},{4,5},{5,6},{6,7},{7,8},{8,9},{9,10},{10,1... | collective-permute-start | bytes 49160 | tf_op jit(solution)/shard_map/ppermute | solution.py:17
  29.6 1.7 fusion.57
  33.5 30.6 %all-to-all-done = bf16[128,6,1664]{2,1,0:T(8,128)(2,1)} async-done(((bf16[128,6,1664]{2,1,0:T(8,128)(2,1)}), bf16[128,6,1664]{2,1,0:T(8,128)(2,1)}, u32[]{:S(2)}, u32[]{:S(2)}) %all-to-all-start) | async-done | bytes 2555936 | tf_op jit(solution)/shard_map/all_to_all | solution.py:159
  65.3 2.1 %slice.242 = bf16[128,6,1536]{2,1,0:T(8,128)(2,1)S(1)} slice(bf16[128,6,1664]{2,1,0:T(8,128)(2,1)} %all-to-all-done), slice={[0:128], [0:6], [0:1536]} | slice | bytes 4718592 | tf_op jit(solution)/shard_map/slice | solution.py:170
  67.4 3.5 %convolution_bitcast_fusion.blk_ref = f32[512,1536]{1,0:T(8,128)} fusion(bf16[128,6,1536]{2,1,0:T(8,128)(2,1)S(1)} %slice.242, s32[128,6]{0,1:T(8,128)S(1)} %fusion.40), kind=kOutput, calls=%fused_computation.1 | convolution fusion | flops 1208352768 | bytes 5508096 | tf_op jit(solution)/shard_map/pcs,pcj->sj/dot_general | solution.py:167
  70.9 13.2 %shard_map.68 = f32[3,32,64,128]{3,2,1,0:T(8,128)} custom-call(f32[512,1536]{1,0:T(8,128)} %convolution_bitcast_fusion.blk_ref), custom_call_target="tpu_custom_call" | custom-call | flops 15728640 | bytes 6291456 | tf_op jit(solution)/shard_map/pallas_call | solution.py:145
  84.2 2.1 %slice_bitcast_fusion.2 = (f32[32,64,128]{2,1,0:T(8,128)S(1)}, f32[32,64,128]{2,1,0:T(8,128)S(1)}, f32[32,64,128]{2,1,0:T(8,128)S(1)}) fusion(f32[3,32,64,128]{3,2,1,0:T(8,128)} %shard_map.68), kind=kLoop, calls=%fused_computation.62 | loop fusion | bytes 6291456 | tf_op jit(solution)/shard_map/squeeze | solution.py:174
  88.6 4.5 %collective-permute-start.3 = (f32[32,128]{1,0:T(8,128)S(1)}, f32[32,128]{1,0:T(8,128)S(1)}, u32[]{:S(2)}, u32[]{:S(2)}) collective-permute-start(f32[32,128]{1,0:T(8,128)S(1)} %bitcast.85), channel_id=1, source_target_pairs={{0,1},{1,2},{2,3},{3,4},{4,5},{5,6},{6,7},{7,8},{8,9},{9,10},{10,1... | collective-permute-start | bytes 49160 | tf_op jit(solution)/shard_map/ppermute | solution.py:17
  94.4 3.0 %collective-permute-start.1 = (f32[1,64,128]{2,1,0:T(8,128)S(1)}, f32[1,64,128]{2,1,0:T(8,128)S(1)}, u32[]{:S(2)}, u32[]{:S(2)}) collective-permute-start(f32[1,64,128]{2,1,0:T(8,128)S(1)} %get-tuple-element.12), channel_id=1, source_target_pairs={{0,16},{16,32},{32,48},{48,64},{64,80},{80,96},{96,112},{1,17},{17... | collective-permute-start | bytes 98312 | tf_op jit(solution)/shard_map/ppermute | solution.py:18
  98.3 3.6 %fusion.43 = (f32[32,64,128]{2,1,0:T(8,128)S(1)}, f32[32,64,128]{2,1,0:T(8,128)S(1)}) fusion(f32[32,64,128]{2,1,0:T(8,128)S(1)} %copy-done.1, f32[32,64,127]{2,1,0:T(8,128)S(1)} %copy-done.4, f32[32,64,127]{2,1,0:T(8,128)S(1)} %copy-done.3, f32[34,64,128]{2,1,0:T(8,128)} %constant_dynamic-update-slice_fusion, f32[32,1,128]{2,1,0:T(1,128)S(1)} %bitcast.75, ...), kind=kLoop, calls=%fused_computation.107 | loop fusion | flops 8126464 | bytes 11763712 | tf_op jit(solution)/shard_map/mul | solution.py:183
  103.2 3.1 %collective-permute-start.9 = (f32[1,64,128]{2,1,0:T(8,128)S(1)}, f32[1,64,128]{2,1,0:T(8,128)S(1)}, u32[]{:S(2)}, u32[]{:S(2)}) collective-permute-start(f32[1,64,128]{2,1,0:T(8,128)S(1)} %get-tuple-element.26), channel_id=1, source_target_pairs={{0,16},{16,32},{32,48},{48,64},{64,80},{80,96},{96,112},{1,17},{17... | collective-permute-start | bytes 98312 | tf_op jit(solution)/shard_map/ppermute | solution.py:18
  107.7 4.5 %collective-permute-start.11 = (f32[32,128]{1,0:T(8,128)S(1)}, f32[32,128]{1,0:T(8,128)S(1)}, u32[]{:S(2)}, u32[]{:S(2)}) collective-permute-start(f32[32,128]{1,0:T(8,128)S(1)} %bitcast.87), channel_id=1, source_target_pairs={{0,1},{1,2},{2,3},{3,4},{4,5},{5,6},{6,7},{7,8},{8,9},{9,10},{10,1... | collective-permute-start | bytes 49160 | tf_op jit(solution)/shard_map/ppermute | solution.py:17
  115.7 3.7 %collective-permute-start.13 = (f32[1,64,128]{2,1,0:T(8,128)S(1)}, f32[1,64,128]{2,1,0:T(8,128)S(1)}, u32[]{:S(2)}, u32[]{:S(2)}) collective-permute-start(f32[1,64,128]{2,1,0:T(8,128)S(1)} %get-tuple-element.20), channel_id=1, source_target_pairs={{0,16},{16,32},{32,48},{48,64},{64,80},{80,96},{96,112},{1,17},{17... | collective-permute-start | bytes 98312 | tf_op jit(solution)/shard_map/ppermute | solution.py:18
  120.8 4.5 %collective-permute-start.15 = (f32[32,128]{1,0:T(8,128)S(1)}, f32[32,128]{1,0:T(8,128)S(1)}, u32[]{:S(2)}, u32[]{:S(2)}) collective-permute-start(f32[32,128]{1,0:T(8,128)S(1)} %bitcast.88), channel_id=1, source_target_pairs={{0,1},{1,2},{2,3},{3,4},{4,5},{5,6},{6,7},{7,8},{8,9},{9,10},{10,1... | collective-permute-start | bytes 49160 | tf_op jit(solution)/shard_map/ppermute | solution.py:17
  126.7 3.3 %multiply_reduce_fusion.3 = (f32[]{:T(128)}, f32[]{:T(128)}, f32[]{:T(128)}, f32[]{:T(128)}, f32[32,64,128]{2,1,0:T(8,128)}) fusion(f32[32,64,128]{2,1,0:T(8,128)S(1)} %get-tuple-element.10, f32[32,64,128]{2,1,0:T(8,128)S(1)} %copy-done.1, f32[32,64,128]{2,1,0:T(8,128)S(1)} %get-tuple-element.8, f32[32,64,128]{2,1,0:T(8,128)S(1)} %get-tuple-element.7, ...), kind=kLoop, calls=%fused_computation.69 | loop fusion | flops 8388604 | bytes 7421968 | tf_op jit(solution)/shard_map/reduce_sum | solution.py:190
  130.1 2.5 %pad_maximum_fusion.20 = f32[4]{0:T(128)S(1)} fusion(f32[1]{0:T(128)} %bitcast.33, f32[1]{0:T(128)} %bitcast.28, f32[1]{0:T(128)} %bitcast.27, f32[1]{0:T(128)} %bitcast.22), kind=kLoop, calls=%fused_computation.101 | loop fusion | flops 12 | bytes 32 | tf_op jit(solution)/shard_map/stack | solution.py:188
  132.6 10.6 %psum.28 = f32[4]{0:T(128)S(1)} all-reduce(f32[4]{0:T(128)S(1)} %pad_maximum_fusion.20), channel_id=1, replica_groups=mesh['gx_0'=4,'gx_1'=2,'gy_0'=4,'gy_1'=4] {'gx_0'}, use_global_device_ids=true, to_apply=%region_7.8 | all-reduce | flops 4 | bytes 32 | tf_op jit(solution)/shard_map/psum | solution.py:43
  143.2 2.5 %psum.29 = f32[4]{0:T(128)S(1)} all-reduce(f32[4]{0:T(128)S(1)} %psum.28), channel_id=1, replica_groups=mesh['gx_0'=4,'gx_1'=2,'gy_0'=4,'gy_1'=4] {'gx_1'}, use_global_device_ids=true, to_apply=%region_8.9 | all-reduce | flops 4 | bytes 32 | tf_op jit(solution)/shard_map/psum | solution.py:43
  145.7 17.9 %psum.30 = f32[4]{0:T(128)S(1)} all-reduce(f32[4]{0:T(128)S(1)} %psum.29), channel_id=1, replica_groups=mesh['gx_0'=4,'gx_1'=2,'gy_0'=4,'gy_1'=4] {'gy_0'}, use_global_device_ids=true, to_apply=%region_9.10 | all-reduce | flops 4 | bytes 32 | tf_op jit(solution)/shard_map/psum | solution.py:43
  163.6 7.7 %psum.31 = f32[4]{0:T(128)S(1)} all-reduce(f32[4]{0:T(128)S(1)} %psum.30), channel_id=1, replica_groups=mesh['gx_0'=4,'gx_1'=2,'gy_0'=4,'gy_1'=4] {'gy_1'}, use_global_device_ids=true, to_apply=%region_10.11 | all-reduce | flops 4 | bytes 32 | tf_op jit(solution)/shard_map/psum | solution.py:43
  176.9 3.5 %multiply_subtract_fusion = (f32[32,64,128]{2,1,0:T(8,128)}, f32[32,64,128]{2,1,0:T(8,128)}) fusion(f32[32,64,128]{2,1,0:T(8,128)} %copy-done.2, f32[32,64,128]{2,1,0:T(8,128)} %get-tuple-element.6, f32[32,64,128]{2,1,0:T(8,128)S(1)} %get-tuple-element.10, f32[]{:T(128)S(6)} %div.18, f32[]{:T(128)S(6)} %div.19, f32[]{:T(128)S(6)} %div.17, ...), kind=kLoop, calls=%fused_computation.63 | loop fusion | flops 4718592 | bytes 7340044 | tf_op jit(solution)/shard_map/sub | solution.py:210
  (70 shorter events, 24.6 us)
Async XLA Ops:
  9.4 11.6 %copy-start = (f32[32,64,128]{2,1,0:T(8,128)S(1)}, f32[32,64,128]{2,1,0:T(8,128)}, u32[]{:S(2)}) copy-start(f32[32,64,128]{2,1,0:T(8,128)} %param.9) | copy-start | bytes 3145732
  9.4 54.7 %all-to-all-start = ((bf16[128,6,1664]{2,1,0:T(8,128)(2,1)}), bf16[128,6,1664]{2,1,0:T(8,128)(2,1)}, u32[]{:S(2)}, u32[]{:S(2)}) async-start(bf16[128,6,1664]{2,1,0:T(8,128)(2,1)} %copy.28), calls=%async_computation | async-start | bytes 6815744 | tf_op jit(solution)/shard_map/all_to_all | solution.py:159
  21.1 10.2 %collective-permute-start.5 = (f32[1,64,128]{2,1,0:T(8,128)S(1)}, f32[1,64,128]{2,1,0:T(8,128)S(1)}, u32[]{:S(2)}, u32[]{:S(2)}) collective-permute-start(f32[1,64,128]{2,1,0:T(8,128)S(1)} %get-tuple-element.37), channel_id=1, source_target_pairs={{0,16},{16,32},{32,48},{48,64},{64,80},{80,96},{96,112},{1,17},{17... | collective-permute-start | bytes 98312 | tf_op jit(solution)/shard_map/ppermute | solution.py:18
  22.4 10.5 %collective-permute-start.4 = (f32[1,64,128]{2,1,0:T(8,128)S(1)}, f32[1,64,128]{2,1,0:T(8,128)S(1)}, u32[]{:S(2)}, u32[]{:S(2)}) collective-permute-start(f32[1,64,128]{2,1,0:T(8,128)S(1)} %get-tuple-element.36), channel_id=1, source_target_pairs={{16,0},{32,16},{48,32},{64,48},{80,64},{96,80},{112,96},{17,1},{33... | collective-permute-start | bytes 98312 | tf_op jit(solution)/shard_map/ppermute | solution.py:18
  23.7 70.7 %collective-permute-start.6 = (f32[32,128]{1,0:T(8,128)S(1)}, f32[32,128]{1,0:T(8,128)S(1)}, u32[]{:S(2)}, u32[]{:S(2)}) collective-permute-start(f32[32,128]{1,0:T(8,128)S(1)} %bitcast.84), channel_id=1, source_target_pairs={{1,0},{2,1},{3,2},{4,3},{5,4},{6,5},{7,6},{8,7},{9,8},{10,9},{11,1... | collective-permute-start | bytes 49160 | tf_op jit(solution)/shard_map/ppermute | solution.py:17
  25.0 72.8 %collective-permute-start.7 = (f32[32,128]{1,0:T(8,128)S(1)}, f32[32,128]{1,0:T(8,128)S(1)}, u32[]{:S(2)}, u32[]{:S(2)}) collective-permute-start(f32[32,128]{1,0:T(8,128)S(1)} %bitcast.83), channel_id=1, source_target_pairs={{0,1},{1,2},{2,3},{3,4},{4,5},{5,6},{6,7},{7,8},{8,9},{9,10},{10,1... | collective-permute-start | bytes 49160 | tf_op jit(solution)/shard_map/ppermute | solution.py:17
  86.3 12.0 %copy-start.1 = (f32[32,64,128]{2,1,0:T(8,128)S(1)}, f32[32,64,128]{2,1,0:T(8,128)}, u32[]{:S(2)}) copy-start(f32[32,64,128]{2,1,0:T(8,128)} %param.8) | copy-start | bytes 3145732
  86.3 12.0 %copy-start.3 = (f32[32,64,127]{2,1,0:T(8,128)S(1)}, f32[32,64,127]{2,1,0:T(8,128)}, u32[]{:S(2)}) copy-start(f32[32,64,127]{2,1,0:T(8,128)} %get-tuple-element.38) | copy-start | bytes 3121156
  86.3 12.0 %copy-start.4 = (f32[32,64,127]{2,1,0:T(8,128)S(1)}, f32[32,64,127]{2,1,0:T(8,128)}, u32[]{:S(2)}) copy-start(f32[32,64,127]{2,1,0:T(8,128)} %get-tuple-element.39) | copy-start | bytes 3121156
  87.3 10.6 %collective-permute-start.2 = (f32[32,128]{1,0:T(8,128)S(1)}, f32[32,128]{1,0:T(8,128)S(1)}, u32[]{:S(2)}, u32[]{:S(2)}) collective-permute-start(f32[32,128]{1,0:T(8,128)S(1)} %bitcast.86), channel_id=1, source_target_pairs={{1,0},{2,1},{3,2},{4,3},{5,4},{6,5},{7,6},{8,7},{9,8},{10,9},{11,1... | collective-permute-start | bytes 49160 | tf_op jit(solution)/shard_map/ppermute | solution.py:17
  88.6 9.3 %collective-permute-start.3 = (f32[32,128]{1,0:T(8,128)S(1)}, f32[32,128]{1,0:T(8,128)S(1)}, u32[]{:S(2)}, u32[]{:S(2)}) collective-permute-start(f32[32,128]{1,0:T(8,128)S(1)} %bitcast.85), channel_id=1, source_target_pairs={{0,1},{1,2},{2,3},{3,4},{4,5},{5,6},{6,7},{7,8},{8,9},{9,10},{10,1... | collective-permute-start | bytes 49160 | tf_op jit(solution)/shard_map/ppermute | solution.py:17
  93.1 4.8 %collective-permute-start = (f32[1,64,128]{2,1,0:T(8,128)S(1)}, f32[1,64,128]{2,1,0:T(8,128)S(1)}, u32[]{:S(2)}, u32[]{:S(2)}) collective-permute-start(f32[1,64,128]{2,1,0:T(8,128)S(1)} %get-tuple-element.11), channel_id=1, source_target_pairs={{16,0},{32,16},{48,32},{64,48},{80,64},{96,80},{112,96},{17,1},{33... | collective-permute-start | bytes 98312 | tf_op jit(solution)/shard_map/ppermute | solution.py:18
  94.4 3.9 %collective-permute-start.1 = (f32[1,64,128]{2,1,0:T(8,128)S(1)}, f32[1,64,128]{2,1,0:T(8,128)S(1)}, u32[]{:S(2)}, u32[]{:S(2)}) collective-permute-start(f32[1,64,128]{2,1,0:T(8,128)S(1)} %get-tuple-element.12), channel_id=1, source_target_pairs={{0,16},{16,32},{32,48},{48,64},{64,80},{80,96},{96,112},{1,17},{17... | collective-permute-start | bytes 98312 | tf_op jit(solution)/shard_map/ppermute | solution.py:18
  101.9 11.7 %collective-permute-start.8 = (f32[1,64,128]{2,1,0:T(8,128)S(1)}, f32[1,64,128]{2,1,0:T(8,128)S(1)}, u32[]{:S(2)}, u32[]{:S(2)}) collective-permute-start(f32[1,64,128]{2,1,0:T(8,128)S(1)} %get-tuple-element.27), channel_id=1, source_target_pairs={{16,0},{32,16},{48,32},{64,48},{80,64},{96,80},{112,96},{17,1},{33... | collective-permute-start | bytes 98312 | tf_op jit(solution)/shard_map/ppermute | solution.py:18
  103.2 10.4 %collective-permute-start.9 = (f32[1,64,128]{2,1,0:T(8,128)S(1)}, f32[1,64,128]{2,1,0:T(8,128)S(1)}, u32[]{:S(2)}, u32[]{:S(2)}) collective-permute-start(f32[1,64,128]{2,1,0:T(8,128)S(1)} %get-tuple-element.26), channel_id=1, source_target_pairs={{0,16},{16,32},{32,48},{48,64},{64,80},{80,96},{96,112},{1,17},{17... | collective-permute-start | bytes 98312 | tf_op jit(solution)/shard_map/ppermute | solution.py:18
  106.4 6.2 %collective-permute-start.10 = (f32[32,128]{1,0:T(8,128)S(1)}, f32[32,128]{1,0:T(8,128)S(1)}, u32[]{:S(2)}, u32[]{:S(2)}) collective-permute-start(f32[32,128]{1,0:T(8,128)S(1)} %bitcast.89), channel_id=1, source_target_pairs={{1,0},{2,1},{3,2},{4,3},{5,4},{6,5},{7,6},{8,7},{9,8},{10,9},{11,1... | collective-permute-start | bytes 49160 | tf_op jit(solution)/shard_map/ppermute | solution.py:17
  107.7 6.0 %collective-permute-start.11 = (f32[32,128]{1,0:T(8,128)S(1)}, f32[32,128]{1,0:T(8,128)S(1)}, u32[]{:S(2)}, u32[]{:S(2)}) collective-permute-start(f32[32,128]{1,0:T(8,128)S(1)} %bitcast.87), channel_id=1, source_target_pairs={{0,1},{1,2},{2,3},{3,4},{4,5},{5,6},{6,7},{7,8},{8,9},{9,10},{10,1... | collective-permute-start | bytes 49160 | tf_op jit(solution)/shard_map/ppermute | solution.py:17
  114.3 15.7 %copy-start.2 = (f32[32,64,128]{2,1,0:T(8,128)}, f32[32,64,128]{2,1,0:T(8,128)S(1)}, u32[]{:S(2)}) copy-start(f32[32,64,128]{2,1,0:T(8,128)S(1)} %get-tuple-element.8) | copy-start | bytes 3145732
  114.4 12.3 %collective-permute-start.12 = (f32[1,64,128]{2,1,0:T(8,128)S(1)}, f32[1,64,128]{2,1,0:T(8,128)S(1)}, u32[]{:S(2)}, u32[]{:S(2)}) collective-permute-start(f32[1,64,128]{2,1,0:T(8,128)S(1)} %get-tuple-element.21), channel_id=1, source_target_pairs={{16,0},{32,16},{48,32},{64,48},{80,64},{96,80},{112,96},{17,1},{33... | collective-permute-start | bytes 98312 | tf_op jit(solution)/shard_map/ppermute | solution.py:18
  115.7 11.0 %collective-permute-start.13 = (f32[1,64,128]{2,1,0:T(8,128)S(1)}, f32[1,64,128]{2,1,0:T(8,128)S(1)}, u32[]{:S(2)}, u32[]{:S(2)}) collective-permute-start(f32[1,64,128]{2,1,0:T(8,128)S(1)} %get-tuple-element.20), channel_id=1, source_target_pairs={{0,16},{16,32},{32,48},{48,64},{64,80},{80,96},{96,112},{1,17},{17... | collective-permute-start | bytes 98312 | tf_op jit(solution)/shard_map/ppermute | solution.py:18
  119.5 6.2 %collective-permute-start.14 = (f32[32,128]{1,0:T(8,128)S(1)}, f32[32,128]{1,0:T(8,128)S(1)}, u32[]{:S(2)}, u32[]{:S(2)}) collective-permute-start(f32[32,128]{1,0:T(8,128)S(1)} %bitcast.90), channel_id=1, source_target_pairs={{1,0},{2,1},{3,2},{4,3},{5,4},{6,5},{7,6},{8,7},{9,8},{10,9},{11,1... | collective-permute-start | bytes 49160 | tf_op jit(solution)/shard_map/ppermute | solution.py:17
  120.8 6.0 %collective-permute-start.15 = (f32[32,128]{1,0:T(8,128)S(1)}, f32[32,128]{1,0:T(8,128)S(1)}, u32[]{:S(2)}, u32[]{:S(2)}) collective-permute-start(f32[32,128]{1,0:T(8,128)S(1)} %bitcast.88), channel_id=1, source_target_pairs={{0,1},{1,2},{2,3},{3,4},{4,5},{5,6},{6,7},{7,8},{8,9},{9,10},{10,1... | collective-permute-start | bytes 49160 | tf_op jit(solution)/shard_map/ppermute | solution.py:17

commit v21 on v20

--- a/solution.py
+++ b/solution.py
@@ -69,13 +69,10 @@
     zero = jnp.zeros((), jnp.bfloat16)
     tag = jnp.where(lanes == 0, high[:, None], jnp.where(lanes == 1, low[:, None], zero))
     rows = jnp.concatenate([bricks, tag], axis=1)
-    chosen = place[None, None, :] == (
-        jnp.arange(peers, dtype=jnp.int32)[:, None, None] * capacity
-        + jnp.arange(capacity, dtype=jnp.int32)[None, :, None]
-    )
+    chosen = place[None, :] == jnp.arange(peers * capacity, dtype=jnp.int32)[:, None]
     payload = jnp.einsum(
-        "pck,kj->pcj", chosen.astype(jnp.bfloat16), rows, preferred_element_type=jnp.float32
-    )
+        "pk,kj->pj", chosen.astype(jnp.bfloat16), rows, preferred_element_type=jnp.float32
+    ).reshape(peers, capacity, rows.shape[1])
     return payload.astype(jnp.bfloat16)
 
 

time: 181 us -> 181 us (level)
  no operation moved by 1% of the time
where the time goes in v21:
time: 181 us; the launch traced here: 180 us
  starting transfers between devices  51.3 us (28%)
  blocking collectives  38.7 us (21%)
  waiting for transfers between devices  33.1 us (18%)
  other arithmetic  16.2 us (9%)
  local copies, waits for them, and re-layouts  15.6 us (9%)
  Pallas kernels  13.2 us (7%)
  between operations  5.99 us (3%)
  matrix products  5.52 us (3%)
    psum x4, blocking collectives, over_axes(): shard = lax.psum(shard, axis)  38.7 us
    all_to_all x1, waiting for transfers between devices, body(): lax.all_to_all(payload, GX_GY, split_axis=0, concat_axis=0, tiled=True)  30.6 us
    ppermute x8, starting transfers between devices, shifted(): return lax.ppermute(flat, axis, pairs).reshape(piece.shape)  23.3 us
    ppermute x8, starting transfers between devices, shifted(): return lax.ppermute(piece, axis, pairs)  16.4 us
    pallas_call x1, Pallas kernels, to_grid(): pl.pallas_call(relayout_kernel, out_shape=jax.ShapeDtypeStruct((3, span_x...  13.2 us
    all_to_all x1, starting transfers between devices, body(): lax.all_to_all(payload, GX_GY, split_axis=0, concat_axis=0, tiled=True)  11.6 us
  transfers between devices with their start and end apart: 17, of which 4 were waited for; matrix products, arithmetic and copies ran while one was open for 8% of the time, Pallas kernels for 7%

profile of v21, /device:TPU:0, one launch (start us, length us, event | category | flops | bytes accessed | tf_op | source)
XLA Modules:
  0.0 179.8 jit_solution(238378892011940896)
XLA Ops:
  4.1 2.0 %convolution_convert_fusion = bf16[768,1664]{1,0:T(8,128)(2,1)S(1)} fusion(bf16[256,128]{1,0:T(8,128)(2,1)S(1)} %select_select_fusion, bf16[256,1536]{1,0:T(8,128)(2,1)} %param.5, s32[256]{0:T(256)S(1)} %multiply_add_fusion.1), kind=kOutput, calls=%fused_computation | convolution fusion | flops 657489920 | bytes 3408896 | tf_op jit(solution)/shard_map/pk,kj->pj/dot_general | solution.py:73
  6.1 2.6 %convert_element_type.36 = bf16[128,6,1664]{2,1,0:T(8,128)(2,1)} reshape(bf16[768,1664]{1,0:T(8,128)(2,1)S(1)} %convolution_convert_fusion) | data formatting | bytes 5111808 | tf_op jit(solution)/shard_map/convert_element_type | solution.py:76
  8.7 11.6 %all-to-all-start = ((bf16[128,6,1664]{2,1,0:T(8,128)(2,1)}), bf16[128,6,1664]{2,1,0:T(8,128)(2,1)}, u32[]{:S(2)}, u32[]{:S(2)}) async-start(bf16[128,6,1664]{2,1,0:T(8,128)(2,1)} %convert_element_type.36), calls=%async_computation | async-start | bytes 6815744 | tf_op jit(solution)/shard_map/all_to_all | solution.py:156
  24.3 4.5 %collective-permute-start.7 = (f32[32,128]{1,0:T(8,128)S(1)}, f32[32,128]{1,0:T(8,128)S(1)}, u32[]{:S(2)}, u32[]{:S(2)}) collective-permute-start(f32[32,128]{1,0:T(8,128)S(1)} %bitcast.80), channel_id=1, source_target_pairs={{0,1},{1,2},{2,3},{3,4},{4,5},{5,6},{6,7},{7,8},{8,9},{9,10},{10,1... | collective-permute-start | bytes 49160 | tf_op jit(solution)/shard_map/ppermute | solution.py:17
  28.9 1.7 fusion.56
  32.9 30.6 %all-to-all-done = bf16[128,6,1664]{2,1,0:T(8,128)(2,1)} async-done(((bf16[128,6,1664]{2,1,0:T(8,128)(2,1)}), bf16[128,6,1664]{2,1,0:T(8,128)(2,1)}, u32[]{:S(2)}, u32[]{:S(2)}) %all-to-all-start) | async-done | bytes 2555936 | tf_op jit(solution)/shard_map/all_to_all | solution.py:156
  64.7 2.1 %slice.242 = bf16[128,6,1536]{2,1,0:T(8,128)(2,1)S(1)} slice(bf16[128,6,1664]{2,1,0:T(8,128)(2,1)} %all-to-all-done), slice={[0:128], [0:6], [0:1536]} | slice | bytes 4718592 | tf_op jit(solution)/shard_map/slice | solution.py:167
  66.8 3.5 %convolution_bitcast_fusion.blk_ref = f32[512,1536]{1,0:T(8,128)} fusion(bf16[128,6,1536]{2,1,0:T(8,128)(2,1)S(1)} %slice.242, s32[128,6]{0,1:T(8,128)S(1)} %fusion.39), kind=kOutput, calls=%fused_computation.1 | convolution fusion | flops 1208352768 | bytes 5508096 | tf_op jit(solution)/shard_map/pcs,pcj->sj/dot_general | solution.py:164
  70.3 13.2 %shard_map.68 = f32[3,32,64,128]{3,2,1,0:T(8,128)} custom-call(f32[512,1536]{1,0:T(8,128)} %convolution_bitcast_fusion.blk_ref), custom_call_target="tpu_custom_call" | custom-call | flops 15728640 | bytes 6291456 | tf_op jit(solution)/shard_map/pallas_call | solution.py:142
  83.5 2.1 %slice_bitcast_fusion.2 = (f32[32,64,128]{2,1,0:T(8,128)S(1)}, f32[32,64,128]{2,1,0:T(8,128)S(1)}, f32[32,64,128]{2,1,0:T(8,128)S(1)}) fusion(f32[3,32,64,128]{3,2,1,0:T(8,128)} %shard_map.68), kind=kLoop, calls=%fused_computation.62 | loop fusion | bytes 6291456 | tf_op jit(solution)/shard_map/squeeze | solution.py:171
  87.9 4.5 %collective-permute-start.3 = (f32[32,128]{1,0:T(8,128)S(1)}, f32[32,128]{1,0:T(8,128)S(1)}, u32[]{:S(2)}, u32[]{:S(2)}) collective-permute-start(f32[32,128]{1,0:T(8,128)S(1)} %bitcast.82), channel_id=1, source_target_pairs={{0,1},{1,2},{2,3},{3,4},{4,5},{5,6},{6,7},{7,8},{8,9},{9,10},{10,1... | collective-permute-start | bytes 49160 | tf_op jit(solution)/shard_map/ppermute | solution.py:17
  93.8 3.0 %collective-permute-start.1 = (f32[1,64,128]{2,1,0:T(8,128)S(1)}, f32[1,64,128]{2,1,0:T(8,128)S(1)}, u32[]{:S(2)}, u32[]{:S(2)}) collective-permute-start(f32[1,64,128]{2,1,0:T(8,128)S(1)} %get-tuple-element.12), channel_id=1, source_target_pairs={{0,16},{16,32},{32,48},{48,64},{64,80},{80,96},{96,112},{1,17},{17... | collective-permute-start | bytes 98312 | tf_op jit(solution)/shard_map/ppermute | solution.py:18
  97.6 3.6 %fusion.42 = (f32[32,64,128]{2,1,0:T(8,128)S(1)}, f32[32,64,128]{2,1,0:T(8,128)S(1)}) fusion(f32[32,64,128]{2,1,0:T(8,128)S(1)} %copy-done.1, f32[32,64,127]{2,1,0:T(8,128)S(1)} %copy-done.4, f32[32,64,127]{2,1,0:T(8,128)S(1)} %copy-done.3, f32[34,64,128]{2,1,0:T(8,128)} %constant_dynamic-update-slice_fusion, f32[32,1,128]{2,1,0:T(1,128)S(1)} %bitcast.72, ...), kind=kLoop, calls=%fused_computation.104 | loop fusion | flops 8126464 | bytes 11763712 | tf_op jit(solution)/shard_map/mul | solution.py:180
  102.6 3.1 %collective-permute-start.9 = (f32[1,64,128]{2,1,0:T(8,128)S(1)}, f32[1,64,128]{2,1,0:T(8,128)S(1)}, u32[]{:S(2)}, u32[]{:S(2)}) collective-permute-start(f32[1,64,128]{2,1,0:T(8,128)S(1)} %get-tuple-element.26), channel_id=1, source_target_pairs={{0,16},{16,32},{32,48},{48,64},{64,80},{80,96},{96,112},{1,17},{17... | collective-permute-start | bytes 98312 | tf_op jit(solution)/shard_map/ppermute | solution.py:18
  107.0 4.5 %collective-permute-start.11 = (f32[32,128]{1,0:T(8,128)S(1)}, f32[32,128]{1,0:T(8,128)S(1)}, u32[]{:S(2)}, u32[]{:S(2)}) collective-permute-start(f32[32,128]{1,0:T(8,128)S(1)} %bitcast.84), channel_id=1, source_target_pairs={{0,1},{1,2},{2,3},{3,4},{4,5},{5,6},{6,7},{7,8},{8,9},{9,10},{10,1... | collective-permute-start | bytes 49160 | tf_op jit(solution)/shard_map/ppermute | solution.py:17
  115.0 3.7 %collective-permute-start.13 = (f32[1,64,128]{2,1,0:T(8,128)S(1)}, f32[1,64,128]{2,1,0:T(8,128)S(1)}, u32[]{:S(2)}, u32[]{:S(2)}) collective-permute-start(f32[1,64,128]{2,1,0:T(8,128)S(1)} %get-tuple-element.20), channel_id=1, source_target_pairs={{0,16},{16,32},{32,48},{48,64},{64,80},{80,96},{96,112},{1,17},{17... | collective-permute-start | bytes 98312 | tf_op jit(solution)/shard_map/ppermute | solution.py:18
  120.1 4.5 %collective-permute-start.15 = (f32[32,128]{1,0:T(8,128)S(1)}, f32[32,128]{1,0:T(8,128)S(1)}, u32[]{:S(2)}, u32[]{:S(2)}) collective-permute-start(f32[32,128]{1,0:T(8,128)S(1)} %bitcast.85), channel_id=1, source_target_pairs={{0,1},{1,2},{2,3},{3,4},{4,5},{5,6},{6,7},{7,8},{8,9},{9,10},{10,1... | collective-permute-start | bytes 49160 | tf_op jit(solution)/shard_map/ppermute | solution.py:17
  126.1 3.3 %multiply_reduce_fusion.3 = (f32[]{:T(128)}, f32[]{:T(128)}, f32[]{:T(128)}, f32[]{:T(128)}, f32[32,64,128]{2,1,0:T(8,128)}) fusion(f32[32,64,128]{2,1,0:T(8,128)S(1)} %get-tuple-element.10, f32[32,64,128]{2,1,0:T(8,128)S(1)} %copy-done.1, f32[32,64,128]{2,1,0:T(8,128)S(1)} %get-tuple-element.8, f32[32,64,128]{2,1,0:T(8,128)S(1)} %get-tuple-element.7, ...), kind=kLoop, calls=%fused_computation.69 | loop fusion | flops 8388604 | bytes 7421968 | tf_op jit(solution)/shard_map/reduce_sum | solution.py:187
  129.4 2.5 %pad_maximum_fusion.20 = f32[4]{0:T(128)S(1)} fusion(f32[1]{0:T(128)} %bitcast.32, f32[1]{0:T(128)} %bitcast.27, f32[1]{0:T(128)} %bitcast.26, f32[1]{0:T(128)} %bitcast.21), kind=kLoop, calls=%fused_computation.99 | loop fusion | flops 12 | bytes 32 | tf_op jit(solution)/shard_map/stack | solution.py:185
  131.9 10.6 %psum.28 = f32[4]{0:T(128)S(1)} all-reduce(f32[4]{0:T(128)S(1)} %pad_maximum_fusion.20), channel_id=1, replica_groups=mesh['gx_0'=4,'gx_1'=2,'gy_0'=4,'gy_1'=4] {'gx_0'}, use_global_device_ids=true, to_apply=%region_7.8 | all-reduce | flops 4 | bytes 32 | tf_op jit(solution)/shard_map/psum | solution.py:43
  142.5 2.5 %psum.29 = f32[4]{0:T(128)S(1)} all-reduce(f32[4]{0:T(128)S(1)} %psum.28), channel_id=1, replica_groups=mesh['gx_0'=4,'gx_1'=2,'gy_0'=4,'gy_1'=4] {'gx_1'}, use_global_device_ids=true, to_apply=%region_8.9 | all-reduce | flops 4 | bytes 32 | tf_op jit(solution)/shard_map/psum | solution.py:43
  145.0 17.9 %psum.30 = f32[4]{0:T(128)S(1)} all-reduce(f32[4]{0:T(128)S(1)} %psum.29), channel_id=1, replica_groups=mesh['gx_0'=4,'gx_1'=2,'gy_0'=4,'gy_1'=4] {'gy_0'}, use_global_device_ids=true, to_apply=%region_9.10 | all-reduce | flops 4 | bytes 32 | tf_op jit(solution)/shard_map/psum | solution.py:43
  162.9 7.7 %psum.31 = f32[4]{0:T(128)S(1)} all-reduce(f32[4]{0:T(128)S(1)} %psum.30), channel_id=1, replica_groups=mesh['gx_0'=4,'gx_1'=2,'gy_0'=4,'gy_1'=4] {'gy_1'}, use_global_device_ids=true, to_apply=%region_10.11 | all-reduce | flops 4 | bytes 32 | tf_op jit(solution)/shard_map/psum | solution.py:43
  176.3 3.5 %multiply_subtract_fusion = (f32[32,64,128]{2,1,0:T(8,128)}, f32[32,64,128]{2,1,0:T(8,128)}) fusion(f32[32,64,128]{2,1,0:T(8,128)} %copy-done.2, f32[32,64,128]{2,1,0:T(8,128)} %get-tuple-element.6, f32[32,64,128]{2,1,0:T(8,128)S(1)} %get-tuple-element.10, f32[]{:T(128)S(6)} %div.18, f32[]{:T(128)S(6)} %div.19, f32[]{:T(128)S(6)} %div.17, ...), kind=kLoop, calls=%fused_computation.63 | loop fusion | flops 4718592 | bytes 7340044 | tf_op jit(solution)/shard_map/sub | solution.py:207
  (68 shorter events, 24.6 us)
Async XLA Ops:
  8.7 11.7 %copy-start = (f32[32,64,128]{2,1,0:T(8,128)S(1)}, f32[32,64,128]{2,1,0:T(8,128)}, u32[]{:S(2)}) copy-start(f32[32,64,128]{2,1,0:T(8,128)} %param.9) | copy-start | bytes 3145732
  8.7 54.7 %all-to-all-start = ((bf16[128,6,1664]{2,1,0:T(8,128)(2,1)}), bf16[128,6,1664]{2,1,0:T(8,128)(2,1)}, u32[]{:S(2)}, u32[]{:S(2)}) async-start(bf16[128,6,1664]{2,1,0:T(8,128)(2,1)} %convert_element_type.36), calls=%async_computation | async-start | bytes 6815744 | tf_op jit(solution)/shard_map/all_to_all | solution.py:156
  20.4 10.2 %collective-permute-start.5 = (f32[1,64,128]{2,1,0:T(8,128)S(1)}, f32[1,64,128]{2,1,0:T(8,128)S(1)}, u32[]{:S(2)}, u32[]{:S(2)}) collective-permute-start(f32[1,64,128]{2,1,0:T(8,128)S(1)} %get-tuple-element.37), channel_id=1, source_target_pairs={{0,16},{16,32},{32,48},{48,64},{64,80},{80,96},{96,112},{1,17},{17... | collective-permute-start | bytes 98312 | tf_op jit(solution)/shard_map/ppermute | solution.py:18
  21.7 10.5 %collective-permute-start.4 = (f32[1,64,128]{2,1,0:T(8,128)S(1)}, f32[1,64,128]{2,1,0:T(8,128)S(1)}, u32[]{:S(2)}, u32[]{:S(2)}) collective-permute-start(f32[1,64,128]{2,1,0:T(8,128)S(1)} %get-tuple-element.36), channel_id=1, source_target_pairs={{16,0},{32,16},{48,32},{64,48},{80,64},{96,80},{112,96},{17,1},{33... | collective-permute-start | bytes 98312 | tf_op jit(solution)/shard_map/ppermute | solution.py:18
  23.0 70.7 %collective-permute-start.6 = (f32[32,128]{1,0:T(8,128)S(1)}, f32[32,128]{1,0:T(8,128)S(1)}, u32[]{:S(2)}, u32[]{:S(2)}) collective-permute-start(f32[32,128]{1,0:T(8,128)S(1)} %bitcast.81), channel_id=1, source_target_pairs={{1,0},{2,1},{3,2},{4,3},{5,4},{6,5},{7,6},{8,7},{9,8},{10,9},{11,1... | collective-permute-start | bytes 49160 | tf_op jit(solution)/shard_map/ppermute | solution.py:17
  24.3 72.8 %collective-permute-start.7 = (f32[32,128]{1,0:T(8,128)S(1)}, f32[32,128]{1,0:T(8,128)S(1)}, u32[]{:S(2)}, u32[]{:S(2)}) collective-permute-start(f32[32,128]{1,0:T(8,128)S(1)} %bitcast.80), channel_id=1, source_target_pairs={{0,1},{1,2},{2,3},{3,4},{4,5},{5,6},{6,7},{7,8},{8,9},{9,10},{10,1... | collective-permute-start | bytes 49160 | tf_op jit(solution)/shard_map/ppermute | solution.py:17
  85.6 12.0 %copy-start.1 = (f32[32,64,128]{2,1,0:T(8,128)S(1)}, f32[32,64,128]{2,1,0:T(8,128)}, u32[]{:S(2)}) copy-start(f32[32,64,128]{2,1,0:T(8,128)} %param.8) | copy-start | bytes 3145732
  85.6 12.0 %copy-start.3 = (f32[32,64,127]{2,1,0:T(8,128)S(1)}, f32[32,64,127]{2,1,0:T(8,128)}, u32[]{:S(2)}) copy-start(f32[32,64,127]{2,1,0:T(8,128)} %get-tuple-element.38) | copy-start | bytes 3121156
  85.6 12.0 %copy-start.4 = (f32[32,64,127]{2,1,0:T(8,128)S(1)}, f32[32,64,127]{2,1,0:T(8,128)}, u32[]{:S(2)}) copy-start(f32[32,64,127]{2,1,0:T(8,128)} %get-tuple-element.39) | copy-start | bytes 3121156
  86.6 10.6 %collective-permute-start.2 = (f32[32,128]{1,0:T(8,128)S(1)}, f32[32,128]{1,0:T(8,128)S(1)}, u32[]{:S(2)}, u32[]{:S(2)}) collective-permute-start(f32[32,128]{1,0:T(8,128)S(1)} %bitcast.83), channel_id=1, source_target_pairs={{1,0},{2,1},{3,2},{4,3},{5,4},{6,5},{7,6},{8,7},{9,8},{10,9},{11,1... | collective-permute-start | bytes 49160 | tf_op jit(solution)/shard_map/ppermute | solution.py:17
  87.9 9.3 %collective-permute-start.3 = (f32[32,128]{1,0:T(8,128)S(1)}, f32[32,128]{1,0:T(8,128)S(1)}, u32[]{:S(2)}, u32[]{:S(2)}) collective-permute-start(f32[32,128]{1,0:T(8,128)S(1)} %bitcast.82), channel_id=1, source_target_pairs={{0,1},{1,2},{2,3},{3,4},{4,5},{5,6},{6,7},{7,8},{8,9},{9,10},{10,1... | collective-permute-start | bytes 49160 | tf_op jit(solution)/shard_map/ppermute | solution.py:17
  92.4 4.8 %collective-permute-start = (f32[1,64,128]{2,1,0:T(8,128)S(1)}, f32[1,64,128]{2,1,0:T(8,128)S(1)}, u32[]{:S(2)}, u32[]{:S(2)}) collective-permute-start(f32[1,64,128]{2,1,0:T(8,128)S(1)} %get-tuple-element.11), channel_id=1, source_target_pairs={{16,0},{32,16},{48,32},{64,48},{80,64},{96,80},{112,96},{17,1},{33... | collective-permute-start | bytes 98312 | tf_op jit(solution)/shard_map/ppermute | solution.py:18
  93.8 3.9 %collective-permute-start.1 = (f32[1,64,128]{2,1,0:T(8,128)S(1)}, f32[1,64,128]{2,1,0:T(8,128)S(1)}, u32[]{:S(2)}, u32[]{:S(2)}) collective-permute-start(f32[1,64,128]{2,1,0:T(8,128)S(1)} %get-tuple-element.12), channel_id=1, source_target_pairs={{0,16},{16,32},{32,48},{48,64},{64,80},{80,96},{96,112},{1,17},{17... | collective-permute-start | bytes 98312 | tf_op jit(solution)/shard_map/ppermute | solution.py:18
  101.3 11.7 %collective-permute-start.8 = (f32[1,64,128]{2,1,0:T(8,128)S(1)}, f32[1,64,128]{2,1,0:T(8,128)S(1)}, u32[]{:S(2)}, u32[]{:S(2)}) collective-permute-start(f32[1,64,128]{2,1,0:T(8,128)S(1)} %get-tuple-element.27), channel_id=1, source_target_pairs={{16,0},{32,16},{48,32},{64,48},{80,64},{96,80},{112,96},{17,1},{33... | collective-permute-start | bytes 98312 | tf_op jit(solution)/shard_map/ppermute | solution.py:18
  102.6 10.4 %collective-permute-start.9 = (f32[1,64,128]{2,1,0:T(8,128)S(1)}, f32[1,64,128]{2,1,0:T(8,128)S(1)}, u32[]{:S(2)}, u32[]{:S(2)}) collective-permute-start(f32[1,64,128]{2,1,0:T(8,128)S(1)} %get-tuple-element.26), channel_id=1, source_target_pairs={{0,16},{16,32},{32,48},{48,64},{64,80},{80,96},{96,112},{1,17},{17... | collective-permute-start | bytes 98312 | tf_op jit(solution)/shard_map/ppermute | solution.py:18
  105.7 6.2 %collective-permute-start.10 = (f32[32,128]{1,0:T(8,128)S(1)}, f32[32,128]{1,0:T(8,128)S(1)}, u32[]{:S(2)}, u32[]{:S(2)}) collective-permute-start(f32[32,128]{1,0:T(8,128)S(1)} %bitcast.86), channel_id=1, source_target_pairs={{1,0},{2,1},{3,2},{4,3},{5,4},{6,5},{7,6},{8,7},{9,8},{10,9},{11,1... | collective-permute-start | bytes 49160 | tf_op jit(solution)/shard_map/ppermute | solution.py:17
  107.0 6.0 %collective-permute-start.11 = (f32[32,128]{1,0:T(8,128)S(1)}, f32[32,128]{1,0:T(8,128)S(1)}, u32[]{:S(2)}, u32[]{:S(2)}) collective-permute-start(f32[32,128]{1,0:T(8,128)S(1)} %bitcast.84), channel_id=1, source_target_pairs={{0,1},{1,2},{2,3},{3,4},{4,5},{5,6},{6,7},{7,8},{8,9},{9,10},{10,1... | collective-permute-start | bytes 49160 | tf_op jit(solution)/shard_map/ppermute | solution.py:17
  113.7 15.7 %copy-start.2 = (f32[32,64,128]{2,1,0:T(8,128)}, f32[32,64,128]{2,1,0:T(8,128)S(1)}, u32[]{:S(2)}) copy-start(f32[32,64,128]{2,1,0:T(8,128)S(1)} %get-tuple-element.8) | copy-start | bytes 3145732
  113.7 12.3 %collective-permute-start.12 = (f32[1,64,128]{2,1,0:T(8,128)S(1)}, f32[1,64,128]{2,1,0:T(8,128)S(1)}, u32[]{:S(2)}, u32[]{:S(2)}) collective-permute-start(f32[1,64,128]{2,1,0:T(8,128)S(1)} %get-tuple-element.21), channel_id=1, source_target_pairs={{16,0},{32,16},{48,32},{64,48},{80,64},{96,80},{112,96},{17,1},{33... | collective-permute-start | bytes 98312 | tf_op jit(solution)/shard_map/ppermute | solution.py:18
  115.0 11.0 %collective-permute-start.13 = (f32[1,64,128]{2,1,0:T(8,128)S(1)}, f32[1,64,128]{2,1,0:T(8,128)S(1)}, u32[]{:S(2)}, u32[]{:S(2)}) collective-permute-start(f32[1,64,128]{2,1,0:T(8,128)S(1)} %get-tuple-element.20), channel_id=1, source_target_pairs={{0,16},{16,32},{32,48},{48,64},{64,80},{80,96},{96,112},{1,17},{17... | collective-permute-start | bytes 98312 | tf_op jit(solution)/shard_map/ppermute | solution.py:18
  118.8 6.2 %collective-permute-start.14 = (f32[32,128]{1,0:T(8,128)S(1)}, f32[32,128]{1,0:T(8,128)S(1)}, u32[]{:S(2)}, u32[]{:S(2)}) collective-permute-start(f32[32,128]{1,0:T(8,128)S(1)} %bitcast.87), channel_id=1, source_target_pairs={{1,0},{2,1},{3,2},{4,3},{5,4},{6,5},{7,6},{8,7},{9,8},{10,9},{11,1... | collective-permute-start | bytes 49160 | tf_op jit(solution)/shard_map/ppermute | solution.py:17
  120.1 6.0 %collective-permute-start.15 = (f32[32,128]{1,0:T(8,128)S(1)}, f32[32,128]{1,0:T(8,128)S(1)}, u32[]{:S(2)}, u32[]{:S(2)}) collective-permute-start(f32[32,128]{1,0:T(8,128)S(1)} %bitcast.85), channel_id=1, source_target_pairs={{0,1},{1,2},{2,3},{3,4},{4,5},{5,6},{6,7},{7,8},{8,9},{9,10},{10,1... | collective-permute-start | bytes 49160 | tf_op jit(solution)/shard_map/ppermute | solution.py:17

commit v22 on v21

--- a/solution.py
+++ b/solution.py
@@ -71,7 +71,7 @@
     rows = jnp.concatenate([bricks, tag], axis=1)
     chosen = place[None, :] == jnp.arange(peers * capacity, dtype=jnp.int32)[:, None]
     payload = jnp.einsum(
-        "pk,kj->pj", chosen.astype(jnp.bfloat16), rows, preferred_element_type=jnp.float32
+        "pk,kj->pj", chosen.astype(jnp.bfloat16), rows, preferred_element_type=jnp.bfloat16
     ).reshape(peers, capacity, rows.shape[1])
     return payload.astype(jnp.bfloat16)
 

time: 181 us -> 181 us (level)
    convert_element_type x1 -> x0, local copies, waits for them, and re-layouts: 2.59 us -> none  [build_send(): return payload.astype(jnp.bfloat16)]
    reshape x0 -> x1, local copies, waits for them, and re-layouts: none -> 2.59 us  [build_send(): payload = jnp.einsum('pk,kj->pj', chosen.astype(jnp.bfloat16), rows, pref...]
where the time goes in v22:
time: 181 us; the launch traced here: 180 us
  starting transfers between devices  50.8 us (28%)
  blocking collectives  38.3 us (21%)
  waiting for transfers between devices  33.1 us (18%)
  local copies, waits for them, and re-layouts  16.4 us (9%)
  other arithmetic  16.2 us (9%)
  Pallas kernels  13.2 us (7%)
  between operations  5.99 us (3%)
  matrix products  5.52 us (3%)
    psum x4, blocking collectives, over_axes(): shard = lax.psum(shard, axis)  38.3 us
    all_to_all x1, waiting for transfers between devices, body(): lax.all_to_all(payload, GX_GY, split_axis=0, concat_axis=0, tiled=True)  30.6 us
    ppermute x8, starting transfers between devices, shifted(): return lax.ppermute(flat, axis, pairs).reshape(piece.shape)  23.6 us
    ppermute x8, starting transfers between devices, shifted(): return lax.ppermute(piece, axis, pairs)  15.6 us
    pallas_call x1, Pallas kernels, to_grid(): pl.pallas_call(relayout_kernel, out_shape=jax.ShapeDtypeStruct((3, span_x...  13.2 us
    all_to_all x1, starting transfers between devices, body(): lax.all_to_all(payload, GX_GY, split_axis=0, concat_axis=0, tiled=True)  11.6 us
  transfers between devices with their start and end apart: 17, of which 4 were waited for; matrix products, arithmetic and copies ran while one was open for 8% of the time, Pallas kernels for 7%

profile of v22, /device:TPU:0, one launch (start us, length us, event | category | flops | bytes accessed | tf_op | source)
XLA Modules:
  0.0 179.6 jit_solution(17091931914513615451)
XLA Ops:
  4.1 2.0 %fusion.29 = bf16[768,1664]{1,0:T(8,128)(2,1)S(1)} fusion(bf16[256,128]{1,0:T(8,128)(2,1)S(1)} %select_select_fusion, bf16[256,1536]{1,0:T(8,128)(2,1)} %param.5, s32[256]{0:T(256)S(1)} %multiply_add_fusion.1), kind=kOutput, calls=%fused_computation.70 | convolution fusion | flops 656211968 | bytes 3408896 | tf_op jit(solution)/shard_map/pk,kj->pj/dot_general | solution.py:73
  6.1 2.6 %reshape.94 = bf16[128,6,1664]{2,1,0:T(8,128)(2,1)} reshape(bf16[768,1664]{1,0:T(8,128)(2,1)S(1)} %fusion.29) | data formatting | bytes 5111808 | tf_op jit(solution)/shard_map/reshape | solution.py:75
  8.7 11.6 %all-to-all-start = ((bf16[128,6,1664]{2,1,0:T(8,128)(2,1)}), bf16[128,6,1664]{2,1,0:T(8,128)(2,1)}, u32[]{:S(2)}, u32[]{:S(2)}) async-start(bf16[128,6,1664]{2,1,0:T(8,128)(2,1)} %reshape.94), calls=%async_computation | async-start | bytes 6815744 | tf_op jit(solution)/shard_map/all_to_all | solution.py:156
  24.3 4.5 %collective-permute-start.7 = (f32[32,128]{1,0:T(8,128)S(1)}, f32[32,128]{1,0:T(8,128)S(1)}, u32[]{:S(2)}, u32[]{:S(2)}) collective-permute-start(f32[32,128]{1,0:T(8,128)S(1)} %bitcast.80), channel_id=1, source_target_pairs={{0,1},{1,2},{2,3},{3,4},{4,5},{5,6},{6,7},{7,8},{8,9},{9,10},{10,1... | collective-permute-start | bytes 49160 | tf_op jit(solution)/shard_map/ppermute | solution.py:17
  28.9 1.7 fusion.57
  32.9 30.6 %all-to-all-done = bf16[128,6,1664]{2,1,0:T(8,128)(2,1)} async-done(((bf16[128,6,1664]{2,1,0:T(8,128)(2,1)}), bf16[128,6,1664]{2,1,0:T(8,128)(2,1)}, u32[]{:S(2)}, u32[]{:S(2)}) %all-to-all-start) | async-done | bytes 2555936 | tf_op jit(solution)/shard_map/all_to_all | solution.py:156
  64.7 2.1 %slice.242 = bf16[128,6,1536]{2,1,0:T(8,128)(2,1)S(1)} slice(bf16[128,6,1664]{2,1,0:T(8,128)(2,1)} %all-to-all-done), slice={[0:128], [0:6], [0:1536]} | slice | bytes 4718592 | tf_op jit(solution)/shard_map/slice | solution.py:167
  66.8 3.5 %convolution_bitcast_fusion.blk_ref = f32[512,1536]{1,0:T(8,128)} fusion(bf16[128,6,1536]{2,1,0:T(8,128)(2,1)S(1)} %slice.242, s32[128,6]{0,1:T(8,128)S(1)} %fusion.40), kind=kOutput, calls=%fused_computation | convolution fusion | flops 1208352768 | bytes 5508096 | tf_op jit(solution)/shard_map/pcs,pcj->sj/dot_general | solution.py:164
  70.3 13.2 %shard_map.68 = f32[3,32,64,128]{3,2,1,0:T(8,128)} custom-call(f32[512,1536]{1,0:T(8,128)} %convolution_bitcast_fusion.blk_ref), custom_call_target="tpu_custom_call" | custom-call | flops 15728640 | bytes 6291456 | tf_op jit(solution)/shard_map/pallas_call | solution.py:142
  83.5 2.1 %slice_bitcast_fusion.2 = (f32[32,64,128]{2,1,0:T(8,128)S(1)}, f32[32,64,128]{2,1,0:T(8,128)S(1)}, f32[32,64,128]{2,1,0:T(8,128)S(1)}) fusion(f32[3,32,64,128]{3,2,1,0:T(8,128)} %shard_map.68), kind=kLoop, calls=%fused_computation.61 | loop fusion | bytes 6291456 | tf_op jit(solution)/shard_map/squeeze | solution.py:171
  87.7 4.5 %collective-permute-start.3 = (f32[32,128]{1,0:T(8,128)S(1)}, f32[32,128]{1,0:T(8,128)S(1)}, u32[]{:S(2)}, u32[]{:S(2)}) collective-permute-start(f32[32,128]{1,0:T(8,128)S(1)} %bitcast.82), channel_id=1, source_target_pairs={{0,1},{1,2},{2,3},{3,4},{4,5},{5,6},{6,7},{7,8},{8,9},{9,10},{10,1... | collective-permute-start | bytes 49160 | tf_op jit(solution)/shard_map/ppermute | solution.py:17
  93.6 3.0 %collective-permute-start.1 = (f32[1,64,128]{2,1,0:T(8,128)S(1)}, f32[1,64,128]{2,1,0:T(8,128)S(1)}, u32[]{:S(2)}, u32[]{:S(2)}) collective-permute-start(f32[1,64,128]{2,1,0:T(8,128)S(1)} %get-tuple-element.12), channel_id=1, source_target_pairs={{0,16},{16,32},{32,48},{48,64},{64,80},{80,96},{96,112},{1,17},{17... | collective-permute-start | bytes 98312 | tf_op jit(solution)/shard_map/ppermute | solution.py:18
  98.5 3.6 %fusion.43 = (f32[32,64,128]{2,1,0:T(8,128)S(1)}, f32[32,64,128]{2,1,0:T(8,128)S(1)}) fusion(f32[32,64,128]{2,1,0:T(8,128)S(1)} %copy-done.1, f32[32,64,127]{2,1,0:T(8,128)S(1)} %copy-done.4, f32[32,64,127]{2,1,0:T(8,128)S(1)} %copy-done.3, f32[34,64,128]{2,1,0:T(8,128)} %constant_dynamic-update-slice_fusion, f32[32,1,128]{2,1,0:T(1,128)S(1)} %bitcast.72, ...), kind=kLoop, calls=%fused_computation.104 | loop fusion | flops 8126464 | bytes 11763712 | tf_op jit(solution)/shard_map/mul | solution.py:180
  103.4 3.0 %collective-permute-start.9 = (f32[1,64,128]{2,1,0:T(8,128)S(1)}, f32[1,64,128]{2,1,0:T(8,128)S(1)}, u32[]{:S(2)}, u32[]{:S(2)}) collective-permute-start(f32[1,64,128]{2,1,0:T(8,128)S(1)} %get-tuple-element.26), channel_id=1, source_target_pairs={{0,16},{16,32},{32,48},{48,64},{64,80},{80,96},{96,112},{1,17},{17... | collective-permute-start | bytes 98312 | tf_op jit(solution)/shard_map/ppermute | solution.py:18
  107.7 4.5 %collective-permute-start.11 = (f32[32,128]{1,0:T(8,128)S(1)}, f32[32,128]{1,0:T(8,128)S(1)}, u32[]{:S(2)}, u32[]{:S(2)}) collective-permute-start(f32[32,128]{1,0:T(8,128)S(1)} %bitcast.84), channel_id=1, source_target_pairs={{0,1},{1,2},{2,3},{3,4},{4,5},{5,6},{6,7},{7,8},{8,9},{9,10},{10,1... | collective-permute-start | bytes 49160 | tf_op jit(solution)/shard_map/ppermute | solution.py:17
  115.8 3.1 %collective-permute-start.13 = (f32[1,64,128]{2,1,0:T(8,128)S(1)}, f32[1,64,128]{2,1,0:T(8,128)S(1)}, u32[]{:S(2)}, u32[]{:S(2)}) collective-permute-start(f32[1,64,128]{2,1,0:T(8,128)S(1)} %get-tuple-element.20), channel_id=1, source_target_pairs={{0,16},{16,32},{32,48},{48,64},{64,80},{80,96},{96,112},{1,17},{17... | collective-permute-start | bytes 98312 | tf_op jit(solution)/shard_map/ppermute | solution.py:18
  120.1 4.8 %collective-permute-start.15 = (f32[32,128]{1,0:T(8,128)S(1)}, f32[32,128]{1,0:T(8,128)S(1)}, u32[]{:S(2)}, u32[]{:S(2)}) collective-permute-start(f32[32,128]{1,0:T(8,128)S(1)} %bitcast.85), channel_id=1, source_target_pairs={{0,1},{1,2},{2,3},{3,4},{4,5},{5,6},{6,7},{7,8},{8,9},{9,10},{10,1... | collective-permute-start | bytes 49160 | tf_op jit(solution)/shard_map/ppermute | solution.py:17
  126.4 3.3 %multiply_reduce_fusion.3 = (f32[]{:T(128)}, f32[]{:T(128)}, f32[]{:T(128)}, f32[]{:T(128)}, f32[32,64,128]{2,1,0:T(8,128)}) fusion(f32[32,64,128]{2,1,0:T(8,128)S(1)} %get-tuple-element.10, f32[32,64,128]{2,1,0:T(8,128)S(1)} %copy-done.1, f32[32,64,128]{2,1,0:T(8,128)S(1)} %get-tuple-element.8, f32[32,64,128]{2,1,0:T(8,128)S(1)} %get-tuple-element.7, ...), kind=kLoop, calls=%fused_computation.68 | loop fusion | flops 8388604 | bytes 7421968 | tf_op jit(solution)/shard_map/reduce_sum | solution.py:187
  129.7 2.5 %pad_maximum_fusion.20 = f32[4]{0:T(128)S(1)} fusion(f32[1]{0:T(128)} %bitcast.32, f32[1]{0:T(128)} %bitcast.27, f32[1]{0:T(128)} %bitcast.26, f32[1]{0:T(128)} %bitcast.21), kind=kLoop, calls=%fused_computation.99 | loop fusion | flops 12 | bytes 32 | tf_op jit(solution)/shard_map/stack | solution.py:185
  132.2 10.1 %psum.28 = f32[4]{0:T(128)S(1)} all-reduce(f32[4]{0:T(128)S(1)} %pad_maximum_fusion.20), channel_id=1, replica_groups=mesh['gx_0'=4,'gx_1'=2,'gy_0'=4,'gy_1'=4] {'gx_0'}, use_global_device_ids=true, to_apply=%region_7.8 | all-reduce | flops 4 | bytes 32 | tf_op jit(solution)/shard_map/psum | solution.py:43
  142.4 2.5 %psum.29 = f32[4]{0:T(128)S(1)} all-reduce(f32[4]{0:T(128)S(1)} %psum.28), channel_id=1, replica_groups=mesh['gx_0'=4,'gx_1'=2,'gy_0'=4,'gy_1'=4] {'gx_1'}, use_global_device_ids=true, to_apply=%region_8.9 | all-reduce | flops 4 | bytes 32 | tf_op jit(solution)/shard_map/psum | solution.py:43
  144.8 17.9 %psum.30 = f32[4]{0:T(128)S(1)} all-reduce(f32[4]{0:T(128)S(1)} %psum.29), channel_id=1, replica_groups=mesh['gx_0'=4,'gx_1'=2,'gy_0'=4,'gy_1'=4] {'gy_0'}, use_global_device_ids=true, to_apply=%region_9.10 | all-reduce | flops 4 | bytes 32 | tf_op jit(solution)/shard_map/psum | solution.py:43
  162.8 7.7 %psum.31 = f32[4]{0:T(128)S(1)} all-reduce(f32[4]{0:T(128)S(1)} %psum.30), channel_id=1, replica_groups=mesh['gx_0'=4,'gx_1'=2,'gy_0'=4,'gy_1'=4] {'gy_1'}, use_global_device_ids=true, to_apply=%region_10.11 | all-reduce | flops 4 | bytes 32 | tf_op jit(solution)/shard_map/psum | solution.py:43
  176.1 3.5 %multiply_subtract_fusion = (f32[32,64,128]{2,1,0:T(8,128)}, f32[32,64,128]{2,1,0:T(8,128)}) fusion(f32[32,64,128]{2,1,0:T(8,128)} %copy-done.2, f32[32,64,128]{2,1,0:T(8,128)} %get-tuple-element.6, f32[32,64,128]{2,1,0:T(8,128)S(1)} %get-tuple-element.10, f32[]{:T(128)S(6)} %div.18, f32[]{:T(128)S(6)} %div.19, f32[]{:T(128)S(6)} %div.17, ...), kind=kLoop, calls=%fused_computation.62 | loop fusion | flops 4718592 | bytes 7340044 | tf_op jit(solution)/shard_map/sub | solution.py:207
  (68 shorter events, 25.4 us)
Async XLA Ops:
  8.7 11.7 %copy-start = (f32[32,64,128]{2,1,0:T(8,128)S(1)}, f32[32,64,128]{2,1,0:T(8,128)}, u32[]{:S(2)}) copy-start(f32[32,64,128]{2,1,0:T(8,128)} %param.9) | copy-start | bytes 3145732
  8.7 54.7 %all-to-all-start = ((bf16[128,6,1664]{2,1,0:T(8,128)(2,1)}), bf16[128,6,1664]{2,1,0:T(8,128)(2,1)}, u32[]{:S(2)}, u32[]{:S(2)}) async-start(bf16[128,6,1664]{2,1,0:T(8,128)(2,1)} %reshape.94), calls=%async_computation | async-start | bytes 6815744 | tf_op jit(solution)/shard_map/all_to_all | solution.py:156
  20.4 10.2 %collective-permute-start.5 = (f32[1,64,128]{2,1,0:T(8,128)S(1)}, f32[1,64,128]{2,1,0:T(8,128)S(1)}, u32[]{:S(2)}, u32[]{:S(2)}) collective-permute-start(f32[1,64,128]{2,1,0:T(8,128)S(1)} %get-tuple-element.37), channel_id=1, source_target_pairs={{0,16},{16,32},{32,48},{48,64},{64,80},{80,96},{96,112},{1,17},{17... | collective-permute-start | bytes 98312 | tf_op jit(solution)/shard_map/ppermute | solution.py:18
  21.7 10.5 %collective-permute-start.4 = (f32[1,64,128]{2,1,0:T(8,128)S(1)}, f32[1,64,128]{2,1,0:T(8,128)S(1)}, u32[]{:S(2)}, u32[]{:S(2)}) collective-permute-start(f32[1,64,128]{2,1,0:T(8,128)S(1)} %get-tuple-element.36), channel_id=1, source_target_pairs={{16,0},{32,16},{48,32},{64,48},{80,64},{96,80},{112,96},{17,1},{33... | collective-permute-start | bytes 98312 | tf_op jit(solution)/shard_map/ppermute | solution.py:18
  23.0 70.5 %collective-permute-start.6 = (f32[32,128]{1,0:T(8,128)S(1)}, f32[32,128]{1,0:T(8,128)S(1)}, u32[]{:S(2)}, u32[]{:S(2)}) collective-permute-start(f32[32,128]{1,0:T(8,128)S(1)} %bitcast.81), channel_id=1, source_target_pairs={{1,0},{2,1},{3,2},{4,3},{5,4},{6,5},{7,6},{8,7},{9,8},{10,9},{11,1... | collective-permute-start | bytes 49160 | tf_op jit(solution)/shard_map/ppermute | solution.py:17
  24.3 72.7 %collective-permute-start.7 = (f32[32,128]{1,0:T(8,128)S(1)}, f32[32,128]{1,0:T(8,128)S(1)}, u32[]{:S(2)}, u32[]{:S(2)}) collective-permute-start(f32[32,128]{1,0:T(8,128)S(1)} %bitcast.80), channel_id=1, source_target_pairs={{0,1},{1,2},{2,3},{3,4},{4,5},{5,6},{6,7},{7,8},{8,9},{9,10},{10,1... | collective-permute-start | bytes 49160 | tf_op jit(solution)/shard_map/ppermute | solution.py:17
  86.4 10.6 %collective-permute-start.2 = (f32[32,128]{1,0:T(8,128)S(1)}, f32[32,128]{1,0:T(8,128)S(1)}, u32[]{:S(2)}, u32[]{:S(2)}) collective-permute-start(f32[32,128]{1,0:T(8,128)S(1)} %bitcast.83), channel_id=1, source_target_pairs={{1,0},{2,1},{3,2},{4,3},{5,4},{6,5},{7,6},{8,7},{9,8},{10,9},{11,1... | collective-permute-start | bytes 49160 | tf_op jit(solution)/shard_map/ppermute | solution.py:17
  87.7 9.3 %collective-permute-start.3 = (f32[32,128]{1,0:T(8,128)S(1)}, f32[32,128]{1,0:T(8,128)S(1)}, u32[]{:S(2)}, u32[]{:S(2)}) collective-permute-start(f32[32,128]{1,0:T(8,128)S(1)} %bitcast.82), channel_id=1, source_target_pairs={{0,1},{1,2},{2,3},{3,4},{4,5},{5,6},{6,7},{7,8},{8,9},{9,10},{10,1... | collective-permute-start | bytes 49160 | tf_op jit(solution)/shard_map/ppermute | solution.py:17
  92.3 4.8 %collective-permute-start = (f32[1,64,128]{2,1,0:T(8,128)S(1)}, f32[1,64,128]{2,1,0:T(8,128)S(1)}, u32[]{:S(2)}, u32[]{:S(2)}) collective-permute-start(f32[1,64,128]{2,1,0:T(8,128)S(1)} %get-tuple-element.11), channel_id=1, source_target_pairs={{16,0},{32,16},{48,32},{64,48},{80,64},{96,80},{112,96},{17,1},{33... | collective-permute-start | bytes 98312 | tf_op jit(solution)/shard_map/ppermute | solution.py:18
  93.6 3.9 %collective-permute-start.1 = (f32[1,64,128]{2,1,0:T(8,128)S(1)}, f32[1,64,128]{2,1,0:T(8,128)S(1)}, u32[]{:S(2)}, u32[]{:S(2)}) collective-permute-start(f32[1,64,128]{2,1,0:T(8,128)S(1)} %get-tuple-element.12), channel_id=1, source_target_pairs={{0,16},{16,32},{32,48},{48,64},{64,80},{80,96},{96,112},{1,17},{17... | collective-permute-start | bytes 98312 | tf_op jit(solution)/shard_map/ppermute | solution.py:18
  96.6 1.2 copy-start.1
  96.6 1.5 copy-start.3
  96.6 1.8 %copy-start.4 = (f32[32,64,127]{2,1,0:T(8,128)S(1)}, f32[32,64,127]{2,1,0:T(8,128)}, u32[]{:S(2)}) copy-start(f32[32,64,127]{2,1,0:T(8,128)} %get-tuple-element.39) | copy-start | bytes 3121156
  102.1 11.6 %collective-permute-start.8 = (f32[1,64,128]{2,1,0:T(8,128)S(1)}, f32[1,64,128]{2,1,0:T(8,128)S(1)}, u32[]{:S(2)}, u32[]{:S(2)}) collective-permute-start(f32[1,64,128]{2,1,0:T(8,128)S(1)} %get-tuple-element.27), channel_id=1, source_target_pairs={{16,0},{32,16},{48,32},{64,48},{80,64},{96,80},{112,96},{17,1},{33... | collective-permute-start | bytes 98312 | tf_op jit(solution)/shard_map/ppermute | solution.py:18
  103.4 10.3 %collective-permute-start.9 = (f32[1,64,128]{2,1,0:T(8,128)S(1)}, f32[1,64,128]{2,1,0:T(8,128)S(1)}, u32[]{:S(2)}, u32[]{:S(2)}) collective-permute-start(f32[1,64,128]{2,1,0:T(8,128)S(1)} %get-tuple-element.26), channel_id=1, source_target_pairs={{0,16},{16,32},{32,48},{48,64},{64,80},{80,96},{96,112},{1,17},{17... | collective-permute-start | bytes 98312 | tf_op jit(solution)/shard_map/ppermute | solution.py:18
  106.4 6.2 %collective-permute-start.10 = (f32[32,128]{1,0:T(8,128)S(1)}, f32[32,128]{1,0:T(8,128)S(1)}, u32[]{:S(2)}, u32[]{:S(2)}) collective-permute-start(f32[32,128]{1,0:T(8,128)S(1)} %bitcast.86), channel_id=1, source_target_pairs={{1,0},{2,1},{3,2},{4,3},{5,4},{6,5},{7,6},{8,7},{9,8},{10,9},{11,1... | collective-permute-start | bytes 49160 | tf_op jit(solution)/shard_map/ppermute | solution.py:17
  107.7 6.0 %collective-permute-start.11 = (f32[32,128]{1,0:T(8,128)S(1)}, f32[32,128]{1,0:T(8,128)S(1)}, u32[]{:S(2)}, u32[]{:S(2)}) collective-permute-start(f32[32,128]{1,0:T(8,128)S(1)} %bitcast.84), channel_id=1, source_target_pairs={{0,1},{1,2},{2,3},{3,4},{4,5},{5,6},{6,7},{7,8},{8,9},{9,10},{10,1... | collective-permute-start | bytes 49160 | tf_op jit(solution)/shard_map/ppermute | solution.py:17
  114.4 12.0 %copy-start.2 = (f32[32,64,128]{2,1,0:T(8,128)}, f32[32,64,128]{2,1,0:T(8,128)S(1)}, u32[]{:S(2)}) copy-start(f32[32,64,128]{2,1,0:T(8,128)S(1)} %get-tuple-element.8) | copy-start | bytes 3145732
  114.5 11.9 %collective-permute-start.12 = (f32[1,64,128]{2,1,0:T(8,128)S(1)}, f32[1,64,128]{2,1,0:T(8,128)S(1)}, u32[]{:S(2)}, u32[]{:S(2)}) collective-permute-start(f32[1,64,128]{2,1,0:T(8,128)S(1)} %get-tuple-element.21), channel_id=1, source_target_pairs={{16,0},{32,16},{48,32},{64,48},{80,64},{96,80},{112,96},{17,1},{33... | collective-permute-start | bytes 98312 | tf_op jit(solution)/shard_map/ppermute | solution.py:18
  115.8 10.6 %collective-permute-start.13 = (f32[1,64,128]{2,1,0:T(8,128)S(1)}, f32[1,64,128]{2,1,0:T(8,128)S(1)}, u32[]{:S(2)}, u32[]{:S(2)}) collective-permute-start(f32[1,64,128]{2,1,0:T(8,128)S(1)} %get-tuple-element.20), channel_id=1, source_target_pairs={{0,16},{16,32},{32,48},{48,64},{64,80},{80,96},{96,112},{1,17},{17... | collective-permute-start | bytes 98312 | tf_op jit(solution)/shard_map/ppermute | solution.py:18
  118.8 6.5 %collective-permute-start.14 = (f32[32,128]{1,0:T(8,128)S(1)}, f32[32,128]{1,0:T(8,128)S(1)}, u32[]{:S(2)}, u32[]{:S(2)}) collective-permute-start(f32[32,128]{1,0:T(8,128)S(1)} %bitcast.87), channel_id=1, source_target_pairs={{1,0},{2,1},{3,2},{4,3},{5,4},{6,5},{7,6},{8,7},{9,8},{10,9},{11,1... | collective-permute-start | bytes 49160 | tf_op jit(solution)/shard_map/ppermute | solution.py:17
  120.1 6.2 %collective-permute-start.15 = (f32[32,128]{1,0:T(8,128)S(1)}, f32[32,128]{1,0:T(8,128)S(1)}, u32[]{:S(2)}, u32[]{:S(2)}) collective-permute-start(f32[32,128]{1,0:T(8,128)S(1)} %bitcast.85), channel_id=1, source_target_pairs={{0,1},{1,2},{2,3},{3,4},{4,5},{5,6},{6,7},{7,8},{8,9},{9,10},{10,1... | collective-permute-start | bytes 49160 | tf_op jit(solution)/shard_map/ppermute | solution.py:17
